TPU v7x, 32 devices: a whole 2x2x4 slice. The times are simulated.
32 devices in a mesh: groups: 2 (over x), blk: 16 (over z, y, core).
Axes of the slice: x: 2, y: 2, z: 4, core: 2. Of those that a mesh axis runs over, the one named last changes fastest.
Arguments:
- embeddings: bfloat16 [30720, 1024], P(('groups', 'blk')), parts along dimension 0, may hold values from -6 to 6
- owners: int32 [30720], P(('groups', 'blk')), parts along dimension 0, may hold values from 0 to 15, as said below
- clusters: int32 [30720], P(('groups', 'blk')), parts along dimension 0, may hold values from 0 to 15
- pairs: int32 [32, 4, 8, 4], P(('groups', 'blk')), parts along dimension 0, may hold values from 0 to 8
Outputs:
- scores: float32 [30720], P(('groups', 'blk')), parts along dimension 0
There are 2 independent parts, one for each index of `groups`. A program takes and returns all parts, laid end to end along the dimension named above; each array names one. Nothing has to cross between parts.
Inputs may be any that keep to these rules, and one draw needn't show every extreme that they name: `owners`: each device sends at most 64 of its rows to one owner; in every draw one owner receives exactly 64 rows from every device.
All inputs are finite; a program needn't handle non-finite values.
Results may differ from a plain program's by a relative error of at most 0.0003.
Values may be sent and summed in bfloat16 or wider, within the bound.
No kernel may reach another device: no remote copies, remote signals or barrier semaphores. Data moves between devices by JAX's collectives and lax.ppermute only.
A program may use at most 64 MiB of HBM per device.

v0:
```python
import jax
import jax.numpy as jnp
from jax import lax
from jax.sharding import PartitionSpec as P

SLOTS = 1024
STEPS = 4


SHARPNESS_KNOB = 32.0


def shifted(shard, axis, by):
    peers = lax.axis_size(axis)
    return lax.ppermute(shard, axis, [(i, (i + by) % peers) for i in range(peers)])


def landing_sequence(owners, device_count):
    onehot = (owners[..., None] == jnp.arange(device_count, dtype=jnp.int32)).astype(jnp.int32)
    prior_rows = jnp.cumsum(onehot, axis=-2) - onehot
    return jnp.sum(prior_rows * onehot, axis=-1)


def add_step(total, local, local_ids, remote, remote_ids, step_pairs, first_step):
    block_count = local.shape[0]
    feature_span = local.shape[2]
    reciprocal_factor = SHARPNESS_KNOB / feature_span
    diagonal = jnp.eye(128, dtype=bool)
    block_index = jnp.arange(block_count, dtype=jnp.int32)
    for which in range(step_pairs.shape[1]):
        partner = step_pairs[:, which]
        live = partner < block_count
        pick = jnp.minimum(partner, block_count - 1)
        tiles = jnp.take(remote, pick, axis=0)
        block_labels = jnp.take(remote_ids, pick, axis=0)
        logits = (
            jnp.einsum("bid,bjd->bij", local, tiles, preferred_element_type=jnp.float32)
            * reciprocal_factor
        )
        keep = (
            live[:, None, None]
            & (local_ids[:, :, None] == block_labels[:, None, :])
            & (local_ids[:, :, None] >= 0)
        )
        if first_step:
            keep = keep & jnp.logical_not((pick == block_index)[:, None, None] & diagonal)
        total = total + jnp.sum(jnp.where(keep, jnp.exp(logits), 0.0), axis=2)
    return total


def body(embeddings, owners, clusters, pairs):
    device_count = lax.axis_size("blk")
    feature_span = embeddings.shape[1]
    slot_count = SLOTS
    capacity = slot_count // device_count
    block_count = slot_count // 128
    value_entries = embeddings.astype(jnp.float32)
    unit = (
        value_entries
        * lax.rsqrt(jnp.mean(value_entries * value_entries, axis=1, keepdims=True) + 1e-06)
    ).astype(jnp.bfloat16)
    arrival = landing_sequence(owners, device_count)
    place = owners * capacity + arrival
    outgoing = jnp.zeros((slot_count, feature_span), jnp.bfloat16).at[place].set(unit)
    departing_row_ids = jnp.full((slot_count,), -1, jnp.int32).at[place].set(clusters)
    held, held_ids = (
        lax.all_to_all(
            outgoing.reshape(device_count, capacity, feature_span),
            "blk",
            split_axis=0,
            concat_axis=0,
            tiled=True,
        ),
        lax.all_to_all(
            departing_row_ids.reshape(device_count, capacity),
            "blk",
            split_axis=0,
            concat_axis=0,
            tiled=True,
        ),
    )
    held = held.reshape(slot_count, feature_span)
    held_ids = held_ids.reshape(slot_count)
    local = held.reshape(block_count, 128, feature_span)
    local_ids = held_ids.reshape(block_count, 128)
    total = jnp.zeros((block_count, 128), jnp.float32)
    remote = held
    remote_ids = held_ids
    for cycle_step in range(STEPS):
        if cycle_step > 0:
            remote, remote_ids = shifted((remote, remote_ids), "blk", 1)
        total = add_step(
            total,
            local,
            local_ids,
            remote.reshape(block_count, 128, feature_span),
            remote_ids.reshape(block_count, 128),
            pairs[0, cycle_step],
            cycle_step == 0,
        )
    slot_scores = jnp.log1p(total).reshape(device_count, capacity)
    returned = lax.all_to_all(slot_scores, "blk", split_axis=0, concat_axis=0, tiled=True)
    return returned.reshape(-1)[place]


def solution(mesh):
    placed = (
        P(("groups", "blk"), None),
        P(("groups", "blk")),
        P(("groups", "blk")),
        P(("groups", "blk"), None, None, None),
    )
    return jax.shard_map(
        body, mesh=mesh, in_specs=placed, out_specs=P(("groups", "blk")), check_vma=False
    )
```

profile of v0, /device:TPU:0, one launch (start us, length us, event | category | flops | bytes accessed | tf_op | source)
XLA Modules:
  0.0 224.5 jit_solution(14846534365585868631)
XLA Ops:
  0.0 0.9 iota_compare_fusion.1
  0.9 4.5 %reduce-window.6 = s32[16,8,128]{2,1,0:T(8,128)S(1)} reduce-window(s32[16,8,128]{2,1,0:T(8,128)S(1)} %bitcast.166, s32[]{:T(128)} %constant.32.clone.1), window={size=1x1x128 pad=0_0x0_0x127_0}, to_apply=%region_0.0 | reduce-window | flops 2080768 | bytes 131076 | tf_op jit(solution)/shard_map/reduce-window
  5.9 0.7 fusion.263
  6.6 0.7 compare_select_fusion
  7.3 5.4 %scatter_custom_fusion = s32[1024]{0:T(1024)S(1)} fusion(s32[960]{0:T(1024)S(1)} %compare_select_fusion, s32[960]{0:T(1024)} %param.10, s32[]{:T(128)} %constant.29.clone.1), kind=kCustom, calls=%fused_computation.235 | custom fusion | bytes 4608 | tf_op jit(solution)/shard_map/scatter | solution.py:65
  12.7 0.7 all_to_all.13
  13.4 7.4 %all-to-all-start = ((s32[16,1,64]{2,1,0:T(1,128)}), s32[16,1,64]{2,1,0:T(1,128)S(1)}, u32[]{:S(2)}, u32[]{:S(2)}) async-start(s32[16,1,64]{2,1,0:T(1,128)} %all_to_all.13), calls=%async_computation | async-start | bytes 16384 | tf_op jit(solution)/shard_map/all_to_all | solution.py:74
  20.8 2.0 fusion
  22.8 8.2 %scatter_custom_fusion.1 = bf16[1024,1024]{1,0:T(8,128)(2,1)} fusion(s32[960]{0:T(1024)S(1)} %compare_select_fusion, bf16[960,1024]{1,0:T(8,128)(2,1)S(1)} %copy-done, f32[960]{0:T(1024)S(1)} %add_rsqrt_fusion, bf16[]{:T(256)} %constant.16.clone.1), kind=kCustom, calls=%fused_computation.87 | custom fusion | flops 2949120 | bytes 4067330 | tf_op jit(solution)/shard_map/scatter | solution.py:64
  31.0 6.0 %all-to-all-start.1 = ((bf16[16,64,1024]{2,1,0:T(8,128)(2,1)}), bf16[16,64,1024]{2,1,0:T(8,128)(2,1)S(1)}, u32[]{:S(2)}, u32[]{:S(2)}) async-start(bf16[16,64,1024]{2,1,0:T(8,128)(2,1)} %bitcast.152), calls=%async_computation.1 | async-start | bytes 4194304 | tf_op jit(solution)/shard_map/all_to_all | solution.py:67
  37.9 0.7 reduce.8
  39.2 0.6 gather_fusion.5
  39.7 0.6 gather_fusion.3
  41.6 34.9 %collective-permute-done = s32[1024]{0:T(1024)S(1)} collective-permute-done((s32[1024]{0:T(1024)S(1)}, s32[1024]{0:T(1024)S(1)}, u32[]{:S(2)}, u32[]{:S(2)}) %collective-permute-start) | collective-permute-done | bytes 4128 | tf_op jit(solution)/shard_map/ppermute | solution.py:15
  77.6 0.6 gather_fusion.11
  78.3 0.6 collective-permute-start.1
  79.6 2.8 %collective-permute-start.2 = (s32[1024]{0:T(1024)S(1)}, s32[1024]{0:T(1024)S(1)}, u32[]{:S(2)}, u32[]{:S(2)}) collective-permute-start(s32[1024]{0:T(1024)S(1)} %collective-permute-done), channel_id=1, source_target_pairs={{0,1},{1,2},{2,3},{3,4},{4,5},{5,6},{6,7},{7,8},{8,9},{9,10},{10,1... | collective-permute-start | bytes 12296 | tf_op jit(solution)/shard_map/ppermute | solution.py:15
  82.4 29.3 %collective-permute-done.2 = s32[1024]{0:T(1024)S(1)} collective-permute-done((s32[1024]{0:T(1024)S(1)}, s32[1024]{0:T(1024)S(1)}, u32[]{:S(2)}, u32[]{:S(2)}) %collective-permute-start.2) | collective-permute-done | bytes 4128 | tf_op jit(solution)/shard_map/ppermute | solution.py:15
  112.8 0.6 gather_fusion.19
  114.3 5.4 %collective-permute-done.4 = s32[1024]{0:T(1024)S(1)} collective-permute-done((s32[1024]{0:T(1024)S(1)}, s32[1024]{0:T(1024)S(1)}, u32[]{:S(2)}, u32[]{:S(2)}) %collective-permute-start.4) | collective-permute-done | bytes 4128 | tf_op jit(solution)/shard_map/ppermute | solution.py:15
  121.4 0.6 gather_fusion.25
  122.2 2.0 gather_fusion.8
  124.2 2.4 %fusion.206 = f32[8,128]{1,0:T(8,128)S(1)} fusion(bf16[8,128,1024]{2,1,0:T(8,128)(2,1)S(1)} %bitcast.133, bf16[8,128,1024]{2,1,0:T(8,128)(2,1)} %gather_fusion.8, pred[8]{0:T(512)(128)(4,1)S(1)} %get-tuple-element.55, s32[8,128]{1,0:T(8,128)S(1)} %broadcast_select_fusion.12, s32[8,128]{1,0:T(8,128)S(1)} %eq.123, pred[8]{0:T(512)(128)(4,1)S(1)} %get-tuple-element.45, ...), kind=kOutput, calls=%fused_computation.140 | convolution fusion | flops 270662656 | bytes 4224024 | tf_op jit(solution)/shard_map/bid,bjd->bij/dot_general | solution.py:37
  126.7 2.0 gather_fusion.6
  128.7 2.1 gather_fusion.4
  130.8 2.0 gather_fusion.2
  132.8 2.6 %fusion.203 = f32[8,128]{1,0:T(8,128)S(1)} fusion(bf16[8,128,1024]{2,1,0:T(8,128)(2,1)S(1)} %bitcast.137, bf16[8,128,1024]{2,1,0:T(8,128)(2,1)} %gather_fusion.6, pred[8]{0:T(512)(128)(4,1)S(1)} %get-tuple-element.52, s32[8,128]{1,0:T(8,128)S(1)} %broadcast_select_fusion.13, s32[8,128]{1,0:T(8,128)S(1)} %eq.123, pred[8]{0:T(512)(128)(4,1)S(1)} %get-tuple-element.46, ...), kind=kOutput, calls=%fused_computation.139 | convolution fusion | flops 270662656 | bytes 4224024 | tf_op jit(solution)/shard_map/bid,bjd->bij/dot_general | solution.py:37
  135.4 0.9 fusion.200
  136.2 0.7 copy-done.3
  137.0 0.9 fusion.197
  137.8 3.6 %gather_fusion.16 = bf16[8,128,1024]{2,1,0:T(8,128)(2,1)} fusion(bf16[8,128,1024]{2,1,0:T(8,128)(2,1)} %bitcast.18, s32[1024]{0:T(1024)S(1)} %get-tuple-element.96), kind=kCustom, calls=%fused_computation.23.clone | custom fusion | bytes 4194336 | tf_op jit(solution)/shard_map/jit(_take)/gather | solution.py:34
  141.4 3.7 %gather_fusion.14 = bf16[8,128,1024]{2,1,0:T(8,128)(2,1)} fusion(bf16[8,128,1024]{2,1,0:T(8,128)(2,1)} %bitcast.18, s32[1024]{0:T(1024)S(1)} %get-tuple-element.97), kind=kCustom, calls=%fused_computation.22.clone | custom fusion | bytes 4194336 | tf_op jit(solution)/shard_map/jit(_take)/gather | solution.py:34
  145.1 3.6 %gather_fusion.12 = bf16[8,128,1024]{2,1,0:T(8,128)(2,1)} fusion(bf16[8,128,1024]{2,1,0:T(8,128)(2,1)} %bitcast.18, s32[1024]{0:T(1024)S(1)} %get-tuple-element.98), kind=kCustom, calls=%fused_computation.21.clone | custom fusion | bytes 4194336 | tf_op jit(solution)/shard_map/jit(_take)/gather | solution.py:34
  148.7 2.5 %fusion.218 = f32[8,128]{1,0:T(8,128)S(1)} fusion(bf16[8,128,1024]{2,1,0:T(8,128)(2,1)S(1)} %bitcast.140, bf16[8,128,1024]{2,1,0:T(8,128)(2,1)} %gather_fusion.16, pred[8]{0:T(512)(128)(4,1)S(1)} %get-tuple-element.66, s32[8,128]{1,0:T(8,128)S(1)} %broadcast_select_fusion.8, s32[8,128]{1,0:T(8,128)S(1)} %eq.123, pred[8]{0:T(512)(128)(4,1)S(1)} %get-tuple-element.59, ...), kind=kOutput, calls=%fused_computation.144 | convolution fusion | flops 270269440 | bytes 4207632 | tf_op jit(solution)/shard_map/bid,bjd->bij/dot_general | solution.py:37
  151.3 0.8 fusion.215
  152.1 0.6 collective-permute-done.3
  152.8 0.8 fusion.212
  153.7 3.6 %gather_fusion.10 = bf16[8,128,1024]{2,1,0:T(8,128)(2,1)} fusion(bf16[8,128,1024]{2,1,0:T(8,128)(2,1)} %bitcast.18, s32[1024]{0:T(1024)S(1)} %get-tuple-element.99), kind=kCustom, calls=%fused_computation.20.clone | custom fusion | bytes 4194336 | tf_op jit(solution)/shard_map/jit(_take)/gather | solution.py:34
  157.3 2.4 %fusion.209 = f32[8,128]{1,0:T(8,128)S(1)} fusion(bf16[8,128,1024]{2,1,0:T(8,128)(2,1)S(1)} %bitcast.143, bf16[8,128,1024]{2,1,0:T(8,128)(2,1)} %gather_fusion.10, pred[8]{0:T(512)(128)(4,1)S(1)} %get-tuple-element.15, s32[8,128]{1,0:T(8,128)S(1)} %broadcast_select_fusion.11, s32[8,128]{1,0:T(8,128)S(1)} %eq.123, pred[8]{0:T(512)(128)(4,1)S(1)} %get-tuple-element.58, ...), kind=kOutput, calls=%fused_computation.141 | convolution fusion | flops 270269440 | bytes 4207632 | tf_op jit(solution)/shard_map/bid,bjd->bij/dot_general | solution.py:37
  159.7 3.6 %gather_fusion.24 = bf16[8,128,1024]{2,1,0:T(8,128)(2,1)} fusion(bf16[8,128,1024]{2,1,0:T(8,128)(2,1)} %bitcast.29, s32[1024]{0:T(1024)S(1)} %get-tuple-element.92), kind=kCustom, calls=%fused_computation.27.clone | custom fusion | bytes 4194336 | tf_op jit(solution)/shard_map/jit(_take)/gather | solution.py:34
  163.2 3.6 %gather_fusion.22 = bf16[8,128,1024]{2,1,0:T(8,128)(2,1)} fusion(bf16[8,128,1024]{2,1,0:T(8,128)(2,1)} %bitcast.29, s32[1024]{0:T(1024)S(1)} %get-tuple-element.93), kind=kCustom, calls=%fused_computation.26.clone | custom fusion | bytes 4194336 | tf_op jit(solution)/shard_map/jit(_take)/gather | solution.py:34
  166.8 3.7 %gather_fusion.20 = bf16[8,128,1024]{2,1,0:T(8,128)(2,1)} fusion(bf16[8,128,1024]{2,1,0:T(8,128)(2,1)} %bitcast.29, s32[1024]{0:T(1024)S(1)} %get-tuple-element.94), kind=kCustom, calls=%fused_computation.25.clone | custom fusion | bytes 4194336 | tf_op jit(solution)/shard_map/jit(_take)/gather | solution.py:34
  170.5 3.6 %gather_fusion.18 = bf16[8,128,1024]{2,1,0:T(8,128)(2,1)} fusion(bf16[8,128,1024]{2,1,0:T(8,128)(2,1)} %bitcast.29, s32[1024]{0:T(1024)S(1)} %get-tuple-element.95), kind=kCustom, calls=%fused_computation.24.clone | custom fusion | bytes 4194336 | tf_op jit(solution)/shard_map/jit(_take)/gather | solution.py:34
  174.1 2.5 %fusion.230 = f32[8,128]{1,0:T(8,128)S(1)} fusion(bf16[8,128,1024]{2,1,0:T(8,128)(2,1)S(1)} %bitcast.144, bf16[8,128,1024]{2,1,0:T(8,128)(2,1)} %gather_fusion.24, pred[8]{0:T(512)(128)(4,1)S(1)} %get-tuple-element.76, s32[8,128]{1,0:T(8,128)S(1)} %broadcast_select_fusion.4, s32[8,128]{1,0:T(8,128)S(1)} %eq.123, pred[8]{0:T(512)(128)(4,1)S(1)} %get-tuple-element.69, ...), kind=kOutput, calls=%fused_computation.148 | convolution fusion | flops 270269440 | bytes 4207632 | tf_op jit(solution)/shard_map/bid,bjd->bij/dot_general | solution.py:37
  176.6 0.8 fusion.227
  177.4 0.8 copy-done.6
  178.2 0.8 fusion.224
  179.0 0.8 copy-done.4
  179.8 0.8 fusion.221
  181.2 3.6 %gather_fusion.32 = bf16[8,128,1024]{2,1,0:T(8,128)(2,1)} fusion(bf16[8,128,1024]{2,1,0:T(8,128)(2,1)} %bitcast.40, s32[1024]{0:T(1024)S(1)} %get-tuple-element.88), kind=kCustom, calls=%fused_computation.31.clone | custom fusion | bytes 4194336 | tf_op jit(solution)/shard_map/jit(_take)/gather | solution.py:34
  184.8 3.6 %gather_fusion.30 = bf16[8,128,1024]{2,1,0:T(8,128)(2,1)} fusion(bf16[8,128,1024]{2,1,0:T(8,128)(2,1)} %bitcast.40, s32[1024]{0:T(1024)S(1)} %get-tuple-element.89), kind=kCustom, calls=%fused_computation.30.clone | custom fusion | bytes 4194336 | tf_op jit(solution)/shard_map/jit(_take)/gather | solution.py:34
  188.4 3.6 %gather_fusion.28 = bf16[8,128,1024]{2,1,0:T(8,128)(2,1)} fusion(bf16[8,128,1024]{2,1,0:T(8,128)(2,1)} %bitcast.40, s32[1024]{0:T(1024)S(1)} %get-tuple-element.90), kind=kCustom, calls=%fused_computation.29.clone | custom fusion | bytes 4194336 | tf_op jit(solution)/shard_map/jit(_take)/gather | solution.py:34
  192.0 3.7 %gather_fusion.26 = bf16[8,128,1024]{2,1,0:T(8,128)(2,1)} fusion(bf16[8,128,1024]{2,1,0:T(8,128)(2,1)} %bitcast.40, s32[1024]{0:T(1024)S(1)} %get-tuple-element.91), kind=kCustom, calls=%fused_computation.28.clone | custom fusion | bytes 4194336 | tf_op jit(solution)/shard_map/jit(_take)/gather | solution.py:34
  195.6 2.5 %fusion.242 = f32[8,128]{1,0:T(8,128)S(1)} fusion(bf16[8,128,1024]{2,1,0:T(8,128)(2,1)S(1)} %bitcast.148, bf16[8,128,1024]{2,1,0:T(8,128)(2,1)} %gather_fusion.32, pred[8]{0:T(512)(128)(4,1)S(1)} %get-tuple-element.86, s32[8,128]{1,0:T(8,128)S(1)} %broadcast_select_fusion, s32[8,128]{1,0:T(8,128)S(1)} %eq.123, pred[8]{0:T(512)(128)(4,1)S(1)} %get-tuple-element.79, ...), kind=kOutput, calls=%fused_computation.152 | convolution fusion | flops 270269440 | bytes 4207632 | tf_op jit(solution)/shard_map/bid,bjd->bij/dot_general | solution.py:37
  198.2 0.8 fusion.239
  199.0 0.8 copy-done.5
  199.8 0.8 fusion.236
  200.6 0.8 copy-done.1
  201.4 0.8 fusion.233
  202.2 0.7 reshape.802
  202.9 5.3 %all-to-all-start.2 = ((f32[16,1,64]{2,1,0:T(1,128)}), f32[16,1,64]{2,1,0:T(1,128)S(1)}, u32[]{:S(2)}, u32[]{:S(2)}) async-start(f32[16,1,64]{2,1,0:T(1,128)} %reshape.802), calls=%async_computation.2 | async-start | bytes 16384 | tf_op jit(solution)/shard_map/all_to_all | solution.py:102
  208.2 6.4 %all-to-all-done.2 = f32[16,1,64]{2,1,0:T(1,128)S(1)} async-done(((f32[16,1,64]{2,1,0:T(1,128)}), f32[16,1,64]{2,1,0:T(1,128)S(1)}, u32[]{:S(2)}, u32[]{:S(2)}) %all-to-all-start.2) | async-done | bytes 4128 | tf_op jit(solution)/shard_map/all_to_all | solution.py:102
  215.1 0.7 reduce.9
  215.8 8.6 %gather_fusion = f32[960]{0:T(1024)} fusion(f32[1024]{0:T(1024)S(1)} %reshape.474, s32[1024]{0:T(1024)S(1)} %pad_clamp_fusion), kind=kCustom, calls=%fused_computation.32 | custom fusion | bytes 11520 | tf_op jit(solution)/shard_map/gather | solution.py:103
  (90 shorter events, 10.4 us)
Async XLA Ops:
  0.0 22.8 %copy-start = (bf16[960,1024]{1,0:T(8,128)(2,1)S(1)}, bf16[960,1024]{1,0:T(8,128)(2,1)}, u32[]{:S(2)}) copy-start(bf16[960,1024]{1,0:T(8,128)(2,1)} %param.8) | copy-start | bytes 5898244
  0.0 22.8 %copy-start.11 = (s32[1,4,8,4]{2,3,1,0:T(4,128)S(1)}, s32[1,4,8,4]{2,3,1,0:T(4,128)}, u32[]{:S(2)}) copy-start(s32[1,4,8,4]{2,3,1,0:T(4,128)} %param.11) | copy-start | bytes 1540
  13.4 17.6 %all-to-all-start = ((s32[16,1,64]{2,1,0:T(1,128)}), s32[16,1,64]{2,1,0:T(1,128)S(1)}, u32[]{:S(2)}, u32[]{:S(2)}) async-start(s32[16,1,64]{2,1,0:T(1,128)} %all_to_all.13), calls=%async_computation | async-start | bytes 16384 | tf_op jit(solution)/shard_map/all_to_all | solution.py:74
  31.0 47.3 %all-to-all-start.1 = ((bf16[16,64,1024]{2,1,0:T(8,128)(2,1)}), bf16[16,64,1024]{2,1,0:T(8,128)(2,1)S(1)}, u32[]{:S(2)}, u32[]{:S(2)}) async-start(bf16[16,64,1024]{2,1,0:T(8,128)(2,1)} %bitcast.152), calls=%async_computation.1 | async-start | bytes 4194304 | tf_op jit(solution)/shard_map/all_to_all | solution.py:67
  40.8 35.7 %collective-permute-start = (s32[1024]{0:T(1024)S(1)}, s32[1024]{0:T(1024)S(1)}, u32[]{:S(2)}, u32[]{:S(2)}) collective-permute-start(s32[1024]{0:T(1024)S(1)} %reshape.466), channel_id=1, source_target_pairs={{0,1},{1,2},{2,3},{3,4},{4,5},{5,6},{6,7},{7,8},{8,9},{9,10},{10,1... | collective-permute-start | bytes 12296 | tf_op jit(solution)/shard_map/ppermute | solution.py:15
  78.3 45.9 %collective-permute-start.1 = (bf16[1024,1024]{1,0:T(8,128)(2,1)S(1)}, bf16[1024,1024]{1,0:T(8,128)(2,1)}, u32[]{:S(2)}, u32[]{:S(2)}) collective-permute-start(bf16[1024,1024]{1,0:T(8,128)(2,1)S(1)} %bitcast.131), channel_id=1, source_target_pairs={{0,1},{1,2},{2,3},{3,4},{4,5},{5,6},{6,7},{7,8},{8,9},{9,10},{10,1... | collective-permute-start | bytes 6291464 | tf_op jit(solution)/shard_map/ppermute | solution.py:15
  79.6 32.1 %collective-permute-start.2 = (s32[1024]{0:T(1024)S(1)}, s32[1024]{0:T(1024)S(1)}, u32[]{:S(2)}, u32[]{:S(2)}) collective-permute-start(s32[1024]{0:T(1024)S(1)} %collective-permute-done), channel_id=1, source_target_pairs={{0,1},{1,2},{2,3},{3,4},{4,5},{5,6},{6,7},{7,8},{8,9},{9,10},{10,1... | collective-permute-start | bytes 12296 | tf_op jit(solution)/shard_map/ppermute | solution.py:15
  113.9 5.8 %collective-permute-start.4 = (s32[1024]{0:T(1024)S(1)}, s32[1024]{0:T(1024)S(1)}, u32[]{:S(2)}, u32[]{:S(2)}) collective-permute-start(s32[1024]{0:T(1024)S(1)} %collective-permute-done.2), channel_id=1, source_target_pairs={{0,1},{1,2},{2,3},{3,4},{4,5},{5,6},{6,7},{7,8},{8,9},{9,10},{10,1... | collective-permute-start | bytes 12296 | tf_op jit(solution)/shard_map/ppermute | solution.py:15
  124.2 28.5 %collective-permute-start.3 = (bf16[1024,1024]{1,0:T(8,128)(2,1)}, bf16[1024,1024]{1,0:T(8,128)(2,1)}, u32[]{:S(2)}, u32[]{:S(2)}) collective-permute-start(bf16[1024,1024]{1,0:T(8,128)(2,1)} %collective-permute-done.1), channel_id=1, source_target_pairs={{0,1},{1,2},{2,3},{3,4},{4,5},{5,6},{6,7},{7,8},{8,9},{9,10},{10,1... | collective-permute-start | bytes 6291464 | tf_op jit(solution)/shard_map/ppermute | solution.py:15
  132.8 2.6 %copy-start.8 = (bf16[8,128,1024]{2,1,0:T(8,128)(2,1)S(1)}, bf16[8,128,1024]{2,1,0:T(8,128)(2,1)}, u32[]{:S(2)}) copy-start(bf16[8,128,1024]{2,1,0:T(8,128)(2,1)} %gather_fusion.4) | copy-start | bytes 6291460
  135.4 1.6 copy-start.3
  148.7 2.6 %copy-start.10 = (bf16[8,128,1024]{2,1,0:T(8,128)(2,1)S(1)}, bf16[8,128,1024]{2,1,0:T(8,128)(2,1)}, u32[]{:S(2)}) copy-start(bf16[8,128,1024]{2,1,0:T(8,128)(2,1)} %gather_fusion.14) | copy-start | bytes 6291460
  151.2 1.6 copy-start.2
  152.7 28.5 %collective-permute-start.5 = (bf16[1024,1024]{1,0:T(8,128)(2,1)}, bf16[1024,1024]{1,0:T(8,128)(2,1)}, u32[]{:S(2)}, u32[]{:S(2)}) collective-permute-start(bf16[1024,1024]{1,0:T(8,128)(2,1)} %collective-permute-done.3), channel_id=1, source_target_pairs={{0,1},{1,2},{2,3},{3,4},{4,5},{5,6},{6,7},{7,8},{8,9},{9,10},{10,1... | collective-permute-start | bytes 6291464 | tf_op jit(solution)/shard_map/ppermute | solution.py:15
  174.1 2.5 %copy-start.9 = (bf16[8,128,1024]{2,1,0:T(8,128)(2,1)S(1)}, bf16[8,128,1024]{2,1,0:T(8,128)(2,1)}, u32[]{:S(2)}) copy-start(bf16[8,128,1024]{2,1,0:T(8,128)(2,1)} %gather_fusion.22) | copy-start | bytes 6291460
  176.6 1.6 copy-start.6
  178.2 1.6 copy-start.4
  195.6 2.5 %copy-start.7 = (bf16[8,128,1024]{2,1,0:T(8,128)(2,1)S(1)}, bf16[8,128,1024]{2,1,0:T(8,128)(2,1)}, u32[]{:S(2)}) copy-start(bf16[8,128,1024]{2,1,0:T(8,128)(2,1)} %gather_fusion.30) | copy-start | bytes 6291460
  198.2 1.6 copy-start.5
  199.8 1.6 copy-start.1
  202.9 11.7 %all-to-all-start.2 = ((f32[16,1,64]{2,1,0:T(1,128)}), f32[16,1,64]{2,1,0:T(1,128)S(1)}, u32[]{:S(2)}, u32[]{:S(2)}) async-start(f32[16,1,64]{2,1,0:T(1,128)} %reshape.802), calls=%async_computation.2 | async-start | bytes 16384 | tf_op jit(solution)/shard_map/all_to_all | solution.py:102
where the time goes:
time: 226 us; the launch traced here: 224 us
  local copies, waits for them, and re-layouts  81.3 us (36%)
  waiting for transfers between devices  77.2 us (34%)
  matrix products  23.2 us (10%)
  starting transfers between devices  22.6 us (10%)
  other arithmetic  19.8 us (9%)
    ppermute x6, waiting for transfers between devices, shifted(): lax.ppermute(shard, axis, [(i, (i + by) % peers) for i in range(peers)])  70.8 us
    gather x16, local copies, waits for them, and re-layouts, add_step(): tiles = jnp.take(remote, pick, axis=0)  51.5 us
    dot_general x16, matrix products, add_step(): jnp.einsum('bid,bjd->bij', local, tiles, preferred_element_type=jnp.float32)  23.2 us
    gather x16, local copies, waits for them, and re-layouts, add_step(): block_labels = jnp.take(remote_ids, pick, axis=0)  8.88 us
    gather x1, local copies, waits for them, and re-layouts, body(): return returned.reshape(-1)[place]  8.63 us
    scatter x1, other arithmetic, body(): jnp.zeros((slot_count, feature_span), jnp.bfloat16).at[place].set(unit)  8.17 us
    all_to_all x1, starting transfers between devices, body(): lax.all_to_all(departing_row_ids.reshape(device_count, capacity), 'blk',...  7.39 us
    all_to_all x1, waiting for transfers between devices, body(): lax.all_to_all(slot_scores, 'blk', split_axis=0, concat_axis=0, tiled=True)  6.39 us
  transfers between devices with their start and end apart: 9, of which 6 were waited for; matrix products, arithmetic and copies ran while one was open for 34% of the time, Pallas kernels for 0%

commit v1 on v0

v1 whole, which is shorter than its diff:
```python
import numpy as np
import jax
import jax.numpy as jnp
from jax import lax
from jax.sharding import PartitionSpec as P

SLOTS = 1024
STEPS = 4
ID_ROWS = 16


SHARPNESS_KNOB = 32.0


def ring_order(n):
    if n == 16:
        chips = [(z, 0) for z in range(4)] + [(z, 1) for z in reversed(range(4))]
        return [chips[p // 2][0] * 4 + chips[p // 2][1] * 2 + p % 2 for p in range(n)]
    return list(range(n))


def moved(x, pos2dev, moves):
    return lax.ppermute(x, "blk", [(pos2dev[a], pos2dev[b]) for a, b in moves])


def step_total(local, local_ids, remote, remote_ids, step_pairs, first_step):
    slot_count, feature_span = local.shape
    block_count = slot_count // 128
    logits = lax.dot_general(
        local, remote, (((1,), (1,)), ((), ())), preferred_element_type=jnp.float32
    ) * (SHARPNESS_KNOB / feature_span)
    keep = (local_ids[:, None] == remote_ids[None, :]) & (local_ids[:, None] >= 0)
    if first_step:
        keep = keep & jnp.logical_not(jnp.eye(slot_count, dtype=bool))
    contrib = jnp.where(keep, jnp.exp(logits), 0.0)
    per_block = contrib.reshape(slot_count, block_count, 128).sum(axis=2)
    counts = jnp.sum(
        step_pairs[:, :, None] == jnp.arange(block_count, dtype=jnp.int32), axis=1
    ).astype(jnp.float32)
    per_block = per_block.reshape(block_count, 128, block_count)
    return jnp.sum(per_block * counts[:, None, :], axis=2)


def pack(held, held_ids):
    feature_span = held.shape[1]
    id_rows = jnp.pad(held_ids.astype(jnp.bfloat16), (0, ID_ROWS * feature_span - held_ids.shape[0]))
    return jnp.concatenate([held, id_rows.reshape(ID_ROWS, feature_span)], axis=0)


def unpack(packed):
    slot_count = packed.shape[0] - ID_ROWS
    return packed[:slot_count], packed[slot_count:].reshape(-1)[:slot_count].astype(jnp.int32)


def body(embeddings, owners, clusters, pairs):
    device_count = lax.axis_size("blk")
    row_count, feature_span = embeddings.shape
    slot_count = SLOTS
    capacity = slot_count // device_count
    block_count = slot_count // 128
    pos2dev = ring_order(device_count)
    dev2pos = np.argsort(np.asarray(pos2dev)).astype(np.int32)
    position = jnp.asarray(dev2pos)[lax.axis_index("blk")]
    odd = (position % 2) == 1

    value_entries = embeddings.astype(jnp.float32)
    unit = (
        value_entries
        * lax.rsqrt(jnp.mean(value_entries * value_entries, axis=1, keepdims=True) + 1e-06)
    ).astype(jnp.bfloat16)
    row_index = jnp.arange(row_count, dtype=jnp.int32)
    earlier = (owners[None, :] == owners[:, None]) & (row_index[None, :] < row_index[:, None])
    arrival = jnp.sum(earlier.astype(jnp.int32), axis=1)
    place = jnp.asarray(np.asarray(pos2dev, np.int32))[owners] * capacity + arrival
    slot_index = jnp.arange(slot_count, dtype=jnp.int32)
    hit = place[None, :] == slot_index[:, None]
    outgoing = jnp.dot(
        hit.astype(jnp.bfloat16), unit, preferred_element_type=jnp.float32
    ).astype(jnp.bfloat16)
    outgoing_ids = jnp.sum(jnp.where(hit, clusters[None, :] + 1, 0), axis=1) - 1
    id_row = jnp.pad(
        outgoing_ids.reshape(device_count, 1, capacity).astype(jnp.bfloat16),
        ((0, 0), (0, 0), (0, feature_span - capacity)),
    )
    payload = jnp.concatenate([outgoing.reshape(device_count, capacity, feature_span), id_row], axis=1)
    arrived = lax.all_to_all(payload, "blk", split_axis=0, concat_axis=0, tiled=True)
    own = arrived[:, :capacity].reshape(slot_count, feature_span)
    own_ids = arrived[:, capacity, :capacity].reshape(slot_count).astype(jnp.int32)

    all_pairs = lax.all_gather(pairs[0], "blk", axis=0, tiled=False)
    my_pairs = all_pairs[position]
    ahead_pairs = all_pairs[(position + 2) % device_count]

    n = device_count
    evens = range(0, n, 2)
    packed = pack(own, own_ids)
    back2 = moved(packed, pos2dev, [(p, (p - 2) % n) for p in evens])
    fwd2 = moved(packed, pos2dev, [(p, (p + 2) % n) for p in range(n)])
    across = moved(packed, pos2dev, [(p, p + 1) for p in evens])
    fwd2_swapped = moved(fwd2, pos2dev, [(p, p ^ 1) for p in range(n)])
    back2_held, back2_ids = unpack(back2)
    fwd2_held, fwd2_ids = unpack(fwd2)
    across_held, across_ids = unpack(across)
    swapped_held, swapped_ids = unpack(fwd2_swapped)

    total = step_total(own, own_ids, own, own_ids, my_pairs[0], True)
    total = total + step_total(
        own,
        own_ids,
        jnp.where(odd, across_held, swapped_held),
        jnp.where(odd, across_ids, swapped_ids),
        my_pairs[1],
        False,
    )
    total = total + step_total(own, own_ids, fwd2_held, fwd2_ids, my_pairs[2], False)
    last = step_total(
        jnp.where(odd, own, back2_held),
        jnp.where(odd, own_ids, back2_ids),
        swapped_held,
        swapped_ids,
        jnp.where(odd, my_pairs[3], ahead_pairs[3]),
        False,
    )
    handed = moved(last, pos2dev, [(p, (p + 2) % n) for p in evens])
    total = total + jnp.where(odd, last, handed)

    slot_scores = jnp.log1p(total).reshape(device_count, capacity)
    returned = lax.all_to_all(slot_scores, "blk", split_axis=0, concat_axis=0, tiled=True).reshape(-1)
    return jnp.sum(jnp.where(place[:, None] == slot_index[None, :], returned[None, :], 0.0), axis=1)


def solution(mesh):
    placed = (
        P(("groups", "blk"), None),
        P(("groups", "blk")),
        P(("groups", "blk")),
        P(("groups", "blk"), None, None, None),
    )
    return jax.shard_map(
        body, mesh=mesh, in_specs=placed, out_specs=P(("groups", "blk")), check_vma=False
    )
```

time: 226 us -> 173 us (0.77)
  blocking collectives: 0 us -> 126 us
  local copies, waits for them, and re-layouts: 81.3 us -> 2.95 us
  waiting for transfers between devices: 77.2 us -> 0.11 us
  starting transfers between devices: 22.6 us -> 8.52 us
  other arithmetic: 19.8 us -> 9.16 us
  between operations: 0.5 us -> 4.17 us
    all_to_all x0 -> x2, blocking collectives: none -> 70.7 us  [the longest x1 61.2 us: body(): lax.all_to_all(payload, 'blk', split_axis=0, concat_axis=0, tiled=True)]
    ppermute x6 -> x5, waiting for transfers between devices: 70.8 us -> 0.11 us  [moved(): return lax.ppermute(x, 'blk', [(pos2dev[a], pos2dev[b]) for a, b in moves])]
    gather x33 -> x0, local copies, waits for them, and re-layouts: 69 us -> none  [the longest x16 51.5 us: add_step(): tiles = jnp.take(remote, pick, axis=0)]
    all_gather x0 -> x1, blocking collectives: none -> 54.8 us  [body(): all_pairs = lax.all_gather(pairs[0], 'blk', axis=0, tiled=False)]
    all_to_all x3 -> x0, starting transfers between devices: 18.7 us -> none  [the longest x1 7.39 us: body(): lax.all_to_all(departing_row_ids.reshape(device_count, capacity), 'blk',...]
    scatter x1 -> x0, other arithmetic: 8.17 us -> none  [body(): jnp.zeros((slot_count, feature_span), jnp.bfloat16).at[place].set(unit)]
    all_to_all x3 -> x0, waiting for transfers between devices: 6.4 us -> none  [the longest x1 6.39 us: body(): lax.all_to_all(slot_scores, 'blk', split_axis=0, concat_axis=0, tiled=True)]
    scatter x1 -> x0, local copies, waits for them, and re-layouts: 5.41 us -> none  [body(): jnp.full((slot_count,), -1, jnp.int32).at[place].set(clusters)]
  transfers between devices with their start and end apart: 9 -> 5, of which waited for: 6 -> 1; matrix products, arithmetic and copies ran while one was open for 34% -> 12% of each run, Pallas kernels for 0% -> 0%
where the time goes in v1:
time: 173 us
  blocking collectives  126 us (73%)
  matrix products  22.2 us (13%)
  other arithmetic  9.16 us (5%)
  starting transfers between devices  8.52 us (5%)
  between operations  4.17 us (2%)
  local copies, waits for them, and re-layouts  2.95 us (2%)
    all_to_all x1, blocking collectives, body(): lax.all_to_all(payload, 'blk', split_axis=0, concat_axis=0, tiled=True)  61.2 us
    all_gather x1, blocking collectives, body(): all_pairs = lax.all_gather(pairs[0], 'blk', axis=0, tiled=False)  54.8 us
    dot_general x4, matrix products, step_total(): lax.dot_general(local, remote, (((1,), (1,)), ((), ())), preferred_elemen...  18.1 us
    all_to_all x1, blocking collectives, body(): lax.all_to_all(slot_scores, 'blk', split_axis=0, concat_axis=0, tiled=True)  9.51 us
    ppermute x5, starting transfers between devices, moved(): return lax.ppermute(x, 'blk', [(pos2dev[a], pos2dev[b]) for a, b in moves])  8.52 us
    dot_general x1, matrix products, body(): jnp.dot(hit.astype(jnp.bfloat16), unit, preferred_element_type=jnp.float32)  4.16 us
  transfers between devices with their start and end apart: 5, of which 1 were waited for; matrix products, arithmetic and copies ran while one was open for 12% of the time, Pallas kernels for 0%

profile of v1, /device:TPU:0, one launch (start us, length us, event | category | flops | bytes accessed | tf_op | source)
XLA Modules:
  0.0 172.7 jit_solution(1247788844349415672)
XLA Ops:
  0.0 2.0 %fusion.3 = f32[960]{0:T(1024)S(1)} fusion(bf16[960,1024]{1,0:T(8,128)(2,1)} %param.6), kind=kLoop, calls=%fused_computation.15 | loop fusion | flops 2948160 | bytes 1969920 | tf_op jit(solution)/shard_map/reduce_sum | solution.py:69
  2.0 1.2 convert_reduce_fusion
  3.3 0.7 fusion.24
  4.0 0.6 select_reduce_fusion.1
  4.6 0.1 convert_element_type.144
  4.7 4.2 %fusion.14 = bf16[1024,1024]{1,0:T(8,128)(2,1)S(1)} fusion(bf16[960,1024]{1,0:T(8,128)(2,1)} %param.6, f32[960]{0:T(1024)S(1)} %add_rsqrt_fusion, s32[960]{0:T(1024)S(1)} %get-tuple-element.12), kind=kOutput, calls=%fused_computation.34 | convolution fusion | flops 2018246656 | bytes 4070912 | tf_op jit(solution)/shard_map/dot_general | solution.py:77
  8.9 0.3 fusion.7
  9.2 61.2 %all_to_all.14 = bf16[16,65,1024]{2,1,0:T(8,128)(2,1)S(1)} all-to-all(bf16[16,65,1024]{2,1,0:T(8,128)(2,1)S(1)} %fusion.7), channel_id=1, replica_groups=mesh['groups'=2,'blk'=16] {'blk'}, dimensions={0} | all-to-all | bytes 4259840 | tf_op jit(solution)/shard_map/all_to_all | solution.py:86
  70.4 0.1 reshape.202
  70.5 0.2 slice.95
  70.7 0.0 copy-start
  70.7 0.0 copy-start.3
  70.8 0.0 copy-start.2
  70.8 1.3 copy-done
  72.1 0.2 pad_maximum_fusion
  72.2 1.3 collective-permute-start.1
  73.5 2.7 %collective-permute-start.3 = (bf16[1040,1024]{1,0:T(8,128)(2,1)S(1)}, bf16[1040,1024]{1,0:T(8,128)(2,1)}, u32[]{:S(2)}, u32[]{:S(2)}) collective-permute-start(bf16[1040,1024]{1,0:T(8,128)(2,1)S(1)} %pad_maximum_fusion), channel_id=1, source_target_pairs={{0,2},{4,0},{8,4},{12,8},{14,12},{10,14},{6,10},{2,6},{16,18},{20,... | collective-permute-start | bytes 6389768 | tf_op jit(solution)/shard_map/ppermute | solution.py:23
  76.2 0.0 copy-done.3
  76.2 0.6 dynamic_slice.9
  80.7 0.0 copy-done.2
  80.7 54.8 %all_gather.3 = s32[16,4,8,4]{2,3,1,0:T(4,128)S(1)} all-gather(s32[1,4,8,4]{2,3,1,0:T(4,128)S(1)} %copy-done.2), channel_id=1, replica_groups=mesh['groups'=2,'blk'=16] {'blk'}, dimensions={0}, use_global_device_ids=true | all-gather | bytes 8704 | tf_op jit(solution)/shard_map/all_gather | solution.py:90
  135.6 0.1 convert_reduce_fusion.3
  135.7 0.1 convert_reduce_fusion.4
  135.7 0.1 convert_reduce_fusion.1
  135.8 0.1 convert_reduce_fusion.2
  135.9 2.6 %collective-permute-start = (bf16[1040,1024]{1,0:T(8,128)(2,1)S(1)}, bf16[1040,1024]{1,0:T(8,128)(2,1)S(1)}, u32[]{:S(2)}, u32[]{:S(2)}) collective-permute-start(bf16[1040,1024]{1,0:T(8,128)(2,1)S(1)} %pad_maximum_fusion), channel_id=1, source_target_pairs={{0,1},{4,5},{8,9},{12,13},{14,15},{10,11},{6,7},{2,3},{16,17},{20,... | collective-permute-start | bytes 6389768 | tf_op jit(solution)/shard_map/ppermute | solution.py:23
  138.5 0.0 collective-permute-done.1
  138.5 0.1 collective-permute-start.2
  138.6 0.0 collective-permute-done.3
  138.6 0.7 slice_convert_fusion.1
  139.3 0.0 copy-start.1
  139.3 5.5 %bitcast_reduce_fusion.3 = f32[1024,8]{0,1:T(8,128)S(1)} fusion(bf16[1024,1024]{1,0:T(8,128)(2,1)} %bitcast.44, s32[1024]{0:T(1024)S(1)} %reshape.202, pred[1024]{0:T(1024)(128)(4,1)S(1)} %get-tuple-element.11), kind=kOutput, calls=%fused_computation.7 | convolution fusion | flops 2155864064 | bytes 2135040 | tf_op jit(solution)/shard_map/dot_general | solution.py:29
  144.9 0.1 fusion.22
  144.9 0.7 slice_convert_fusion.2
  145.7 0.0 copy-done.1
  145.7 4.6 %bitcast_reduce_fusion.1 = f32[1024,8]{0,1:T(8,128)S(1)} fusion(bf16[1024,1024]{1,0:T(8,128)(2,1)S(1)} %bitcast.45, bf16[1040,1024]{1,0:T(8,128)(2,1)} %collective-permute-done.1, s32[1024]{0:T(1024)S(1)} %reshape.202, s32[1024]{0:T(1024)S(1)} %bitcast.52, pred[1024]{0:T(1024)(128)(4,1)S(1)} %get-tuple-element.11), kind=kOutput, calls=%fused_computation.5 | convolution fusion | flops 2152718336 | bytes 4236288 | tf_op jit(solution)/shard_map/dot_general | solution.py:29
  150.3 0.1 fusion.20
  150.4 0.0 collective-permute-done.2
  150.4 4.6 %bitcast_reduce_fusion = f32[1024,8]{0,1:T(8,128)S(1)} fusion(bf16[1024,1024]{1,0:T(8,128)(2,1)S(1)} %bitcast.46, bf16[1040,1024]{1,0:T(8,128)(2,1)} %collective-permute-done.3, s32[1024]{0:T(1024)S(1)} %get-tuple-element.6, s32[1024]{0:T(1024)S(1)} %bitcast.51, pred[1024]{0:T(1024)(128)(4,1)S(1)} %get-tuple-element.5, pred[]{:T(512)S(6)} %eq.180, ...), kind=kOutput, calls=%fused_computation.4 | convolution fusion | flops 2153766912 | bytes 6333441 | tf_op jit(solution)/shard_map/dot_general | solution.py:29
  155.0 0.1 fusion.19
  155.1 1.9 %collective-permute-start.4 = (f32[8,128]{1,0:T(8,128)S(1)}, f32[8,128]{1,0:T(8,128)S(1)}, u32[]{:S(2)}, u32[]{:S(2)}) collective-permute-start(f32[8,128]{1,0:T(8,128)S(1)} %fusion.19), channel_id=1, source_target_pairs={{0,4},{4,8},{8,12},{12,14},{14,10},{10,6},{6,2},{2,0},{16,20},{20,... | collective-permute-start | bytes 12296 | tf_op jit(solution)/shard_map/ppermute | solution.py:23
  157.0 0.0 collective-permute-done
  157.0 3.3 %bitcast_reduce_fusion.2 = f32[1024,8]{0,1:T(8,128)S(1)} fusion(bf16[1024,1024]{1,0:T(8,128)(2,1)S(1)} %bitcast.47, bf16[1040,1024]{1,0:T(8,128)(2,1)S(1)} %collective-permute-done, s32[1024]{0:T(1024)S(1)} %reshape.202, s32[1024]{0:T(1024)S(1)} %bitcast.50, pred[]{:T(512)S(6)} %eq.180, pred[1024]{0:T(1024)(128)(4,1)S(1)} %get-tuple-element.11, ...), kind=kOutput, calls=%fused_computation.6 | convolution fusion | flops 2153766912 | bytes 6333441 | tf_op jit(solution)/shard_map/dot_general | solution.py:29
  160.4 0.1 fusion.21
  160.5 0.1 collective-permute-done.4
  160.6 0.1 all_to_all.10
  160.7 9.5 %all_to_all.15 = f32[16,1,64]{2,1,0:T(1,128)S(1)} all-to-all(f32[16,1,64]{2,1,0:T(1,128)S(1)} %all_to_all.10), channel_id=1, replica_groups=mesh['groups'=2,'blk'=16] {'blk'}, dimensions={0} | all-to-all | bytes 8192 | tf_op jit(solution)/shard_map/all_to_all | solution.py:128
  170.2 0.5 broadcast.153
  170.7 0.7 reduce.23
  171.4 0.1 broadcast_in_dim.35
  171.4 1.2 select_reduce_fusion
  (15 shorter events, 0.2 us)
Async XLA Ops:
  70.7 1.3 copy-start
  70.7 5.5 %copy-start.3 = (s32[16]{0:T(128)S(1)}, s32[16]{0:T(128)}, u32[]{:S(2)}) copy-start(s32[16]{0:T(128)} %constant.53.clone) | copy-start | bytes 196
  70.8 10.0 %copy-start.2 = (s32[1,4,8,4]{2,3,1,0:T(4,128)S(1)}, s32[1,4,8,4]{2,3,1,0:T(4,128)}, u32[]{:S(2)}) copy-start(s32[1,4,8,4]{2,3,1,0:T(4,128)} %param.9) | copy-start | bytes 1540
  72.2 66.2 %collective-permute-start.1 = (bf16[1040,1024]{1,0:T(8,128)(2,1)S(1)}, bf16[1040,1024]{1,0:T(8,128)(2,1)}, u32[]{:S(2)}, u32[]{:S(2)}) collective-permute-start(bf16[1040,1024]{1,0:T(8,128)(2,1)S(1)} %pad_maximum_fusion), channel_id=1, source_target_pairs={{0,4},{1,5},{4,8},{5,9},{8,12},{9,13},{12,14},{13,15},{14,10},{15,... | collective-permute-start | bytes 6389768 | tf_op jit(solution)/shard_map/ppermute | solution.py:23
  73.5 65.0 %collective-permute-start.3 = (bf16[1040,1024]{1,0:T(8,128)(2,1)S(1)}, bf16[1040,1024]{1,0:T(8,128)(2,1)}, u32[]{:S(2)}, u32[]{:S(2)}) collective-permute-start(bf16[1040,1024]{1,0:T(8,128)(2,1)S(1)} %pad_maximum_fusion), channel_id=1, source_target_pairs={{0,2},{4,0},{8,4},{12,8},{14,12},{10,14},{6,10},{2,6},{16,18},{20,... | collective-permute-start | bytes 6389768 | tf_op jit(solution)/shard_map/ppermute | solution.py:23
  135.9 21.1 %collective-permute-start = (bf16[1040,1024]{1,0:T(8,128)(2,1)S(1)}, bf16[1040,1024]{1,0:T(8,128)(2,1)S(1)}, u32[]{:S(2)}, u32[]{:S(2)}) collective-permute-start(bf16[1040,1024]{1,0:T(8,128)(2,1)S(1)} %pad_maximum_fusion), channel_id=1, source_target_pairs={{0,1},{4,5},{8,9},{12,13},{14,15},{10,11},{6,7},{2,3},{16,17},{20,... | collective-permute-start | bytes 6389768 | tf_op jit(solution)/shard_map/ppermute | solution.py:23
  138.5 11.9 %collective-permute-start.2 = (bf16[1040,1024]{1,0:T(8,128)(2,1)}, bf16[1040,1024]{1,0:T(8,128)(2,1)S(1)}, u32[]{:S(2)}, u32[]{:S(2)}) collective-permute-start(bf16[1040,1024]{1,0:T(8,128)(2,1)} %collective-permute-done.1), channel_id=1, source_target_pairs={{0,1},{1,0},{4,5},{5,4},{8,9},{9,8},{12,13},{13,12},{14,15},{15,14... | collective-permute-start | bytes 6389768 | tf_op jit(solution)/shard_map/ppermute | solution.py:23
  139.3 6.4 %copy-start.1 = (bf16[16,64,1024]{2,1,0:T(8,128)(2,1)S(1)}, bf16[16,64,1024]{2,1,0:T(8,128)(2,1)}, u32[]{:S(2)}) copy-start(bf16[16,64,1024]{2,1,0:T(8,128)(2,1)} %copy-done) | copy-start | bytes 6291460
  155.1 5.5 %collective-permute-start.4 = (f32[8,128]{1,0:T(8,128)S(1)}, f32[8,128]{1,0:T(8,128)S(1)}, u32[]{:S(2)}, u32[]{:S(2)}) collective-permute-start(f32[8,128]{1,0:T(8,128)S(1)} %fusion.19), channel_id=1, source_target_pairs={{0,4},{4,8},{8,12},{12,14},{14,10},{10,6},{6,2},{2,0},{16,20},{20,... | collective-permute-start | bytes 12296 | tf_op jit(solution)/shard_map/ppermute | solution.py:23

commit v2 on v1

--- a/solution.py
+++ b/solution.py
@@ -78,16 +78,23 @@
         hit.astype(jnp.bfloat16), unit, preferred_element_type=jnp.float32
     ).astype(jnp.bfloat16)
     outgoing_ids = jnp.sum(jnp.where(hit, clusters[None, :] + 1, 0), axis=1) - 1
-    id_row = jnp.pad(
-        outgoing_ids.reshape(device_count, 1, capacity).astype(jnp.bfloat16),
-        ((0, 0), (0, 0), (0, feature_span - capacity)),
-    )
+    pair_count = pairs[0].size
+    side = jnp.concatenate(
+        [
+            outgoing_ids.reshape(device_count, capacity),
+            jnp.broadcast_to(pairs[0].reshape(1, pair_count), (device_count, pair_count)),
+        ],
+        axis=1,
+    ).astype(jnp.bfloat16)
+    id_row = jnp.pad(side, ((0, 0), (0, feature_span - capacity - pair_count)))[:, None, :]
     payload = jnp.concatenate([outgoing.reshape(device_count, capacity, feature_span), id_row], axis=1)
     arrived = lax.all_to_all(payload, "blk", split_axis=0, concat_axis=0, tiled=True)
     own = arrived[:, :capacity].reshape(slot_count, feature_span)
     own_ids = arrived[:, capacity, :capacity].reshape(slot_count).astype(jnp.int32)
 
-    all_pairs = lax.all_gather(pairs[0], "blk", axis=0, tiled=False)
+    all_pairs = (
+        arrived[:, capacity, capacity : capacity + pair_count].astype(jnp.int32).reshape((device_count,) + pairs.shape[1:])
+    )
     my_pairs = all_pairs[position]
     ahead_pairs = all_pairs[(position + 2) % device_count]
 
@@ -97,13 +104,14 @@
     back2 = moved(packed, pos2dev, [(p, (p - 2) % n) for p in evens])
     fwd2 = moved(packed, pos2dev, [(p, (p + 2) % n) for p in range(n)])
     across = moved(packed, pos2dev, [(p, p + 1) for p in evens])
+    total = step_total(own, own_ids, own, own_ids, my_pairs[0], True)
+    total, back2, fwd2, across = lax.optimization_barrier((total, back2, fwd2, across))
     fwd2_swapped = moved(fwd2, pos2dev, [(p, p ^ 1) for p in range(n)])
     back2_held, back2_ids = unpack(back2)
     fwd2_held, fwd2_ids = unpack(fwd2)
     across_held, across_ids = unpack(across)
     swapped_held, swapped_ids = unpack(fwd2_swapped)
 
-    total = step_total(own, own_ids, own, own_ids, my_pairs[0], True)
     total = total + step_total(
         own,
         own_ids,

time: 173 us -> 160 us (0.925)
  blocking collectives: 126 us -> 70.5 us
  waiting for transfers between devices: 0.11 us -> 31.9 us
  other arithmetic: 9.16 us -> 12.9 us
  matrix products: 22.2 us -> 24.8 us
  starting transfers between devices: 8.52 us -> 11 us
    all_gather x1 -> x0, blocking collectives: 54.8 us -> none  [body(): all_pairs = lax.all_gather(pairs[0], 'blk', axis=0, tiled=False)]
    ppermute x5, waiting for transfers between devices: 0.11 us -> 31.9 us  [moved(): return lax.ppermute(x, 'blk', [(pos2dev[a], pos2dev[b]) for a, b in moves])]
    dot_general x4, matrix products: 18.1 us -> 20.6 us  [step_total(): lax.dot_general(local, remote, (((1,), (1,)), ((), ())), preferred_elemen...]
    ppermute x5, starting transfers between devices: 8.52 us -> 11 us  [moved(): return lax.ppermute(x, 'blk', [(pos2dev[a], pos2dev[b]) for a, b in moves])]
where the time goes in v2:
time: 160 us; the launch traced here: 159 us
  blocking collectives  70.5 us (44%)
  waiting for transfers between devices  31.9 us (20%)
  matrix products  24.8 us (16%)
  other arithmetic  12.9 us (8%)
  starting transfers between devices  11 us (7%)
  between operations  4.13 us (3%)
  local copies, waits for them, and re-layouts  3.96 us (2%)
    all_to_all x1, blocking collectives, body(): lax.all_to_all(payload, 'blk', split_axis=0, concat_axis=0, tiled=True)  61.2 us
    ppermute x5, waiting for transfers between devices, moved(): return lax.ppermute(x, 'blk', [(pos2dev[a], pos2dev[b]) for a, b in moves])  31.9 us
    dot_general x4, matrix products, step_total(): lax.dot_general(local, remote, (((1,), (1,)), ((), ())), preferred_elemen...  20.6 us
    ppermute x5, starting transfers between devices, moved(): return lax.ppermute(x, 'blk', [(pos2dev[a], pos2dev[b]) for a, b in moves])  11 us
    all_to_all x1, blocking collectives, body(): lax.all_to_all(slot_scores, 'blk', split_axis=0, concat_axis=0, tiled=True)  9.37 us
    dot_general x1, matrix products, body(): jnp.dot(hit.astype(jnp.bfloat16), unit, preferred_element_type=jnp.float32)  4.16 us
  transfers between devices with their start and end apart: 5, of which 1 were waited for; matrix products, arithmetic and copies ran while one was open for 12% of the time, Pallas kernels for 0%

profile of v2, /device:TPU:0, one launch (start us, length us, event | category | flops | bytes accessed | tf_op | source)
XLA Modules:
  0.0 159.2 jit_solution(806107788722209914)
XLA Ops:
  0.0 0.7 convert.14
  0.7 0.1 copy.67
  0.8 0.1 reshape.233
  0.9 2.0 %fusion.2 = f32[960]{0:T(1024)S(1)} fusion(bf16[960,1024]{1,0:T(8,128)(2,1)} %param.6), kind=kLoop, calls=%fused_computation.13 | loop fusion | flops 2948160 | bytes 1969920 | tf_op jit(solution)/shard_map/reduce_sum | solution.py:69
  2.9 1.2 convert_reduce_fusion
  4.2 0.7 fusion.26
  4.9 0.6 select_reduce_fusion.1
  5.6 0.1 sub.7
  5.6 0.1 pad.15.clone
  5.7 0.1 copy.68
  5.8 4.2 %fusion.16 = bf16[1024,1024]{1,0:T(8,128)(2,1)S(1)} fusion(bf16[960,1024]{1,0:T(8,128)(2,1)} %param.6, f32[960]{0:T(1024)S(1)} %add_rsqrt_fusion, s32[960]{0:T(1024)S(1)} %get-tuple-element.19), kind=kOutput, calls=%fused_computation.34 | convolution fusion | flops 2018246656 | bytes 4070912 | tf_op jit(solution)/shard_map/dot_general | solution.py:77
  10.0 0.3 pad_maximum_fusion
  10.3 61.2 %all_to_all.14 = bf16[16,65,1024]{2,1,0:T(8,128)(2,1)S(1)} all-to-all(bf16[16,65,1024]{2,1,0:T(8,128)(2,1)S(1)} %pad_maximum_fusion), channel_id=1, replica_groups=mesh['groups'=2,'blk'=16] {'blk'}, dimensions={0} | all-to-all | bytes 4259840 | tf_op jit(solution)/shard_map/all_to_all | solution.py:91
  71.5 0.1 reshape.193
  71.6 0.2 slice.99
  71.9 0.0 copy-start
  71.9 0.0 copy-start.2
  71.9 1.3 copy-done
  73.2 1.5 pad_maximum_fusion.1
  74.8 4.0 %collective-permute-start.2 = (bf16[1040,1024]{1,0:T(8,128)(2,1)}, bf16[1040,1024]{1,0:T(8,128)(2,1)}, u32[]{:S(2)}, u32[]{:S(2)}) collective-permute-start(bf16[1040,1024]{1,0:T(8,128)(2,1)} %pad_maximum_fusion.1), channel_id=1, source_target_pairs={{0,1},{4,5},{8,9},{12,13},{14,15},{10,11},{6,7},{2,3},{16,17},{20,... | collective-permute-start | bytes 6389768 | tf_op jit(solution)/shard_map/ppermute | solution.py:23
  78.8 1.0 collective-permute-start.1
  79.8 3.1 %collective-permute-start = (bf16[1040,1024]{1,0:T(8,128)(2,1)}, bf16[1040,1024]{1,0:T(8,128)(2,1)}, u32[]{:S(2)}, u32[]{:S(2)}) collective-permute-start(bf16[1040,1024]{1,0:T(8,128)(2,1)} %pad_maximum_fusion.1), channel_id=1, source_target_pairs={{0,2},{4,0},{8,4},{12,8},{14,12},{10,14},{6,10},{2,6},{16,18},{20,... | collective-permute-start | bytes 6389768 | tf_op jit(solution)/shard_map/ppermute | solution.py:23
  82.9 0.0 copy-done.2
  82.9 0.6 dynamic_slice.9
  87.4 0.1 slice.100
  87.5 0.1 copy.70
  87.6 0.1 constant_dynamic-slice_fusion.1
  87.7 0.1 copy.71
  87.8 0.1 convert_reduce_fusion.4
  87.9 0.0 copy-start.1
  87.9 5.5 %bitcast_reduce_fusion.3 = f32[1024,8]{0,1:T(8,128)S(1)} fusion(bf16[1024,1024]{1,0:T(8,128)(2,1)} %bitcast.45, s32[1024]{0:T(1024)S(1)} %reshape.193, pred[1024]{0:T(1024)(128)(4,1)S(1)} %broadcast_compare_fusion.1), kind=kOutput, calls=%fused_computation.5 | convolution fusion | flops 2155864064 | bytes 2135040 | tf_op jit(solution)/shard_map/dot_general | solution.py:29
  93.5 0.1 fusion.24
  93.6 0.0 collective-permute-done.2
  93.6 31.9 %collective-permute-done.1 = bf16[1040,1024]{1,0:T(8,128)(2,1)} collective-permute-done((bf16[1040,1024]{1,0:T(8,128)(2,1)}, bf16[1040,1024]{1,0:T(8,128)(2,1)}, u32[]{:S(2)}, u32[]{:S(2)}) %collective-permute-start.1) | collective-permute-done | bytes 2129952 | tf_op jit(solution)/shard_map/ppermute | solution.py:23
  125.4 0.0 collective-permute-done
  125.4 0.0 collective-permute-start.3
  125.4 0.1 copy.72
  125.5 0.1 convert_reduce_fusion.3
  125.6 0.1 copy.74
  125.7 0.1 convert_reduce_fusion.1
  125.8 0.1 copy.73
  125.9 0.1 convert_reduce_fusion.2
  126.0 0.7 slice_convert_fusion.3
  126.7 0.0 copy-done.1
  126.7 4.6 %bitcast_reduce_fusion.1 = f32[1024,8]{0,1:T(8,128)S(1)} fusion(bf16[1024,1024]{1,0:T(8,128)(2,1)S(1)} %bitcast.46, bf16[1040,1024]{1,0:T(8,128)(2,1)} %collective-permute-done.1, s32[1024]{0:T(1024)S(1)} %reshape.193, s32[1024]{0:T(1024)S(1)} %bitcast.58, pred[1024]{0:T(1024)(128)(4,1)S(1)} %broadcast_compare_fusion.1), kind=kOutput, calls=%fused_computation.3 | convolution fusion | flops 2152718336 | bytes 4236288 | tf_op jit(solution)/shard_map/dot_general | solution.py:29
  131.3 0.1 fusion.22
  131.4 0.7 slice_convert_fusion.2
  132.2 0.0 collective-permute-done.3
  132.2 0.7 slice_convert_fusion.1
  132.9 5.2 %bitcast_reduce_fusion = f32[1024,8]{0,1:T(8,128)S(1)} fusion(bf16[1024,1024]{1,0:T(8,128)(2,1)S(1)} %bitcast.47, bf16[1040,1024]{1,0:T(8,128)(2,1)} %collective-permute-done, s32[1024]{0:T(1024)S(1)} %get-tuple-element.14, s32[1024]{0:T(1024)S(1)} %bitcast.57, pred[1024]{0:T(1024)(128)(4,1)S(1)} %get-tuple-element.13, pred[]{:T(512)S(6)} %eq.180, ...), kind=kOutput, calls=%fused_computation.2 | convolution fusion | flops 2153766912 | bytes 6333441 | tf_op jit(solution)/shard_map/dot_general | solution.py:29
  138.1 0.1 fusion.21
  138.2 2.9 %collective-permute-start.4 = (f32[8,128]{1,0:T(8,128)S(1)}, f32[8,128]{1,0:T(8,128)S(1)}, u32[]{:S(2)}, u32[]{:S(2)}) collective-permute-start(f32[8,128]{1,0:T(8,128)S(1)} %fusion.21), channel_id=1, source_target_pairs={{0,4},{4,8},{8,12},{12,14},{14,10},{10,6},{6,2},{2,0},{16,20},{20,... | collective-permute-start | bytes 12296 | tf_op jit(solution)/shard_map/ppermute | solution.py:23
  141.1 0.7 broadcast_select_fusion
  141.9 5.2 %bitcast_reduce_fusion.2 = f32[1024,8]{0,1:T(8,128)S(1)} fusion(bf16[1024,1024]{1,0:T(8,128)(2,1)S(1)} %bitcast.48, bf16[1040,1024]{1,0:T(8,128)(2,1)} %collective-permute-done.2, s32[1024]{0:T(1024)S(1)} %reshape.193, s32[1024]{0:T(1024)S(1)} %bitcast.56, pred[]{:T(512)S(6)} %eq.180, pred[1024]{0:T(1024)(128)(4,1)S(1)} %broadcast_compare_fusion.1, ...), kind=kOutput, calls=%fused_computation.4 | convolution fusion | flops 2153766912 | bytes 6333441 | tf_op jit(solution)/shard_map/dot_general | solution.py:29
  147.1 0.1 fusion.23
  147.2 0.0 collective-permute-done.4
  147.2 0.1 all_to_all.10
  147.3 9.4 %all_to_all.15 = f32[16,1,64]{2,1,0:T(1,128)S(1)} all-to-all(f32[16,1,64]{2,1,0:T(1,128)S(1)} %all_to_all.10), channel_id=1, replica_groups=mesh['groups'=2,'blk'=16] {'blk'}, dimensions={0} | all-to-all | bytes 8192 | tf_op jit(solution)/shard_map/all_to_all | solution.py:136
  156.7 0.5 broadcast.145
  157.2 0.7 reduce.23
  157.9 0.1 broadcast_in_dim.44
  157.9 1.2 select_reduce_fusion
  (16 shorter events, 0.2 us)
Async XLA Ops:
  71.9 1.4 copy-start
  71.9 11.0 %copy-start.2 = (s32[16]{0:T(128)S(1)}, s32[16]{0:T(128)}, u32[]{:S(2)}) copy-start(s32[16]{0:T(128)} %constant.53.clone) | copy-start | bytes 196
  74.8 18.8 %collective-permute-start.2 = (bf16[1040,1024]{1,0:T(8,128)(2,1)}, bf16[1040,1024]{1,0:T(8,128)(2,1)}, u32[]{:S(2)}, u32[]{:S(2)}) collective-permute-start(bf16[1040,1024]{1,0:T(8,128)(2,1)} %pad_maximum_fusion.1), channel_id=1, source_target_pairs={{0,1},{4,5},{8,9},{12,13},{14,15},{10,11},{6,7},{2,3},{16,17},{20,... | collective-permute-start | bytes 6389768 | tf_op jit(solution)/shard_map/ppermute | solution.py:23
  78.8 46.6 %collective-permute-start.1 = (bf16[1040,1024]{1,0:T(8,128)(2,1)}, bf16[1040,1024]{1,0:T(8,128)(2,1)}, u32[]{:S(2)}, u32[]{:S(2)}) collective-permute-start(bf16[1040,1024]{1,0:T(8,128)(2,1)} %pad_maximum_fusion.1), channel_id=1, source_target_pairs={{0,4},{1,5},{4,8},{5,9},{8,12},{9,13},{12,14},{13,15},{14,10},{15,... | collective-permute-start | bytes 6389768 | tf_op jit(solution)/shard_map/ppermute | solution.py:23
  79.8 45.7 %collective-permute-start = (bf16[1040,1024]{1,0:T(8,128)(2,1)}, bf16[1040,1024]{1,0:T(8,128)(2,1)}, u32[]{:S(2)}, u32[]{:S(2)}) collective-permute-start(bf16[1040,1024]{1,0:T(8,128)(2,1)} %pad_maximum_fusion.1), channel_id=1, source_target_pairs={{0,2},{4,0},{8,4},{12,8},{14,12},{10,14},{6,10},{2,6},{16,18},{20,... | collective-permute-start | bytes 6389768 | tf_op jit(solution)/shard_map/ppermute | solution.py:23
  87.9 38.8 %copy-start.1 = (bf16[16,64,1024]{2,1,0:T(8,128)(2,1)S(1)}, bf16[16,64,1024]{2,1,0:T(8,128)(2,1)}, u32[]{:S(2)}) copy-start(bf16[16,64,1024]{2,1,0:T(8,128)(2,1)} %copy-done) | copy-start | bytes 6291460
  125.4 6.7 %collective-permute-start.3 = (bf16[1040,1024]{1,0:T(8,128)(2,1)}, bf16[1040,1024]{1,0:T(8,128)(2,1)}, u32[]{:S(2)}, u32[]{:S(2)}) collective-permute-start(bf16[1040,1024]{1,0:T(8,128)(2,1)} %collective-permute-done.1), channel_id=1, source_target_pairs={{0,1},{1,0},{4,5},{5,4},{8,9},{9,8},{12,13},{13,12},{14,15},{15,14... | collective-permute-start | bytes 6389768 | tf_op jit(solution)/shard_map/ppermute | solution.py:23
  138.2 9.0 %collective-permute-start.4 = (f32[8,128]{1,0:T(8,128)S(1)}, f32[8,128]{1,0:T(8,128)S(1)}, u32[]{:S(2)}, u32[]{:S(2)}) collective-permute-start(f32[8,128]{1,0:T(8,128)S(1)} %fusion.21), channel_id=1, source_target_pairs={{0,4},{4,8},{8,12},{12,14},{14,10},{10,6},{6,2},{2,0},{16,20},{20,... | collective-permute-start | bytes 12296 | tf_op jit(solution)/shard_map/ppermute | solution.py:23

commit v3 on v2

--- a/solution.py
+++ b/solution.py
@@ -129,12 +129,19 @@
         jnp.where(odd, my_pairs[3], ahead_pairs[3]),
         False,
     )
-    handed = moved(last, pos2dev, [(p, (p + 2) % n) for p in evens])
-    total = total + jnp.where(odd, last, handed)
-
-    slot_scores = jnp.log1p(total).reshape(device_count, capacity)
-    returned = lax.all_to_all(slot_scores, "blk", split_axis=0, concat_axis=0, tiled=True).reshape(-1)
-    return jnp.sum(jnp.where(place[:, None] == slot_index[None, :], returned[None, :], 0.0), axis=1)
+    total = total + jnp.where(odd, last, 0.0)
+    forward_part = jnp.where(odd, 0.0, last)
+    totals = jnp.stack([total.reshape(device_count, capacity), forward_part.reshape(device_count, capacity)], axis=1)
+    returned = lax.all_to_all(totals, "blk", split_axis=0, concat_axis=0, tiled=True)
+    owner_sum = jnp.sum(
+        jnp.where(place[:, None] == slot_index[None, :], returned[:, 0].reshape(-1)[None, :], 0.0), axis=1
+    )
+    behind = jnp.asarray(np.asarray(pos2dev, np.int32))[(owners - 2) % device_count] * capacity + arrival
+    behind = jnp.where(owners % 2 == 0, behind, -1)
+    handed_sum = jnp.sum(
+        jnp.where(behind[:, None] == slot_index[None, :], returned[:, 1].reshape(-1)[None, :], 0.0), axis=1
+    )
+    return jnp.log1p(owner_sum + handed_sum)
 
 
 def solution(mesh):

time: 160 us -> 160 us (level)
  starting transfers between devices: 11 us -> 8.13 us
    ppermute x5 -> x4, starting transfers between devices: 11 us -> 8.13 us  [moved(): return lax.ppermute(x, 'blk', [(pos2dev[a], pos2dev[b]) for a, b in moves])]
    ppermute x5 -> x4, waiting for transfers between devices: 31.9 us -> 31.9 us  [moved(): return lax.ppermute(x, 'blk', [(pos2dev[a], pos2dev[b]) for a, b in moves])]
  transfers between devices with their start and end apart: 5 -> 4, of which waited for: 1 -> 1; matrix products, arithmetic and copies ran while one was open for 12% -> 8% of each run, Pallas kernels for 0% -> 0%
where the time goes in v3:
time: 160 us; the launch traced here: 159 us
  blocking collectives  71.1 us (44%)
  waiting for transfers between devices  31.9 us (20%)
  matrix products  24.7 us (15%)
  other arithmetic  14.4 us (9%)
  starting transfers between devices  8.13 us (5%)
  local copies, waits for them, and re-layouts  4.32 us (3%)
  between operations  4.14 us (3%)
    all_to_all x1, blocking collectives, body(): lax.all_to_all(payload, 'blk', split_axis=0, concat_axis=0, tiled=True)  61.2 us
    ppermute x4, waiting for transfers between devices, moved(): return lax.ppermute(x, 'blk', [(pos2dev[a], pos2dev[b]) for a, b in moves])  31.9 us
    dot_general x4, matrix products, step_total(): lax.dot_general(local, remote, (((1,), (1,)), ((), ())), preferred_elemen...  20.6 us
    all_to_all x1, blocking collectives, body(): lax.all_to_all(totals, 'blk', split_axis=0, concat_axis=0, tiled=True)  9.88 us
    ppermute x4, starting transfers between devices, moved(): return lax.ppermute(x, 'blk', [(pos2dev[a], pos2dev[b]) for a, b in moves])  8.13 us
    dot_general x1, matrix products, body(): jnp.dot(hit.astype(jnp.bfloat16), unit, preferred_element_type=jnp.float32)  4.16 us
  transfers between devices with their start and end apart: 4, of which 1 were waited for; matrix products, arithmetic and copies ran while one was open for 8% of the time, Pallas kernels for 0%

profile of v3, /device:TPU:0, one launch (start us, length us, event | category | flops | bytes accessed | tf_op | source)
XLA Modules:
  0.0 158.7 jit_solution(12537210157948387975)
XLA Ops:
  0.0 0.7 broadcast_add_fusion
  0.7 0.7 convert.14
  1.4 0.1 copy.68
  1.5 0.1 reshape.276
  1.6 2.0 %fusion.2 = f32[960]{0:T(1024)S(1)} fusion(bf16[960,1024]{1,0:T(8,128)(2,1)} %param.7), kind=kLoop, calls=%fused_computation.13 | loop fusion | flops 2948160 | bytes 1969920 | tf_op jit(solution)/shard_map/reduce_sum | solution.py:69
  3.6 1.2 convert_reduce_fusion
  4.9 0.7 fusion.30
  5.6 0.6 select_reduce_fusion.2
  6.2 0.1 sub.11
  6.3 0.1 pad.17.clone
  6.4 0.1 copy.69
  6.5 4.2 %fusion.16 = bf16[1024,1024]{1,0:T(8,128)(2,1)S(1)} fusion(bf16[960,1024]{1,0:T(8,128)(2,1)} %param.7, f32[960]{0:T(1024)S(1)} %add_rsqrt_fusion, s32[960]{0:T(1024)S(1)} %get-tuple-element.22), kind=kOutput, calls=%fused_computation.36 | convolution fusion | flops 2018246656 | bytes 4070912 | tf_op jit(solution)/shard_map/dot_general | solution.py:77
  10.6 0.3 pad_maximum_fusion
  11.0 61.2 %all_to_all.10 = bf16[16,65,1024]{2,1,0:T(8,128)(2,1)S(1)} all-to-all(bf16[16,65,1024]{2,1,0:T(8,128)(2,1)S(1)} %pad_maximum_fusion), channel_id=1, replica_groups=mesh['groups'=2,'blk'=16] {'blk'}, dimensions={0} | all-to-all | bytes 4259840 | tf_op jit(solution)/shard_map/all_to_all | solution.py:91
  72.2 0.1 reshape.207
  72.3 0.2 slice.124
  72.6 0.0 copy-start
  72.6 0.0 copy-start.2
  72.6 1.3 copy-done
  73.9 1.5 pad_maximum_fusion.1
  75.5 4.0 %collective-permute-start.2 = (bf16[1040,1024]{1,0:T(8,128)(2,1)}, bf16[1040,1024]{1,0:T(8,128)(2,1)}, u32[]{:S(2)}, u32[]{:S(2)}) collective-permute-start(bf16[1040,1024]{1,0:T(8,128)(2,1)} %pad_maximum_fusion.1), channel_id=1, source_target_pairs={{0,1},{4,5},{8,9},{12,13},{14,15},{10,11},{6,7},{2,3},{16,17},{20,... | collective-permute-start | bytes 6389768 | tf_op jit(solution)/shard_map/ppermute | solution.py:23
  79.5 1.0 collective-permute-start.1
  80.4 3.1 %collective-permute-start = (bf16[1040,1024]{1,0:T(8,128)(2,1)}, bf16[1040,1024]{1,0:T(8,128)(2,1)}, u32[]{:S(2)}, u32[]{:S(2)}) collective-permute-start(bf16[1040,1024]{1,0:T(8,128)(2,1)} %pad_maximum_fusion.1), channel_id=1, source_target_pairs={{0,2},{4,0},{8,4},{12,8},{14,12},{10,14},{6,10},{2,6},{16,18},{20,... | collective-permute-start | bytes 6389768 | tf_op jit(solution)/shard_map/ppermute | solution.py:23
  83.6 0.6 dynamic_slice.9
  88.1 0.1 slice.125
  88.2 0.1 copy.71
  88.3 0.1 constant_dynamic-slice_fusion.1
  88.4 0.1 copy.72
  88.5 0.1 convert_reduce_fusion.4
  88.6 5.5 %bitcast_reduce_fusion.3 = f32[1024,8]{0,1:T(8,128)S(1)} fusion(bf16[1024,1024]{1,0:T(8,128)(2,1)} %bitcast.45, s32[1024]{0:T(1024)S(1)} %reshape.207, pred[1024]{0:T(1024)(128)(4,1)S(1)} %broadcast_compare_fusion.1), kind=kOutput, calls=%fused_computation.5 | convolution fusion | flops 2155864064 | bytes 2135040 | tf_op jit(solution)/shard_map/dot_general | solution.py:29
  94.2 0.1 fusion.24
  94.3 0.0 collective-permute-done.2
  94.3 31.9 %collective-permute-done.1 = bf16[1040,1024]{1,0:T(8,128)(2,1)} collective-permute-done((bf16[1040,1024]{1,0:T(8,128)(2,1)}, bf16[1040,1024]{1,0:T(8,128)(2,1)}, u32[]{:S(2)}, u32[]{:S(2)}) %collective-permute-start.1) | collective-permute-done | bytes 2129952 | tf_op jit(solution)/shard_map/ppermute | solution.py:23
  126.1 0.0 collective-permute-done
  126.1 0.0 collective-permute-start.3
  126.1 0.1 copy.73
  126.2 0.1 convert_reduce_fusion.3
  126.3 0.1 copy.75
  126.4 0.1 convert_reduce_fusion.1
  126.5 0.1 copy.74
  126.6 0.1 convert_reduce_fusion.2
  126.7 0.7 slice_convert_fusion.3
  127.4 0.0 copy-done.1
  127.4 4.6 %bitcast_reduce_fusion.1 = f32[1024,8]{0,1:T(8,128)S(1)} fusion(bf16[1024,1024]{1,0:T(8,128)(2,1)S(1)} %bitcast.46, bf16[1040,1024]{1,0:T(8,128)(2,1)} %collective-permute-done.1, s32[1024]{0:T(1024)S(1)} %reshape.207, s32[1024]{0:T(1024)S(1)} %bitcast.58, pred[1024]{0:T(1024)(128)(4,1)S(1)} %broadcast_compare_fusion.1), kind=kOutput, calls=%fused_computation.3 | convolution fusion | flops 2152718336 | bytes 4236288 | tf_op jit(solution)/shard_map/dot_general | solution.py:29
  132.0 0.1 fusion.22
  132.1 0.7 slice_convert_fusion.2
  132.8 0.0 collective-permute-done.3
  132.9 0.7 broadcast_select_fusion
  133.6 5.2 %bitcast_reduce_fusion.2 = f32[1024,8]{0,1:T(8,128)S(1)} fusion(bf16[1024,1024]{1,0:T(8,128)(2,1)S(1)} %bitcast.47, bf16[1040,1024]{1,0:T(8,128)(2,1)} %collective-permute-done.2, s32[1024]{0:T(1024)S(1)} %reshape.207, s32[1024]{0:T(1024)S(1)} %bitcast.56, pred[]{:T(512)S(6)} %eq.199, pred[1024]{0:T(1024)(128)(4,1)S(1)} %broadcast_compare_fusion.1, ...), kind=kOutput, calls=%fused_computation.4 | convolution fusion | flops 2153766912 | bytes 6333441 | tf_op jit(solution)/shard_map/dot_general | solution.py:29
  138.9 0.1 fusion.23
  138.9 0.7 slice_convert_fusion.1
  139.7 5.2 %bitcast_reduce_fusion = f32[1024,8]{0,1:T(8,128)S(1)} fusion(bf16[1024,1024]{1,0:T(8,128)(2,1)S(1)} %bitcast.48, bf16[1040,1024]{1,0:T(8,128)(2,1)} %collective-permute-done, s32[1024]{0:T(1024)S(1)} %get-tuple-element.16, s32[1024]{0:T(1024)S(1)} %bitcast.57, pred[1024]{0:T(1024)(128)(4,1)S(1)} %get-tuple-element.15, pred[]{:T(512)S(6)} %eq.199, ...), kind=kOutput, calls=%fused_computation.2 | convolution fusion | flops 2153766912 | bytes 6333441 | tf_op jit(solution)/shard_map/dot_general | solution.py:29
  144.9 0.1 fusion.21
  145.0 0.1 stack_reshape.4
  145.1 0.1 select_n.161
  145.2 0.1 reshape.279
  145.3 9.9 %all_to_all.11 = f32[16,1,128]{2,1,0:T(1,128)S(1)} all-to-all(f32[16,1,128]{2,1,0:T(1,128)S(1)} %reshape.279), channel_id=1, replica_groups=mesh['groups'=2,'blk'=16] {'blk'}, dimensions={0} | all-to-all | bytes 16384 | tf_op jit(solution)/shard_map/all_to_all | solution.py:135
  155.2 0.5 broadcast.245
  155.7 0.7 reduce.28
  156.3 0.1 reshape.280
  156.5 0.1 broadcast_in_dim.113
  156.5 0.1 broadcast_in_dim.108
  156.6 1.5 select_reduce_fusion
  158.1 0.6 add_log-plus-one_fusion
  (20 shorter events, 0.2 us)
Async XLA Ops:
  72.6 1.4 copy-start
  72.6 11.0 %copy-start.2 = (s32[16]{0:T(128)S(1)}, s32[16]{0:T(128)}, u32[]{:S(2)}) copy-start(s32[16]{0:T(128)} %constant.70.clone) | copy-start | bytes 196
  75.5 18.8 %collective-permute-start.2 = (bf16[1040,1024]{1,0:T(8,128)(2,1)}, bf16[1040,1024]{1,0:T(8,128)(2,1)}, u32[]{:S(2)}, u32[]{:S(2)}) collective-permute-start(bf16[1040,1024]{1,0:T(8,128)(2,1)} %pad_maximum_fusion.1), channel_id=1, source_target_pairs={{0,1},{4,5},{8,9},{12,13},{14,15},{10,11},{6,7},{2,3},{16,17},{20,... | collective-permute-start | bytes 6389768 | tf_op jit(solution)/shard_map/ppermute | solution.py:23
  79.5 46.6 %collective-permute-start.1 = (bf16[1040,1024]{1,0:T(8,128)(2,1)}, bf16[1040,1024]{1,0:T(8,128)(2,1)}, u32[]{:S(2)}, u32[]{:S(2)}) collective-permute-start(bf16[1040,1024]{1,0:T(8,128)(2,1)} %pad_maximum_fusion.1), channel_id=1, source_target_pairs={{0,4},{1,5},{4,8},{5,9},{8,12},{9,13},{12,14},{13,15},{14,10},{15,... | collective-permute-start | bytes 6389768 | tf_op jit(solution)/shard_map/ppermute | solution.py:23
  80.4 45.7 %collective-permute-start = (bf16[1040,1024]{1,0:T(8,128)(2,1)}, bf16[1040,1024]{1,0:T(8,128)(2,1)}, u32[]{:S(2)}, u32[]{:S(2)}) collective-permute-start(bf16[1040,1024]{1,0:T(8,128)(2,1)} %pad_maximum_fusion.1), channel_id=1, source_target_pairs={{0,2},{4,0},{8,4},{12,8},{14,12},{10,14},{6,10},{2,6},{16,18},{20,... | collective-permute-start | bytes 6389768 | tf_op jit(solution)/shard_map/ppermute | solution.py:23
  88.6 38.8 %copy-start.1 = (bf16[16,64,1024]{2,1,0:T(8,128)(2,1)S(1)}, bf16[16,64,1024]{2,1,0:T(8,128)(2,1)}, u32[]{:S(2)}) copy-start(bf16[16,64,1024]{2,1,0:T(8,128)(2,1)} %copy-done) | copy-start | bytes 6291460
  126.1 6.7 %collective-permute-start.3 = (bf16[1040,1024]{1,0:T(8,128)(2,1)}, bf16[1040,1024]{1,0:T(8,128)(2,1)}, u32[]{:S(2)}, u32[]{:S(2)}) collective-permute-start(bf16[1040,1024]{1,0:T(8,128)(2,1)} %collective-permute-done.1), channel_id=1, source_target_pairs={{0,1},{1,0},{4,5},{5,4},{8,9},{9,8},{12,13},{13,12},{14,15},{15,14... | collective-permute-start | bytes 6389768 | tf_op jit(solution)/shard_map/ppermute | solution.py:23

commit v4 on v3

--- a/solution.py
+++ b/solution.py
@@ -6,7 +6,6 @@
 
 SLOTS = 1024
 STEPS = 4
-ID_ROWS = 16
 
 
 SHARPNESS_KNOB = 32.0
@@ -41,15 +40,10 @@
     return jnp.sum(per_block * counts[:, None, :], axis=2)
 
 
-def pack(held, held_ids):
-    feature_span = held.shape[1]
-    id_rows = jnp.pad(held_ids.astype(jnp.bfloat16), (0, ID_ROWS * feature_span - held_ids.shape[0]))
-    return jnp.concatenate([held, id_rows.reshape(ID_ROWS, feature_span)], axis=0)
-
-
-def unpack(packed):
-    slot_count = packed.shape[0] - ID_ROWS
-    return packed[:slot_count], packed[slot_count:].reshape(-1)[:slot_count].astype(jnp.int32)
+def unpack(packed, capacity):
+    chunks = packed.reshape(-1, capacity + 1, packed.shape[-1])
+    held = chunks[:, :capacity].reshape(-1, packed.shape[-1])
+    return held, chunks[:, capacity, :capacity].reshape(-1).astype(jnp.int32)
 
 
 def body(embeddings, owners, clusters, pairs):
@@ -89,9 +83,6 @@
     id_row = jnp.pad(side, ((0, 0), (0, feature_span - capacity - pair_count)))[:, None, :]
     payload = jnp.concatenate([outgoing.reshape(device_count, capacity, feature_span), id_row], axis=1)
     arrived = lax.all_to_all(payload, "blk", split_axis=0, concat_axis=0, tiled=True)
-    own = arrived[:, :capacity].reshape(slot_count, feature_span)
-    own_ids = arrived[:, capacity, :capacity].reshape(slot_count).astype(jnp.int32)
-
     all_pairs = (
         arrived[:, capacity, capacity : capacity + pair_count].astype(jnp.int32).reshape((device_count,) + pairs.shape[1:])
     )
@@ -100,17 +91,17 @@
 
     n = device_count
     evens = range(0, n, 2)
-    packed = pack(own, own_ids)
-    back2 = moved(packed, pos2dev, [(p, (p - 2) % n) for p in evens])
-    fwd2 = moved(packed, pos2dev, [(p, (p + 2) % n) for p in range(n)])
-    across = moved(packed, pos2dev, [(p, p + 1) for p in evens])
+    fwd2 = moved(arrived, pos2dev, [(p, (p + 2) % n) for p in range(n)])
+    back2 = moved(arrived, pos2dev, [(p, (p - 2) % n) for p in evens])
+    across = moved(arrived, pos2dev, [(p, p + 1) for p in evens])
+    own, own_ids = unpack(arrived, capacity)
     total = step_total(own, own_ids, own, own_ids, my_pairs[0], True)
     total, back2, fwd2, across = lax.optimization_barrier((total, back2, fwd2, across))
     fwd2_swapped = moved(fwd2, pos2dev, [(p, p ^ 1) for p in range(n)])
-    back2_held, back2_ids = unpack(back2)
-    fwd2_held, fwd2_ids = unpack(fwd2)
-    across_held, across_ids = unpack(across)
-    swapped_held, swapped_ids = unpack(fwd2_swapped)
+    back2_held, back2_ids = unpack(back2, capacity)
+    fwd2_held, fwd2_ids = unpack(fwd2, capacity)
+    across_held, across_ids = unpack(across, capacity)
+    swapped_held, swapped_ids = unpack(fwd2_swapped, capacity)
 
     total = total + step_total(
         own,

time: 160 us -> 173 us (1.081)
  local copies, waits for them, and re-layouts: 4.32 us -> 22.3 us
  matrix products: 24.7 us -> 16.5 us
  other arithmetic: 14.4 us -> 17.9 us
    optimization_barrier x0 -> x3, local copies, waits for them, and re-layouts: none -> 12.6 us  [body(): lax.optimization_barrier((total, back2, fwd2, across))]
    dot_general x4, matrix products: 20.6 us -> 12.3 us  [step_total(): lax.dot_general(local, remote, (((1,), (1,)), ((), ())), preferred_elemen...]
    select_n x0 -> x2, other arithmetic: none -> 4.28 us  [the longest x1 2.66 us: body(): jnp.where(odd, across_held, swapped_held)]
    slice x2 -> x4, local copies, waits for them, and re-layouts: 0.31 us -> 3.52 us  [unpack(): held = chunks[:, :capacity].reshape(-1, packed.shape[-1])]
    all_to_all x0 -> x1, local copies, waits for them, and re-layouts: none -> 2.52 us  [body(): lax.all_to_all(payload, 'blk', split_axis=0, concat_axis=0, tiled=True)]
  transfers between devices with their start and end apart: 4 -> 4, of which waited for: 1 -> 1; matrix products, arithmetic and copies ran while one was open for 8% -> 15% of each run, Pallas kernels for 0% -> 0%
where the time goes in v4:
time: 173 us
  blocking collectives  71 us (41%)
  waiting for transfers between devices  32.7 us (19%)
  local copies, waits for them, and re-layouts  22.3 us (13%)
  other arithmetic  17.9 us (10%)
  matrix products  16.5 us (10%)
  starting transfers between devices  8.17 us (5%)
  between operations  4.2 us (2%)
    all_to_all x1, blocking collectives, body(): lax.all_to_all(payload, 'blk', split_axis=0, concat_axis=0, tiled=True)  61.2 us
    ppermute x4, waiting for transfers between devices, moved(): return lax.ppermute(x, 'blk', [(pos2dev[a], pos2dev[b]) for a, b in moves])  32.7 us
    optimization_barrier x3, local copies, waits for them, and re-layouts, body(): lax.optimization_barrier((total, back2, fwd2, across))  12.6 us
    dot_general x4, matrix products, step_total(): lax.dot_general(local, remote, (((1,), (1,)), ((), ())), preferred_elemen...  12.3 us
    all_to_all x1, blocking collectives, body(): lax.all_to_all(totals, 'blk', split_axis=0, concat_axis=0, tiled=True)  9.87 us
    ppermute x4, starting transfers between devices, moved(): return lax.ppermute(x, 'blk', [(pos2dev[a], pos2dev[b]) for a, b in moves])  8.17 us
    dot_general x1, matrix products, body(): jnp.dot(hit.astype(jnp.bfloat16), unit, preferred_element_type=jnp.float32)  4.16 us
    slice x4, local copies, waits for them, and re-layouts, unpack(): held = chunks[:, :capacity].reshape(-1, packed.shape[-1])  3.52 us
  transfers between devices with their start and end apart: 4, of which 1 were waited for; matrix products, arithmetic and copies ran while one was open for 15% of the time, Pallas kernels for 0%

profile of v4, /device:TPU:0, one launch (start us, length us, event | category | flops | bytes accessed | tf_op | source)
XLA Modules:
  0.0 172.7 jit_solution(3470502388822408427)
XLA Ops:
  0.0 0.7 broadcast_add_fusion
  0.7 0.7 convert.16
  1.4 0.1 copy.90
  1.5 0.1 reshape.303
  1.6 2.0 %fusion.2 = f32[960]{0:T(1024)S(1)} fusion(bf16[960,1024]{1,0:T(8,128)(2,1)} %param.7), kind=kLoop, calls=%fused_computation.13 | loop fusion | flops 2948160 | bytes 1969920 | tf_op jit(solution)/shard_map/reduce_sum | solution.py:63
  3.6 1.2 convert_reduce_fusion
  4.9 0.7 fusion.21
  5.6 0.6 select_reduce_fusion.2
  6.2 0.1 sub.11
  6.3 0.1 pad.10.clone
  6.5 4.2 %fusion.9 = bf16[1024,1024]{1,0:T(8,128)(2,1)S(1)} fusion(bf16[960,1024]{1,0:T(8,128)(2,1)} %param.7, f32[960]{0:T(1024)S(1)} %add_rsqrt_fusion, s32[960]{0:T(1024)S(1)} %get-tuple-element.24), kind=kOutput, calls=%fused_computation.30 | convolution fusion | flops 2018246656 | bytes 4070912 | tf_op jit(solution)/shard_map/dot_general | solution.py:71
  10.6 0.3 pad_maximum_fusion
  11.0 61.2 %all_to_all.10 = bf16[16,65,1024]{2,1,0:T(8,128)(2,1)S(1)} all-to-all(bf16[16,65,1024]{2,1,0:T(8,128)(2,1)S(1)} %pad_maximum_fusion), channel_id=1, replica_groups=mesh['groups'=2,'blk'=16] {'blk'}, dimensions={0} | all-to-all | bytes 4259840 | tf_op jit(solution)/shard_map/all_to_all | solution.py:85
  72.2 2.5 %copy.92 = bf16[16,65,1024]{2,0,1:T(8,128)(2,1)} copy(bf16[16,65,1024]{2,1,0:T(8,128)(2,1)S(1)} %all_to_all.10) | data formatting | bytes 4259840 | tf_op jit(solution)/shard_map/all_to_all | solution.py:85
  74.7 4.1 %collective-permute-start.2 = (bf16[16,65,1024]{2,0,1:T(8,128)(2,1)}, bf16[16,65,1024]{2,0,1:T(8,128)(2,1)}, u32[]{:S(2)}, u32[]{:S(2)}) collective-permute-start(bf16[16,65,1024]{2,0,1:T(8,128)(2,1)} %copy.92), channel_id=1, source_target_pairs={{0,1},{4,5},{8,9},{12,13},{14,15},{10,11},{6,7},{2,3},{16,17},{20,... | collective-permute-start | bytes 6389768 | tf_op jit(solution)/shard_map/ppermute | solution.py:22
  78.8 1.0 collective-permute-start.1
  79.7 3.1 %collective-permute-start = (bf16[16,65,1024]{2,0,1:T(8,128)(2,1)}, bf16[16,65,1024]{2,0,1:T(8,128)(2,1)}, u32[]{:S(2)}, u32[]{:S(2)}) collective-permute-start(bf16[16,65,1024]{2,0,1:T(8,128)(2,1)} %copy.92), channel_id=1, source_target_pairs={{0,2},{4,0},{8,4},{12,8},{14,12},{10,14},{6,10},{2,6},{16,18},{20,... | collective-permute-start | bytes 6389768 | tf_op jit(solution)/shard_map/ppermute | solution.py:22
  82.9 0.6 dynamic_slice.9
  87.5 0.8 slice_convert_fusion.2
  88.3 0.1 copy.93
  88.4 0.1 constant_dynamic-slice_fusion.1
  88.5 0.1 copy.100
  88.6 0.1 convert_reduce_fusion.3
  88.7 0.1 copy.94
  88.8 0.1 convert_reduce_fusion.4
  88.9 0.1 copy.104
  89.0 0.1 convert_reduce_fusion.1
  89.1 0.1 copy.102
  89.2 0.2 slice.112
  89.4 3.2 %bitcast_reduce_fusion.3 = f32[1024,8]{0,1:T(8,128)S(1)} fusion(bf16[1024,1024]{1,0:T(8,128)(2,1)S(1)} %bitcast.58, s32[1024]{0:T(1024)S(1)} %reshape.232, pred[1024]{0:T(1024)(128)(4,1)S(1)} %broadcast_compare_fusion.1), kind=kOutput, calls=%fused_computation.5 | convolution fusion | flops 2155864064 | bytes 2135040 | tf_op jit(solution)/shard_map/dot_general | solution.py:28
  92.6 0.1 fusion.15
  92.7 32.7 %collective-permute-done.1 = bf16[16,65,1024]{2,0,1:T(8,128)(2,1)} collective-permute-done((bf16[16,65,1024]{2,0,1:T(8,128)(2,1)}, bf16[16,65,1024]{2,0,1:T(8,128)(2,1)}, u32[]{:S(2)}, u32[]{:S(2)}) %collective-permute-start.1) | collective-permute-done | bytes 2129952 | tf_op jit(solution)/shard_map/ppermute | solution.py:22
  125.4 0.1 convert_reduce_fusion.2
  125.4 4.2 %copy.101 = bf16[16,65,1024]{2,1,0:T(8,128)(2,1)} copy(bf16[16,65,1024]{2,0,1:T(8,128)(2,1)} %collective-permute-done.1) | data formatting | bytes 4259840 | tf_op jit(solution)/shard_map/optimization_barrier | solution.py:99
  129.6 4.2 %copy.98 = bf16[16,65,1024]{2,1,0:T(8,128)(2,1)} copy(bf16[16,65,1024]{2,0,1:T(8,128)(2,1)} %collective-permute-done.2) | data formatting | bytes 4259840 | tf_op jit(solution)/shard_map/optimization_barrier | solution.py:99
  133.8 0.7 slice_convert_fusion.5
  134.5 0.1 reshape.234
  134.6 4.2 %copy.103 = bf16[16,65,1024]{2,1,0:T(8,128)(2,1)} copy(bf16[16,65,1024]{2,0,1:T(8,128)(2,1)} %collective-permute-done) | data formatting | bytes 4259840 | tf_op jit(solution)/shard_map/optimization_barrier | solution.py:99
  138.8 0.7 slice_convert_fusion.3
  139.5 0.1 reshape.237
  139.6 0.7 slice_convert_fusion.4
  140.3 0.1 reshape.236
  140.4 1.6 slice-done
  141.9 0.6 copy-done.4
  142.6 3.0 %bitcast_reduce_fusion.1 = f32[1024,8]{0,1:T(8,128)S(1)} fusion(bf16[1024,1024]{1,0:T(8,128)(2,1)S(1)} %bitcast.59, bf16[1024,1024]{1,0:T(8,128)(2,1)S(1)} %bitcast.56, s32[1024]{0:T(1024)S(1)} %reshape.232, s32[1024]{0:T(1024)S(1)} %reshape.236, pred[1024]{0:T(1024)(128)(4,1)S(1)} %broadcast_compare_fusion.1), kind=kOutput, calls=%fused_computation.3 | convolution fusion | flops 2152718336 | bytes 4236288 | tf_op jit(solution)/shard_map/dot_general | solution.py:28
  145.6 0.1 fusion.13
  145.7 1.6 slice_select_fusion
  147.4 0.8 slice_convert_fusion.1
  148.2 0.1 reshape.235
  148.3 1.8 %slice.116 = bf16[16,64,1024]{2,0,1:T(8,128)(2,1)S(1)} slice(bf16[16,65,1024]{2,0,1:T(8,128)(2,1)} %collective-permute-done.3), slice={[0:16], [0:64], [0:1024]} | slice | bytes 4194304 | tf_op jit(solution)/shard_map/slice | solution.py:45
  150.1 2.7 %slice_select_fusion.1 = (bf16[16,64,1024]{2,1,0:T(8,128)(2,1)S(1)}, bf16[16,64,1024]{2,1,0:T(8,128)(2,1)S(1)}) fusion(bf16[16,65,1024]{2,1,0:T(8,128)(2,1)S(1)} %copy-done.1, pred[]{:T(512)S(6)} %eq.190, bf16[16,64,1024]{2,0,1:T(8,128)(2,1)S(1)} %slice.116), kind=kLoop, calls=%fused_computation.27 | loop fusion | flops 1048576 | bytes 8388609 | tf_op jit(solution)/shard_map/jit(_where)/select_n | solution.py:109
  152.7 3.0 %bitcast_reduce_fusion.2 = f32[1024,8]{0,1:T(8,128)S(1)} fusion(bf16[1024,1024]{1,0:T(8,128)(2,1)S(1)} %bitcast.60, bf16[1024,1024]{1,0:T(8,128)(2,1)S(1)} %bitcast.63, s32[1024]{0:T(1024)S(1)} %reshape.232, s32[1024]{0:T(1024)S(1)} %broadcast_select_fusion.2, pred[1024]{0:T(1024)(128)(4,1)S(1)} %broadcast_compare_fusion.1), kind=kOutput, calls=%fused_computation.4 | convolution fusion | flops 2152718336 | bytes 4236288 | tf_op jit(solution)/shard_map/dot_general | solution.py:28
  155.8 0.1 fusion.14
  155.9 3.1 %bitcast_reduce_fusion = f32[1024,8]{0,1:T(8,128)S(1)} fusion(bf16[1024,1024]{1,0:T(8,128)(2,1)S(1)} %bitcast.57, bf16[1024,1024]{1,0:T(8,128)(2,1)S(1)} %bitcast.62, s32[1024]{0:T(1024)S(1)} %get-tuple-element.16, s32[1024]{0:T(1024)S(1)} %reshape.235, pred[1024]{0:T(1024)(128)(4,1)S(1)} %get-tuple-element.15), kind=kOutput, calls=%fused_computation.2 | convolution fusion | flops 2152718336 | bytes 4236288 | tf_op jit(solution)/shard_map/dot_general | solution.py:28
  159.0 0.1 fusion.12
  159.1 0.1 stack_reshape.4
  159.2 0.1 select_n.169
  159.3 0.1 reshape.306
  159.3 9.9 %all_to_all.11 = f32[16,1,128]{2,1,0:T(1,128)S(1)} all-to-all(f32[16,1,128]{2,1,0:T(1,128)S(1)} %reshape.306), channel_id=1, replica_groups=mesh['groups'=2,'blk'=16] {'blk'}, dimensions={0} | all-to-all | bytes 16384 | tf_op jit(solution)/shard_map/all_to_all | solution.py:126
  169.2 0.5 broadcast.248
  169.7 0.7 reduce.28
  170.4 0.1 reshape.307
  170.7 1.5 select_reduce_fusion
  172.1 0.6 add_log-plus-one_fusion
  (37 shorter events, 0.5 us)
Async XLA Ops:
  72.2 10.7 %copy-start.6 = (s32[16]{0:T(128)S(1)}, s32[16]{0:T(128)}, u32[]{:S(2)}) copy-start(s32[16]{0:T(128)} %constant.70.clone) | copy-start | bytes 196
  74.7 18.0 %collective-permute-start.2 = (bf16[16,65,1024]{2,0,1:T(8,128)(2,1)}, bf16[16,65,1024]{2,0,1:T(8,128)(2,1)}, u32[]{:S(2)}, u32[]{:S(2)}) collective-permute-start(bf16[16,65,1024]{2,0,1:T(8,128)(2,1)} %copy.92), channel_id=1, source_target_pairs={{0,1},{4,5},{8,9},{12,13},{14,15},{10,11},{6,7},{2,3},{16,17},{20,... | collective-permute-start | bytes 6389768 | tf_op jit(solution)/shard_map/ppermute | solution.py:22
  78.8 46.6 %collective-permute-start.1 = (bf16[16,65,1024]{2,0,1:T(8,128)(2,1)}, bf16[16,65,1024]{2,0,1:T(8,128)(2,1)}, u32[]{:S(2)}, u32[]{:S(2)}) collective-permute-start(bf16[16,65,1024]{2,0,1:T(8,128)(2,1)} %copy.92), channel_id=1, source_target_pairs={{0,4},{1,5},{4,8},{5,9},{8,12},{9,13},{12,14},{13,15},{14,10},{15,... | collective-permute-start | bytes 6389768 | tf_op jit(solution)/shard_map/ppermute | solution.py:22
  79.7 45.6 %collective-permute-start = (bf16[16,65,1024]{2,0,1:T(8,128)(2,1)}, bf16[16,65,1024]{2,0,1:T(8,128)(2,1)}, u32[]{:S(2)}, u32[]{:S(2)}) collective-permute-start(bf16[16,65,1024]{2,0,1:T(8,128)(2,1)} %copy.92), channel_id=1, source_target_pairs={{0,2},{4,0},{8,4},{12,8},{14,12},{10,14},{6,10},{2,6},{16,18},{20,... | collective-permute-start | bytes 6389768 | tf_op jit(solution)/shard_map/ppermute | solution.py:22
  89.3 3.2 %copy-start.3 = (bf16[16,64,1024]{2,1,0:T(8,128)(2,1)}, bf16[16,64,1024]{2,1,0:T(8,128)(2,1)S(1)}, u32[]{:S(2)}) copy-start(bf16[16,64,1024]{2,1,0:T(8,128)(2,1)S(1)} %slice.112) | copy-start | bytes 6291460
  125.4 22.0 %collective-permute-start.3 = (bf16[16,65,1024]{2,0,1:T(8,128)(2,1)}, bf16[16,65,1024]{2,0,1:T(8,128)(2,1)}, u32[]{:S(2)}, u32[]{:S(2)}) collective-permute-start(bf16[16,65,1024]{2,0,1:T(8,128)(2,1)} %collective-permute-done.1), channel_id=1, source_target_pairs={{0,1},{1,0},{4,5},{5,4},{8,9},{9,8},{12,13},{13,12},{14,15},{15,14... | collective-permute-start | bytes 6389768 | tf_op jit(solution)/shard_map/ppermute | solution.py:22
  140.3 1.6 slice-start
  140.4 2.2 %copy-start.4 = (bf16[16,64,1024]{2,1,0:T(8,128)(2,1)S(1)}, bf16[16,64,1024]{2,1,0:T(8,128)(2,1)}, u32[]{:S(2)}) copy-start(bf16[16,64,1024]{2,1,0:T(8,128)(2,1)} %copy-done.3) | copy-start | bytes 6291460
  142.6 3.1 %copy-start = (bf16[16,65,1024]{2,1,0:T(8,128)(2,1)S(1)}, bf16[16,65,1024]{2,1,0:T(8,128)(2,1)}, u32[]{:S(2)}) copy-start(bf16[16,65,1024]{2,1,0:T(8,128)(2,1)} %copy.103) | copy-start | bytes 6389764
  147.4 2.7 %copy-start.1 = (bf16[16,65,1024]{2,1,0:T(8,128)(2,1)S(1)}, bf16[16,65,1024]{2,1,0:T(8,128)(2,1)}, u32[]{:S(2)}) copy-start(bf16[16,65,1024]{2,1,0:T(8,128)(2,1)} %copy.98) | copy-start | bytes 6389764
  150.0 2.7 %copy-start.5 = (bf16[16,64,1024]{2,1,0:T(8,128)(2,1)S(1)}, bf16[16,64,1024]{2,1,0:T(8,128)(2,1)}, u32[]{:S(2)}) copy-start(bf16[16,64,1024]{2,1,0:T(8,128)(2,1)} %copy-done.3) | copy-start | bytes 6291460
  152.7 3.1 %copy-start.2 = (bf16[16,64,1024]{2,1,0:T(8,128)(2,1)S(1)}, bf16[16,64,1024]{2,1,0:T(8,128)(2,1)}, u32[]{:S(2)}) copy-start(bf16[16,64,1024]{2,1,0:T(8,128)(2,1)} %slice_select_fusion) | copy-start | bytes 6291460

commit v5 on v3

--- a/solution.py
+++ b/solution.py
@@ -132,7 +132,8 @@
     total = total + jnp.where(odd, last, 0.0)
     forward_part = jnp.where(odd, 0.0, last)
     totals = jnp.stack([total.reshape(device_count, capacity), forward_part.reshape(device_count, capacity)], axis=1)
-    returned = lax.all_to_all(totals, "blk", split_axis=0, concat_axis=0, tiled=True)
+    gathered = lax.all_gather(totals, "blk", axis=0, tiled=False)
+    returned = gathered[:, lax.axis_index("blk")]
     owner_sum = jnp.sum(
         jnp.where(place[:, None] == slot_index[None, :], returned[:, 0].reshape(-1)[None, :], 0.0), axis=1
     )

time: 160 us -> 168 us (1.050)
  blocking collectives: 71.1 us -> 81.2 us
    all_gather x0 -> x1, blocking collectives: none -> 20 us  [body(): gathered = lax.all_gather(totals, 'blk', axis=0, tiled=False)]
    all_to_all x1 -> x0, blocking collectives: 9.88 us -> none  [body(): lax.all_to_all(totals, 'blk', split_axis=0, concat_axis=0, tiled=True)]
where the time goes in v5:
time: 168 us; the launch traced here: 167 us
  blocking collectives  81.2 us (48%)
  waiting for transfers between devices  31.9 us (19%)
  matrix products  24.7 us (15%)
  other arithmetic  13.7 us (8%)
  starting transfers between devices  8.13 us (5%)
  between operations  4.13 us (2%)
  local copies, waits for them, and re-layouts  3.6 us (2%)
    all_to_all x1, blocking collectives, body(): lax.all_to_all(payload, 'blk', split_axis=0, concat_axis=0, tiled=True)  61.2 us
    ppermute x4, waiting for transfers between devices, moved(): return lax.ppermute(x, 'blk', [(pos2dev[a], pos2dev[b]) for a, b in moves])  31.9 us
    dot_general x4, matrix products, step_total(): lax.dot_general(local, remote, (((1,), (1,)), ((), ())), preferred_elemen...  20.6 us
    all_gather x1, blocking collectives, body(): gathered = lax.all_gather(totals, 'blk', axis=0, tiled=False)  20 us
    ppermute x4, starting transfers between devices, moved(): return lax.ppermute(x, 'blk', [(pos2dev[a], pos2dev[b]) for a, b in moves])  8.13 us
    dot_general x1, matrix products, body(): jnp.dot(hit.astype(jnp.bfloat16), unit, preferred_element_type=jnp.float32)  4.16 us
  transfers between devices with their start and end apart: 4, of which 1 were waited for; matrix products, arithmetic and copies ran while one was open for 8% of the time, Pallas kernels for 0%

profile of v5, /device:TPU:0, one launch (start us, length us, event | category | flops | bytes accessed | tf_op | source)
XLA Modules:
  0.0 167.4 jit_solution(11449285792742456386)
XLA Ops:
  0.0 0.7 broadcast_add_fusion
  0.7 0.7 convert.14
  1.4 0.1 copy.68
  1.5 0.1 reshape.266
  1.6 2.0 %fusion.2 = f32[960]{0:T(1024)S(1)} fusion(bf16[960,1024]{1,0:T(8,128)(2,1)} %param.7), kind=kLoop, calls=%fused_computation.13 | loop fusion | flops 2948160 | bytes 1969920 | tf_op jit(solution)/shard_map/reduce_sum | solution.py:69
  3.6 1.2 convert_reduce_fusion
  4.9 0.7 fusion.30
  5.6 0.6 select_reduce_fusion.2
  6.2 0.1 sub.11
  6.3 0.1 pad.17.clone
  6.4 0.1 copy.69
  6.5 4.2 %fusion.16 = bf16[1024,1024]{1,0:T(8,128)(2,1)S(1)} fusion(bf16[960,1024]{1,0:T(8,128)(2,1)} %param.7, f32[960]{0:T(1024)S(1)} %add_rsqrt_fusion, s32[960]{0:T(1024)S(1)} %get-tuple-element.22), kind=kOutput, calls=%fused_computation.36 | convolution fusion | flops 2018246656 | bytes 4070912 | tf_op jit(solution)/shard_map/dot_general | solution.py:77
  10.6 0.3 pad_maximum_fusion
  11.0 61.2 %all_to_all.5 = bf16[16,65,1024]{2,1,0:T(8,128)(2,1)S(1)} all-to-all(bf16[16,65,1024]{2,1,0:T(8,128)(2,1)S(1)} %pad_maximum_fusion), channel_id=1, replica_groups=mesh['groups'=2,'blk'=16] {'blk'}, dimensions={0} | all-to-all | bytes 4259840 | tf_op jit(solution)/shard_map/all_to_all | solution.py:91
  72.2 0.1 reshape.207
  72.3 0.2 slice.124
  72.6 0.0 copy-start
  72.6 0.0 copy-start.2
  72.6 1.3 copy-done
  73.9 1.5 pad_maximum_fusion.1
  75.5 4.0 %collective-permute-start.2 = (bf16[1040,1024]{1,0:T(8,128)(2,1)}, bf16[1040,1024]{1,0:T(8,128)(2,1)}, u32[]{:S(2)}, u32[]{:S(2)}) collective-permute-start(bf16[1040,1024]{1,0:T(8,128)(2,1)} %pad_maximum_fusion.1), channel_id=1, source_target_pairs={{0,1},{4,5},{8,9},{12,13},{14,15},{10,11},{6,7},{2,3},{16,17},{20,... | collective-permute-start | bytes 6389768 | tf_op jit(solution)/shard_map/ppermute | solution.py:23
  79.5 1.0 collective-permute-start.1
  80.4 3.1 %collective-permute-start = (bf16[1040,1024]{1,0:T(8,128)(2,1)}, bf16[1040,1024]{1,0:T(8,128)(2,1)}, u32[]{:S(2)}, u32[]{:S(2)}) collective-permute-start(bf16[1040,1024]{1,0:T(8,128)(2,1)} %pad_maximum_fusion.1), channel_id=1, source_target_pairs={{0,2},{4,0},{8,4},{12,8},{14,12},{10,14},{6,10},{2,6},{16,18},{20,... | collective-permute-start | bytes 6389768 | tf_op jit(solution)/shard_map/ppermute | solution.py:23
  83.6 0.0 copy-done.2
  83.6 0.6 dynamic_slice.12
  88.1 0.1 slice.125
  88.2 0.1 copy.71
  88.3 0.1 constant_dynamic-slice_fusion.1
  88.4 0.1 copy.72
  88.5 0.1 convert_reduce_fusion.4
  88.6 0.0 copy-start.1
  88.6 5.5 %bitcast_reduce_fusion.3 = f32[1024,8]{0,1:T(8,128)S(1)} fusion(bf16[1024,1024]{1,0:T(8,128)(2,1)} %bitcast.51, s32[1024]{0:T(1024)S(1)} %reshape.207, pred[1024]{0:T(1024)(128)(4,1)S(1)} %broadcast_compare_fusion.1), kind=kOutput, calls=%fused_computation.5 | convolution fusion | flops 2155864064 | bytes 2135040 | tf_op jit(solution)/shard_map/dot_general | solution.py:29
  94.2 0.1 fusion.24
  94.3 0.0 collective-permute-done.2
  94.3 31.9 %collective-permute-done.1 = bf16[1040,1024]{1,0:T(8,128)(2,1)} collective-permute-done((bf16[1040,1024]{1,0:T(8,128)(2,1)}, bf16[1040,1024]{1,0:T(8,128)(2,1)}, u32[]{:S(2)}, u32[]{:S(2)}) %collective-permute-start.1) | collective-permute-done | bytes 2129952 | tf_op jit(solution)/shard_map/ppermute | solution.py:23
  126.1 0.0 collective-permute-done
  126.1 0.0 collective-permute-start.3
  126.1 0.1 copy.73
  126.2 0.1 convert_reduce_fusion.3
  126.3 0.1 copy.75
  126.4 0.1 convert_reduce_fusion.1
  126.5 0.1 copy.74
  126.6 0.1 convert_reduce_fusion.2
  126.7 0.7 slice_convert_fusion.3
  127.4 0.0 copy-done.1
  127.4 4.6 %bitcast_reduce_fusion.1 = f32[1024,8]{0,1:T(8,128)S(1)} fusion(bf16[1024,1024]{1,0:T(8,128)(2,1)S(1)} %bitcast.52, bf16[1040,1024]{1,0:T(8,128)(2,1)} %collective-permute-done.1, s32[1024]{0:T(1024)S(1)} %reshape.207, s32[1024]{0:T(1024)S(1)} %bitcast.66, pred[1024]{0:T(1024)(128)(4,1)S(1)} %broadcast_compare_fusion.1), kind=kOutput, calls=%fused_computation.3 | convolution fusion | flops 2152718336 | bytes 4236288 | tf_op jit(solution)/shard_map/dot_general | solution.py:29
  132.0 0.1 fusion.22
  132.1 0.7 slice_convert_fusion.2
  132.8 0.0 collective-permute-done.3
  132.9 0.7 broadcast_select_fusion
  133.6 5.2 %bitcast_reduce_fusion.2 = f32[1024,8]{0,1:T(8,128)S(1)} fusion(bf16[1024,1024]{1,0:T(8,128)(2,1)S(1)} %bitcast.53, bf16[1040,1024]{1,0:T(8,128)(2,1)} %collective-permute-done.2, s32[1024]{0:T(1024)S(1)} %reshape.207, s32[1024]{0:T(1024)S(1)} %bitcast.64, pred[]{:T(512)S(6)} %eq.199, pred[1024]{0:T(1024)(128)(4,1)S(1)} %broadcast_compare_fusion.1, ...), kind=kOutput, calls=%fused_computation.4 | convolution fusion | flops 2153766912 | bytes 6333441 | tf_op jit(solution)/shard_map/dot_general | solution.py:29
  138.9 0.1 fusion.23
  138.9 0.7 slice_convert_fusion.1
  139.7 5.2 %bitcast_reduce_fusion = f32[1024,8]{0,1:T(8,128)S(1)} fusion(bf16[1024,1024]{1,0:T(8,128)(2,1)S(1)} %bitcast.54, bf16[1040,1024]{1,0:T(8,128)(2,1)} %collective-permute-done, s32[1024]{0:T(1024)S(1)} %get-tuple-element.14, s32[1024]{0:T(1024)S(1)} %bitcast.65, pred[1024]{0:T(1024)(128)(4,1)S(1)} %get-tuple-element.13, pred[]{:T(512)S(6)} %eq.199, ...), kind=kOutput, calls=%fused_computation.2 | convolution fusion | flops 2153766912 | bytes 6333441 | tf_op jit(solution)/shard_map/dot_general | solution.py:29
  144.9 0.1 fusion.21
  145.0 0.1 stack_reshape.4
  145.1 0.1 select_n.162
  145.2 20.0 %all-gather = f32[256,2,64]{2,0,1:T(8,128)S(1)} all-gather(f32[16,2,64]{2,0,1:T(8,128)S(1)} %pad_maximum_fusion.2), channel_id=2, replica_groups=mesh['groups'=2,'blk'=16] {'blk'}, dimensions={0}, use_global_device_ids=true | all-gather | bytes 139264 | tf_op jit(solution)/shard_map/all_gather | solution.py:135
  165.2 0.1 broadcast_in_dim.113
  165.2 0.1 broadcast_in_dim.108
  165.3 1.5 select_reduce_fusion
  166.8 0.6 add_log-plus-one_fusion
  (19 shorter events, 0.2 us)
Async XLA Ops:
  72.6 1.4 copy-start
  72.6 11.0 %copy-start.2 = (s32[16]{0:T(128)S(1)}, s32[16]{0:T(128)}, u32[]{:S(2)}) copy-start(s32[16]{0:T(128)} %constant.70.clone) | copy-start | bytes 196
  75.5 18.8 %collective-permute-start.2 = (bf16[1040,1024]{1,0:T(8,128)(2,1)}, bf16[1040,1024]{1,0:T(8,128)(2,1)}, u32[]{:S(2)}, u32[]{:S(2)}) collective-permute-start(bf16[1040,1024]{1,0:T(8,128)(2,1)} %pad_maximum_fusion.1), channel_id=1, source_target_pairs={{0,1},{4,5},{8,9},{12,13},{14,15},{10,11},{6,7},{2,3},{16,17},{20,... | collective-permute-start | bytes 6389768 | tf_op jit(solution)/shard_map/ppermute | solution.py:23
  79.5 46.6 %collective-permute-start.1 = (bf16[1040,1024]{1,0:T(8,128)(2,1)}, bf16[1040,1024]{1,0:T(8,128)(2,1)}, u32[]{:S(2)}, u32[]{:S(2)}) collective-permute-start(bf16[1040,1024]{1,0:T(8,128)(2,1)} %pad_maximum_fusion.1), channel_id=1, source_target_pairs={{0,4},{1,5},{4,8},{5,9},{8,12},{9,13},{12,14},{13,15},{14,10},{15,... | collective-permute-start | bytes 6389768 | tf_op jit(solution)/shard_map/ppermute | solution.py:23
  80.4 45.7 %collective-permute-start = (bf16[1040,1024]{1,0:T(8,128)(2,1)}, bf16[1040,1024]{1,0:T(8,128)(2,1)}, u32[]{:S(2)}, u32[]{:S(2)}) collective-permute-start(bf16[1040,1024]{1,0:T(8,128)(2,1)} %pad_maximum_fusion.1), channel_id=1, source_target_pairs={{0,2},{4,0},{8,4},{12,8},{14,12},{10,14},{6,10},{2,6},{16,18},{20,... | collective-permute-start | bytes 6389768 | tf_op jit(solution)/shard_map/ppermute | solution.py:23
  88.6 38.8 %copy-start.1 = (bf16[16,64,1024]{2,1,0:T(8,128)(2,1)S(1)}, bf16[16,64,1024]{2,1,0:T(8,128)(2,1)}, u32[]{:S(2)}) copy-start(bf16[16,64,1024]{2,1,0:T(8,128)(2,1)} %copy-done) | copy-start | bytes 6291460
  126.1 6.7 %collective-permute-start.3 = (bf16[1040,1024]{1,0:T(8,128)(2,1)}, bf16[1040,1024]{1,0:T(8,128)(2,1)}, u32[]{:S(2)}, u32[]{:S(2)}) collective-permute-start(bf16[1040,1024]{1,0:T(8,128)(2,1)} %collective-permute-done.1), channel_id=1, source_target_pairs={{0,1},{1,0},{4,5},{5,4},{8,9},{9,8},{12,13},{13,12},{14,15},{15,14... | collective-permute-start | bytes 6389768 | tf_op jit(solution)/shard_map/ppermute | solution.py:23

commit v6 on v3

--- a/solution.py
+++ b/solution.py
@@ -23,9 +23,10 @@
     return lax.ppermute(x, "blk", [(pos2dev[a], pos2dev[b]) for a, b in moves])
 
 
-def step_total(local, local_ids, remote, remote_ids, step_pairs, first_step):
+def step_total(local, local_ids, remote, remote_ids, step_pairs, first_step, first_block=0):
     slot_count, feature_span = local.shape
     block_count = slot_count // 128
+    remote_blocks = remote.shape[0] // 128
     logits = lax.dot_general(
         local, remote, (((1,), (1,)), ((), ())), preferred_element_type=jnp.float32
     ) * (SHARPNESS_KNOB / feature_span)
@@ -33,11 +34,10 @@
     if first_step:
         keep = keep & jnp.logical_not(jnp.eye(slot_count, dtype=bool))
     contrib = jnp.where(keep, jnp.exp(logits), 0.0)
-    per_block = contrib.reshape(slot_count, block_count, 128).sum(axis=2)
-    counts = jnp.sum(
-        step_pairs[:, :, None] == jnp.arange(block_count, dtype=jnp.int32), axis=1
-    ).astype(jnp.float32)
-    per_block = per_block.reshape(block_count, 128, block_count)
+    per_block = contrib.reshape(slot_count, remote_blocks, 128).sum(axis=2)
+    named = first_block + jnp.arange(remote_blocks, dtype=jnp.int32)
+    counts = jnp.sum(step_pairs[:, :, None] == named, axis=1).astype(jnp.float32)
+    per_block = per_block.reshape(block_count, 128, remote_blocks)
     return jnp.sum(per_block * counts[:, None, :], axis=2)
 
 
@@ -100,35 +100,47 @@
 
     n = device_count
     evens = range(0, n, 2)
+    half = slot_count // 2
+    half_blocks = block_count // 2
     packed = pack(own, own_ids)
+    first_half = pack(own[:half], own_ids[:half])
     back2 = moved(packed, pos2dev, [(p, (p - 2) % n) for p in evens])
-    fwd2 = moved(packed, pos2dev, [(p, (p + 2) % n) for p in range(n)])
+    fwd_a = moved(first_half, pos2dev, [(p, (p + 2) % n) for p in range(n)])
     across = moved(packed, pos2dev, [(p, p + 1) for p in evens])
     total = step_total(own, own_ids, own, own_ids, my_pairs[0], True)
-    total, back2, fwd2, across = lax.optimization_barrier((total, back2, fwd2, across))
-    fwd2_swapped = moved(fwd2, pos2dev, [(p, p ^ 1) for p in range(n)])
-    back2_held, back2_ids = unpack(back2)
-    fwd2_held, fwd2_ids = unpack(fwd2)
+    total, fwd_a, across, back2 = lax.optimization_barrier((total, fwd_a, across, back2))
+    _, second_half = lax.optimization_barrier((fwd_a, pack(own[half:], own_ids[half:])))
+    fwd_b = moved(second_half, pos2dev, [(p, (p + 2) % n) for p in range(n)])
     across_held, across_ids = unpack(across)
-    swapped_held, swapped_ids = unpack(fwd2_swapped)
-
-    total = total + step_total(
-        own,
-        own_ids,
-        jnp.where(odd, across_held, swapped_held),
-        jnp.where(odd, across_ids, swapped_ids),
-        my_pairs[1],
-        False,
-    )
-    total = total + step_total(own, own_ids, fwd2_held, fwd2_ids, my_pairs[2], False)
-    last = step_total(
-        jnp.where(odd, own, back2_held),
-        jnp.where(odd, own_ids, back2_ids),
-        swapped_held,
-        swapped_ids,
-        jnp.where(odd, my_pairs[3], ahead_pairs[3]),
-        False,
-    )
+    swap = [(p, p ^ 1) for p in range(n)]
+    last = 0.0
+    fwd = fwd_a
+    for lo in (0, half):
+        if lo:
+            fwd, total, last = lax.optimization_barrier((fwd_b, total, last))
+        swapped_held, swapped_ids = unpack(moved(fwd, pos2dev, swap))
+        fwd_held, fwd_ids = unpack(fwd)
+        q0 = lo // 128
+        total = total + step_total(own, own_ids, fwd_held, fwd_ids, my_pairs[2], False, q0)
+        total = total + step_total(
+            own,
+            own_ids,
+            jnp.where(odd, across_held[lo : lo + half], swapped_held),
+            jnp.where(odd, across_ids[lo : lo + half], swapped_ids),
+            my_pairs[1],
+            False,
+            q0,
+        )
+        back2_held, back2_ids = unpack(back2)
+        last = last + step_total(
+            jnp.where(odd, own, back2_held),
+            jnp.where(odd, own_ids, back2_ids),
+            swapped_held,
+            swapped_ids,
+            jnp.where(odd, my_pairs[3], ahead_pairs[3]),
+            False,
+            q0,
+        )
     total = total + jnp.where(odd, last, 0.0)
     forward_part = jnp.where(odd, 0.0, last)
     totals = jnp.stack([total.reshape(device_count, capacity), forward_part.reshape(device_count, capacity)], axis=1)

time: 160 us -> 158 us (0.988)
  blocking collectives: 71.1 us -> 11.3 us
  waiting for transfers between devices: 31.9 us -> 77.7 us
  starting transfers between devices: 8.13 us -> 23.7 us
  matrix products: 24.7 us -> 21.3 us
    all_to_all x1 -> x0, blocking collectives: 61.2 us -> none  [body(): lax.all_to_all(payload, 'blk', split_axis=0, concat_axis=0, tiled=True)]
    all_to_all x0 -> x1, waiting for transfers between devices: none -> 41.1 us  [body(): lax.all_to_all(payload, 'blk', split_axis=0, concat_axis=0, tiled=True)]
    ppermute x4 -> x6, starting transfers between devices: 8.13 us -> 16.2 us  [moved(): return lax.ppermute(x, 'blk', [(pos2dev[a], pos2dev[b]) for a, b in moves])]
    all_to_all x0 -> x1, starting transfers between devices: none -> 7.52 us  [body(): lax.all_to_all(payload, 'blk', split_axis=0, concat_axis=0, tiled=True)]
    ppermute x4 -> x6, waiting for transfers between devices: 31.9 us -> 36.5 us  [moved(): return lax.ppermute(x, 'blk', [(pos2dev[a], pos2dev[b]) for a, b in moves])]
    dot_general x4 -> x7, matrix products: 20.6 us -> 18.7 us  [step_total(): lax.dot_general(local, remote, (((1,), (1,)), ((), ())), preferred_elemen...]
  transfers between devices with their start and end apart: 4 -> 7, of which waited for: 1 -> 4; matrix products, arithmetic and copies ran while one was open for 8% -> 11% of each run, Pallas kernels for 0% -> 0%
where the time goes in v6:
time: 158 us; the launch traced here: 157 us
  waiting for transfers between devices  77.7 us (49%)
  starting transfers between devices  23.7 us (15%)
  matrix products  21.3 us (13%)
  other arithmetic  14.8 us (9%)
  blocking collectives  11.3 us (7%)
  between operations  4.3 us (3%)
  local copies, waits for them, and re-layouts  3.82 us (2%)
    all_to_all x1, waiting for transfers between devices, body(): lax.all_to_all(payload, 'blk', split_axis=0, concat_axis=0, tiled=True)  41.1 us
    ppermute x6, waiting for transfers between devices, moved(): return lax.ppermute(x, 'blk', [(pos2dev[a], pos2dev[b]) for a, b in moves])  36.5 us
    dot_general x7, matrix products, step_total(): lax.dot_general(local, remote, (((1,), (1,)), ((), ())), preferred_elemen...  18.7 us
    ppermute x6, starting transfers between devices, moved(): return lax.ppermute(x, 'blk', [(pos2dev[a], pos2dev[b]) for a, b in moves])  16.2 us
    all_to_all x1, blocking collectives, body(): lax.all_to_all(totals, 'blk', split_axis=0, concat_axis=0, tiled=True)  11.3 us
    all_to_all x1, starting transfers between devices, body(): lax.all_to_all(payload, 'blk', split_axis=0, concat_axis=0, tiled=True)  7.52 us
  transfers between devices with their start and end apart: 7, of which 4 were waited for; matrix products, arithmetic and copies ran while one was open for 11% of the time, Pallas kernels for 0%

profile of v6, /device:TPU:0, one launch (start us, length us, event | category | flops | bytes accessed | tf_op | source)
XLA Modules:
  0.0 157.0 jit_solution(9291329973190318882)
XLA Ops:
  0.0 0.8 broadcast_add_fusion
  0.8 0.7 convert.17
  1.5 0.1 copy.74
  1.7 0.1 reshape.352
  1.8 2.0 %fusion.2 = f32[960]{0:T(1024)S(1)} fusion(bf16[960,1024]{1,0:T(8,128)(2,1)} %param.7), kind=kLoop, calls=%fused_computation.7 | loop fusion | flops 2948160 | bytes 1969920 | tf_op jit(solution)/shard_map/reduce_sum | solution.py:69
  3.8 1.2 convert_reduce_fusion
  5.0 0.7 fusion.37
  5.7 0.6 select_reduce_fusion.2
  6.4 0.1 sub.11
  6.5 0.1 pad.30.clone
  6.6 2.6 %fusion.9 = bf16[1024,1024]{1,0:T(8,128)(2,1)S(1)} fusion(bf16[960,1024]{1,0:T(8,128)(2,1)S(1)} %copy-done.2, f32[960]{0:T(1024)S(1)} %add_rsqrt_fusion, s32[960]{0:T(1024)S(1)} %get-tuple-element.44), kind=kOutput, calls=%fused_computation.36 | convolution fusion | flops 2018246656 | bytes 4070912 | tf_op jit(solution)/shard_map/dot_general | solution.py:77
  9.2 1.7 %pad_maximum_fusion = bf16[16,65,1024]{2,1,0:T(8,128)(2,1)} fusion(bf16[16,1,1024]{2,1,0:T(2,128)(2,1)S(1)} %copy.75, bf16[16,64,1024]{2,1,0:T(8,128)(2,1)S(1)} %bitcast.105), kind=kLoop, calls=%fused_computation.19 | loop fusion | flops 4259840 | bytes 4259840 | tf_op jit(solution)/shard_map/concatenate | solution.py:90
  10.9 7.5 %all-to-all-start = ((bf16[16,65,1024]{2,1,0:T(8,128)(2,1)}), bf16[16,65,1024]{2,1,0:T(8,128)(2,1)S(1)}, u32[]{:S(2)}, u32[]{:S(2)}) async-start(bf16[16,65,1024]{2,1,0:T(8,128)(2,1)} %pad_maximum_fusion), calls=%async_computation | async-start | bytes 4718592 | tf_op jit(solution)/shard_map/all_to_all | solution.py:91
  18.5 0.6 dynamic_slice.9
  23.0 41.1 %all-to-all-done = bf16[16,65,1024]{2,1,0:T(8,128)(2,1)S(1)} async-done(((bf16[16,65,1024]{2,1,0:T(8,128)(2,1)}), bf16[16,65,1024]{2,1,0:T(8,128)(2,1)S(1)}, u32[]{:S(2)}, u32[]{:S(2)}) %all-to-all-start) | async-done | bytes 2129952 | tf_op jit(solution)/shard_map/all_to_all | solution.py:91
  64.3 0.2 slice.210
  64.5 1.7 %pad_maximum_fusion.1 = bf16[1040,1024]{1,0:T(8,128)(2,1)} fusion(bf16[16,1024]{1,0:T(8,128)(2,1)S(1)} %reshape.270, bf16[1024,1024]{1,0:T(8,128)(2,1)S(1)} %bitcast.95), kind=kLoop, calls=%fused_computation.20 | loop fusion | flops 4259840 | bytes 4259840 | tf_op jit(solution)/shard_map/concatenate | solution.py:47
  66.2 0.3 copy-done
  66.5 5.6 %collective-permute-start.2 = (bf16[1040,1024]{1,0:T(8,128)(2,1)}, bf16[1040,1024]{1,0:T(8,128)(2,1)}, u32[]{:S(2)}, u32[]{:S(2)}) collective-permute-start(bf16[1040,1024]{1,0:T(8,128)(2,1)} %pad_maximum_fusion.1), channel_id=1, source_target_pairs={{0,2},{4,0},{8,4},{12,8},{14,12},{10,14},{6,10},{2,6},{16,18},{20,... | collective-permute-start | bytes 6389768 | tf_op jit(solution)/shard_map/ppermute | solution.py:23
  72.2 2.6 %collective-permute-start.1 = (bf16[1040,1024]{1,0:T(8,128)(2,1)}, bf16[1040,1024]{1,0:T(8,128)(2,1)}, u32[]{:S(2)}, u32[]{:S(2)}) collective-permute-start(bf16[1040,1024]{1,0:T(8,128)(2,1)} %pad_maximum_fusion.1), channel_id=1, source_target_pairs={{0,1},{4,5},{8,9},{12,13},{14,15},{10,11},{6,7},{2,3},{16,17},{20,... | collective-permute-start | bytes 6389768 | tf_op jit(solution)/shard_map/ppermute | solution.py:23
  74.9 0.1 convert_element_type.174
  74.9 0.1 convert_element_type.172
  75.1 0.1 slice.211
  75.2 0.1 copy.77
  75.3 0.1 dynamic-slice_select_fusion
  75.4 0.1 copy.81
  75.5 0.1 copy.79
  75.6 0.1 copy.78
  75.7 0.1 convert_reduce_fusion.1
  75.8 0.1 copy.80
  75.9 0.1 convert_reduce_fusion.4
  76.0 0.2 fusion.40
  76.2 0.1 pad_maximum_fusion.2
  76.3 4.7 %collective-permute-start = (bf16[528,1024]{1,0:T(8,128)(2,1)S(1)}, bf16[528,1024]{1,0:T(8,128)(2,1)S(1)}, u32[]{:S(2)}, u32[]{:S(2)}) collective-permute-start(bf16[528,1024]{1,0:T(8,128)(2,1)S(1)} %pad_maximum_fusion.2), channel_id=1, source_target_pairs={{0,4},{1,5},{4,8},{5,9},{8,12},{9,13},{12,14},{13,15},{14,10},{15,... | collective-permute-start | bytes 3244040 | tf_op jit(solution)/shard_map/ppermute | solution.py:23
  81.0 3.2 %bitcast_reduce_fusion = f32[1024,8]{0,1:T(8,128)S(1)} fusion(bf16[1024,1024]{1,0:T(8,128)(2,1)S(1)} %bitcast.96, s32[1024]{0:T(1024)S(1)} %convert_element_type.167, pred[1024]{0:T(1024)(128)(4,1)S(1)} %broadcast_compare_fusion.1), kind=kOutput, calls=%fused_computation.2 | convolution fusion | flops 2155864064 | bytes 2135040 | tf_op jit(solution)/shard_map/dot_general | solution.py:30
  84.2 0.1 fusion.24
  84.3 0.1 pad_maximum_fusion.3
  84.4 18.0 %collective-permute-done = bf16[528,1024]{1,0:T(8,128)(2,1)S(1)} collective-permute-done((bf16[528,1024]{1,0:T(8,128)(2,1)S(1)}, bf16[528,1024]{1,0:T(8,128)(2,1)S(1)}, u32[]{:S(2)}, u32[]{:S(2)}) %collective-permute-start) | collective-permute-done | bytes 1081376 | tf_op jit(solution)/shard_map/ppermute | solution.py:23
  102.5 1.6 %bitcast_reduce_fusion.6 = f32[1024,4]{0,1:T(4,128)S(1)} fusion(bf16[1024,1024]{1,0:T(8,128)(2,1)S(1)} %bitcast.97, bf16[528,1024]{1,0:T(8,128)(2,1)S(1)} %collective-permute-done, s32[1024]{0:T(1024)S(1)} %convert_element_type.167, s32[512]{0:T(512)S(1)} %slice_convert_fusion.6, pred[1024]{0:T(1024)(128)(4,1)S(1)} %broadcast_compare_fusion.1), kind=kOutput, calls=%fused_computation.26 | convolution fusion | flops 1076359168 | bytes 3169280 | tf_op jit(solution)/shard_map/dot_general | solution.py:30
  104.1 3.2 %collective-permute-start.3 = (bf16[528,1024]{1,0:T(8,128)(2,1)S(1)}, bf16[528,1024]{1,0:T(8,128)(2,1)S(1)}, u32[]{:S(2)}, u32[]{:S(2)}) collective-permute-start(bf16[528,1024]{1,0:T(8,128)(2,1)S(1)} %pad_maximum_fusion.3), channel_id=1, source_target_pairs={{0,4},{1,5},{4,8},{5,9},{8,12},{9,13},{12,14},{13,15},{14,10},{15,... | collective-permute-start | bytes 3244040 | tf_op jit(solution)/shard_map/ppermute | solution.py:23
  107.3 0.1 fusion.30
  107.4 0.7 slice_convert_fusion.2
  108.1 0.7 slice_convert_fusion.1
  108.9 2.9 %bitcast_reduce_fusion.5 = f32[1024,4]{0,1:T(4,128)S(1)} fusion(bf16[1024,1024]{1,0:T(8,128)(2,1)S(1)} %bitcast.98, bf16[1040,1024]{1,0:T(8,128)(2,1)} %collective-permute-done.1, s32[1024]{0:T(1024)S(1)} %convert_element_type.167, s32[512]{0:T(512)S(1)} %broadcast_select_fusion.3, pred[]{:T(512)S(6)} %eq.265, ...), kind=kOutput, calls=%fused_computation.25 | convolution fusion | flops 1076883456 | bytes 4217857 | tf_op jit(solution)/shard_map/dot_general | solution.py:30
  111.8 0.1 fusion.29
  111.9 3.3 %bitcast_reduce_fusion.4 = f32[1024,4]{0,1:T(4,128)S(1)} fusion(s32[1024]{0:T(1024)S(1)} %get-tuple-element.36, s32[512]{0:T(512)S(1)} %slice_convert_fusion.5, pred[1024]{0:T(1024)(128)(4,1)S(1)} %get-tuple-element.35, bf16[528,1024]{1,0:T(8,128)(2,1)S(1)} %collective-permute-done.4, bf16[1024,1024]{1,0:T(8,128)(2,1)S(1)} %bitcast.99, ...), kind=kOutput, calls=%fused_computation.24 | convolution fusion | flops 1077407744 | bytes 5266433 | tf_op jit(solution)/shard_map/dot_general | solution.py:30
  115.1 0.1 fusion.28
  115.2 17.6 %collective-permute-done.3 = bf16[528,1024]{1,0:T(8,128)(2,1)S(1)} collective-permute-done((bf16[528,1024]{1,0:T(8,128)(2,1)S(1)}, bf16[528,1024]{1,0:T(8,128)(2,1)S(1)}, u32[]{:S(2)}, u32[]{:S(2)}) %collective-permute-start.3) | collective-permute-done | bytes 1081376 | tf_op jit(solution)/shard_map/ppermute | solution.py:23
  132.9 1.6 %bitcast_reduce_fusion.3 = f32[1024,4]{0,1:T(4,128)S(1)} fusion(bf16[1024,1024]{1,0:T(8,128)(2,1)S(1)} %bitcast.100, bf16[528,1024]{1,0:T(8,128)(2,1)S(1)} %collective-permute-done.3, s32[1024]{0:T(1024)S(1)} %convert_element_type.167, s32[512]{0:T(512)S(1)} %slice_convert_fusion.4, pred[1024]{0:T(1024)(128)(4,1)S(1)} %broadcast_compare_fusion.1), kind=kOutput, calls=%fused_computation.23 | convolution fusion | flops 1076359168 | bytes 3169280 | tf_op jit(solution)/shard_map/dot_general | solution.py:30
  134.6 0.1 fusion.27
  134.6 0.9 collective-permute-done.5
  135.6 3.3 %bitcast_reduce_fusion.1 = f32[1024,4]{0,1:T(4,128)S(1)} fusion(s32[1024]{0:T(1024)S(1)} %get-tuple-element.36, s32[512]{0:T(512)S(1)} %slice_convert_fusion.3, pred[1024]{0:T(1024)(128)(4,1)S(1)} %get-tuple-element.35, bf16[528,1024]{1,0:T(8,128)(2,1)S(1)} %collective-permute-done.5, bf16[1024,1024]{1,0:T(8,128)(2,1)S(1)} %bitcast.101, ...), kind=kOutput, calls=%fused_computation.21 | convolution fusion | flops 1077407744 | bytes 5266433 | tf_op jit(solution)/shard_map/dot_general | solution.py:30
  138.9 0.1 fusion.25
  138.9 2.9 %bitcast_reduce_fusion.2 = f32[1024,4]{0,1:T(4,128)S(1)} fusion(bf16[1024,1024]{1,0:T(8,128)(2,1)S(1)} %bitcast.102, bf16[1040,1024]{1,0:T(8,128)(2,1)} %collective-permute-done.1, s32[1024]{0:T(1024)S(1)} %convert_element_type.167, s32[512]{0:T(512)S(1)} %broadcast_select_fusion.2, pred[]{:T(512)S(6)} %eq.265, ...), kind=kOutput, calls=%fused_computation.22 | convolution fusion | flops 1076883456 | bytes 4217857 | tf_op jit(solution)/shard_map/dot_general | solution.py:30
  141.8 0.1 fusion.26
  141.9 0.1 stack_reshape.6
  142.0 0.1 stack_reshape.7
  142.1 0.1 reshape.355
  142.2 11.3 %all_to_all.10 = f32[16,1,128]{2,1,0:T(1,128)S(1)} all-to-all(f32[16,1,128]{2,1,0:T(1,128)S(1)} %reshape.355), channel_id=1, replica_groups=mesh['groups'=2,'blk'=16] {'blk'}, dimensions={0} | all-to-all | bytes 16384 | tf_op jit(solution)/shard_map/all_to_all | solution.py:147
  153.5 0.5 broadcast.258
  154.0 0.7 reduce.44
  154.7 0.1 reshape.356
  155.0 1.5 select_reduce_fusion
  156.4 0.6 add_log-plus-one_fusion
  (60 shorter events, 0.8 us)
Async XLA Ops:
  0.0 6.6 %copy-start.2 = (bf16[960,1024]{1,0:T(8,128)(2,1)S(1)}, bf16[960,1024]{1,0:T(8,128)(2,1)}, u32[]{:S(2)}) copy-start(bf16[960,1024]{1,0:T(8,128)(2,1)} %param.7) | copy-start | bytes 5898244
  10.9 7.5 %copy-start.3 = (s32[16]{0:T(128)S(1)}, s32[16]{0:T(128)}, u32[]{:S(2)}) copy-start(s32[16]{0:T(128)} %constant.73.clone) | copy-start | bytes 196
  10.9 53.2 %all-to-all-start = ((bf16[16,65,1024]{2,1,0:T(8,128)(2,1)}), bf16[16,65,1024]{2,1,0:T(8,128)(2,1)S(1)}, u32[]{:S(2)}, u32[]{:S(2)}) async-start(bf16[16,65,1024]{2,1,0:T(8,128)(2,1)} %pad_maximum_fusion), calls=%async_computation | async-start | bytes 4718592 | tf_op jit(solution)/shard_map/all_to_all | solution.py:91
  64.5 2.0 %copy-start = (bf16[16,64,1024]{2,1,0:T(8,128)(2,1)}, bf16[16,64,1024]{2,1,0:T(8,128)(2,1)S(1)}, u32[]{:S(2)}) copy-start(bf16[16,64,1024]{2,1,0:T(8,128)(2,1)S(1)} %slice.210) | copy-start | bytes 6291460
  66.5 35.8 %collective-permute-start.2 = (bf16[1040,1024]{1,0:T(8,128)(2,1)}, bf16[1040,1024]{1,0:T(8,128)(2,1)}, u32[]{:S(2)}, u32[]{:S(2)}) collective-permute-start(bf16[1040,1024]{1,0:T(8,128)(2,1)} %pad_maximum_fusion.1), channel_id=1, source_target_pairs={{0,2},{4,0},{8,4},{12,8},{14,12},{10,14},{6,10},{2,6},{16,18},{20,... | collective-permute-start | bytes 6389768 | tf_op jit(solution)/shard_map/ppermute | solution.py:23
  72.2 30.2 %collective-permute-start.1 = (bf16[1040,1024]{1,0:T(8,128)(2,1)}, bf16[1040,1024]{1,0:T(8,128)(2,1)}, u32[]{:S(2)}, u32[]{:S(2)}) collective-permute-start(bf16[1040,1024]{1,0:T(8,128)(2,1)} %pad_maximum_fusion.1), channel_id=1, source_target_pairs={{0,1},{4,5},{8,9},{12,13},{14,15},{10,11},{6,7},{2,3},{16,17},{20,... | collective-permute-start | bytes 6389768 | tf_op jit(solution)/shard_map/ppermute | solution.py:23
  76.2 4.8 %copy-start.1 = (bf16[16,64,1024]{2,1,0:T(8,128)(2,1)S(1)}, bf16[16,64,1024]{2,1,0:T(8,128)(2,1)}, u32[]{:S(2)}) copy-start(bf16[16,64,1024]{2,1,0:T(8,128)(2,1)} %copy-done) | copy-start | bytes 6291460
  76.3 26.0 %collective-permute-start = (bf16[528,1024]{1,0:T(8,128)(2,1)S(1)}, bf16[528,1024]{1,0:T(8,128)(2,1)S(1)}, u32[]{:S(2)}, u32[]{:S(2)}) collective-permute-start(bf16[528,1024]{1,0:T(8,128)(2,1)S(1)} %pad_maximum_fusion.2), channel_id=1, source_target_pairs={{0,4},{1,5},{4,8},{5,9},{8,12},{9,13},{12,14},{13,15},{14,10},{15,... | collective-permute-start | bytes 3244040 | tf_op jit(solution)/shard_map/ppermute | solution.py:23
  102.4 6.5 %collective-permute-start.4 = (bf16[528,1024]{1,0:T(8,128)(2,1)S(1)}, bf16[528,1024]{1,0:T(8,128)(2,1)S(1)}, u32[]{:S(2)}, u32[]{:S(2)}) collective-permute-start(bf16[528,1024]{1,0:T(8,128)(2,1)S(1)} %collective-permute-done), channel_id=1, source_target_pairs={{0,1},{1,0},{4,5},{5,4},{8,9},{9,8},{12,13},{13,12},{14,15},{15,14... | collective-permute-start | bytes 3244040 | tf_op jit(solution)/shard_map/ppermute | solution.py:23
  104.1 28.7 %collective-permute-start.3 = (bf16[528,1024]{1,0:T(8,128)(2,1)S(1)}, bf16[528,1024]{1,0:T(8,128)(2,1)S(1)}, u32[]{:S(2)}, u32[]{:S(2)}) collective-permute-start(bf16[528,1024]{1,0:T(8,128)(2,1)S(1)} %pad_maximum_fusion.3), channel_id=1, source_target_pairs={{0,4},{1,5},{4,8},{5,9},{8,12},{9,13},{12,14},{13,15},{14,10},{15,... | collective-permute-start | bytes 3244040 | tf_op jit(solution)/shard_map/ppermute | solution.py:23
  132.8 2.7 %collective-permute-start.5 = (bf16[528,1024]{1,0:T(8,128)(2,1)S(1)}, bf16[528,1024]{1,0:T(8,128)(2,1)S(1)}, u32[]{:S(2)}, u32[]{:S(2)}) collective-permute-start(bf16[528,1024]{1,0:T(8,128)(2,1)S(1)} %collective-permute-done.3), channel_id=1, source_target_pairs={{0,1},{1,0},{4,5},{5,4},{8,9},{9,8},{12,13},{13,12},{14,15},{15,14... | collective-permute-start | bytes 3244040 | tf_op jit(solution)/shard_map/ppermute | solution.py:23

commit v7 on v6

--- a/solution.py
+++ b/solution.py
@@ -101,28 +101,26 @@
     n = device_count
     evens = range(0, n, 2)
     half = slot_count // 2
-    half_blocks = block_count // 2
-    packed = pack(own, own_ids)
-    first_half = pack(own[:half], own_ids[:half])
+    forward = [(p, (p + 2) % n) for p in range(n)]
+    swap = [(p, p ^ 1) for p in range(n)]
+    fwd_a = moved(pack(own[:half], own_ids[:half]), pos2dev, forward)
+    total = step_total(own, own_ids, own, own_ids, my_pairs[0], True)
+    total, fwd_a = lax.optimization_barrier((total, fwd_a))
+    _, second_half, packed = lax.optimization_barrier(
+        (fwd_a, pack(own[half:], own_ids[half:]), pack(own, own_ids))
+    )
+    fwd_b = moved(second_half, pos2dev, forward)
     back2 = moved(packed, pos2dev, [(p, (p - 2) % n) for p in evens])
-    fwd_a = moved(first_half, pos2dev, [(p, (p + 2) % n) for p in range(n)])
     across = moved(packed, pos2dev, [(p, p + 1) for p in evens])
-    total = step_total(own, own_ids, own, own_ids, my_pairs[0], True)
-    total, fwd_a, across, back2 = lax.optimization_barrier((total, fwd_a, across, back2))
-    _, second_half = lax.optimization_barrier((fwd_a, pack(own[half:], own_ids[half:])))
-    fwd_b = moved(second_half, pos2dev, [(p, (p + 2) % n) for p in range(n)])
+    swapped_a = moved(fwd_a, pos2dev, swap)
     across_held, across_ids = unpack(across)
-    swap = [(p, p ^ 1) for p in range(n)]
-    last = 0.0
-    fwd = fwd_a
-    for lo in (0, half):
-        if lo:
-            fwd, total, last = lax.optimization_barrier((fwd_b, total, last))
-        swapped_held, swapped_ids = unpack(moved(fwd, pos2dev, swap))
+
+    def half_steps(fwd, swapped, lo, total):
         fwd_held, fwd_ids = unpack(fwd)
+        swapped_held, swapped_ids = unpack(swapped)
         q0 = lo // 128
         total = total + step_total(own, own_ids, fwd_held, fwd_ids, my_pairs[2], False, q0)
-        total = total + step_total(
+        return total + step_total(
             own,
             own_ids,
             jnp.where(odd, across_held[lo : lo + half], swapped_held),
@@ -131,16 +129,25 @@
             False,
             q0,
         )
+
+    def last_step(swapped, lo):
         back2_held, back2_ids = unpack(back2)
-        last = last + step_total(
+        swapped_held, swapped_ids = unpack(swapped)
+        return step_total(
             jnp.where(odd, own, back2_held),
             jnp.where(odd, own_ids, back2_ids),
             swapped_held,
             swapped_ids,
             jnp.where(odd, my_pairs[3], ahead_pairs[3]),
             False,
-            q0,
+            lo // 128,
         )
+
+    total = half_steps(fwd_a, swapped_a, 0, total)
+    fwd_b, total = lax.optimization_barrier((fwd_b, total))
+    swapped_b = moved(fwd_b, pos2dev, swap)
+    total = half_steps(fwd_b, swapped_b, half, total)
+    last = last_step(swapped_a, 0) + last_step(swapped_b, half)
     total = total + jnp.where(odd, last, 0.0)
     forward_part = jnp.where(odd, 0.0, last)
     totals = jnp.stack([total.reshape(device_count, capacity), forward_part.reshape(device_count, capacity)], axis=1)

time: 158 us -> 156 us (0.987)
  waiting for transfers between devices: 77.7 us -> 75 us
  other arithmetic: 14.8 us -> 16.4 us
    ppermute x6, waiting for transfers between devices: 36.5 us -> 33.3 us  [moved(): return lax.ppermute(x, 'blk', [(pos2dev[a], pos2dev[b]) for a, b in moves])]
  transfers between devices with their start and end apart: 7 -> 7, of which waited for: 4 -> 3; matrix products, arithmetic and copies ran while one was open for 11% -> 11% of each run, Pallas kernels for 0% -> 0%
where the time goes in v7:
time: 156 us
  waiting for transfers between devices  75 us (48%)
  starting transfers between devices  24.5 us (16%)
  matrix products  20.1 us (13%)
  other arithmetic  16.4 us (11%)
  blocking collectives  11.1 us (7%)
  local copies, waits for them, and re-layouts  4.71 us (3%)
  between operations  3.8 us (2%)
    all_to_all x1, waiting for transfers between devices, body(): lax.all_to_all(payload, 'blk', split_axis=0, concat_axis=0, tiled=True)  41.7 us
    ppermute x6, waiting for transfers between devices, moved(): return lax.ppermute(x, 'blk', [(pos2dev[a], pos2dev[b]) for a, b in moves])  33.3 us
    dot_general x7, matrix products, step_total(): lax.dot_general(local, remote, (((1,), (1,)), ((), ())), preferred_elemen...  17.5 us
    ppermute x6, starting transfers between devices, moved(): return lax.ppermute(x, 'blk', [(pos2dev[a], pos2dev[b]) for a, b in moves])  17 us
    all_to_all x1, blocking collectives, body(): lax.all_to_all(totals, 'blk', split_axis=0, concat_axis=0, tiled=True)  11.1 us
    all_to_all x1, starting transfers between devices, body(): lax.all_to_all(payload, 'blk', split_axis=0, concat_axis=0, tiled=True)  7.52 us
  transfers between devices with their start and end apart: 7, of which 3 were waited for; matrix products, arithmetic and copies ran while one was open for 11% of the time, Pallas kernels for 0%

profile of v7, /device:TPU:0, one launch (start us, length us, event | category | flops | bytes accessed | tf_op | source)
XLA Modules:
  0.0 155.6 jit_solution(17045039497615205638)
XLA Ops:
  0.0 0.8 broadcast_add_fusion
  0.8 1.2 convert_reduce_fusion
  2.1 1.3 fusion.33
  3.4 0.6 select_reduce_fusion.2
  4.0 0.1 sub.11
  4.1 0.7 convert.17
  4.8 0.1 copy.74
  4.9 0.1 reshape.386
  5.0 0.1 pad.30.clone
  5.2 2.0 %fusion.2 = f32[960]{0:T(1024)S(1)} fusion(bf16[960,1024]{1,0:T(8,128)(2,1)} %param.7), kind=kLoop, calls=%fused_computation.7 | loop fusion | flops 2948160 | bytes 1969920 | tf_op jit(solution)/shard_map/reduce_sum | solution.py:69
  7.2 2.6 %fusion.9 = bf16[1024,1024]{1,0:T(8,128)(2,1)S(1)} fusion(bf16[960,1024]{1,0:T(8,128)(2,1)S(1)} %copy-done.2, f32[960]{0:T(1024)S(1)} %add_rsqrt_fusion, s32[960]{0:T(1024)S(1)} %get-tuple-element.40), kind=kOutput, calls=%fused_computation.36 | convolution fusion | flops 2018246656 | bytes 4070912 | tf_op jit(solution)/shard_map/dot_general | solution.py:77
  9.8 1.7 %pad_maximum_fusion = bf16[16,65,1024]{2,1,0:T(8,128)(2,1)} fusion(bf16[16,1,1024]{2,1,0:T(2,128)(2,1)S(1)} %copy.75, bf16[16,64,1024]{2,1,0:T(8,128)(2,1)S(1)} %bitcast.105), kind=kLoop, calls=%fused_computation.19 | loop fusion | flops 4259840 | bytes 4259840 | tf_op jit(solution)/shard_map/concatenate | solution.py:90
  11.5 7.5 %all-to-all-start = ((bf16[16,65,1024]{2,1,0:T(8,128)(2,1)}), bf16[16,65,1024]{2,1,0:T(8,128)(2,1)S(1)}, u32[]{:S(2)}, u32[]{:S(2)}) async-start(bf16[16,65,1024]{2,1,0:T(8,128)(2,1)} %pad_maximum_fusion), calls=%async_computation | async-start | bytes 4718592 | tf_op jit(solution)/shard_map/all_to_all | solution.py:91
  19.0 0.6 dynamic_slice.9
  23.0 41.7 %all-to-all-done = bf16[16,65,1024]{2,1,0:T(8,128)(2,1)S(1)} async-done(((bf16[16,65,1024]{2,1,0:T(8,128)(2,1)}), bf16[16,65,1024]{2,1,0:T(8,128)(2,1)S(1)}, u32[]{:S(2)}, u32[]{:S(2)}) %all-to-all-start) | async-done | bytes 2129952 | tf_op jit(solution)/shard_map/all_to_all | solution.py:91
  64.8 0.5 broadcast_compare_fusion.1
  65.4 0.1 slice.217
  65.5 0.1 copy.77
  65.6 0.7 dynamic-slice_select_fusion
  66.3 0.1 copy.78
  66.4 0.1 convert_reduce_fusion.1
  66.5 0.1 convert_element_type.174
  66.6 0.2 fusion.36
  66.8 1.1 pad_maximum_fusion.2
  67.9 7.8 %collective-permute-start = (bf16[528,1024]{1,0:T(8,128)(2,1)}, bf16[528,1024]{1,0:T(8,128)(2,1)}, u32[]{:S(2)}, u32[]{:S(2)}) collective-permute-start(bf16[528,1024]{1,0:T(8,128)(2,1)} %pad_maximum_fusion.2), channel_id=1, source_target_pairs={{0,4},{1,5},{4,8},{5,9},{8,12},{9,13},{12,14},{13,15},{14,10},{15,... | collective-permute-start | bytes 3244040 | tf_op jit(solution)/shard_map/ppermute | solution.py:23
  75.6 0.1 convert_element_type.175
  75.8 0.2 slice.216
  76.0 0.4 copy-done.6
  76.4 3.2 %bitcast_reduce_fusion = f32[1024,8]{0,1:T(8,128)S(1)} fusion(bf16[1024,1024]{1,0:T(8,128)(2,1)S(1)} %bitcast.95, s32[1024]{0:T(1024)S(1)} %convert_element_type.169, pred[1024]{0:T(1024)(128)(4,1)S(1)} %copy-done.6), kind=kOutput, calls=%fused_computation.2 | convolution fusion | flops 2155864064 | bytes 2135040 | tf_op jit(solution)/shard_map/dot_general | solution.py:30
  79.6 0.1 fusion.20
  79.7 1.1 pad_maximum_fusion.3
  80.8 0.2 pad_maximum_fusion.1
  81.0 18.2 %collective-permute-done = bf16[528,1024]{1,0:T(8,128)(2,1)} collective-permute-done((bf16[528,1024]{1,0:T(8,128)(2,1)}, bf16[528,1024]{1,0:T(8,128)(2,1)}, u32[]{:S(2)}, u32[]{:S(2)}) %collective-permute-start) | collective-permute-done | bytes 1081376 | tf_op jit(solution)/shard_map/ppermute | solution.py:23
  99.1 2.6 %collective-permute-start.2 = (bf16[1040,1024]{1,0:T(8,128)(2,1)S(1)}, bf16[1040,1024]{1,0:T(8,128)(2,1)}, u32[]{:S(2)}, u32[]{:S(2)}) collective-permute-start(bf16[1040,1024]{1,0:T(8,128)(2,1)S(1)} %pad_maximum_fusion.1), channel_id=1, source_target_pairs={{0,1},{4,5},{8,9},{12,13},{14,15},{10,11},{6,7},{2,3},{16,17},{20,... | collective-permute-start | bytes 6389768 | tf_op jit(solution)/shard_map/ppermute | solution.py:23
  101.8 0.1 copy.79
  101.9 0.1 copy.80
  102.0 0.1 copy.81
  102.1 0.1 convert_reduce_fusion.5
  102.2 6.3 %collective-permute-start.5 = (bf16[1040,1024]{1,0:T(8,128)(2,1)S(1)}, bf16[1040,1024]{1,0:T(8,128)(2,1)S(1)}, u32[]{:S(2)}, u32[]{:S(2)}) collective-permute-start(bf16[1040,1024]{1,0:T(8,128)(2,1)S(1)} %pad_maximum_fusion.1), channel_id=1, source_target_pairs={{0,2},{4,0},{8,4},{12,8},{14,12},{10,14},{6,10},{2,6},{16,18},{20,... | collective-permute-start | bytes 6389768 | tf_op jit(solution)/shard_map/ppermute | solution.py:23
  108.6 0.2 collective-permute-start.1
  108.8 0.8 slice_bitcast_fusion.3
  109.6 3.6 %bitcast_reduce_fusion.6 = f32[1024,4]{0,1:T(4,128)S(1)} fusion(bf16[1024,1024]{1,0:T(8,128)(2,1)} %bitcast.97, bf16[528,1024]{1,0:T(8,128)(2,1)} %collective-permute-done, s32[1024]{0:T(1024)S(1)} %convert_element_type.169, s32[512]{0:T(512)S(1)} %slice_convert_fusion.6, pred[1024]{0:T(1024)(128)(4,1)S(1)} %copy-done.7), kind=kOutput, calls=%fused_computation.27 | convolution fusion | flops 1076359168 | bytes 3169280 | tf_op jit(solution)/shard_map/dot_general | solution.py:30
  113.3 0.1 fusion.26
  113.4 0.7 slice_convert_fusion.2
  114.1 2.9 %bitcast_reduce_fusion.5 = f32[1024,4]{0,1:T(4,128)S(1)} fusion(bf16[1024,1024]{1,0:T(8,128)(2,1)S(1)} %bitcast.98, bf16[1040,1024]{1,0:T(8,128)(2,1)} %collective-permute-done.2, s32[1024]{0:T(1024)S(1)} %convert_element_type.169, s32[512]{0:T(512)S(1)} %broadcast_select_fusion.3, pred[]{:T(512)S(6)} %eq.265, pred[1024]{0:T(1024)(128)(4,1)S(1)} %copy-done.7, ...), kind=kOutput, calls=%fused_computation.26 | convolution fusion | flops 1076883456 | bytes 4217857 | tf_op jit(solution)/shard_map/dot_general | solution.py:30
  117.0 0.1 fusion.25
  117.1 15.1 %collective-permute-done.1 = bf16[528,1024]{1,0:T(8,128)(2,1)S(1)} collective-permute-done((bf16[528,1024]{1,0:T(8,128)(2,1)S(1)}, bf16[528,1024]{1,0:T(8,128)(2,1)S(1)}, u32[]{:S(2)}, u32[]{:S(2)}) %collective-permute-start.1) | collective-permute-done | bytes 1081376 | tf_op jit(solution)/shard_map/ppermute | solution.py:23
  132.3 1.6 %bitcast_reduce_fusion.4 = f32[1024,4]{0,1:T(4,128)S(1)} fusion(bf16[1024,1024]{1,0:T(8,128)(2,1)S(1)} %bitcast.99, bf16[528,1024]{1,0:T(8,128)(2,1)S(1)} %collective-permute-done.1, s32[1024]{0:T(1024)S(1)} %convert_element_type.169, s32[512]{0:T(512)S(1)} %slice_convert_fusion.4, pred[1024]{0:T(1024)(128)(4,1)S(1)} %copy-done.7), kind=kOutput, calls=%fused_computation.25 | convolution fusion | flops 1076359168 | bytes 3169280 | tf_op jit(solution)/shard_map/dot_general | solution.py:30
  133.9 0.1 fusion.24
  134.0 1.7 %bitcast_reduce_fusion.2 = f32[1024,4]{0,1:T(4,128)S(1)} fusion(s32[1024]{0:T(1024)S(1)} %get-tuple-element.32, s32[512]{0:T(512)S(1)} %slice_convert_fusion.5, pred[1024]{0:T(1024)(128)(4,1)S(1)} %get-tuple-element.31, bf16[528,1024]{1,0:T(8,128)(2,1)S(1)} %collective-permute-done.3, bf16[1024,1024]{1,0:T(8,128)(2,1)S(1)} %bitcast.100, ...), kind=kOutput, calls=%fused_computation.23 | convolution fusion | flops 1077407744 | bytes 5266433 | tf_op jit(solution)/shard_map/dot_general | solution.py:30
  135.7 0.1 fusion.22
  135.8 2.9 %bitcast_reduce_fusion.3 = f32[1024,4]{0,1:T(4,128)S(1)} fusion(bf16[1024,1024]{1,0:T(8,128)(2,1)S(1)} %bitcast.101, bf16[1040,1024]{1,0:T(8,128)(2,1)} %collective-permute-done.2, s32[1024]{0:T(1024)S(1)} %convert_element_type.169, s32[512]{0:T(512)S(1)} %broadcast_select_fusion.2, pred[]{:T(512)S(6)} %eq.265, pred[1024]{0:T(1024)(128)(4,1)S(1)} %copy-done.7, ...), kind=kOutput, calls=%fused_computation.24 | convolution fusion | flops 1076883456 | bytes 4217857 | tf_op jit(solution)/shard_map/dot_general | solution.py:30
  138.7 0.1 fusion.23
  138.8 1.7 %bitcast_reduce_fusion.1 = f32[1024,4]{0,1:T(4,128)S(1)} fusion(s32[1024]{0:T(1024)S(1)} %get-tuple-element.32, s32[512]{0:T(512)S(1)} %slice_convert_fusion.3, pred[1024]{0:T(1024)(128)(4,1)S(1)} %get-tuple-element.31, bf16[528,1024]{1,0:T(8,128)(2,1)S(1)} %collective-permute-done.4, bf16[1024,1024]{1,0:T(8,128)(2,1)S(1)} %bitcast.102, ...), kind=kOutput, calls=%fused_computation.22 | convolution fusion | flops 1077407744 | bytes 5266433 | tf_op jit(solution)/shard_map/dot_general | solution.py:30
  140.5 0.1 fusion.21
  140.5 0.1 select_n.196
  140.6 0.1 stack_reshape.4
  140.7 0.1 reshape.389
  140.8 11.1 %all_to_all.10 = f32[16,1,128]{2,1,0:T(1,128)S(1)} all-to-all(f32[16,1,128]{2,1,0:T(1,128)S(1)} %reshape.389), channel_id=1, replica_groups=mesh['groups'=2,'blk'=16] {'blk'}, dimensions={0} | all-to-all | bytes 16384 | tf_op jit(solution)/shard_map/all_to_all | solution.py:154
  151.9 0.6 broadcast.276
  152.5 0.7 reduce.44
  153.3 0.1 reshape.390
  153.5 1.5 select_reduce_fusion
  155.0 0.6 add_log-plus-one_fusion
  (70 shorter events, 0.8 us)
Async XLA Ops:
  0.0 7.2 %copy-start.2 = (bf16[960,1024]{1,0:T(8,128)(2,1)S(1)}, bf16[960,1024]{1,0:T(8,128)(2,1)}, u32[]{:S(2)}) copy-start(bf16[960,1024]{1,0:T(8,128)(2,1)} %param.7) | copy-start | bytes 5898244
  11.5 7.5 %copy-start.8 = (s32[16]{0:T(128)S(1)}, s32[16]{0:T(128)}, u32[]{:S(2)}) copy-start(s32[16]{0:T(128)} %constant.73.clone) | copy-start | bytes 196
  11.5 53.2 %all-to-all-start = ((bf16[16,65,1024]{2,1,0:T(8,128)(2,1)}), bf16[16,65,1024]{2,1,0:T(8,128)(2,1)S(1)}, u32[]{:S(2)}, u32[]{:S(2)}) async-start(bf16[16,65,1024]{2,1,0:T(8,128)(2,1)} %pad_maximum_fusion), calls=%async_computation | async-start | bytes 4718592 | tf_op jit(solution)/shard_map/all_to_all | solution.py:91
  67.9 31.3 %collective-permute-start = (bf16[528,1024]{1,0:T(8,128)(2,1)}, bf16[528,1024]{1,0:T(8,128)(2,1)}, u32[]{:S(2)}, u32[]{:S(2)}) collective-permute-start(bf16[528,1024]{1,0:T(8,128)(2,1)} %pad_maximum_fusion.2), channel_id=1, source_target_pairs={{0,4},{1,5},{4,8},{5,9},{8,12},{9,13},{12,14},{13,15},{14,10},{15,... | collective-permute-start | bytes 3244040 | tf_op jit(solution)/shard_map/ppermute | solution.py:23
  75.8 0.6 copy-start.6
  76.0 4.7 %copy-start = (bf16[16,64,1024]{2,1,0:T(8,128)(2,1)}, bf16[16,64,1024]{2,1,0:T(8,128)(2,1)S(1)}, u32[]{:S(2)}) copy-start(bf16[16,64,1024]{2,1,0:T(8,128)(2,1)S(1)} %slice.216) | copy-start | bytes 6291460
  80.8 21.0 %copy-start.4 = (s32[1,1,8,4]{0,3,2,1:T(4,128)S(1)}, s32[1,1,8,4]{0,3,2,1:T(4,128)}, u32[]{:S(2)}) copy-start(s32[1,1,8,4]{0,3,2,1:T(4,128)} %get-tuple-element.36) | copy-start | bytes 388
  80.8 27.8 %copy-start.3 = (bf16[528,1024]{1,0:T(8,128)(2,1)S(1)}, bf16[528,1024]{1,0:T(8,128)(2,1)}, u32[]{:S(2)}) copy-start(bf16[528,1024]{1,0:T(8,128)(2,1)} %pad_maximum_fusion.3) | copy-start | bytes 3244036
  80.8 28.8 %copy-start.7 = (pred[1024]{0:T(1024)(128)(4,1)S(1)}, pred[1024]{0:T(1024)(128)(4,1)}, u32[]{:S(2)}) copy-start(pred[1024]{0:T(1024)(128)(4,1)} %broadcast_compare_fusion.1) | copy-start | bytes 3076
  99.1 14.3 %collective-permute-start.2 = (bf16[1040,1024]{1,0:T(8,128)(2,1)S(1)}, bf16[1040,1024]{1,0:T(8,128)(2,1)}, u32[]{:S(2)}, u32[]{:S(2)}) collective-permute-start(bf16[1040,1024]{1,0:T(8,128)(2,1)S(1)} %pad_maximum_fusion.1), channel_id=1, source_target_pairs={{0,1},{4,5},{8,9},{12,13},{14,15},{10,11},{6,7},{2,3},{16,17},{20,... | collective-permute-start | bytes 6389768 | tf_op jit(solution)/shard_map/ppermute | solution.py:23
  102.1 11.3 %collective-permute-start.3 = (bf16[528,1024]{1,0:T(8,128)(2,1)}, bf16[528,1024]{1,0:T(8,128)(2,1)S(1)}, u32[]{:S(2)}, u32[]{:S(2)}) collective-permute-start(bf16[528,1024]{1,0:T(8,128)(2,1)} %collective-permute-done), channel_id=1, source_target_pairs={{0,1},{1,0},{4,5},{5,4},{8,9},{9,8},{12,13},{13,12},{14,15},{15,14... | collective-permute-start | bytes 3244040 | tf_op jit(solution)/shard_map/ppermute | solution.py:23
  102.2 31.7 %collective-permute-start.5 = (bf16[1040,1024]{1,0:T(8,128)(2,1)S(1)}, bf16[1040,1024]{1,0:T(8,128)(2,1)S(1)}, u32[]{:S(2)}, u32[]{:S(2)}) collective-permute-start(bf16[1040,1024]{1,0:T(8,128)(2,1)S(1)} %pad_maximum_fusion.1), channel_id=1, source_target_pairs={{0,2},{4,0},{8,4},{12,8},{14,12},{10,14},{6,10},{2,6},{16,18},{20,... | collective-permute-start | bytes 6389768 | tf_op jit(solution)/shard_map/ppermute | solution.py:23
  108.6 23.7 %collective-permute-start.1 = (bf16[528,1024]{1,0:T(8,128)(2,1)S(1)}, bf16[528,1024]{1,0:T(8,128)(2,1)S(1)}, u32[]{:S(2)}, u32[]{:S(2)}) collective-permute-start(bf16[528,1024]{1,0:T(8,128)(2,1)S(1)} %copy-done.3), channel_id=1, source_target_pairs={{0,4},{1,5},{4,8},{5,9},{8,12},{9,13},{12,14},{13,15},{14,10},{15,... | collective-permute-start | bytes 3244040 | tf_op jit(solution)/shard_map/ppermute | solution.py:23
  109.6 4.5 %copy-start.1 = (bf16[16,64,1024]{2,1,0:T(8,128)(2,1)S(1)}, bf16[16,64,1024]{2,1,0:T(8,128)(2,1)}, u32[]{:S(2)}) copy-start(bf16[16,64,1024]{2,1,0:T(8,128)(2,1)} %copy-done) | copy-start | bytes 6291460
  132.2 3.5 %collective-permute-start.4 = (bf16[528,1024]{1,0:T(8,128)(2,1)S(1)}, bf16[528,1024]{1,0:T(8,128)(2,1)S(1)}, u32[]{:S(2)}, u32[]{:S(2)}) collective-permute-start(bf16[528,1024]{1,0:T(8,128)(2,1)S(1)} %collective-permute-done.1), channel_id=1, source_target_pairs={{0,1},{1,0},{4,5},{5,4},{8,9},{9,8},{12,13},{13,12},{14,15},{15,14... | collective-permute-start | bytes 3244040 | tf_op jit(solution)/shard_map/ppermute | solution.py:23
  138.8 14.7 %copy-start.5 = (s32[960]{0:T(1024)S(1)}, s32[960]{0:T(1024)}, u32[]{:S(2)}) copy-start(s32[960]{0:T(1024)} %get-tuple-element.39) | copy-start | bytes 11524

commit v8 on v7

--- a/solution.py
+++ b/solution.py
@@ -104,14 +104,14 @@
     forward = [(p, (p + 2) % n) for p in range(n)]
     swap = [(p, p ^ 1) for p in range(n)]
     fwd_a = moved(pack(own[:half], own_ids[:half]), pos2dev, forward)
+    across = moved(pack(own, own_ids), pos2dev, [(p, p + 1) for p in evens])
     total = step_total(own, own_ids, own, own_ids, my_pairs[0], True)
-    total, fwd_a = lax.optimization_barrier((total, fwd_a))
+    total, fwd_a, across = lax.optimization_barrier((total, fwd_a, across))
     _, second_half, packed = lax.optimization_barrier(
         (fwd_a, pack(own[half:], own_ids[half:]), pack(own, own_ids))
     )
     fwd_b = moved(second_half, pos2dev, forward)
     back2 = moved(packed, pos2dev, [(p, (p - 2) % n) for p in evens])
-    across = moved(packed, pos2dev, [(p, p + 1) for p in evens])
     swapped_a = moved(fwd_a, pos2dev, swap)
     across_held, across_ids = unpack(across)
 

time: 156 us -> 154 us (0.987)
  waiting for transfers between devices: 75 us -> 77.7 us
  other arithmetic: 16.4 us -> 14.1 us
  matrix products: 20.1 us -> 18.1 us
    ppermute x6, waiting for transfers between devices: 33.3 us -> 36.6 us  [moved(): return lax.ppermute(x, 'blk', [(pos2dev[a], pos2dev[b]) for a, b in moves])]
    dot_general x7, matrix products: 17.5 us -> 15.5 us  [step_total(): lax.dot_general(local, remote, (((1,), (1,)), ((), ())), preferred_elemen...]
  transfers between devices with their start and end apart: 7 -> 7, of which waited for: 3 -> 4; matrix products, arithmetic and copies ran while one was open for 11% -> 9% of each run, Pallas kernels for 0% -> 0%
where the time goes in v8:
time: 154 us; the launch traced here: 153 us
  waiting for transfers between devices  77.7 us (50%)
  starting transfers between devices  24.6 us (16%)
  matrix products  18.1 us (12%)
  other arithmetic  14.1 us (9%)
  blocking collectives  10.8 us (7%)
  between operations  4.3 us (3%)
  local copies, waits for them, and re-layouts  3.76 us (2%)
    all_to_all x1, waiting for transfers between devices, body(): lax.all_to_all(payload, 'blk', split_axis=0, concat_axis=0, tiled=True)  41.1 us
    ppermute x6, waiting for transfers between devices, moved(): return lax.ppermute(x, 'blk', [(pos2dev[a], pos2dev[b]) for a, b in moves])  36.6 us
    ppermute x6, starting transfers between devices, moved(): return lax.ppermute(x, 'blk', [(pos2dev[a], pos2dev[b]) for a, b in moves])  17.1 us
    dot_general x7, matrix products, step_total(): lax.dot_general(local, remote, (((1,), (1,)), ((), ())), preferred_elemen...  15.5 us
    all_to_all x1, blocking collectives, body(): lax.all_to_all(totals, 'blk', split_axis=0, concat_axis=0, tiled=True)  10.8 us
    all_to_all x1, starting transfers between devices, body(): lax.all_to_all(payload, 'blk', split_axis=0, concat_axis=0, tiled=True)  7.52 us
  transfers between devices with their start and end apart: 7, of which 4 were waited for; matrix products, arithmetic and copies ran while one was open for 9% of the time, Pallas kernels for 0%

profile of v8, /device:TPU:0, one launch (start us, length us, event | category | flops | bytes accessed | tf_op | source)
XLA Modules:
  0.0 153.4 jit_solution(2236842557865552131)
XLA Ops:
  0.0 0.8 broadcast_add_fusion
  0.8 0.7 convert.17
  1.5 0.1 copy.74
  1.7 0.1 reshape.387
  1.8 2.0 %fusion.2 = f32[960]{0:T(1024)S(1)} fusion(bf16[960,1024]{1,0:T(8,128)(2,1)} %param.7), kind=kLoop, calls=%fused_computation.7 | loop fusion | flops 2948160 | bytes 1969920 | tf_op jit(solution)/shard_map/reduce_sum | solution.py:69
  3.8 1.2 convert_reduce_fusion
  5.0 0.7 fusion.37
  5.7 0.6 select_reduce_fusion.2
  6.4 0.1 sub.11
  6.5 0.1 pad.31.clone
  6.6 2.6 %fusion.9 = bf16[1024,1024]{1,0:T(8,128)(2,1)S(1)} fusion(bf16[960,1024]{1,0:T(8,128)(2,1)S(1)} %copy-done.2, f32[960]{0:T(1024)S(1)} %add_rsqrt_fusion, s32[960]{0:T(1024)S(1)} %get-tuple-element.42), kind=kOutput, calls=%fused_computation.36 | convolution fusion | flops 2018246656 | bytes 4070912 | tf_op jit(solution)/shard_map/dot_general | solution.py:77
  9.2 1.7 %pad_maximum_fusion = bf16[16,65,1024]{2,1,0:T(8,128)(2,1)} fusion(bf16[16,1,1024]{2,1,0:T(2,128)(2,1)S(1)} %copy.75, bf16[16,64,1024]{2,1,0:T(8,128)(2,1)S(1)} %bitcast.105), kind=kLoop, calls=%fused_computation.19 | loop fusion | flops 4259840 | bytes 4259840 | tf_op jit(solution)/shard_map/concatenate | solution.py:90
  10.9 7.5 %all-to-all-start = ((bf16[16,65,1024]{2,1,0:T(8,128)(2,1)}), bf16[16,65,1024]{2,1,0:T(8,128)(2,1)S(1)}, u32[]{:S(2)}, u32[]{:S(2)}) async-start(bf16[16,65,1024]{2,1,0:T(8,128)(2,1)} %pad_maximum_fusion), calls=%async_computation | async-start | bytes 4718592 | tf_op jit(solution)/shard_map/all_to_all | solution.py:91
  18.5 0.6 dynamic_slice.9
  23.0 41.1 %all-to-all-done = bf16[16,65,1024]{2,1,0:T(8,128)(2,1)S(1)} async-done(((bf16[16,65,1024]{2,1,0:T(8,128)(2,1)}), bf16[16,65,1024]{2,1,0:T(8,128)(2,1)S(1)}, u32[]{:S(2)}, u32[]{:S(2)}) %all-to-all-start) | async-done | bytes 2129952 | tf_op jit(solution)/shard_map/all_to_all | solution.py:91
  64.2 0.1 convert_element_type.178
  64.3 0.1 convert_element_type.176
  64.4 0.1 convert_element_type.171
  64.6 0.2 slice.216
  64.8 1.6 %pad_maximum_fusion.1 = bf16[1040,1024]{1,0:T(8,128)(2,1)} fusion(bf16[16,1024]{1,0:T(8,128)(2,1)S(1)} %reshape.305, bf16[1024,1024]{1,0:T(8,128)(2,1)S(1)} %bitcast.95), kind=kLoop, calls=%fused_computation.20 | loop fusion | flops 4259840 | bytes 4259840 | tf_op jit(solution)/shard_map/concatenate | solution.py:47
  66.5 0.3 copy-done
  66.8 4.0 %collective-permute-start.1 = (bf16[1040,1024]{1,0:T(8,128)(2,1)}, bf16[1040,1024]{1,0:T(8,128)(2,1)}, u32[]{:S(2)}, u32[]{:S(2)}) collective-permute-start(bf16[1040,1024]{1,0:T(8,128)(2,1)} %pad_maximum_fusion.1), channel_id=1, source_target_pairs={{0,1},{4,5},{8,9},{12,13},{14,15},{10,11},{6,7},{2,3},{16,17},{20,... | collective-permute-start | bytes 6389768 | tf_op jit(solution)/shard_map/ppermute | solution.py:23
  70.8 0.1 slice.217
  70.9 0.1 copy.77
  71.0 0.1 dynamic-slice_select_fusion
  71.1 0.1 copy.81
  71.2 0.1 copy.79
  71.3 0.1 copy.78
  71.4 0.1 convert_reduce_fusion.1
  71.5 0.1 copy.80
  71.6 0.1 convert_reduce_fusion.5
  71.7 0.2 fusion.40
  71.9 0.1 pad_maximum_fusion.2
  72.0 6.9 %collective-permute-start = (bf16[528,1024]{1,0:T(8,128)(2,1)S(1)}, bf16[528,1024]{1,0:T(8,128)(2,1)S(1)}, u32[]{:S(2)}, u32[]{:S(2)}) collective-permute-start(bf16[528,1024]{1,0:T(8,128)(2,1)S(1)} %pad_maximum_fusion.2), channel_id=1, source_target_pairs={{0,4},{1,5},{4,8},{5,9},{8,12},{9,13},{12,14},{13,15},{14,10},{15,... | collective-permute-start | bytes 3244040 | tf_op jit(solution)/shard_map/ppermute | solution.py:23
  79.0 3.2 %bitcast_reduce_fusion = f32[1024,8]{0,1:T(8,128)S(1)} fusion(bf16[1024,1024]{1,0:T(8,128)(2,1)S(1)} %bitcast.96, s32[1024]{0:T(1024)S(1)} %convert_element_type.171, pred[1024]{0:T(1024)(128)(4,1)S(1)} %broadcast_compare_fusion.1), kind=kOutput, calls=%fused_computation.2 | convolution fusion | flops 2155864064 | bytes 2135040 | tf_op jit(solution)/shard_map/dot_general | solution.py:30
  82.1 0.1 fusion.24
  82.2 0.1 pad_maximum_fusion.3
  82.3 18.0 %collective-permute-done = bf16[528,1024]{1,0:T(8,128)(2,1)S(1)} collective-permute-done((bf16[528,1024]{1,0:T(8,128)(2,1)S(1)}, bf16[528,1024]{1,0:T(8,128)(2,1)S(1)}, u32[]{:S(2)}, u32[]{:S(2)}) %collective-permute-start) | collective-permute-done | bytes 1081376 | tf_op jit(solution)/shard_map/ppermute | solution.py:23
  100.3 3.0 %collective-permute-start.2 = (bf16[528,1024]{1,0:T(8,128)(2,1)S(1)}, bf16[528,1024]{1,0:T(8,128)(2,1)S(1)}, u32[]{:S(2)}, u32[]{:S(2)}) collective-permute-start(bf16[528,1024]{1,0:T(8,128)(2,1)S(1)} %pad_maximum_fusion.3), channel_id=1, source_target_pairs={{0,4},{1,5},{4,8},{5,9},{8,12},{9,13},{12,14},{13,15},{14,10},{15,... | collective-permute-start | bytes 3244040 | tf_op jit(solution)/shard_map/ppermute | solution.py:23
  103.4 3.1 %collective-permute-start.5 = (bf16[1040,1024]{1,0:T(8,128)(2,1)}, bf16[1040,1024]{1,0:T(8,128)(2,1)S(1)}, u32[]{:S(2)}, u32[]{:S(2)}) collective-permute-start(bf16[1040,1024]{1,0:T(8,128)(2,1)} %pad_maximum_fusion.1), channel_id=1, source_target_pairs={{0,2},{4,0},{8,4},{12,8},{14,12},{10,14},{6,10},{2,6},{16,18},{20,... | collective-permute-start | bytes 6389768 | tf_op jit(solution)/shard_map/ppermute | solution.py:23
  106.5 1.6 %bitcast_reduce_fusion.6 = f32[1024,4]{0,1:T(4,128)S(1)} fusion(bf16[1024,1024]{1,0:T(8,128)(2,1)S(1)} %bitcast.97, bf16[528,1024]{1,0:T(8,128)(2,1)S(1)} %collective-permute-done, s32[1024]{0:T(1024)S(1)} %convert_element_type.171, s32[512]{0:T(512)S(1)} %slice_convert_fusion.6, pred[1024]{0:T(1024)(128)(4,1)S(1)} %broadcast_compare_fusion.1), kind=kOutput, calls=%fused_computation.27 | convolution fusion | flops 1076359168 | bytes 3169280 | tf_op jit(solution)/shard_map/dot_general | solution.py:30
  108.2 0.1 fusion.30
  108.2 0.7 slice_convert_fusion.2
  109.0 2.9 %bitcast_reduce_fusion.5 = f32[1024,4]{0,1:T(4,128)S(1)} fusion(bf16[1024,1024]{1,0:T(8,128)(2,1)S(1)} %bitcast.98, bf16[1040,1024]{1,0:T(8,128)(2,1)} %collective-permute-done.1, s32[1024]{0:T(1024)S(1)} %convert_element_type.171, s32[512]{0:T(512)S(1)} %broadcast_select_fusion.3, pred[]{:T(512)S(6)} %eq.265, ...), kind=kOutput, calls=%fused_computation.26 | convolution fusion | flops 1076883456 | bytes 4217857 | tf_op jit(solution)/shard_map/dot_general | solution.py:30
  111.9 0.1 fusion.29
  112.0 16.9 %collective-permute-done.2 = bf16[528,1024]{1,0:T(8,128)(2,1)S(1)} collective-permute-done((bf16[528,1024]{1,0:T(8,128)(2,1)S(1)}, bf16[528,1024]{1,0:T(8,128)(2,1)S(1)}, u32[]{:S(2)}, u32[]{:S(2)}) %collective-permute-start.2) | collective-permute-done | bytes 1081376 | tf_op jit(solution)/shard_map/ppermute | solution.py:23
  128.9 1.6 %bitcast_reduce_fusion.4 = f32[1024,4]{0,1:T(4,128)S(1)} fusion(bf16[1024,1024]{1,0:T(8,128)(2,1)S(1)} %bitcast.99, bf16[528,1024]{1,0:T(8,128)(2,1)S(1)} %collective-permute-done.2, s32[1024]{0:T(1024)S(1)} %convert_element_type.171, s32[512]{0:T(512)S(1)} %slice_convert_fusion.4, pred[1024]{0:T(1024)(128)(4,1)S(1)} %broadcast_compare_fusion.1), kind=kOutput, calls=%fused_computation.25 | convolution fusion | flops 1076359168 | bytes 3169280 | tf_op jit(solution)/shard_map/dot_general | solution.py:30
  130.6 0.1 fusion.28
  130.7 1.6 %collective-permute-done.5 = bf16[1040,1024]{1,0:T(8,128)(2,1)S(1)} collective-permute-done((bf16[1040,1024]{1,0:T(8,128)(2,1)}, bf16[1040,1024]{1,0:T(8,128)(2,1)S(1)}, u32[]{:S(2)}, u32[]{:S(2)}) %collective-permute-start.5) | collective-permute-done | bytes 2129952 | tf_op jit(solution)/shard_map/ppermute | solution.py:23
  132.3 1.7 %bitcast_reduce_fusion.2 = f32[1024,4]{0,1:T(4,128)S(1)} fusion(s32[1024]{0:T(1024)S(1)} %get-tuple-element.34, s32[512]{0:T(512)S(1)} %slice_convert_fusion.5, pred[1024]{0:T(1024)(128)(4,1)S(1)} %get-tuple-element.33, bf16[528,1024]{1,0:T(8,128)(2,1)S(1)} %collective-permute-done.3, bf16[1024,1024]{1,0:T(8,128)(2,1)S(1)} %bitcast.100, ...), kind=kOutput, calls=%fused_computation.23 | convolution fusion | flops 1077407744 | bytes 5266433 | tf_op jit(solution)/shard_map/dot_general | solution.py:30
  134.0 0.1 fusion.26
  134.1 2.9 %bitcast_reduce_fusion.3 = f32[1024,4]{0,1:T(4,128)S(1)} fusion(bf16[1024,1024]{1,0:T(8,128)(2,1)S(1)} %bitcast.101, bf16[1040,1024]{1,0:T(8,128)(2,1)} %collective-permute-done.1, s32[1024]{0:T(1024)S(1)} %convert_element_type.171, s32[512]{0:T(512)S(1)} %broadcast_select_fusion.2, pred[]{:T(512)S(6)} %eq.265, ...), kind=kOutput, calls=%fused_computation.24 | convolution fusion | flops 1076883456 | bytes 4217857 | tf_op jit(solution)/shard_map/dot_general | solution.py:30
  137.0 0.1 fusion.27
  137.1 1.7 %bitcast_reduce_fusion.1 = f32[1024,4]{0,1:T(4,128)S(1)} fusion(s32[1024]{0:T(1024)S(1)} %get-tuple-element.34, s32[512]{0:T(512)S(1)} %slice_convert_fusion.3, pred[1024]{0:T(1024)(128)(4,1)S(1)} %get-tuple-element.33, bf16[528,1024]{1,0:T(8,128)(2,1)S(1)} %collective-permute-done.4, bf16[1024,1024]{1,0:T(8,128)(2,1)S(1)} %bitcast.102, ...), kind=kOutput, calls=%fused_computation.22 | convolution fusion | flops 1077407744 | bytes 5266433 | tf_op jit(solution)/shard_map/dot_general | solution.py:30
  138.7 0.1 fusion.25
  138.8 0.1 stack_reshape.4
  138.9 0.1 select_n.196
  139.0 0.1 reshape.390
  139.1 10.8 %all_to_all.10 = f32[16,1,128]{2,1,0:T(1,128)S(1)} all-to-all(f32[16,1,128]{2,1,0:T(1,128)S(1)} %reshape.390), channel_id=1, replica_groups=mesh['groups'=2,'blk'=16] {'blk'}, dimensions={0} | all-to-all | bytes 16384 | tf_op jit(solution)/shard_map/all_to_all | solution.py:154
  149.9 0.5 broadcast.276
  150.4 0.7 reduce.44
  151.1 0.1 reshape.391
  151.3 1.5 select_reduce_fusion
  152.8 0.6 add_log-plus-one_fusion
  (60 shorter events, 0.7 us)
Async XLA Ops:
  0.0 6.6 %copy-start.2 = (bf16[960,1024]{1,0:T(8,128)(2,1)S(1)}, bf16[960,1024]{1,0:T(8,128)(2,1)}, u32[]{:S(2)}) copy-start(bf16[960,1024]{1,0:T(8,128)(2,1)} %param.7) | copy-start | bytes 5898244
  10.9 7.5 %copy-start.3 = (s32[16]{0:T(128)S(1)}, s32[16]{0:T(128)}, u32[]{:S(2)}) copy-start(s32[16]{0:T(128)} %constant.73.clone) | copy-start | bytes 196
  10.9 53.2 %all-to-all-start = ((bf16[16,65,1024]{2,1,0:T(8,128)(2,1)}), bf16[16,65,1024]{2,1,0:T(8,128)(2,1)S(1)}, u32[]{:S(2)}, u32[]{:S(2)}) async-start(bf16[16,65,1024]{2,1,0:T(8,128)(2,1)} %pad_maximum_fusion), calls=%async_computation | async-start | bytes 4718592 | tf_op jit(solution)/shard_map/all_to_all | solution.py:91
  64.8 1.9 %copy-start = (bf16[16,64,1024]{2,1,0:T(8,128)(2,1)}, bf16[16,64,1024]{2,1,0:T(8,128)(2,1)S(1)}, u32[]{:S(2)}) copy-start(bf16[16,64,1024]{2,1,0:T(8,128)(2,1)S(1)} %slice.216) | copy-start | bytes 6291460
  66.8 33.5 %collective-permute-start.1 = (bf16[1040,1024]{1,0:T(8,128)(2,1)}, bf16[1040,1024]{1,0:T(8,128)(2,1)}, u32[]{:S(2)}, u32[]{:S(2)}) collective-permute-start(bf16[1040,1024]{1,0:T(8,128)(2,1)} %pad_maximum_fusion.1), channel_id=1, source_target_pairs={{0,1},{4,5},{8,9},{12,13},{14,15},{10,11},{6,7},{2,3},{16,17},{20,... | collective-permute-start | bytes 6389768 | tf_op jit(solution)/shard_map/ppermute | solution.py:23
  71.9 7.0 %copy-start.1 = (bf16[16,64,1024]{2,1,0:T(8,128)(2,1)S(1)}, bf16[16,64,1024]{2,1,0:T(8,128)(2,1)}, u32[]{:S(2)}) copy-start(bf16[16,64,1024]{2,1,0:T(8,128)(2,1)} %copy-done) | copy-start | bytes 6291460
  72.0 28.3 %collective-permute-start = (bf16[528,1024]{1,0:T(8,128)(2,1)S(1)}, bf16[528,1024]{1,0:T(8,128)(2,1)S(1)}, u32[]{:S(2)}, u32[]{:S(2)}) collective-permute-start(bf16[528,1024]{1,0:T(8,128)(2,1)S(1)} %pad_maximum_fusion.2), channel_id=1, source_target_pairs={{0,4},{1,5},{4,8},{5,9},{8,12},{9,13},{12,14},{13,15},{14,10},{15,... | collective-permute-start | bytes 3244040 | tf_op jit(solution)/shard_map/ppermute | solution.py:23
  100.3 8.7 %collective-permute-start.3 = (bf16[528,1024]{1,0:T(8,128)(2,1)S(1)}, bf16[528,1024]{1,0:T(8,128)(2,1)S(1)}, u32[]{:S(2)}, u32[]{:S(2)}) collective-permute-start(bf16[528,1024]{1,0:T(8,128)(2,1)S(1)} %collective-permute-done), channel_id=1, source_target_pairs={{0,1},{1,0},{4,5},{5,4},{8,9},{9,8},{12,13},{13,12},{14,15},{15,14... | collective-permute-start | bytes 3244040 | tf_op jit(solution)/shard_map/ppermute | solution.py:23
  100.3 28.6 %collective-permute-start.2 = (bf16[528,1024]{1,0:T(8,128)(2,1)S(1)}, bf16[528,1024]{1,0:T(8,128)(2,1)S(1)}, u32[]{:S(2)}, u32[]{:S(2)}) collective-permute-start(bf16[528,1024]{1,0:T(8,128)(2,1)S(1)} %pad_maximum_fusion.3), channel_id=1, source_target_pairs={{0,4},{1,5},{4,8},{5,9},{8,12},{9,13},{12,14},{13,15},{14,10},{15,... | collective-permute-start | bytes 3244040 | tf_op jit(solution)/shard_map/ppermute | solution.py:23
  103.4 28.9 %collective-permute-start.5 = (bf16[1040,1024]{1,0:T(8,128)(2,1)}, bf16[1040,1024]{1,0:T(8,128)(2,1)S(1)}, u32[]{:S(2)}, u32[]{:S(2)}) collective-permute-start(bf16[1040,1024]{1,0:T(8,128)(2,1)} %pad_maximum_fusion.1), channel_id=1, source_target_pairs={{0,2},{4,0},{8,4},{12,8},{14,12},{10,14},{6,10},{2,6},{16,18},{20,... | collective-permute-start | bytes 6389768 | tf_op jit(solution)/shard_map/ppermute | solution.py:23
  128.9 5.2 %collective-permute-start.4 = (bf16[528,1024]{1,0:T(8,128)(2,1)S(1)}, bf16[528,1024]{1,0:T(8,128)(2,1)S(1)}, u32[]{:S(2)}, u32[]{:S(2)}) collective-permute-start(bf16[528,1024]{1,0:T(8,128)(2,1)S(1)} %collective-permute-done.2), channel_id=1, source_target_pairs={{0,1},{1,0},{4,5},{5,4},{8,9},{9,8},{12,13},{13,12},{14,15},{15,14... | collective-permute-start | bytes 3244040 | tf_op jit(solution)/shard_map/ppermute | solution.py:23

commit v9 on v7

--- a/solution.py
+++ b/solution.py
@@ -103,51 +103,57 @@
     half = slot_count // 2
     forward = [(p, (p + 2) % n) for p in range(n)]
     swap = [(p, p ^ 1) for p in range(n)]
-    fwd_a = moved(pack(own[:half], own_ids[:half]), pos2dev, forward)
+    packed = pack(own, own_ids)
+    packed = jnp.concatenate([packed[:half], packed[slot_count:], packed[half:slot_count]], axis=0)
+    lead = half + packed.shape[0] - slot_count
+
+    def ids_of(rows):
+        return rows.reshape(-1)[:slot_count].astype(jnp.int32)
+
+    fwd_a = moved(packed[:lead], pos2dev, forward)
     total = step_total(own, own_ids, own, own_ids, my_pairs[0], True)
     total, fwd_a = lax.optimization_barrier((total, fwd_a))
-    _, second_half, packed = lax.optimization_barrier(
-        (fwd_a, pack(own[half:], own_ids[half:]), pack(own, own_ids))
-    )
+    _, second_half, late = lax.optimization_barrier((fwd_a, own[half:], packed))
     fwd_b = moved(second_half, pos2dev, forward)
-    back2 = moved(packed, pos2dev, [(p, (p - 2) % n) for p in evens])
-    across = moved(packed, pos2dev, [(p, p + 1) for p in evens])
-    swapped_a = moved(fwd_a, pos2dev, swap)
-    across_held, across_ids = unpack(across)
+    back2 = moved(late, pos2dev, [(p, (p - 2) % n) for p in evens])
+    partner = moved(jnp.concatenate([fwd_a, late], axis=0), pos2dev, swap)
+    swapped_a, across = partner[:lead], partner[lead:]
+    across_ids = ids_of(across[half:lead])
+    fwd_ids = ids_of(fwd_a[half:lead])
 
-    def half_steps(fwd, swapped, lo, total):
-        fwd_held, fwd_ids = unpack(fwd)
-        swapped_held, swapped_ids = unpack(swapped)
+    def half_steps(fwd, swapped, swapped_ids, lo, total):
         q0 = lo // 128
-        total = total + step_total(own, own_ids, fwd_held, fwd_ids, my_pairs[2], False, q0)
+        total = total + step_total(own, own_ids, fwd[:half], fwd_ids[lo : lo + half], my_pairs[2], False, q0)
+        across_rows = across[:half] if lo == 0 else across[lead:]
         return total + step_total(
             own,
             own_ids,
-            jnp.where(odd, across_held[lo : lo + half], swapped_held),
-            jnp.where(odd, across_ids[lo : lo + half], swapped_ids),
+            jnp.where(odd, across_rows, swapped[:half]),
+            jnp.where(odd, across_ids[lo : lo + half], swapped_ids[lo : lo + half]),
             my_pairs[1],
             False,
             q0,
         )
 
-    def last_step(swapped, lo):
-        back2_held, back2_ids = unpack(back2)
-        swapped_held, swapped_ids = unpack(swapped)
+    def last_step(swapped, swapped_ids, lo):
+        back2_held = jnp.concatenate([back2[:half], back2[lead:]], axis=0)
+        back2_ids = ids_of(back2[half:lead])
         return step_total(
             jnp.where(odd, own, back2_held),
             jnp.where(odd, own_ids, back2_ids),
-            swapped_held,
-            swapped_ids,
+            swapped[:half],
+            swapped_ids[lo : lo + half],
             jnp.where(odd, my_pairs[3], ahead_pairs[3]),
             False,
             lo // 128,
         )
 
-    total = half_steps(fwd_a, swapped_a, 0, total)
+    swapped_ids = ids_of(swapped_a[half:lead])
+    total = half_steps(fwd_a, swapped_a, swapped_ids, 0, total)
     fwd_b, total = lax.optimization_barrier((fwd_b, total))
     swapped_b = moved(fwd_b, pos2dev, swap)
-    total = half_steps(fwd_b, swapped_b, half, total)
-    last = last_step(swapped_a, 0) + last_step(swapped_b, half)
+    total = half_steps(fwd_b, swapped_b, swapped_ids, half, total)
+    last = last_step(swapped_a, swapped_ids, 0) + last_step(swapped_b, swapped_ids, half)
     total = total + jnp.where(odd, last, 0.0)
     forward_part = jnp.where(odd, 0.0, last)
     totals = jnp.stack([total.reshape(device_count, capacity), forward_part.reshape(device_count, capacity)], axis=1)

time: 156 us -> 161 us (1.032)
  waiting for transfers between devices: 75 us -> 79.5 us
  starting transfers between devices: 24.5 us -> 21.5 us
    ppermute x6 -> x5, waiting for transfers between devices: 33.3 us -> 38.4 us  [moved(): return lax.ppermute(x, 'blk', [(pos2dev[a], pos2dev[b]) for a, b in moves])]
    ppermute x6 -> x5, starting transfers between devices: 17 us -> 14 us  [moved(): return lax.ppermute(x, 'blk', [(pos2dev[a], pos2dev[b]) for a, b in moves])]
    slice x2 -> x4, local copies, waits for them, and re-layouts: 0.21 us -> 2.1 us  [the longest x1 1.86 us: last_step(): back2_held = jnp.concatenate([back2[:half], back2[lead:]], axis=0)]
  transfers between devices with their start and end apart: 7 -> 6, of which waited for: 3 -> 3; matrix products, arithmetic and copies ran while one was open for 11% -> 13% of each run, Pallas kernels for 0% -> 0%
where the time goes in v9:
time: 161 us; the launch traced here: 160 us
  waiting for transfers between devices  79.5 us (49%)
  matrix products  21.6 us (13%)
  starting transfers between devices  21.5 us (13%)
  other arithmetic  16.1 us (10%)
  blocking collectives  12.3 us (8%)
  local copies, waits for them, and re-layouts  5.04 us (3%)
  between operations  4.27 us (3%)
    all_to_all x1, waiting for transfers between devices, body(): lax.all_to_all(payload, 'blk', split_axis=0, concat_axis=0, tiled=True)  41.2 us
    ppermute x5, waiting for transfers between devices, moved(): return lax.ppermute(x, 'blk', [(pos2dev[a], pos2dev[b]) for a, b in moves])  38.4 us
    dot_general x7, matrix products, step_total(): lax.dot_general(local, remote, (((1,), (1,)), ((), ())), preferred_elemen...  19 us
    ppermute x5, starting transfers between devices, moved(): return lax.ppermute(x, 'blk', [(pos2dev[a], pos2dev[b]) for a, b in moves])  14 us
    all_to_all x1, blocking collectives, body(): lax.all_to_all(totals, 'blk', split_axis=0, concat_axis=0, tiled=True)  12.3 us
    all_to_all x1, starting transfers between devices, body(): lax.all_to_all(payload, 'blk', split_axis=0, concat_axis=0, tiled=True)  7.52 us
  transfers between devices with their start and end apart: 6, of which 3 were waited for; matrix products, arithmetic and copies ran while one was open for 13% of the time, Pallas kernels for 0%

profile of v9, /device:TPU:0, one launch (start us, length us, event | category | flops | bytes accessed | tf_op | source)
XLA Modules:
  0.0 160.4 jit_solution(7479832786927569366)
XLA Ops:
  0.0 0.8 broadcast_add_fusion
  0.8 0.7 convert.13
  1.5 0.1 copy.72
  1.7 0.1 reshape.366
  1.8 2.0 %fusion.2 = f32[960]{0:T(1024)S(1)} fusion(bf16[960,1024]{1,0:T(8,128)(2,1)} %param.7), kind=kLoop, calls=%fused_computation.7 | loop fusion | flops 2948160 | bytes 1969920 | tf_op jit(solution)/shard_map/reduce_sum | solution.py:69
  3.8 1.2 convert_reduce_fusion
  5.0 0.7 fusion.29
  5.7 0.6 select_reduce_fusion.2
  6.4 0.1 sub.11
  6.5 0.1 pad.24.clone
  6.6 2.6 %fusion.9 = bf16[1024,1024]{1,0:T(8,128)(2,1)S(1)} fusion(bf16[960,1024]{1,0:T(8,128)(2,1)S(1)} %copy-done.2, f32[960]{0:T(1024)S(1)} %add_rsqrt_fusion, s32[960]{0:T(1024)S(1)} %get-tuple-element.42), kind=kOutput, calls=%fused_computation.37 | convolution fusion | flops 2018246656 | bytes 4070912 | tf_op jit(solution)/shard_map/dot_general | solution.py:77
  9.2 1.7 %pad_maximum_fusion.1 = bf16[16,65,1024]{2,1,0:T(8,128)(2,1)} fusion(bf16[16,1,1024]{2,1,0:T(2,128)(2,1)S(1)} %copy.73, bf16[16,64,1024]{2,1,0:T(8,128)(2,1)S(1)} %bitcast.100), kind=kLoop, calls=%fused_computation.20 | loop fusion | flops 4259840 | bytes 4259840 | tf_op jit(solution)/shard_map/concatenate | solution.py:90
  10.9 7.5 %all-to-all-start = ((bf16[16,65,1024]{2,1,0:T(8,128)(2,1)}), bf16[16,65,1024]{2,1,0:T(8,128)(2,1)S(1)}, u32[]{:S(2)}, u32[]{:S(2)}) async-start(bf16[16,65,1024]{2,1,0:T(8,128)(2,1)} %pad_maximum_fusion.1), calls=%async_computation | async-start | bytes 4718592 | tf_op jit(solution)/shard_map/all_to_all | solution.py:91
  18.5 0.6 dynamic_slice.9
  23.0 41.2 %all-to-all-done = bf16[16,65,1024]{2,1,0:T(8,128)(2,1)S(1)} async-done(((bf16[16,65,1024]{2,1,0:T(8,128)(2,1)}), bf16[16,65,1024]{2,1,0:T(8,128)(2,1)S(1)}, u32[]{:S(2)}, u32[]{:S(2)}) %all-to-all-start) | async-done | bytes 2129952 | tf_op jit(solution)/shard_map/all_to_all | solution.py:91
  64.2 0.1 reshape.298
  64.2 0.1 slice.220
  64.4 0.1 copy.75
  64.5 0.1 dynamic-slice_select_fusion
  64.6 0.1 copy.76
  64.7 0.1 convert_reduce_fusion.1
  64.8 0.2 fusion.34
  65.0 0.1 pad_maximum_fusion.3
  65.1 7.8 %collective-permute-start = (bf16[528,1024]{1,0:T(8,128)(2,1)S(1)}, bf16[528,1024]{1,0:T(8,128)(2,1)S(1)}, u32[]{:S(2)}, u32[]{:S(2)}) collective-permute-start(bf16[528,1024]{1,0:T(8,128)(2,1)S(1)} %pad_maximum_fusion.3), channel_id=1, source_target_pairs={{0,4},{1,5},{4,8},{5,9},{8,12},{9,13},{12,14},{13,15},{14,10},{15,... | collective-permute-start | bytes 3244040 | tf_op jit(solution)/shard_map/ppermute | solution.py:23
  72.9 0.2 slice.219
  73.1 3.2 %bitcast_reduce_fusion = f32[1024,8]{0,1:T(8,128)S(1)} fusion(bf16[1024,1024]{1,0:T(8,128)(2,1)S(1)} %bitcast.93, s32[1024]{0:T(1024)S(1)} %reshape.298, pred[1024]{0:T(1024)(128)(4,1)S(1)} %broadcast_compare_fusion.1), kind=kOutput, calls=%fused_computation.2 | convolution fusion | flops 2155864064 | bytes 2135040 | tf_op jit(solution)/shard_map/dot_general | solution.py:30
  76.3 0.1 fusion.17
  76.4 0.2 pad_maximum_fusion.2
  76.6 19.5 %collective-permute-done = bf16[528,1024]{1,0:T(8,128)(2,1)S(1)} collective-permute-done((bf16[528,1024]{1,0:T(8,128)(2,1)S(1)}, bf16[528,1024]{1,0:T(8,128)(2,1)S(1)}, u32[]{:S(2)}, u32[]{:S(2)}) %collective-permute-start) | collective-permute-done | bytes 1081376 | tf_op jit(solution)/shard_map/ppermute | solution.py:23
  96.1 2.1 %pad_maximum_fusion = bf16[1568,1024]{1,0:T(8,128)(2,1)} fusion(bf16[1040,1024]{1,0:T(8,128)(2,1)S(1)} %pad_maximum_fusion.2, bf16[528,1024]{1,0:T(8,128)(2,1)S(1)} %collective-permute-done), kind=kLoop, calls=%fused_computation.19 | loop fusion | flops 6422528 | bytes 6422528 | tf_op jit(solution)/shard_map/concatenate | solution.py:119
  98.2 5.9 %collective-permute-start.4 = (bf16[1040,1024]{1,0:T(8,128)(2,1)S(1)}, bf16[1040,1024]{1,0:T(8,128)(2,1)}, u32[]{:S(2)}, u32[]{:S(2)}) collective-permute-start(bf16[1040,1024]{1,0:T(8,128)(2,1)S(1)} %pad_maximum_fusion.2), channel_id=1, source_target_pairs={{0,2},{4,0},{8,4},{12,8},{14,12},{10,14},{6,10},{2,6},{16,18},{20,... | collective-permute-start | bytes 6389768 | tf_op jit(solution)/shard_map/ppermute | solution.py:23
  104.2 0.1 copy.79
  104.3 0.1 copy.77
  104.4 0.1 copy.78
  104.5 0.1 convert_reduce_fusion.5
  104.6 0.2 collective-permute-start.1
  104.9 0.7 slice_convert_fusion.4
  105.6 3.5 %bitcast_reduce_fusion.6 = f32[1024,4]{0,1:T(4,128)S(1)} fusion(bf16[1024,1024]{1,0:T(8,128)(2,1)} %bitcast.94, bf16[528,1024]{1,0:T(8,128)(2,1)} %copy-done.3, s32[1024]{0:T(1024)S(1)} %reshape.298, s32[512]{0:T(512)S(1)} %bitcast.120, pred[1024]{0:T(1024)(128)(4,1)S(1)} %broadcast_compare_fusion.1), kind=kOutput, calls=%fused_computation.28 | convolution fusion | flops 1076359168 | bytes 3169280 | tf_op jit(solution)/shard_map/dot_general | solution.py:30
  109.1 0.1 fusion.23
  109.2 18.9 %collective-permute-done.4 = bf16[1040,1024]{1,0:T(8,128)(2,1)} collective-permute-done((bf16[1040,1024]{1,0:T(8,128)(2,1)S(1)}, bf16[1040,1024]{1,0:T(8,128)(2,1)}, u32[]{:S(2)}, u32[]{:S(2)}) %collective-permute-start.4) | collective-permute-done | bytes 2129952 | tf_op jit(solution)/shard_map/ppermute | solution.py:23
  128.0 0.7 slice_convert_fusion.1
  128.8 1.9 %fusion.35 = (bf16[512,1024]{1,0:T(8,128)(2,1)S(1)}, bf16[512,1024]{1,0:T(8,128)(2,1)S(1)}) fusion(bf16[1040,1024]{1,0:T(8,128)(2,1)} %collective-permute-done.4), kind=kLoop, calls=%fused_computation.120 | loop fusion | bytes 4194304 | tf_op jit(solution)/shard_map/slice | solution.py:139
  130.6 0.7 slice_convert_fusion.3
  131.4 3.2 %bitcast_reduce_fusion.5 = f32[1024,4]{0,1:T(4,128)S(1)} fusion(bf16[1024,1024]{1,0:T(8,128)(2,1)S(1)} %bitcast.95, bf16[1568,1024]{1,0:T(8,128)(2,1)} %collective-permute-done.2, s32[1024]{0:T(1024)S(1)} %reshape.298, s32[512]{0:T(512)S(1)} %broadcast_select_fusion.3, pred[]{:T(512)S(6)} %eq.265, pred[1024]{0:T(1024)(128)(4,1)S(1)} %broadcast_compare_fusion.1), kind=kOutput, calls=%fused_computation.27 | convolution fusion | flops 1076883456 | bytes 4217857 | tf_op jit(solution)/shard_map/dot_general | solution.py:30
  134.6 0.1 fusion.22
  134.7 0.1 collective-permute-start.3
  134.8 2.9 %bitcast_reduce_fusion.2 = f32[1024,4]{0,1:T(4,128)S(1)} fusion(s32[1024]{0:T(1024)S(1)} %get-tuple-element.30, s32[512]{0:T(512)S(1)} %bitcast.117, pred[1024]{0:T(1024)(128)(4,1)S(1)} %get-tuple-element.29, bf16[1568,1024]{1,0:T(8,128)(2,1)} %collective-permute-done.2, bf16[1024,1024]{1,0:T(8,128)(2,1)S(1)} %bitcast.96, ...), kind=kOutput, calls=%fused_computation.24 | convolution fusion | flops 1081602048 | bytes 5266433 | tf_op jit(solution)/shard_map/dot_general | solution.py:30
  137.7 0.1 fusion.19
  137.8 1.6 %bitcast_reduce_fusion.4 = f32[1024,4]{0,1:T(4,128)S(1)} fusion(bf16[1024,1024]{1,0:T(8,128)(2,1)S(1)} %bitcast.97, bf16[512,1024]{1,0:T(8,128)(2,1)S(1)} %collective-permute-done.1, s32[1024]{0:T(1024)S(1)} %reshape.298, s32[512]{0:T(512)S(1)} %bitcast.119, pred[1024]{0:T(1024)(128)(4,1)S(1)} %broadcast_compare_fusion.1), kind=kOutput, calls=%fused_computation.26 | convolution fusion | flops 1076359168 | bytes 3169280 | tf_op jit(solution)/shard_map/dot_general | solution.py:30
  139.5 0.1 fusion.21
  139.5 1.7 %bitcast_reduce_fusion.1 = f32[1024,4]{0,1:T(4,128)S(1)} fusion(bf16[512,1024]{1,0:T(8,128)(2,1)S(1)} %collective-permute-done.3, s32[1024]{0:T(1024)S(1)} %get-tuple-element.30, s32[512]{0:T(512)S(1)} %bitcast.114, pred[1024]{0:T(1024)(128)(4,1)S(1)} %get-tuple-element.29, bf16[1024,1024]{1,0:T(8,128)(2,1)S(1)} %bitcast.98, ...), kind=kOutput, calls=%fused_computation.23 | convolution fusion | flops 1081602048 | bytes 5266433 | tf_op jit(solution)/shard_map/dot_general | solution.py:30
  141.3 0.1 fusion.18
  141.3 2.9 %bitcast_reduce_fusion.3 = f32[1024,4]{0,1:T(4,128)S(1)} fusion(bf16[1024,1024]{1,0:T(8,128)(2,1)S(1)} %bitcast.99, bf16[512,1024]{1,0:T(8,128)(2,1)S(1)} %collective-permute-done.3, bf16[1568,1024]{1,0:T(8,128)(2,1)} %collective-permute-done.2, s32[1024]{0:T(1024)S(1)} %reshape.298, s32[512]{0:T(512)S(1)} %broadcast_select_fusion.2, pred[]{:T(512)S(6)} %eq.265, ...), kind=kOutput, calls=%fused_computation.25 | convolution fusion | flops 1076883456 | bytes 4217857 | tf_op jit(solution)/shard_map/dot_general | solution.py:30
  144.2 0.1 fusion.20
  144.3 0.1 stack_reshape.4
  144.4 0.1 select_n.196
  144.5 0.1 reshape.369
  144.6 12.3 %all_to_all.10 = f32[16,1,128]{2,1,0:T(1,128)S(1)} all-to-all(f32[16,1,128]{2,1,0:T(1,128)S(1)} %reshape.369), channel_id=1, replica_groups=mesh['groups'=2,'blk'=16] {'blk'}, dimensions={0} | all-to-all | bytes 16384 | tf_op jit(solution)/shard_map/all_to_all | solution.py:160
  156.9 0.5 broadcast.270
  157.4 0.7 reduce.40
  158.0 0.1 reshape.370
  158.2 0.1 broadcast_in_dim.136
  158.3 1.5 select_reduce_fusion
  159.8 0.6 add_log-plus-one_fusion
  (44 shorter events, 0.4 us)
Async XLA Ops:
  0.0 6.6 %copy-start.2 = (bf16[960,1024]{1,0:T(8,128)(2,1)S(1)}, bf16[960,1024]{1,0:T(8,128)(2,1)}, u32[]{:S(2)}) copy-start(bf16[960,1024]{1,0:T(8,128)(2,1)} %param.7) | copy-start | bytes 5898244
  10.9 7.5 %copy-start.4 = (s32[16]{0:T(128)S(1)}, s32[16]{0:T(128)}, u32[]{:S(2)}) copy-start(s32[16]{0:T(128)} %constant.73.clone) | copy-start | bytes 196
  10.9 53.2 %all-to-all-start = ((bf16[16,65,1024]{2,1,0:T(8,128)(2,1)}), bf16[16,65,1024]{2,1,0:T(8,128)(2,1)S(1)}, u32[]{:S(2)}, u32[]{:S(2)}) async-start(bf16[16,65,1024]{2,1,0:T(8,128)(2,1)} %pad_maximum_fusion.1), calls=%async_computation | async-start | bytes 4718592 | tf_op jit(solution)/shard_map/all_to_all | solution.py:91
  65.1 31.0 %collective-permute-start = (bf16[528,1024]{1,0:T(8,128)(2,1)S(1)}, bf16[528,1024]{1,0:T(8,128)(2,1)S(1)}, u32[]{:S(2)}, u32[]{:S(2)}) collective-permute-start(bf16[528,1024]{1,0:T(8,128)(2,1)S(1)} %pad_maximum_fusion.3), channel_id=1, source_target_pairs={{0,4},{1,5},{4,8},{5,9},{8,12},{9,13},{12,14},{13,15},{14,10},{15,... | collective-permute-start | bytes 3244040 | tf_op jit(solution)/shard_map/ppermute | solution.py:23
  73.1 3.2 %copy-start = (bf16[16,64,1024]{2,1,0:T(8,128)(2,1)}, bf16[16,64,1024]{2,1,0:T(8,128)(2,1)S(1)}, u32[]{:S(2)}) copy-start(bf16[16,64,1024]{2,1,0:T(8,128)(2,1)S(1)} %slice.219) | copy-start | bytes 6291460
  96.1 2.1 %copy-start.3 = (bf16[528,1024]{1,0:T(8,128)(2,1)}, bf16[528,1024]{1,0:T(8,128)(2,1)S(1)}, u32[]{:S(2)}) copy-start(bf16[528,1024]{1,0:T(8,128)(2,1)S(1)} %collective-permute-done) | copy-start | bytes 3244036
  98.2 32.4 %collective-permute-start.2 = (bf16[1568,1024]{1,0:T(8,128)(2,1)}, bf16[1568,1024]{1,0:T(8,128)(2,1)}, u32[]{:S(2)}, u32[]{:S(2)}) collective-permute-start(bf16[1568,1024]{1,0:T(8,128)(2,1)} %pad_maximum_fusion), channel_id=1, source_target_pairs={{0,1},{1,0},{4,5},{5,4},{8,9},{9,8},{12,13},{13,12},{14,15},{15,14... | collective-permute-start | bytes 9633800 | tf_op jit(solution)/shard_map/ppermute | solution.py:23
  98.2 29.8 %collective-permute-start.4 = (bf16[1040,1024]{1,0:T(8,128)(2,1)S(1)}, bf16[1040,1024]{1,0:T(8,128)(2,1)}, u32[]{:S(2)}, u32[]{:S(2)}) collective-permute-start(bf16[1040,1024]{1,0:T(8,128)(2,1)S(1)} %pad_maximum_fusion.2), channel_id=1, source_target_pairs={{0,2},{4,0},{8,4},{12,8},{14,12},{10,14},{6,10},{2,6},{16,18},{20,... | collective-permute-start | bytes 6389768 | tf_op jit(solution)/shard_map/ppermute | solution.py:23
  104.6 30.1 %collective-permute-start.1 = (bf16[512,1024]{1,0:T(8,128)(2,1)S(1)}, bf16[512,1024]{1,0:T(8,128)(2,1)S(1)}, u32[]{:S(2)}, u32[]{:S(2)}) collective-permute-start(bf16[512,1024]{1,0:T(8,128)(2,1)S(1)} %bitcast.92), channel_id=1, source_target_pairs={{0,4},{1,5},{4,8},{5,9},{8,12},{9,13},{12,14},{13,15},{14,10},{15,... | collective-permute-start | bytes 3145736 | tf_op jit(solution)/shard_map/ppermute | solution.py:23
  128.8 2.7 %copy-start.1 = (bf16[16,64,1024]{2,1,0:T(8,128)(2,1)S(1)}, bf16[16,64,1024]{2,1,0:T(8,128)(2,1)}, u32[]{:S(2)}) copy-start(bf16[16,64,1024]{2,1,0:T(8,128)(2,1)} %copy-done) | copy-start | bytes 6291460
  134.7 4.8 %collective-permute-start.3 = (bf16[512,1024]{1,0:T(8,128)(2,1)S(1)}, bf16[512,1024]{1,0:T(8,128)(2,1)S(1)}, u32[]{:S(2)}, u32[]{:S(2)}) collective-permute-start(bf16[512,1024]{1,0:T(8,128)(2,1)S(1)} %collective-permute-done.1), channel_id=1, source_target_pairs={{0,1},{1,0},{4,5},{5,4},{8,9},{9,8},{12,13},{13,12},{14,15},{15,14... | collective-permute-start | bytes 3145736 | tf_op jit(solution)/shard_map/ppermute | solution.py:23

commit v10 on v8

--- a/solution.py
+++ b/solution.py
@@ -111,7 +111,7 @@
         (fwd_a, pack(own[half:], own_ids[half:]), pack(own, own_ids))
     )
     fwd_b = moved(second_half, pos2dev, forward)
-    back2 = moved(packed, pos2dev, [(p, (p - 2) % n) for p in evens])
+    back2 = moved(packed, pos2dev, [(p, (p - 2) % n) for p in evens] + [(p, p) for p in range(1, n, 2)])
     swapped_a = moved(fwd_a, pos2dev, swap)
     across_held, across_ids = unpack(across)
 
@@ -134,8 +134,8 @@
         back2_held, back2_ids = unpack(back2)
         swapped_held, swapped_ids = unpack(swapped)
         return step_total(
-            jnp.where(odd, own, back2_held),
-            jnp.where(odd, own_ids, back2_ids),
+            back2_held,
+            back2_ids,
             swapped_held,
             swapped_ids,
             jnp.where(odd, my_pairs[3], ahead_pairs[3]),
@@ -152,15 +152,14 @@
     forward_part = jnp.where(odd, 0.0, last)
     totals = jnp.stack([total.reshape(device_count, capacity), forward_part.reshape(device_count, capacity)], axis=1)
     returned = lax.all_to_all(totals, "blk", split_axis=0, concat_axis=0, tiled=True)
-    owner_sum = jnp.sum(
-        jnp.where(place[:, None] == slot_index[None, :], returned[:, 0].reshape(-1)[None, :], 0.0), axis=1
-    )
     behind = jnp.asarray(np.asarray(pos2dev, np.int32))[(owners - 2) % device_count] * capacity + arrival
     behind = jnp.where(owners % 2 == 0, behind, -1)
-    handed_sum = jnp.sum(
-        jnp.where(behind[:, None] == slot_index[None, :], returned[:, 1].reshape(-1)[None, :], 0.0), axis=1
+    both = jnp.sum(
+        jnp.where(place[:, None] == slot_index[None, :], returned[:, 0].reshape(-1)[None, :], 0.0)
+        + jnp.where(behind[:, None] == slot_index[None, :], returned[:, 1].reshape(-1)[None, :], 0.0),
+        axis=1,
     )
-    return jnp.log1p(owner_sum + handed_sum)
+    return jnp.log1p(both)
 
 
 def solution(mesh):

time: 154 us -> 153 us (level)
  no operation moved by 1% of the time
where the time goes in v10:
time: 153 us
  waiting for transfers between devices  77.7 us (51%)
  starting transfers between devices  24.6 us (16%)
  matrix products  18.2 us (12%)
  other arithmetic  12.8 us (8%)
  blocking collectives  10.8 us (7%)
  local copies, waits for them, and re-layouts  4.37 us (3%)
  between operations  4.3 us (3%)
    all_to_all x1, waiting for transfers between devices, body(): lax.all_to_all(payload, 'blk', split_axis=0, concat_axis=0, tiled=True)  41.1 us
    ppermute x6, waiting for transfers between devices, moved(): return lax.ppermute(x, 'blk', [(pos2dev[a], pos2dev[b]) for a, b in moves])  36.6 us
    ppermute x6, starting transfers between devices, moved(): return lax.ppermute(x, 'blk', [(pos2dev[a], pos2dev[b]) for a, b in moves])  17.1 us
    dot_general x7, matrix products, step_total(): lax.dot_general(local, remote, (((1,), (1,)), ((), ())), preferred_elemen...  15.5 us
    all_to_all x1, blocking collectives, body(): lax.all_to_all(totals, 'blk', split_axis=0, concat_axis=0, tiled=True)  10.8 us
    all_to_all x1, starting transfers between devices, body(): lax.all_to_all(payload, 'blk', split_axis=0, concat_axis=0, tiled=True)  7.52 us
  transfers between devices with their start and end apart: 7, of which 4 were waited for; matrix products, arithmetic and copies ran while one was open for 9% of the time, Pallas kernels for 0%

profile of v10, /device:TPU:0, one launch (start us, length us, event | category | flops | bytes accessed | tf_op | source)
XLA Modules:
  0.0 152.8 jit_solution(3914944694660425657)
XLA Ops:
  0.0 0.8 convert.17
  0.8 0.1 copy.74
  1.0 0.1 reshape.380
  1.1 2.0 %fusion.2 = f32[960]{0:T(1024)S(1)} fusion(bf16[960,1024]{1,0:T(8,128)(2,1)} %param.7), kind=kLoop, calls=%fused_computation.7 | loop fusion | flops 2948160 | bytes 1969920 | tf_op jit(solution)/shard_map/reduce_sum | solution.py:69
  3.1 1.2 convert_reduce_fusion
  4.3 0.7 fusion.45
  5.1 0.6 select_reduce_fusion
  5.7 0.1 sub.11
  5.8 0.1 pad.31.clone
  6.0 2.6 %fusion.9 = bf16[1024,1024]{1,0:T(8,128)(2,1)S(1)} fusion(bf16[960,1024]{1,0:T(8,128)(2,1)S(1)} %copy-done.2, f32[960]{0:T(1024)S(1)} %add_rsqrt_fusion, s32[960]{0:T(1024)S(1)} %get-tuple-element.40), kind=kOutput, calls=%fused_computation.34 | convolution fusion | flops 2018246656 | bytes 4070912 | tf_op jit(solution)/shard_map/dot_general | solution.py:77
  8.6 1.7 %pad_maximum_fusion = bf16[16,65,1024]{2,1,0:T(8,128)(2,1)} fusion(bf16[16,1,1024]{2,1,0:T(2,128)(2,1)S(1)} %copy.75, bf16[16,64,1024]{2,1,0:T(8,128)(2,1)S(1)} %bitcast.103), kind=kLoop, calls=%fused_computation.18 | loop fusion | flops 4259840 | bytes 4259840 | tf_op jit(solution)/shard_map/concatenate | solution.py:90
  10.3 7.5 %all-to-all-start = ((bf16[16,65,1024]{2,1,0:T(8,128)(2,1)}), bf16[16,65,1024]{2,1,0:T(8,128)(2,1)S(1)}, u32[]{:S(2)}, u32[]{:S(2)}) async-start(bf16[16,65,1024]{2,1,0:T(8,128)(2,1)} %pad_maximum_fusion), calls=%async_computation | async-start | bytes 4718592 | tf_op jit(solution)/shard_map/all_to_all | solution.py:91
  17.8 0.6 dynamic_slice.9
  22.3 41.1 %all-to-all-done = bf16[16,65,1024]{2,1,0:T(8,128)(2,1)S(1)} async-done(((bf16[16,65,1024]{2,1,0:T(8,128)(2,1)}), bf16[16,65,1024]{2,1,0:T(8,128)(2,1)S(1)}, u32[]{:S(2)}, u32[]{:S(2)}) %all-to-all-start) | async-done | bytes 2129952 | tf_op jit(solution)/shard_map/all_to_all | solution.py:91
  63.5 0.1 convert_element_type.172
  63.6 0.1 convert_element_type.170
  63.7 0.1 convert_element_type.165
  63.9 0.2 slice.216
  64.2 1.6 %pad_maximum_fusion.1 = bf16[1040,1024]{1,0:T(8,128)(2,1)} fusion(bf16[16,1024]{1,0:T(8,128)(2,1)S(1)} %reshape.298, bf16[1024,1024]{1,0:T(8,128)(2,1)S(1)} %bitcast.95), kind=kLoop, calls=%fused_computation.19 | loop fusion | flops 4259840 | bytes 4259840 | tf_op jit(solution)/shard_map/concatenate | solution.py:47
  65.8 0.3 copy-done
  66.1 4.0 %collective-permute-start.1 = (bf16[1040,1024]{1,0:T(8,128)(2,1)}, bf16[1040,1024]{1,0:T(8,128)(2,1)}, u32[]{:S(2)}, u32[]{:S(2)}) collective-permute-start(bf16[1040,1024]{1,0:T(8,128)(2,1)} %pad_maximum_fusion.1), channel_id=1, source_target_pairs={{0,1},{4,5},{8,9},{12,13},{14,15},{10,11},{6,7},{2,3},{16,17},{20,... | collective-permute-start | bytes 6389768 | tf_op jit(solution)/shard_map/ppermute | solution.py:23
  70.1 0.1 slice.217
  70.2 0.1 copy.77
  70.3 0.1 dynamic-slice_select_fusion
  70.4 0.1 copy.81
  70.5 0.1 copy.79
  70.6 0.1 copy.78
  70.7 0.1 convert_reduce_fusion.1
  70.8 0.1 copy.80
  70.9 0.1 convert_reduce_fusion.5
  71.1 0.2 fusion.48
  71.3 0.1 pad_maximum_fusion.2
  71.3 6.9 %collective-permute-start = (bf16[528,1024]{1,0:T(8,128)(2,1)S(1)}, bf16[528,1024]{1,0:T(8,128)(2,1)S(1)}, u32[]{:S(2)}, u32[]{:S(2)}) collective-permute-start(bf16[528,1024]{1,0:T(8,128)(2,1)S(1)} %pad_maximum_fusion.2), channel_id=1, source_target_pairs={{0,4},{1,5},{4,8},{5,9},{8,12},{9,13},{12,14},{13,15},{14,10},{15,... | collective-permute-start | bytes 3244040 | tf_op jit(solution)/shard_map/ppermute | solution.py:23
  78.3 3.2 %bitcast_reduce_fusion = f32[1024,8]{0,1:T(8,128)S(1)} fusion(bf16[1024,1024]{1,0:T(8,128)(2,1)S(1)} %bitcast.96, s32[1024]{0:T(1024)S(1)} %convert_element_type.165, pred[1024]{0:T(1024)(128)(4,1)S(1)} %broadcast_compare_fusion.1), kind=kOutput, calls=%fused_computation.2 | convolution fusion | flops 2155864064 | bytes 2135040 | tf_op jit(solution)/shard_map/dot_general | solution.py:30
  81.5 0.1 fusion.32
  81.6 0.1 pad_maximum_fusion.3
  81.6 18.0 %collective-permute-done = bf16[528,1024]{1,0:T(8,128)(2,1)S(1)} collective-permute-done((bf16[528,1024]{1,0:T(8,128)(2,1)S(1)}, bf16[528,1024]{1,0:T(8,128)(2,1)S(1)}, u32[]{:S(2)}, u32[]{:S(2)}) %collective-permute-start) | collective-permute-done | bytes 1081376 | tf_op jit(solution)/shard_map/ppermute | solution.py:23
  99.7 3.0 %collective-permute-start.2 = (bf16[528,1024]{1,0:T(8,128)(2,1)S(1)}, bf16[528,1024]{1,0:T(8,128)(2,1)S(1)}, u32[]{:S(2)}, u32[]{:S(2)}) collective-permute-start(bf16[528,1024]{1,0:T(8,128)(2,1)S(1)} %pad_maximum_fusion.3), channel_id=1, source_target_pairs={{0,4},{1,5},{4,8},{5,9},{8,12},{9,13},{12,14},{13,15},{14,10},{15,... | collective-permute-start | bytes 3244040 | tf_op jit(solution)/shard_map/ppermute | solution.py:23
  102.7 3.1 %collective-permute-start.5 = (bf16[1040,1024]{1,0:T(8,128)(2,1)}, bf16[1040,1024]{1,0:T(8,128)(2,1)S(1)}, u32[]{:S(2)}, u32[]{:S(2)}) collective-permute-start(bf16[1040,1024]{1,0:T(8,128)(2,1)} %pad_maximum_fusion.1), channel_id=1, source_target_pairs={{0,2},{4,0},{8,4},{12,8},{14,12},{10,14},{6,10},{2,6},{1,1},{5,5},... | collective-permute-start | bytes 6389768 | tf_op jit(solution)/shard_map/ppermute | solution.py:23
  105.8 1.6 %bitcast_reduce_fusion.6 = f32[1024,4]{0,1:T(4,128)S(1)} fusion(bf16[1024,1024]{1,0:T(8,128)(2,1)S(1)} %bitcast.97, bf16[528,1024]{1,0:T(8,128)(2,1)S(1)} %collective-permute-done, s32[1024]{0:T(1024)S(1)} %convert_element_type.165, s32[512]{0:T(512)S(1)} %slice_convert_fusion.6, pred[1024]{0:T(1024)(128)(4,1)S(1)} %broadcast_compare_fusion.1), kind=kOutput, calls=%fused_computation.25 | convolution fusion | flops 1076359168 | bytes 3169280 | tf_op jit(solution)/shard_map/dot_general | solution.py:30
  107.5 0.1 fusion.38
  107.6 0.7 slice_convert_fusion.2
  108.3 2.9 %bitcast_reduce_fusion.5 = f32[1024,4]{0,1:T(4,128)S(1)} fusion(bf16[1024,1024]{1,0:T(8,128)(2,1)S(1)} %bitcast.98, bf16[1040,1024]{1,0:T(8,128)(2,1)} %collective-permute-done.1, s32[1024]{0:T(1024)S(1)} %convert_element_type.165, s32[512]{0:T(512)S(1)} %broadcast_select_fusion.2, pred[]{:T(512)S(6)} %eq.265, ...), kind=kOutput, calls=%fused_computation.24 | convolution fusion | flops 1076883456 | bytes 4217857 | tf_op jit(solution)/shard_map/dot_general | solution.py:30
  111.2 0.1 fusion.37
  111.3 16.9 %collective-permute-done.2 = bf16[528,1024]{1,0:T(8,128)(2,1)S(1)} collective-permute-done((bf16[528,1024]{1,0:T(8,128)(2,1)S(1)}, bf16[528,1024]{1,0:T(8,128)(2,1)S(1)}, u32[]{:S(2)}, u32[]{:S(2)}) %collective-permute-start.2) | collective-permute-done | bytes 1081376 | tf_op jit(solution)/shard_map/ppermute | solution.py:23
  128.3 1.6 %bitcast_reduce_fusion.4 = f32[1024,4]{0,1:T(4,128)S(1)} fusion(bf16[1024,1024]{1,0:T(8,128)(2,1)S(1)} %bitcast.99, bf16[528,1024]{1,0:T(8,128)(2,1)S(1)} %collective-permute-done.2, s32[1024]{0:T(1024)S(1)} %convert_element_type.165, s32[512]{0:T(512)S(1)} %slice_convert_fusion.4, pred[1024]{0:T(1024)(128)(4,1)S(1)} %broadcast_compare_fusion.1), kind=kOutput, calls=%fused_computation.23 | convolution fusion | flops 1076359168 | bytes 3169280 | tf_op jit(solution)/shard_map/dot_general | solution.py:30
  129.9 0.1 fusion.36
  130.0 1.6 %collective-permute-done.5 = bf16[1040,1024]{1,0:T(8,128)(2,1)S(1)} collective-permute-done((bf16[1040,1024]{1,0:T(8,128)(2,1)}, bf16[1040,1024]{1,0:T(8,128)(2,1)S(1)}, u32[]{:S(2)}, u32[]{:S(2)}) %collective-permute-start.5) | collective-permute-done | bytes 2129952 | tf_op jit(solution)/shard_map/ppermute | solution.py:23
  131.7 1.6 %bitcast_reduce_fusion.2 = f32[1024,4]{0,1:T(4,128)S(1)} fusion(bf16[1040,1024]{1,0:T(8,128)(2,1)S(1)} %collective-permute-done.5, s32[1024]{0:T(1024)S(1)} %bitcast.112, s32[512]{0:T(512)S(1)} %slice_convert_fusion.5, pred[1024]{0:T(1024)(128)(4,1)S(1)} %broadcast_compare_fusion, bf16[528,1024]{1,0:T(8,128)(2,1)S(1)} %collective-permute-done.3), kind=kOutput, calls=%fused_computation.21 | convolution fusion | flops 1076359168 | bytes 3169280 | tf_op jit(solution)/shard_map/dot_general | solution.py:30
  133.3 0.1 fusion.34
  133.4 2.9 %bitcast_reduce_fusion.3 = f32[1024,4]{0,1:T(4,128)S(1)} fusion(bf16[1024,1024]{1,0:T(8,128)(2,1)S(1)} %bitcast.100, bf16[1040,1024]{1,0:T(8,128)(2,1)} %collective-permute-done.1, s32[1024]{0:T(1024)S(1)} %convert_element_type.165, s32[512]{0:T(512)S(1)} %broadcast_select_fusion.1, pred[]{:T(512)S(6)} %eq.265, ...), kind=kOutput, calls=%fused_computation.22 | convolution fusion | flops 1076883456 | bytes 4217857 | tf_op jit(solution)/shard_map/dot_general | solution.py:30
  136.3 0.1 fusion.35
  136.4 1.7 %bitcast_reduce_fusion.1 = f32[1024,4]{0,1:T(4,128)S(1)} fusion(bf16[1040,1024]{1,0:T(8,128)(2,1)S(1)} %collective-permute-done.5, s32[1024]{0:T(1024)S(1)} %bitcast.113, s32[512]{0:T(512)S(1)} %slice_convert_fusion.3, pred[1024]{0:T(1024)(128)(4,1)S(1)} %broadcast_compare_fusion, bf16[528,1024]{1,0:T(8,128)(2,1)S(1)} %collective-permute-done.4), kind=kOutput, calls=%fused_computation.20 | convolution fusion | flops 1076359168 | bytes 3169280 | tf_op jit(solution)/shard_map/dot_general | solution.py:30
  138.1 0.1 fusion.33
  138.2 0.1 stack_reshape.4
  138.3 0.1 select_n.165
  138.4 0.1 reshape.383
  138.5 10.8 %all_to_all.10 = f32[16,1,128]{2,1,0:T(1,128)S(1)} all-to-all(f32[16,1,128]{2,1,0:T(1,128)S(1)} %reshape.383), channel_id=1, replica_groups=mesh['groups'=2,'blk'=16] {'blk'}, dimensions={0} | all-to-all | bytes 16384 | tf_op jit(solution)/shard_map/all_to_all | solution.py:154
  149.2 0.5 broadcast.269
  149.7 0.7 reduce.44
  150.4 0.1 reshape.384
  150.5 0.1 broadcast_in_dim.72
  150.7 1.5 add_reduce_fusion
  152.2 0.6 log1p.3
  (59 shorter events, 0.6 us)
Async XLA Ops:
  0.0 5.9 %copy-start.2 = (bf16[960,1024]{1,0:T(8,128)(2,1)S(1)}, bf16[960,1024]{1,0:T(8,128)(2,1)}, u32[]{:S(2)}) copy-start(bf16[960,1024]{1,0:T(8,128)(2,1)} %param.7) | copy-start | bytes 5898244
  10.3 7.5 %copy-start.3 = (s32[16]{0:T(128)S(1)}, s32[16]{0:T(128)}, u32[]{:S(2)}) copy-start(s32[16]{0:T(128)} %constant.73.clone) | copy-start | bytes 196
  10.3 53.2 %all-to-all-start = ((bf16[16,65,1024]{2,1,0:T(8,128)(2,1)}), bf16[16,65,1024]{2,1,0:T(8,128)(2,1)S(1)}, u32[]{:S(2)}, u32[]{:S(2)}) async-start(bf16[16,65,1024]{2,1,0:T(8,128)(2,1)} %pad_maximum_fusion), calls=%async_computation | async-start | bytes 4718592 | tf_op jit(solution)/shard_map/all_to_all | solution.py:91
  64.2 1.9 %copy-start = (bf16[16,64,1024]{2,1,0:T(8,128)(2,1)}, bf16[16,64,1024]{2,1,0:T(8,128)(2,1)S(1)}, u32[]{:S(2)}) copy-start(bf16[16,64,1024]{2,1,0:T(8,128)(2,1)S(1)} %slice.216) | copy-start | bytes 6291460
  66.1 33.5 %collective-permute-start.1 = (bf16[1040,1024]{1,0:T(8,128)(2,1)}, bf16[1040,1024]{1,0:T(8,128)(2,1)}, u32[]{:S(2)}, u32[]{:S(2)}) collective-permute-start(bf16[1040,1024]{1,0:T(8,128)(2,1)} %pad_maximum_fusion.1), channel_id=1, source_target_pairs={{0,1},{4,5},{8,9},{12,13},{14,15},{10,11},{6,7},{2,3},{16,17},{20,... | collective-permute-start | bytes 6389768 | tf_op jit(solution)/shard_map/ppermute | solution.py:23
  71.2 7.0 %copy-start.1 = (bf16[16,64,1024]{2,1,0:T(8,128)(2,1)S(1)}, bf16[16,64,1024]{2,1,0:T(8,128)(2,1)}, u32[]{:S(2)}) copy-start(bf16[16,64,1024]{2,1,0:T(8,128)(2,1)} %copy-done) | copy-start | bytes 6291460
  71.3 28.3 %collective-permute-start = (bf16[528,1024]{1,0:T(8,128)(2,1)S(1)}, bf16[528,1024]{1,0:T(8,128)(2,1)S(1)}, u32[]{:S(2)}, u32[]{:S(2)}) collective-permute-start(bf16[528,1024]{1,0:T(8,128)(2,1)S(1)} %pad_maximum_fusion.2), channel_id=1, source_target_pairs={{0,4},{1,5},{4,8},{5,9},{8,12},{9,13},{12,14},{13,15},{14,10},{15,... | collective-permute-start | bytes 3244040 | tf_op jit(solution)/shard_map/ppermute | solution.py:23
  99.6 8.7 %collective-permute-start.3 = (bf16[528,1024]{1,0:T(8,128)(2,1)S(1)}, bf16[528,1024]{1,0:T(8,128)(2,1)S(1)}, u32[]{:S(2)}, u32[]{:S(2)}) collective-permute-start(bf16[528,1024]{1,0:T(8,128)(2,1)S(1)} %collective-permute-done), channel_id=1, source_target_pairs={{0,1},{1,0},{4,5},{5,4},{8,9},{9,8},{12,13},{13,12},{14,15},{15,14... | collective-permute-start | bytes 3244040 | tf_op jit(solution)/shard_map/ppermute | solution.py:23
  99.7 28.6 %collective-permute-start.2 = (bf16[528,1024]{1,0:T(8,128)(2,1)S(1)}, bf16[528,1024]{1,0:T(8,128)(2,1)S(1)}, u32[]{:S(2)}, u32[]{:S(2)}) collective-permute-start(bf16[528,1024]{1,0:T(8,128)(2,1)S(1)} %pad_maximum_fusion.3), channel_id=1, source_target_pairs={{0,4},{1,5},{4,8},{5,9},{8,12},{9,13},{12,14},{13,15},{14,10},{15,... | collective-permute-start | bytes 3244040 | tf_op jit(solution)/shard_map/ppermute | solution.py:23
  102.7 28.9 %collective-permute-start.5 = (bf16[1040,1024]{1,0:T(8,128)(2,1)}, bf16[1040,1024]{1,0:T(8,128)(2,1)S(1)}, u32[]{:S(2)}, u32[]{:S(2)}) collective-permute-start(bf16[1040,1024]{1,0:T(8,128)(2,1)} %pad_maximum_fusion.1), channel_id=1, source_target_pairs={{0,2},{4,0},{8,4},{12,8},{14,12},{10,14},{6,10},{2,6},{1,1},{5,5},... | collective-permute-start | bytes 6389768 | tf_op jit(solution)/shard_map/ppermute | solution.py:23
  128.2 5.1 %collective-permute-start.4 = (bf16[528,1024]{1,0:T(8,128)(2,1)S(1)}, bf16[528,1024]{1,0:T(8,128)(2,1)S(1)}, u32[]{:S(2)}, u32[]{:S(2)}) collective-permute-start(bf16[528,1024]{1,0:T(8,128)(2,1)S(1)} %collective-permute-done.2), channel_id=1, source_target_pairs={{0,1},{1,0},{4,5},{5,4},{8,9},{9,8},{12,13},{13,12},{14,15},{15,14... | collective-permute-start | bytes 3244040 | tf_op jit(solution)/shard_map/ppermute | solution.py:23

commit v11 on v10

--- a/solution.py
+++ b/solution.py
@@ -106,29 +106,27 @@
     fwd_a = moved(pack(own[:half], own_ids[:half]), pos2dev, forward)
     across = moved(pack(own, own_ids), pos2dev, [(p, p + 1) for p in evens])
     total = step_total(own, own_ids, own, own_ids, my_pairs[0], True)
-    total, fwd_a, across = lax.optimization_barrier((total, fwd_a, across))
+    total, across = lax.optimization_barrier((total, across))
+    across_held, across_ids = unpack(across)
+    from_across = [
+        step_total(own, own_ids, across_held[lo : lo + half], across_ids[lo : lo + half], my_pairs[1], False, lo // 128)
+        for lo in (0, half)
+    ]
+    total, fwd_a, from_across = lax.optimization_barrier((total, fwd_a, from_across))
     _, second_half, packed = lax.optimization_barrier(
         (fwd_a, pack(own[half:], own_ids[half:]), pack(own, own_ids))
     )
     fwd_b = moved(second_half, pos2dev, forward)
     back2 = moved(packed, pos2dev, [(p, (p - 2) % n) for p in evens] + [(p, p) for p in range(1, n, 2)])
     swapped_a = moved(fwd_a, pos2dev, swap)
-    across_held, across_ids = unpack(across)
 
     def half_steps(fwd, swapped, lo, total):
         fwd_held, fwd_ids = unpack(fwd)
         swapped_held, swapped_ids = unpack(swapped)
         q0 = lo // 128
         total = total + step_total(own, own_ids, fwd_held, fwd_ids, my_pairs[2], False, q0)
-        return total + step_total(
-            own,
-            own_ids,
-            jnp.where(odd, across_held[lo : lo + half], swapped_held),
-            jnp.where(odd, across_ids[lo : lo + half], swapped_ids),
-            my_pairs[1],
-            False,
-            q0,
-        )
+        from_swap = step_total(own, own_ids, swapped_held, swapped_ids, my_pairs[1], False, q0)
+        return total + jnp.where(odd, from_across[lo // half], from_swap)
 
     def last_step(swapped, lo):
         back2_held, back2_ids = unpack(back2)

time: 153 us -> 152 us (level)
  waiting for transfers between devices: 77.7 us -> 73.3 us
  matrix products: 18.2 us -> 21.4 us
    ppermute x6, waiting for transfers between devices: 36.6 us -> 32.2 us  [moved(): return lax.ppermute(x, 'blk', [(pos2dev[a], pos2dev[b]) for a, b in moves])]
    dot_general x7 -> x9, matrix products: 15.5 us -> 18.8 us  [step_total(): lax.dot_general(local, remote, (((1,), (1,)), ((), ())), preferred_elemen...]
  transfers between devices with their start and end apart: 7 -> 7, of which waited for: 4 -> 4; matrix products, arithmetic and copies ran while one was open for 9% -> 12% of each run, Pallas kernels for 0% -> 0%
where the time goes in v11:
time: 152 us
  waiting for transfers between devices  73.3 us (48%)
  starting transfers between devices  24.6 us (16%)
  matrix products  21.4 us (14%)
  other arithmetic  13 us (9%)
  blocking collectives  10.8 us (7%)
  local copies, waits for them, and re-layouts  4.37 us (3%)
  between operations  4.29 us (3%)
    all_to_all x1, waiting for transfers between devices, body(): lax.all_to_all(payload, 'blk', split_axis=0, concat_axis=0, tiled=True)  41.1 us
    ppermute x6, waiting for transfers between devices, moved(): return lax.ppermute(x, 'blk', [(pos2dev[a], pos2dev[b]) for a, b in moves])  32.2 us
    dot_general x9, matrix products, step_total(): lax.dot_general(local, remote, (((1,), (1,)), ((), ())), preferred_elemen...  18.8 us
    ppermute x6, starting transfers between devices, moved(): return lax.ppermute(x, 'blk', [(pos2dev[a], pos2dev[b]) for a, b in moves])  17.1 us
    all_to_all x1, blocking collectives, body(): lax.all_to_all(totals, 'blk', split_axis=0, concat_axis=0, tiled=True)  10.8 us
    all_to_all x1, starting transfers between devices, body(): lax.all_to_all(payload, 'blk', split_axis=0, concat_axis=0, tiled=True)  7.52 us
  transfers between devices with their start and end apart: 7, of which 4 were waited for; matrix products, arithmetic and copies ran while one was open for 12% of the time, Pallas kernels for 0%

profile of v11, /device:TPU:0, one launch (start us, length us, event | category | flops | bytes accessed | tf_op | source)
XLA Modules:
  0.0 151.7 jit_solution(671386362016385702)
XLA Ops:
  0.0 0.8 convert.17
  0.8 0.1 copy.74
  1.0 0.1 reshape.410
  1.1 2.0 %fusion.2 = f32[960]{0:T(1024)S(1)} fusion(bf16[960,1024]{1,0:T(8,128)(2,1)} %param.7), kind=kLoop, calls=%fused_computation.7 | loop fusion | flops 2948160 | bytes 1969920 | tf_op jit(solution)/shard_map/reduce_sum | solution.py:69
  3.1 1.2 convert_reduce_fusion
  4.3 0.7 fusion.43
  5.1 0.6 select_reduce_fusion
  5.7 0.1 sub.11
  5.8 0.1 pad.31.clone
  6.0 2.6 %fusion.9 = bf16[1024,1024]{1,0:T(8,128)(2,1)S(1)} fusion(bf16[960,1024]{1,0:T(8,128)(2,1)S(1)} %copy-done.2, f32[960]{0:T(1024)S(1)} %add_rsqrt_fusion, s32[960]{0:T(1024)S(1)} %get-tuple-element.46), kind=kOutput, calls=%fused_computation.38 | convolution fusion | flops 2018246656 | bytes 4070912 | tf_op jit(solution)/shard_map/dot_general | solution.py:77
  8.6 1.7 %pad_maximum_fusion = bf16[16,65,1024]{2,1,0:T(8,128)(2,1)} fusion(bf16[16,1,1024]{2,1,0:T(2,128)(2,1)S(1)} %copy.75, bf16[16,64,1024]{2,1,0:T(8,128)(2,1)S(1)} %bitcast.125), kind=kLoop, calls=%fused_computation.18 | loop fusion | flops 4259840 | bytes 4259840 | tf_op jit(solution)/shard_map/concatenate | solution.py:90
  10.3 7.5 %all-to-all-start = ((bf16[16,65,1024]{2,1,0:T(8,128)(2,1)}), bf16[16,65,1024]{2,1,0:T(8,128)(2,1)S(1)}, u32[]{:S(2)}, u32[]{:S(2)}) async-start(bf16[16,65,1024]{2,1,0:T(8,128)(2,1)} %pad_maximum_fusion), calls=%async_computation | async-start | bytes 4718592 | tf_op jit(solution)/shard_map/all_to_all | solution.py:91
  17.8 0.6 dynamic_slice.9
  22.3 41.1 %all-to-all-done = bf16[16,65,1024]{2,1,0:T(8,128)(2,1)S(1)} async-done(((bf16[16,65,1024]{2,1,0:T(8,128)(2,1)}), bf16[16,65,1024]{2,1,0:T(8,128)(2,1)S(1)}, u32[]{:S(2)}, u32[]{:S(2)}) %all-to-all-start) | async-done | bytes 2129952 | tf_op jit(solution)/shard_map/all_to_all | solution.py:91
  63.6 0.2 slice.218
  63.9 1.6 %pad_maximum_fusion.1 = bf16[1040,1024]{1,0:T(8,128)(2,1)} fusion(bf16[16,1024]{1,0:T(8,128)(2,1)S(1)} %reshape.325, bf16[1024,1024]{1,0:T(8,128)(2,1)S(1)} %bitcast.115), kind=kLoop, calls=%fused_computation.19 | loop fusion | flops 4259840 | bytes 4259840 | tf_op jit(solution)/shard_map/concatenate | solution.py:47
  65.5 0.3 copy-done
  65.8 4.0 %collective-permute-start = (bf16[1040,1024]{1,0:T(8,128)(2,1)}, bf16[1040,1024]{1,0:T(8,128)(2,1)}, u32[]{:S(2)}, u32[]{:S(2)}) collective-permute-start(bf16[1040,1024]{1,0:T(8,128)(2,1)} %pad_maximum_fusion.1), channel_id=1, source_target_pairs={{0,1},{4,5},{8,9},{12,13},{14,15},{10,11},{6,7},{2,3},{16,17},{20,... | collective-permute-start | bytes 6389768 | tf_op jit(solution)/shard_map/ppermute | solution.py:23
  69.8 0.1 convert_element_type.181
  69.9 0.1 convert_element_type.175
  70.1 0.1 slice.219
  70.2 0.1 copy.77
  70.3 0.1 constant_dynamic-slice_fusion.1
  70.4 0.1 copy.79
  70.5 0.1 copy.78
  70.6 0.1 convert_reduce_fusion.1
  70.7 0.1 copy.81
  70.8 0.1 copy.80
  70.9 0.1 convert_reduce_fusion.4
  71.1 0.2 fusion.46
  71.3 6.9 %collective-permute-start.1 = (bf16[528,1024]{1,0:T(8,128)(2,1)S(1)}, bf16[528,1024]{1,0:T(8,128)(2,1)S(1)}, u32[]{:S(2)}, u32[]{:S(2)}) collective-permute-start(bf16[528,1024]{1,0:T(8,128)(2,1)S(1)} %pad_maximum_fusion.2), channel_id=1, source_target_pairs={{0,4},{1,5},{4,8},{5,9},{8,12},{9,13},{12,14},{13,15},{14,10},{15,... | collective-permute-start | bytes 3244040 | tf_op jit(solution)/shard_map/ppermute | solution.py:23
  78.3 3.2 %bitcast_reduce_fusion = f32[1024,8]{0,1:T(8,128)S(1)} fusion(bf16[1024,1024]{1,0:T(8,128)(2,1)S(1)} %bitcast.116, s32[1024]{0:T(1024)S(1)} %convert_element_type.169, pred[1024]{0:T(1024)(128)(4,1)S(1)} %broadcast_compare_fusion.1), kind=kOutput, calls=%fused_computation.2 | convolution fusion | flops 2155864064 | bytes 2135040 | tf_op jit(solution)/shard_map/dot_general | solution.py:30
  81.5 0.1 fusion.28
  81.6 0.7 slice_convert_fusion.2
  82.3 2.9 %bitcast_reduce_fusion.7 = f32[1024,4]{0,1:T(4,128)S(1)} fusion(bf16[1024,1024]{1,0:T(8,128)(2,1)S(1)} %bitcast.117, bf16[1040,1024]{1,0:T(8,128)(2,1)} %collective-permute-done, s32[1024]{0:T(1024)S(1)} %convert_element_type.169, s32[512]{0:T(512)S(1)} %bitcast.147, pred[1024]{0:T(1024)(128)(4,1)S(1)} %broadcast_compare_fusion.1), kind=kOutput, calls=%fused_computation.26 | convolution fusion | flops 1076359168 | bytes 3169280 | tf_op jit(solution)/shard_map/dot_general | solution.py:30
  85.2 0.1 fusion.35
  85.2 2.9 %bitcast_reduce_fusion.8 = f32[1024,4]{0,1:T(4,128)S(1)} fusion(bf16[1024,1024]{1,0:T(8,128)(2,1)S(1)} %bitcast.118, bf16[1040,1024]{1,0:T(8,128)(2,1)} %collective-permute-done, s32[1024]{0:T(1024)S(1)} %convert_element_type.169, s32[512]{0:T(512)S(1)} %bitcast.146, pred[1024]{0:T(1024)(128)(4,1)S(1)} %broadcast_compare_fusion.1), kind=kOutput, calls=%fused_computation.27 | convolution fusion | flops 1076359168 | bytes 3169280 | tf_op jit(solution)/shard_map/dot_general | solution.py:30
  88.1 0.1 fusion.36
  88.2 11.4 %collective-permute-done.1 = bf16[528,1024]{1,0:T(8,128)(2,1)S(1)} collective-permute-done((bf16[528,1024]{1,0:T(8,128)(2,1)S(1)}, bf16[528,1024]{1,0:T(8,128)(2,1)S(1)}, u32[]{:S(2)}, u32[]{:S(2)}) %collective-permute-start.1) | collective-permute-done | bytes 1081376 | tf_op jit(solution)/shard_map/ppermute | solution.py:23
  99.7 3.2 %collective-permute-start.2 = (bf16[528,1024]{1,0:T(8,128)(2,1)S(1)}, bf16[528,1024]{1,0:T(8,128)(2,1)S(1)}, u32[]{:S(2)}, u32[]{:S(2)}) collective-permute-start(bf16[528,1024]{1,0:T(8,128)(2,1)S(1)} %pad_maximum_fusion.3), channel_id=1, source_target_pairs={{0,4},{1,5},{4,8},{5,9},{8,12},{9,13},{12,14},{13,15},{14,10},{15,... | collective-permute-start | bytes 3244040 | tf_op jit(solution)/shard_map/ppermute | solution.py:23
  102.9 2.9 %collective-permute-start.5 = (bf16[1040,1024]{1,0:T(8,128)(2,1)}, bf16[1040,1024]{1,0:T(8,128)(2,1)S(1)}, u32[]{:S(2)}, u32[]{:S(2)}) collective-permute-start(bf16[1040,1024]{1,0:T(8,128)(2,1)} %pad_maximum_fusion.1), channel_id=1, source_target_pairs={{0,2},{4,0},{8,4},{12,8},{14,12},{10,14},{6,10},{2,6},{1,1},{5,5},... | collective-permute-start | bytes 6389768 | tf_op jit(solution)/shard_map/ppermute | solution.py:23
  105.9 1.6 %bitcast_reduce_fusion.6 = f32[1024,4]{0,1:T(4,128)S(1)} fusion(bf16[1024,1024]{1,0:T(8,128)(2,1)S(1)} %bitcast.119, bf16[528,1024]{1,0:T(8,128)(2,1)S(1)} %collective-permute-done.1, s32[1024]{0:T(1024)S(1)} %convert_element_type.169, s32[512]{0:T(512)S(1)} %slice_convert_fusion.6, pred[1024]{0:T(1024)(128)(4,1)S(1)} %broadcast_compare_fusion.1), kind=kOutput, calls=%fused_computation.25 | convolution fusion | flops 1076359168 | bytes 3169280 | tf_op jit(solution)/shard_map/dot_general | solution.py:30
  107.5 0.1 fusion.34
  107.7 1.6 %bitcast_reduce_fusion.5 = f32[1024,4]{0,1:T(4,128)S(1)} fusion(bf16[1024,1024]{1,0:T(8,128)(2,1)S(1)} %bitcast.120, s32[1024]{0:T(1024)S(1)} %convert_element_type.169, s32[512]{0:T(512)S(1)} %slice_convert_fusion.5, pred[1024]{0:T(1024)(128)(4,1)S(1)} %broadcast_compare_fusion.1, bf16[528,1024]{1,0:T(8,128)(2,1)S(1)} %collective-permute-done.3), kind=kOutput, calls=%fused_computation.24 | convolution fusion | flops 1076359168 | bytes 3169280 | tf_op jit(solution)/shard_map/dot_general | solution.py:30
  109.3 0.1 fusion.33
  109.4 19.1 %collective-permute-done.2 = bf16[528,1024]{1,0:T(8,128)(2,1)S(1)} collective-permute-done((bf16[528,1024]{1,0:T(8,128)(2,1)S(1)}, bf16[528,1024]{1,0:T(8,128)(2,1)S(1)}, u32[]{:S(2)}, u32[]{:S(2)}) %collective-permute-start.2) | collective-permute-done | bytes 1081376 | tf_op jit(solution)/shard_map/ppermute | solution.py:23
  128.5 1.6 %bitcast_reduce_fusion.4 = f32[1024,4]{0,1:T(4,128)S(1)} fusion(bf16[1024,1024]{1,0:T(8,128)(2,1)S(1)} %bitcast.121, bf16[528,1024]{1,0:T(8,128)(2,1)S(1)} %collective-permute-done.2, s32[1024]{0:T(1024)S(1)} %convert_element_type.169, s32[512]{0:T(512)S(1)} %slice_convert_fusion.4, pred[1024]{0:T(1024)(128)(4,1)S(1)} %broadcast_compare_fusion.1), kind=kOutput, calls=%fused_computation.23 | convolution fusion | flops 1076359168 | bytes 3169280 | tf_op jit(solution)/shard_map/dot_general | solution.py:30
  130.2 0.1 fusion.32
  130.2 1.6 %collective-permute-done.5 = bf16[1040,1024]{1,0:T(8,128)(2,1)S(1)} collective-permute-done((bf16[1040,1024]{1,0:T(8,128)(2,1)}, bf16[1040,1024]{1,0:T(8,128)(2,1)S(1)}, u32[]{:S(2)}, u32[]{:S(2)}) %collective-permute-start.5) | collective-permute-done | bytes 2129952 | tf_op jit(solution)/shard_map/ppermute | solution.py:23
  131.9 1.6 %bitcast_reduce_fusion.2 = f32[1024,4]{0,1:T(4,128)S(1)} fusion(bf16[1040,1024]{1,0:T(8,128)(2,1)S(1)} %collective-permute-done.5, s32[1024]{0:T(1024)S(1)} %bitcast.132, s32[512]{0:T(512)S(1)} %slice_convert_fusion.5, pred[1024]{0:T(1024)(128)(4,1)S(1)} %broadcast_compare_fusion, bf16[528,1024]{1,0:T(8,128)(2,1)S(1)} %collective-permute-done.3), kind=kOutput, calls=%fused_computation.21 | convolution fusion | flops 1076359168 | bytes 3169280 | tf_op jit(solution)/shard_map/dot_general | solution.py:30
  133.5 0.1 fusion.30
  133.7 1.6 %bitcast_reduce_fusion.3 = f32[1024,4]{0,1:T(4,128)S(1)} fusion(bf16[1024,1024]{1,0:T(8,128)(2,1)S(1)} %bitcast.122, s32[1024]{0:T(1024)S(1)} %convert_element_type.169, s32[512]{0:T(512)S(1)} %slice_convert_fusion.3, pred[1024]{0:T(1024)(128)(4,1)S(1)} %broadcast_compare_fusion.1, bf16[528,1024]{1,0:T(8,128)(2,1)S(1)} %collective-permute-done.4), kind=kOutput, calls=%fused_computation.22 | convolution fusion | flops 1076359168 | bytes 3169280 | tf_op jit(solution)/shard_map/dot_general | solution.py:30
  135.3 0.1 fusion.31
  135.4 1.7 %bitcast_reduce_fusion.1 = f32[1024,4]{0,1:T(4,128)S(1)} fusion(bf16[1040,1024]{1,0:T(8,128)(2,1)S(1)} %collective-permute-done.5, s32[1024]{0:T(1024)S(1)} %bitcast.133, s32[512]{0:T(512)S(1)} %slice_convert_fusion.3, pred[1024]{0:T(1024)(128)(4,1)S(1)} %broadcast_compare_fusion, bf16[528,1024]{1,0:T(8,128)(2,1)S(1)} %collective-permute-done.4), kind=kOutput, calls=%fused_computation.20 | convolution fusion | flops 1076359168 | bytes 3169280 | tf_op jit(solution)/shard_map/dot_general | solution.py:30
  137.0 0.1 fusion.29
  137.1 0.1 stack_reshape.4
  137.2 0.1 select_n.155
  137.3 0.1 reshape.413
  137.4 10.8 %all_to_all.10 = f32[16,1,128]{2,1,0:T(1,128)S(1)} all-to-all(f32[16,1,128]{2,1,0:T(1,128)S(1)} %reshape.413), channel_id=1, replica_groups=mesh['groups'=2,'blk'=16] {'blk'}, dimensions={0} | all-to-all | bytes 16384 | tf_op jit(solution)/shard_map/all_to_all | solution.py:152
  148.2 0.5 broadcast.275
  148.7 0.7 reduce.52
  149.4 0.1 reshape.414
  149.6 1.5 add_reduce_fusion
  151.1 0.6 log1p.3
  (61 shorter events, 0.9 us)
Async XLA Ops:
  0.0 5.9 %copy-start.2 = (bf16[960,1024]{1,0:T(8,128)(2,1)S(1)}, bf16[960,1024]{1,0:T(8,128)(2,1)}, u32[]{:S(2)}) copy-start(bf16[960,1024]{1,0:T(8,128)(2,1)} %param.7) | copy-start | bytes 5898244
  10.3 7.5 %copy-start.3 = (s32[16]{0:T(128)S(1)}, s32[16]{0:T(128)}, u32[]{:S(2)}) copy-start(s32[16]{0:T(128)} %constant.73.clone) | copy-start | bytes 196
  10.3 53.2 %all-to-all-start = ((bf16[16,65,1024]{2,1,0:T(8,128)(2,1)}), bf16[16,65,1024]{2,1,0:T(8,128)(2,1)S(1)}, u32[]{:S(2)}, u32[]{:S(2)}) async-start(bf16[16,65,1024]{2,1,0:T(8,128)(2,1)} %pad_maximum_fusion), calls=%async_computation | async-start | bytes 4718592 | tf_op jit(solution)/shard_map/all_to_all | solution.py:91
  63.8 1.9 %copy-start = (bf16[16,64,1024]{2,1,0:T(8,128)(2,1)}, bf16[16,64,1024]{2,1,0:T(8,128)(2,1)S(1)}, u32[]{:S(2)}) copy-start(bf16[16,64,1024]{2,1,0:T(8,128)(2,1)S(1)} %slice.218) | copy-start | bytes 6291460
  65.8 15.8 %collective-permute-start = (bf16[1040,1024]{1,0:T(8,128)(2,1)}, bf16[1040,1024]{1,0:T(8,128)(2,1)}, u32[]{:S(2)}, u32[]{:S(2)}) collective-permute-start(bf16[1040,1024]{1,0:T(8,128)(2,1)} %pad_maximum_fusion.1), channel_id=1, source_target_pairs={{0,1},{4,5},{8,9},{12,13},{14,15},{10,11},{6,7},{2,3},{16,17},{20,... | collective-permute-start | bytes 6389768 | tf_op jit(solution)/shard_map/ppermute | solution.py:23
  71.2 7.0 %copy-start.1 = (bf16[16,64,1024]{2,1,0:T(8,128)(2,1)S(1)}, bf16[16,64,1024]{2,1,0:T(8,128)(2,1)}, u32[]{:S(2)}) copy-start(bf16[16,64,1024]{2,1,0:T(8,128)(2,1)} %copy-done) | copy-start | bytes 6291460
  71.3 28.3 %collective-permute-start.1 = (bf16[528,1024]{1,0:T(8,128)(2,1)S(1)}, bf16[528,1024]{1,0:T(8,128)(2,1)S(1)}, u32[]{:S(2)}, u32[]{:S(2)}) collective-permute-start(bf16[528,1024]{1,0:T(8,128)(2,1)S(1)} %pad_maximum_fusion.2), channel_id=1, source_target_pairs={{0,4},{1,5},{4,8},{5,9},{8,12},{9,13},{12,14},{13,15},{14,10},{15,... | collective-permute-start | bytes 3244040 | tf_op jit(solution)/shard_map/ppermute | solution.py:23
  99.6 8.0 %collective-permute-start.3 = (bf16[528,1024]{1,0:T(8,128)(2,1)S(1)}, bf16[528,1024]{1,0:T(8,128)(2,1)S(1)}, u32[]{:S(2)}, u32[]{:S(2)}) collective-permute-start(bf16[528,1024]{1,0:T(8,128)(2,1)S(1)} %collective-permute-done.1), channel_id=1, source_target_pairs={{0,1},{1,0},{4,5},{5,4},{8,9},{9,8},{12,13},{13,12},{14,15},{15,14... | collective-permute-start | bytes 3244040 | tf_op jit(solution)/shard_map/ppermute | solution.py:23
  99.7 28.8 %collective-permute-start.2 = (bf16[528,1024]{1,0:T(8,128)(2,1)S(1)}, bf16[528,1024]{1,0:T(8,128)(2,1)S(1)}, u32[]{:S(2)}, u32[]{:S(2)}) collective-permute-start(bf16[528,1024]{1,0:T(8,128)(2,1)S(1)} %pad_maximum_fusion.3), channel_id=1, source_target_pairs={{0,4},{1,5},{4,8},{5,9},{8,12},{9,13},{12,14},{13,15},{14,10},{15,... | collective-permute-start | bytes 3244040 | tf_op jit(solution)/shard_map/ppermute | solution.py:23
  102.9 28.9 %collective-permute-start.5 = (bf16[1040,1024]{1,0:T(8,128)(2,1)}, bf16[1040,1024]{1,0:T(8,128)(2,1)S(1)}, u32[]{:S(2)}, u32[]{:S(2)}) collective-permute-start(bf16[1040,1024]{1,0:T(8,128)(2,1)} %pad_maximum_fusion.1), channel_id=1, source_target_pairs={{0,2},{4,0},{8,4},{12,8},{14,12},{10,14},{6,10},{2,6},{1,1},{5,5},... | collective-permute-start | bytes 6389768 | tf_op jit(solution)/shard_map/ppermute | solution.py:23
  128.5 5.1 %collective-permute-start.4 = (bf16[528,1024]{1,0:T(8,128)(2,1)S(1)}, bf16[528,1024]{1,0:T(8,128)(2,1)S(1)}, u32[]{:S(2)}, u32[]{:S(2)}) collective-permute-start(bf16[528,1024]{1,0:T(8,128)(2,1)S(1)} %collective-permute-done.2), channel_id=1, source_target_pairs={{0,1},{1,0},{4,5},{5,4},{8,9},{9,8},{12,13},{13,12},{14,15},{15,14... | collective-permute-start | bytes 3244040 | tf_op jit(solution)/shard_map/ppermute | solution.py:23

commit v12 on v11

--- a/solution.py
+++ b/solution.py
@@ -150,13 +150,15 @@
     forward_part = jnp.where(odd, 0.0, last)
     totals = jnp.stack([total.reshape(device_count, capacity), forward_part.reshape(device_count, capacity)], axis=1)
     returned = lax.all_to_all(totals, "blk", split_axis=0, concat_axis=0, tiled=True)
-    behind = jnp.asarray(np.asarray(pos2dev, np.int32))[(owners - 2) % device_count] * capacity + arrival
-    behind = jnp.where(owners % 2 == 0, behind, -1)
-    both = jnp.sum(
-        jnp.where(place[:, None] == slot_index[None, :], returned[:, 0].reshape(-1)[None, :], 0.0)
-        + jnp.where(behind[:, None] == slot_index[None, :], returned[:, 1].reshape(-1)[None, :], 0.0),
-        axis=1,
-    )
+    ring_dev = jnp.asarray(np.asarray(pos2dev, np.int32))
+    source_dev = jnp.stack([ring_dev[owners], jnp.where(owners % 2 == 0, ring_dev[(owners - 2) % device_count], -1)], axis=1)
+    dev_index = jnp.arange(device_count, dtype=jnp.int32)
+    slot_in = jnp.arange(capacity, dtype=jnp.int32)
+    pick = (
+        (source_dev[:, None, :, None] == dev_index[None, :, None, None])
+        & (arrival[:, None, None, None] == slot_in[None, None, None, :])
+    ).astype(jnp.float32)
+    both = jnp.einsum("rePa,ePa->r", pick, returned, precision=lax.Precision.HIGHEST)
     return jnp.log1p(both)
 
 

time: 152 us -> 154 us (1.013)
  blocking collectives: 10.8 us -> 0 us
  waiting for transfers between devices: 73.3 us -> 79.5 us
  starting transfers between devices: 24.6 us -> 29.2 us
  matrix products: 21.4 us -> 23.6 us
    all_to_all x1 -> x0, blocking collectives: 10.8 us -> none  [body(): lax.all_to_all(totals, 'blk', split_axis=0, concat_axis=0, tiled=True)]
    all_to_all x0 -> x1, waiting for transfers between devices: none -> 6.3 us  [body(): lax.all_to_all(totals, 'blk', split_axis=0, concat_axis=0, tiled=True)]
    all_to_all x0 -> x1, starting transfers between devices: none -> 4.57 us  [body(): lax.all_to_all(totals, 'blk', split_axis=0, concat_axis=0, tiled=True)]
    dot_general x0 -> x1, matrix products: none -> 2.22 us  [body(): jnp.einsum('rePa,ePa->r', pick, returned, precision=lax.Precision.HIGHEST)]
  transfers between devices with their start and end apart: 7 -> 8, of which waited for: 4 -> 5; matrix products, arithmetic and copies ran while one was open for 12% -> 12% of each run, Pallas kernels for 0% -> 0%
where the time goes in v12:
time: 154 us; the launch traced here: 153 us
  waiting for transfers between devices  79.5 us (52%)
  starting transfers between devices  29.2 us (19%)
  matrix products  23.6 us (15%)
  other arithmetic  11.5 us (7%)
  local copies, waits for them, and re-layouts  4.86 us (3%)
  between operations  4.32 us (3%)
    all_to_all x1, waiting for transfers between devices, body(): lax.all_to_all(payload, 'blk', split_axis=0, concat_axis=0, tiled=True)  41.1 us
    ppermute x6, waiting for transfers between devices, moved(): return lax.ppermute(x, 'blk', [(pos2dev[a], pos2dev[b]) for a, b in moves])  32.2 us
    dot_general x9, matrix products, step_total(): lax.dot_general(local, remote, (((1,), (1,)), ((), ())), preferred_elemen...  18.8 us
    ppermute x6, starting transfers between devices, moved(): return lax.ppermute(x, 'blk', [(pos2dev[a], pos2dev[b]) for a, b in moves])  17.1 us
    all_to_all x1, starting transfers between devices, body(): lax.all_to_all(payload, 'blk', split_axis=0, concat_axis=0, tiled=True)  7.52 us
    all_to_all x1, waiting for transfers between devices, body(): lax.all_to_all(totals, 'blk', split_axis=0, concat_axis=0, tiled=True)  6.3 us
    all_to_all x1, starting transfers between devices, body(): lax.all_to_all(totals, 'blk', split_axis=0, concat_axis=0, tiled=True)  4.57 us
  transfers between devices with their start and end apart: 8, of which 5 were waited for; matrix products, arithmetic and copies ran while one was open for 12% of the time, Pallas kernels for 0%

profile of v12, /device:TPU:0, one launch (start us, length us, event | category | flops | bytes accessed | tf_op | source)
XLA Modules:
  0.0 153.0 jit_solution(13019405039133656842)
XLA Ops:
  0.0 1.3 convert_reduce_fusion
  1.3 0.7 convert.17
  2.0 0.1 copy.89
  2.1 0.1 reshape.421
  2.3 2.0 %fusion.4 = f32[960]{0:T(1024)S(1)} fusion(bf16[960,1024]{1,0:T(8,128)(2,1)} %param.7), kind=kLoop, calls=%fused_computation.10 | loop fusion | flops 2948160 | bytes 1969920 | tf_op jit(solution)/shard_map/reduce_sum | solution.py:69
  4.3 0.7 multiply_add_fusion
  5.0 0.6 select_reduce_fusion
  5.7 0.1 sub.12
  5.9 2.6 %fusion.11 = bf16[1024,1024]{1,0:T(8,128)(2,1)S(1)} fusion(bf16[960,1024]{1,0:T(8,128)(2,1)S(1)} %copy-done.2, f32[960]{0:T(1024)S(1)} %add_rsqrt_fusion, s32[960]{0:T(1024)S(1)} %get-tuple-element.37), kind=kOutput, calls=%fused_computation.38 | convolution fusion | flops 2018246656 | bytes 4070912 | tf_op jit(solution)/shard_map/dot_general | solution.py:77
  8.5 1.7 %pad_maximum_fusion = bf16[16,65,1024]{2,1,0:T(8,128)(2,1)} fusion(bf16[16,1,1024]{2,1,0:T(2,128)(2,1)S(1)} %copy.90, bf16[16,64,1024]{2,1,0:T(8,128)(2,1)S(1)} %bitcast.131), kind=kLoop, calls=%fused_computation.18 | loop fusion | flops 4259840 | bytes 4259840 | tf_op jit(solution)/shard_map/concatenate | solution.py:90
  10.2 7.5 %all-to-all-start = ((bf16[16,65,1024]{2,1,0:T(8,128)(2,1)}), bf16[16,65,1024]{2,1,0:T(8,128)(2,1)S(1)}, u32[]{:S(2)}, u32[]{:S(2)}) async-start(bf16[16,65,1024]{2,1,0:T(8,128)(2,1)} %pad_maximum_fusion), calls=%async_computation | async-start | bytes 4718592 | tf_op jit(solution)/shard_map/all_to_all | solution.py:91
  17.7 0.6 dynamic_slice.9
  22.3 41.1 %all-to-all-done = bf16[16,65,1024]{2,1,0:T(8,128)(2,1)S(1)} async-done(((bf16[16,65,1024]{2,1,0:T(8,128)(2,1)}), bf16[16,65,1024]{2,1,0:T(8,128)(2,1)S(1)}, u32[]{:S(2)}, u32[]{:S(2)}) %all-to-all-start) | async-done | bytes 2129952 | tf_op jit(solution)/shard_map/all_to_all | solution.py:91
  63.5 0.2 slice.210
  63.8 1.6 %pad_maximum_fusion.1 = bf16[1040,1024]{1,0:T(8,128)(2,1)} fusion(bf16[16,1024]{1,0:T(8,128)(2,1)S(1)} %reshape.345, bf16[1024,1024]{1,0:T(8,128)(2,1)S(1)} %bitcast.121), kind=kLoop, calls=%fused_computation.19 | loop fusion | flops 4259840 | bytes 4259840 | tf_op jit(solution)/shard_map/concatenate | solution.py:47
  65.4 0.3 copy-done
  65.7 4.0 %collective-permute-start = (bf16[1040,1024]{1,0:T(8,128)(2,1)}, bf16[1040,1024]{1,0:T(8,128)(2,1)}, u32[]{:S(2)}, u32[]{:S(2)}) collective-permute-start(bf16[1040,1024]{1,0:T(8,128)(2,1)} %pad_maximum_fusion.1), channel_id=1, source_target_pairs={{0,1},{4,5},{8,9},{12,13},{14,15},{10,11},{6,7},{2,3},{16,17},{20,... | collective-permute-start | bytes 6389768 | tf_op jit(solution)/shard_map/ppermute | solution.py:23
  69.8 0.1 convert_element_type.182
  69.9 0.1 convert_element_type.176
  70.0 0.1 slice.211
  70.1 0.1 copy.92
  70.2 0.1 constant_dynamic-slice_fusion
  70.3 0.1 copy.94
  70.4 0.1 copy.93
  70.5 0.1 convert_reduce_fusion.1
  70.6 0.1 copy.96
  70.7 0.1 copy.95
  70.8 0.1 convert_reduce_fusion.4
  71.0 0.2 fusion.46
  71.3 6.9 %collective-permute-start.1 = (bf16[528,1024]{1,0:T(8,128)(2,1)S(1)}, bf16[528,1024]{1,0:T(8,128)(2,1)S(1)}, u32[]{:S(2)}, u32[]{:S(2)}) collective-permute-start(bf16[528,1024]{1,0:T(8,128)(2,1)S(1)} %pad_maximum_fusion.2), channel_id=1, source_target_pairs={{0,4},{1,5},{4,8},{5,9},{8,12},{9,13},{12,14},{13,15},{14,10},{15,... | collective-permute-start | bytes 3244040 | tf_op jit(solution)/shard_map/ppermute | solution.py:23
  78.2 3.2 %bitcast_reduce_fusion = f32[1024,8]{0,1:T(8,128)S(1)} fusion(bf16[1024,1024]{1,0:T(8,128)(2,1)S(1)} %bitcast.122, s32[1024]{0:T(1024)S(1)} %convert_element_type.170, pred[1024]{0:T(1024)(128)(4,1)S(1)} %broadcast_compare_fusion.1), kind=kOutput, calls=%fused_computation.4 | convolution fusion | flops 2155864064 | bytes 2135040 | tf_op jit(solution)/shard_map/dot_general | solution.py:30
  81.4 0.1 fusion.30
  81.5 0.7 slice_convert_fusion.2
  82.2 2.9 %bitcast_reduce_fusion.7 = f32[1024,4]{0,1:T(4,128)S(1)} fusion(bf16[1024,1024]{1,0:T(8,128)(2,1)S(1)} %bitcast.123, bf16[1040,1024]{1,0:T(8,128)(2,1)} %collective-permute-done, s32[1024]{0:T(1024)S(1)} %convert_element_type.170, s32[512]{0:T(512)S(1)} %bitcast.157, pred[1024]{0:T(1024)(128)(4,1)S(1)} %broadcast_compare_fusion.1), kind=kOutput, calls=%fused_computation.26 | convolution fusion | flops 1076359168 | bytes 3169280 | tf_op jit(solution)/shard_map/dot_general | solution.py:30
  85.1 0.1 fusion.37
  85.2 2.9 %bitcast_reduce_fusion.8 = f32[1024,4]{0,1:T(4,128)S(1)} fusion(bf16[1024,1024]{1,0:T(8,128)(2,1)S(1)} %bitcast.124, bf16[1040,1024]{1,0:T(8,128)(2,1)} %collective-permute-done, s32[1024]{0:T(1024)S(1)} %convert_element_type.170, s32[512]{0:T(512)S(1)} %bitcast.156, pred[1024]{0:T(1024)(128)(4,1)S(1)} %broadcast_compare_fusion.1), kind=kOutput, calls=%fused_computation.27 | convolution fusion | flops 1076359168 | bytes 3169280 | tf_op jit(solution)/shard_map/dot_general | solution.py:30
  88.1 0.1 fusion.38
  88.1 11.4 %collective-permute-done.1 = bf16[528,1024]{1,0:T(8,128)(2,1)S(1)} collective-permute-done((bf16[528,1024]{1,0:T(8,128)(2,1)S(1)}, bf16[528,1024]{1,0:T(8,128)(2,1)S(1)}, u32[]{:S(2)}, u32[]{:S(2)}) %collective-permute-start.1) | collective-permute-done | bytes 1081376 | tf_op jit(solution)/shard_map/ppermute | solution.py:23
  99.7 3.2 %collective-permute-start.2 = (bf16[528,1024]{1,0:T(8,128)(2,1)S(1)}, bf16[528,1024]{1,0:T(8,128)(2,1)S(1)}, u32[]{:S(2)}, u32[]{:S(2)}) collective-permute-start(bf16[528,1024]{1,0:T(8,128)(2,1)S(1)} %pad_maximum_fusion.3), channel_id=1, source_target_pairs={{0,4},{1,5},{4,8},{5,9},{8,12},{9,13},{12,14},{13,15},{14,10},{15,... | collective-permute-start | bytes 3244040 | tf_op jit(solution)/shard_map/ppermute | solution.py:23
  102.9 2.9 %collective-permute-start.5 = (bf16[1040,1024]{1,0:T(8,128)(2,1)}, bf16[1040,1024]{1,0:T(8,128)(2,1)S(1)}, u32[]{:S(2)}, u32[]{:S(2)}) collective-permute-start(bf16[1040,1024]{1,0:T(8,128)(2,1)} %pad_maximum_fusion.1), channel_id=1, source_target_pairs={{0,2},{4,0},{8,4},{12,8},{14,12},{10,14},{6,10},{2,6},{1,1},{5,5},... | collective-permute-start | bytes 6389768 | tf_op jit(solution)/shard_map/ppermute | solution.py:23
  105.8 1.6 %bitcast_reduce_fusion.6 = f32[1024,4]{0,1:T(4,128)S(1)} fusion(bf16[1024,1024]{1,0:T(8,128)(2,1)S(1)} %bitcast.125, bf16[528,1024]{1,0:T(8,128)(2,1)S(1)} %collective-permute-done.1, s32[1024]{0:T(1024)S(1)} %convert_element_type.170, s32[512]{0:T(512)S(1)} %slice_convert_fusion.6, pred[1024]{0:T(1024)(128)(4,1)S(1)} %broadcast_compare_fusion.1), kind=kOutput, calls=%fused_computation.25 | convolution fusion | flops 1076359168 | bytes 3169280 | tf_op jit(solution)/shard_map/dot_general | solution.py:30
  107.5 0.1 fusion.36
  107.6 1.6 %bitcast_reduce_fusion.5 = f32[1024,4]{0,1:T(4,128)S(1)} fusion(bf16[1024,1024]{1,0:T(8,128)(2,1)S(1)} %bitcast.126, s32[1024]{0:T(1024)S(1)} %convert_element_type.170, s32[512]{0:T(512)S(1)} %slice_convert_fusion.5, pred[1024]{0:T(1024)(128)(4,1)S(1)} %broadcast_compare_fusion.1, bf16[528,1024]{1,0:T(8,128)(2,1)S(1)} %collective-permute-done.3), kind=kOutput, calls=%fused_computation.24 | convolution fusion | flops 1076359168 | bytes 3169280 | tf_op jit(solution)/shard_map/dot_general | solution.py:30
  109.2 0.1 fusion.35
  109.3 19.1 %collective-permute-done.2 = bf16[528,1024]{1,0:T(8,128)(2,1)S(1)} collective-permute-done((bf16[528,1024]{1,0:T(8,128)(2,1)S(1)}, bf16[528,1024]{1,0:T(8,128)(2,1)S(1)}, u32[]{:S(2)}, u32[]{:S(2)}) %collective-permute-start.2) | collective-permute-done | bytes 1081376 | tf_op jit(solution)/shard_map/ppermute | solution.py:23
  128.5 1.6 %bitcast_reduce_fusion.4 = f32[1024,4]{0,1:T(4,128)S(1)} fusion(bf16[1024,1024]{1,0:T(8,128)(2,1)S(1)} %bitcast.127, bf16[528,1024]{1,0:T(8,128)(2,1)S(1)} %collective-permute-done.2, s32[1024]{0:T(1024)S(1)} %convert_element_type.170, s32[512]{0:T(512)S(1)} %slice_convert_fusion.4, pred[1024]{0:T(1024)(128)(4,1)S(1)} %broadcast_compare_fusion.1), kind=kOutput, calls=%fused_computation.23 | convolution fusion | flops 1076359168 | bytes 3169280 | tf_op jit(solution)/shard_map/dot_general | solution.py:30
  130.1 0.1 fusion.34
  130.2 1.6 %collective-permute-done.5 = bf16[1040,1024]{1,0:T(8,128)(2,1)S(1)} collective-permute-done((bf16[1040,1024]{1,0:T(8,128)(2,1)}, bf16[1040,1024]{1,0:T(8,128)(2,1)S(1)}, u32[]{:S(2)}, u32[]{:S(2)}) %collective-permute-start.5) | collective-permute-done | bytes 2129952 | tf_op jit(solution)/shard_map/ppermute | solution.py:23
  131.8 1.6 %bitcast_reduce_fusion.2 = f32[1024,4]{0,1:T(4,128)S(1)} fusion(bf16[1040,1024]{1,0:T(8,128)(2,1)S(1)} %collective-permute-done.5, s32[1024]{0:T(1024)S(1)} %bitcast.139, s32[512]{0:T(512)S(1)} %slice_convert_fusion.5, pred[1024]{0:T(1024)(128)(4,1)S(1)} %broadcast_compare_fusion, bf16[528,1024]{1,0:T(8,128)(2,1)S(1)} %collective-permute-done.3), kind=kOutput, calls=%fused_computation.21 | convolution fusion | flops 1076359168 | bytes 3169280 | tf_op jit(solution)/shard_map/dot_general | solution.py:30
  133.5 0.1 fusion.32
  133.6 1.6 %bitcast_reduce_fusion.3 = f32[1024,4]{0,1:T(4,128)S(1)} fusion(bf16[1024,1024]{1,0:T(8,128)(2,1)S(1)} %bitcast.128, s32[1024]{0:T(1024)S(1)} %convert_element_type.170, s32[512]{0:T(512)S(1)} %slice_convert_fusion.3, pred[1024]{0:T(1024)(128)(4,1)S(1)} %broadcast_compare_fusion.1, bf16[528,1024]{1,0:T(8,128)(2,1)S(1)} %collective-permute-done.4), kind=kOutput, calls=%fused_computation.22 | convolution fusion | flops 1076359168 | bytes 3169280 | tf_op jit(solution)/shard_map/dot_general | solution.py:30
  135.3 0.1 fusion.33
  135.3 1.6 %bitcast_reduce_fusion.1 = f32[1024,4]{0,1:T(4,128)S(1)} fusion(bf16[1040,1024]{1,0:T(8,128)(2,1)S(1)} %collective-permute-done.5, s32[1024]{0:T(1024)S(1)} %bitcast.140, s32[512]{0:T(512)S(1)} %slice_convert_fusion.3, pred[1024]{0:T(1024)(128)(4,1)S(1)} %broadcast_compare_fusion, bf16[528,1024]{1,0:T(8,128)(2,1)S(1)} %collective-permute-done.4), kind=kOutput, calls=%fused_computation.20 | convolution fusion | flops 1076359168 | bytes 3169280 | tf_op jit(solution)/shard_map/dot_general | solution.py:30
  137.0 0.1 fusion.31
  137.1 0.1 stack_reshape.4
  137.1 0.1 select_n.153
  137.3 0.7 reshape.423
  137.9 4.6 %all-to-all-start.1 = ((f32[16,1,128]{2,1,0:T(1,128)}), f32[16,1,128]{2,1,0:T(1,128)S(1)}, u32[]{:S(2)}, u32[]{:S(2)}) async-start(f32[16,1,128]{2,1,0:T(1,128)} %reshape.423), calls=%async_computation.1 | async-start | bytes 16384 | tf_op jit(solution)/shard_map/all_to_all | solution.py:152
  142.6 6.3 %all-to-all-done.1 = f32[16,1,128]{2,1,0:T(1,128)S(1)} async-done(((f32[16,1,128]{2,1,0:T(1,128)}), f32[16,1,128]{2,1,0:T(1,128)S(1)}, u32[]{:S(2)}, u32[]{:S(2)}) %all-to-all-start.1) | async-done | bytes 8224 | tf_op jit(solution)/shard_map/all_to_all | solution.py:152
  148.9 0.5 broadcast.298
  149.4 0.7 reduce.44
  150.1 0.1 reshape.424
  150.2 2.2 %fusion = f32[1,960,1,1]{1,0,3,2:T(1,128)S(1)} fusion(f32[16,2,64,1]{2,1,0,3:T(2,128)S(1)} %bitcast.137, pred[960,64]{0,1:T(8,128)(4,1)S(1)} %iota_compare_fusion.6, pred[960,16,2]{0,2,1:T(4,128)(4,1)S(1)} %copy.88), kind=kOutput, calls=%fused_computation | convolution fusion | flops 25559040 | bytes 104192 | tf_op jit(solution)/shard_map/rePa,ePa->r/dot_general | solution.py:161
  152.4 0.6 log1p.3
  (63 shorter events, 0.9 us)
Async XLA Ops:
  0.0 5.9 %copy-start.2 = (bf16[960,1024]{1,0:T(8,128)(2,1)S(1)}, bf16[960,1024]{1,0:T(8,128)(2,1)}, u32[]{:S(2)}) copy-start(bf16[960,1024]{1,0:T(8,128)(2,1)} %param.7) | copy-start | bytes 5898244
  10.2 7.5 %copy-start.3 = (s32[16]{0:T(128)S(1)}, s32[16]{0:T(128)}, u32[]{:S(2)}) copy-start(s32[16]{0:T(128)} %constant.73.clone) | copy-start | bytes 196
  10.2 53.2 %all-to-all-start = ((bf16[16,65,1024]{2,1,0:T(8,128)(2,1)}), bf16[16,65,1024]{2,1,0:T(8,128)(2,1)S(1)}, u32[]{:S(2)}, u32[]{:S(2)}) async-start(bf16[16,65,1024]{2,1,0:T(8,128)(2,1)} %pad_maximum_fusion), calls=%async_computation | async-start | bytes 4718592 | tf_op jit(solution)/shard_map/all_to_all | solution.py:91
  63.8 1.9 %copy-start = (bf16[16,64,1024]{2,1,0:T(8,128)(2,1)}, bf16[16,64,1024]{2,1,0:T(8,128)(2,1)S(1)}, u32[]{:S(2)}) copy-start(bf16[16,64,1024]{2,1,0:T(8,128)(2,1)S(1)} %slice.210) | copy-start | bytes 6291460
  65.7 15.8 %collective-permute-start = (bf16[1040,1024]{1,0:T(8,128)(2,1)}, bf16[1040,1024]{1,0:T(8,128)(2,1)}, u32[]{:S(2)}, u32[]{:S(2)}) collective-permute-start(bf16[1040,1024]{1,0:T(8,128)(2,1)} %pad_maximum_fusion.1), channel_id=1, source_target_pairs={{0,1},{4,5},{8,9},{12,13},{14,15},{10,11},{6,7},{2,3},{16,17},{20,... | collective-permute-start | bytes 6389768 | tf_op jit(solution)/shard_map/ppermute | solution.py:23
  71.2 7.0 %copy-start.1 = (bf16[16,64,1024]{2,1,0:T(8,128)(2,1)S(1)}, bf16[16,64,1024]{2,1,0:T(8,128)(2,1)}, u32[]{:S(2)}) copy-start(bf16[16,64,1024]{2,1,0:T(8,128)(2,1)} %copy-done) | copy-start | bytes 6291460
  71.3 28.3 %collective-permute-start.1 = (bf16[528,1024]{1,0:T(8,128)(2,1)S(1)}, bf16[528,1024]{1,0:T(8,128)(2,1)S(1)}, u32[]{:S(2)}, u32[]{:S(2)}) collective-permute-start(bf16[528,1024]{1,0:T(8,128)(2,1)S(1)} %pad_maximum_fusion.2), channel_id=1, source_target_pairs={{0,4},{1,5},{4,8},{5,9},{8,12},{9,13},{12,14},{13,15},{14,10},{15,... | collective-permute-start | bytes 3244040 | tf_op jit(solution)/shard_map/ppermute | solution.py:23
  99.6 8.0 %collective-permute-start.3 = (bf16[528,1024]{1,0:T(8,128)(2,1)S(1)}, bf16[528,1024]{1,0:T(8,128)(2,1)S(1)}, u32[]{:S(2)}, u32[]{:S(2)}) collective-permute-start(bf16[528,1024]{1,0:T(8,128)(2,1)S(1)} %collective-permute-done.1), channel_id=1, source_target_pairs={{0,1},{1,0},{4,5},{5,4},{8,9},{9,8},{12,13},{13,12},{14,15},{15,14... | collective-permute-start | bytes 3244040 | tf_op jit(solution)/shard_map/ppermute | solution.py:23
  99.7 28.8 %collective-permute-start.2 = (bf16[528,1024]{1,0:T(8,128)(2,1)S(1)}, bf16[528,1024]{1,0:T(8,128)(2,1)S(1)}, u32[]{:S(2)}, u32[]{:S(2)}) collective-permute-start(bf16[528,1024]{1,0:T(8,128)(2,1)S(1)} %pad_maximum_fusion.3), channel_id=1, source_target_pairs={{0,4},{1,5},{4,8},{5,9},{8,12},{9,13},{12,14},{13,15},{14,10},{15,... | collective-permute-start | bytes 3244040 | tf_op jit(solution)/shard_map/ppermute | solution.py:23
  102.9 28.9 %collective-permute-start.5 = (bf16[1040,1024]{1,0:T(8,128)(2,1)}, bf16[1040,1024]{1,0:T(8,128)(2,1)S(1)}, u32[]{:S(2)}, u32[]{:S(2)}) collective-permute-start(bf16[1040,1024]{1,0:T(8,128)(2,1)} %pad_maximum_fusion.1), channel_id=1, source_target_pairs={{0,2},{4,0},{8,4},{12,8},{14,12},{10,14},{6,10},{2,6},{1,1},{5,5},... | collective-permute-start | bytes 6389768 | tf_op jit(solution)/shard_map/ppermute | solution.py:23
  128.4 5.1 %collective-permute-start.4 = (bf16[528,1024]{1,0:T(8,128)(2,1)S(1)}, bf16[528,1024]{1,0:T(8,128)(2,1)S(1)}, u32[]{:S(2)}, u32[]{:S(2)}) collective-permute-start(bf16[528,1024]{1,0:T(8,128)(2,1)S(1)} %collective-permute-done.2), channel_id=1, source_target_pairs={{0,1},{1,0},{4,5},{5,4},{8,9},{9,8},{12,13},{13,12},{14,15},{15,14... | collective-permute-start | bytes 3244040 | tf_op jit(solution)/shard_map/ppermute | solution.py:23
  137.9 11.0 %all-to-all-start.1 = ((f32[16,1,128]{2,1,0:T(1,128)}), f32[16,1,128]{2,1,0:T(1,128)S(1)}, u32[]{:S(2)}, u32[]{:S(2)}) async-start(f32[16,1,128]{2,1,0:T(1,128)} %reshape.423), calls=%async_computation.1 | async-start | bytes 16384 | tf_op jit(solution)/shard_map/all_to_all | solution.py:152

commit v13 on v11

--- a/solution.py
+++ b/solution.py
@@ -105,8 +105,9 @@
     swap = [(p, p ^ 1) for p in range(n)]
     fwd_a = moved(pack(own[:half], own_ids[:half]), pos2dev, forward)
     across = moved(pack(own, own_ids), pos2dev, [(p, p + 1) for p in evens])
+    back2 = moved(pack(own, own_ids), pos2dev, [(p, (p - 2) % n) for p in evens] + [(p, p) for p in range(1, n, 2)])
     total = step_total(own, own_ids, own, own_ids, my_pairs[0], True)
-    total, across = lax.optimization_barrier((total, across))
+    total, across, back2 = lax.optimization_barrier((total, across, back2))
     across_held, across_ids = unpack(across)
     from_across = [
         step_total(own, own_ids, across_held[lo : lo + half], across_ids[lo : lo + half], my_pairs[1], False, lo // 128)
@@ -117,7 +118,6 @@
         (fwd_a, pack(own[half:], own_ids[half:]), pack(own, own_ids))
     )
     fwd_b = moved(second_half, pos2dev, forward)
-    back2 = moved(packed, pos2dev, [(p, (p - 2) % n) for p in evens] + [(p, p) for p in range(1, n, 2)])
     swapped_a = moved(fwd_a, pos2dev, swap)
 
     def half_steps(fwd, swapped, lo, total):
@@ -142,10 +142,11 @@
         )
 
     total = half_steps(fwd_a, swapped_a, 0, total)
-    fwd_b, total = lax.optimization_barrier((fwd_b, total))
+    last = last_step(swapped_a, 0)
+    fwd_b, total, last = lax.optimization_barrier((fwd_b, total, last))
     swapped_b = moved(fwd_b, pos2dev, swap)
     total = half_steps(fwd_b, swapped_b, half, total)
-    last = last_step(swapped_a, 0) + last_step(swapped_b, half)
+    last = last + last_step(swapped_b, half)
     total = total + jnp.where(odd, last, 0.0)
     forward_part = jnp.where(odd, 0.0, last)
     totals = jnp.stack([total.reshape(device_count, capacity), forward_part.reshape(device_count, capacity)], axis=1)

time: 152 us -> 171 us (1.12)
  starting transfers between devices: 24.6 us -> 39.5 us
  matrix products: 21.4 us -> 24.6 us
  waiting for transfers between devices: 73.3 us -> 71.4 us
    ppermute x6, starting transfers between devices: 17.1 us -> 31.9 us  [moved(): return lax.ppermute(x, 'blk', [(pos2dev[a], pos2dev[b]) for a, b in moves])]
    dot_general x9, matrix products: 18.8 us -> 22 us  [step_total(): lax.dot_general(local, remote, (((1,), (1,)), ((), ())), preferred_elemen...]
    ppermute x6, waiting for transfers between devices: 32.2 us -> 30.3 us  [moved(): return lax.ppermute(x, 'blk', [(pos2dev[a], pos2dev[b]) for a, b in moves])]
  transfers between devices with their start and end apart: 7 -> 7, of which waited for: 4 -> 5; matrix products, arithmetic and copies ran while one was open for 12% -> 13% of each run, Pallas kernels for 0% -> 0%
where the time goes in v13:
time: 171 us; the launch traced here: 169 us
  waiting for transfers between devices  71.4 us (42%)
  starting transfers between devices  39.5 us (23%)
  matrix products  24.6 us (14%)
  other arithmetic  13.7 us (8%)
  blocking collectives  11.3 us (7%)
  local copies, waits for them, and re-layouts  4.43 us (3%)
  between operations  4.27 us (2%)
    all_to_all x1, waiting for transfers between devices, body(): lax.all_to_all(payload, 'blk', split_axis=0, concat_axis=0, tiled=True)  41.1 us
    ppermute x6, starting transfers between devices, moved(): return lax.ppermute(x, 'blk', [(pos2dev[a], pos2dev[b]) for a, b in moves])  31.9 us
    ppermute x6, waiting for transfers between devices, moved(): return lax.ppermute(x, 'blk', [(pos2dev[a], pos2dev[b]) for a, b in moves])  30.3 us
    dot_general x9, matrix products, step_total(): lax.dot_general(local, remote, (((1,), (1,)), ((), ())), preferred_elemen...  22 us
    all_to_all x1, blocking collectives, body(): lax.all_to_all(totals, 'blk', split_axis=0, concat_axis=0, tiled=True)  11.3 us
    all_to_all x1, starting transfers between devices, body(): lax.all_to_all(payload, 'blk', split_axis=0, concat_axis=0, tiled=True)  7.52 us
  transfers between devices with their start and end apart: 7, of which 5 were waited for; matrix products, arithmetic and copies ran while one was open for 13% of the time, Pallas kernels for 0%

profile of v13, /device:TPU:0, one launch (start us, length us, event | category | flops | bytes accessed | tf_op | source)
XLA Modules:
  0.0 169.2 jit_solution(9139227244161785092)
XLA Ops:
  0.0 0.8 convert.17
  0.8 0.1 copy.74
  1.0 0.1 reshape.379
  1.1 2.0 %fusion.2 = f32[960]{0:T(1024)S(1)} fusion(bf16[960,1024]{1,0:T(8,128)(2,1)} %param.7), kind=kLoop, calls=%fused_computation.7 | loop fusion | flops 2948160 | bytes 1969920 | tf_op jit(solution)/shard_map/reduce_sum | solution.py:69
  3.1 1.2 convert_reduce_fusion
  4.3 0.7 fusion.43
  5.1 0.6 select_reduce_fusion
  5.7 0.1 sub.11
  6.0 2.6 %fusion.9 = bf16[1024,1024]{1,0:T(8,128)(2,1)S(1)} fusion(bf16[960,1024]{1,0:T(8,128)(2,1)S(1)} %copy-done.2, f32[960]{0:T(1024)S(1)} %add_rsqrt_fusion, s32[960]{0:T(1024)S(1)} %get-tuple-element.48), kind=kOutput, calls=%fused_computation.38 | convolution fusion | flops 2018246656 | bytes 4070912 | tf_op jit(solution)/shard_map/dot_general | solution.py:77
  8.6 1.7 pad_maximum_fusion
  10.3 7.5 %all-to-all-start = ((bf16[16,65,1024]{2,1,0:T(8,128)(2,1)}), bf16[16,65,1024]{2,1,0:T(8,128)(2,1)S(1)}, u32[]{:S(2)}, u32[]{:S(2)}) async-start(bf16[16,65,1024]{2,1,0:T(8,128)(2,1)} %pad_maximum_fusion), calls=%async_computation | async-start | bytes 4718592 | tf_op jit(solution)/shard_map/all_to_all | solution.py:91
  17.8 0.6 dynamic_slice.9
  22.3 41.1 %all-to-all-done = bf16[16,65,1024]{2,1,0:T(8,128)(2,1)S(1)} async-done(((bf16[16,65,1024]{2,1,0:T(8,128)(2,1)}), bf16[16,65,1024]{2,1,0:T(8,128)(2,1)S(1)}, u32[]{:S(2)}, u32[]{:S(2)}) %all-to-all-start) | async-done | bytes 2129952 | tf_op jit(solution)/shard_map/all_to_all | solution.py:91
  63.6 0.2 slice.218
  63.9 1.6 pad_maximum_fusion.1
  65.5 0.3 copy-done
  65.8 5.6 %collective-permute-start.1 = (bf16[1040,1024]{1,0:T(8,128)(2,1)}, bf16[1040,1024]{1,0:T(8,128)(2,1)}, u32[]{:S(2)}, u32[]{:S(2)}) collective-permute-start(bf16[1040,1024]{1,0:T(8,128)(2,1)} %pad_maximum_fusion.1), channel_id=1, source_target_pairs={{0,2},{4,0},{8,4},{12,8},{14,12},{10,14},{6,10},{2,6},{1,1},{5,5},... | collective-permute-start | bytes 6389768 | tf_op jit(solution)/shard_map/ppermute | solution.py:23
  71.5 16.0 %collective-permute-start = (bf16[1040,1024]{1,0:T(8,128)(2,1)}, bf16[1040,1024]{1,0:T(8,128)(2,1)}, u32[]{:S(2)}, u32[]{:S(2)}) collective-permute-start(bf16[1040,1024]{1,0:T(8,128)(2,1)} %pad_maximum_fusion.1), channel_id=1, source_target_pairs={{0,1},{4,5},{8,9},{12,13},{14,15},{10,11},{6,7},{2,3},{16,17},{20,... | collective-permute-start | bytes 6389768 | tf_op jit(solution)/shard_map/ppermute | solution.py:23
  87.5 0.1 convert_element_type.183
  87.5 0.1 convert_element_type.177
  87.7 0.1 slice.219
  87.8 0.1 copy.77
  87.9 0.1 constant_dynamic-slice_fusion.1
  88.0 0.1 copy.79
  88.1 0.1 copy.78
  88.2 0.1 convert_reduce_fusion.1
  88.3 0.1 copy.81
  88.4 0.1 copy.80
  88.5 0.1 convert_reduce_fusion.3
  88.7 0.2 fusion.46
  88.9 7.1 %collective-permute-start.2 = (bf16[528,1024]{1,0:T(8,128)(2,1)S(1)}, bf16[528,1024]{1,0:T(8,128)(2,1)S(1)}, u32[]{:S(2)}, u32[]{:S(2)}) collective-permute-start(bf16[528,1024]{1,0:T(8,128)(2,1)S(1)} %pad_maximum_fusion.2), channel_id=1, source_target_pairs={{0,4},{1,5},{4,8},{5,9},{8,12},{9,13},{12,14},{13,15},{14,10},{15,... | collective-permute-start | bytes 3244040 | tf_op jit(solution)/shard_map/ppermute | solution.py:23
  96.1 3.2 %bitcast_reduce_fusion = f32[1024,8]{0,1:T(8,128)S(1)} fusion(bf16[1024,1024]{1,0:T(8,128)(2,1)S(1)} %bitcast.116, s32[1024]{0:T(1024)S(1)} %convert_element_type.171, pred[1024]{0:T(1024)(128)(4,1)S(1)} %broadcast_compare_fusion.1), kind=kOutput, calls=%fused_computation.2 | convolution fusion | flops 2155864064 | bytes 2135040 | tf_op jit(solution)/shard_map/dot_general | solution.py:30
  99.2 0.1 fusion.28
  99.4 0.7 collective-permute-done.1
  100.2 0.7 slice_convert_fusion.2
  100.9 2.9 %bitcast_reduce_fusion.7 = f32[1024,4]{0,1:T(4,128)S(1)} fusion(bf16[1024,1024]{1,0:T(8,128)(2,1)S(1)} %bitcast.117, bf16[1040,1024]{1,0:T(8,128)(2,1)} %collective-permute-done, s32[1024]{0:T(1024)S(1)} %convert_element_type.171, s32[512]{0:T(512)S(1)} %bitcast.147, pred[1024]{0:T(1024)(128)(4,1)S(1)} %broadcast_compare_fusion.1), kind=kOutput, calls=%fused_computation.26 | convolution fusion | flops 1076359168 | bytes 3169280 | tf_op jit(solution)/shard_map/dot_general | solution.py:30
  103.8 0.1 fusion.35
  103.8 2.9 %bitcast_reduce_fusion.8 = f32[1024,4]{0,1:T(4,128)S(1)} fusion(bf16[1024,1024]{1,0:T(8,128)(2,1)S(1)} %bitcast.118, bf16[1040,1024]{1,0:T(8,128)(2,1)} %collective-permute-done, s32[1024]{0:T(1024)S(1)} %convert_element_type.171, s32[512]{0:T(512)S(1)} %bitcast.146, pred[1024]{0:T(1024)(128)(4,1)S(1)} %broadcast_compare_fusion.1), kind=kOutput, calls=%fused_computation.27 | convolution fusion | flops 1076359168 | bytes 3169280 | tf_op jit(solution)/shard_map/dot_general | solution.py:30
  106.7 0.1 fusion.36
  106.8 10.6 %collective-permute-done.2 = bf16[528,1024]{1,0:T(8,128)(2,1)S(1)} collective-permute-done((bf16[528,1024]{1,0:T(8,128)(2,1)S(1)}, bf16[528,1024]{1,0:T(8,128)(2,1)S(1)}, u32[]{:S(2)}, u32[]{:S(2)}) %collective-permute-start.2) | collective-permute-done | bytes 1081376 | tf_op jit(solution)/shard_map/ppermute | solution.py:23
  117.4 3.2 %collective-permute-start.3 = (bf16[528,1024]{1,0:T(8,128)(2,1)S(1)}, bf16[528,1024]{1,0:T(8,128)(2,1)S(1)}, u32[]{:S(2)}, u32[]{:S(2)}) collective-permute-start(bf16[528,1024]{1,0:T(8,128)(2,1)S(1)} %pad_maximum_fusion.3), channel_id=1, source_target_pairs={{0,4},{1,5},{4,8},{5,9},{8,12},{9,13},{12,14},{13,15},{14,10},{15,... | collective-permute-start | bytes 3244040 | tf_op jit(solution)/shard_map/ppermute | solution.py:23
  120.7 1.6 bitcast_reduce_fusion.6
  122.3 0.1 fusion.34
  122.4 0.7 slice_convert_fusion.1
  123.2 1.6 bitcast_reduce_fusion.5
  124.8 0.1 fusion.33
  124.9 3.2 %bitcast_reduce_fusion.4 = f32[1024,4]{0,1:T(4,128)S(1)} fusion(bf16[1040,1024]{1,0:T(8,128)(2,1)} %collective-permute-done.1, s32[1024]{0:T(1024)S(1)} %bitcast.132, s32[512]{0:T(512)S(1)} %slice_convert_fusion.5, pred[1024]{0:T(1024)(128)(4,1)S(1)} %broadcast_compare_fusion, bf16[528,1024]{1,0:T(8,128)(2,1)S(1)} %collective-permute-done.4), kind=kOutput, calls=%fused_computation.23 | convolution fusion | flops 1076359168 | bytes 3169280 | tf_op jit(solution)/shard_map/dot_general | solution.py:30
  128.1 0.1 fusion.32
  128.2 18.0 %collective-permute-done.3 = bf16[528,1024]{1,0:T(8,128)(2,1)S(1)} collective-permute-done((bf16[528,1024]{1,0:T(8,128)(2,1)S(1)}, bf16[528,1024]{1,0:T(8,128)(2,1)S(1)}, u32[]{:S(2)}, u32[]{:S(2)}) %collective-permute-start.3) | collective-permute-done | bytes 1081376 | tf_op jit(solution)/shard_map/ppermute | solution.py:23
  146.3 1.6 bitcast_reduce_fusion.3
  147.9 0.1 fusion.31
  148.0 0.9 collective-permute-done.5
  149.0 1.6 bitcast_reduce_fusion.2
  150.6 0.1 fusion.30
  150.7 3.2 %bitcast_reduce_fusion.1 = f32[1024,4]{0,1:T(4,128)S(1)} fusion(bf16[1040,1024]{1,0:T(8,128)(2,1)} %collective-permute-done.1, s32[1024]{0:T(1024)S(1)} %bitcast.133, s32[512]{0:T(512)S(1)} %slice_convert_fusion.3, pred[1024]{0:T(1024)(128)(4,1)S(1)} %broadcast_compare_fusion, bf16[528,1024]{1,0:T(8,128)(2,1)S(1)} %collective-permute-done.5), kind=kOutput, calls=%fused_computation.20 | convolution fusion | flops 1076359168 | bytes 3169280 | tf_op jit(solution)/shard_map/dot_general | solution.py:30
  154.0 0.1 stack_reshape.6
  154.1 0.1 stack_reshape.7
  154.2 0.1 reshape.382
  154.3 11.3 %all_to_all.10 = f32[16,1,128]{2,1,0:T(1,128)S(1)} all-to-all(f32[16,1,128]{2,1,0:T(1,128)S(1)} %reshape.382), channel_id=1, replica_groups=mesh['groups'=2,'blk'=16] {'blk'}, dimensions={0} | all-to-all | bytes 16384 | tf_op jit(solution)/shard_map/all_to_all | solution.py:153
  165.6 0.5 broadcast.257
  166.1 0.7 reduce.52
  166.8 0.1 reshape.383
  167.1 1.5 add_reduce_fusion
  168.6 0.6 log1p.3
  (61 shorter events, 1.0 us)
Async XLA Ops:
  0.0 5.9 %copy-start.2 = (bf16[960,1024]{1,0:T(8,128)(2,1)S(1)}, bf16[960,1024]{1,0:T(8,128)(2,1)}, u32[]{:S(2)}) copy-start(bf16[960,1024]{1,0:T(8,128)(2,1)} %param.7) | copy-start | bytes 5898244
  10.3 7.5 %copy-start.3 = (s32[16]{0:T(128)S(1)}, s32[16]{0:T(128)}, u32[]{:S(2)}) copy-start(s32[16]{0:T(128)} %constant.73.clone) | copy-start | bytes 196
  10.3 53.2 %all-to-all-start = ((bf16[16,65,1024]{2,1,0:T(8,128)(2,1)}), bf16[16,65,1024]{2,1,0:T(8,128)(2,1)S(1)}, u32[]{:S(2)}, u32[]{:S(2)}) async-start(bf16[16,65,1024]{2,1,0:T(8,128)(2,1)} %pad_maximum_fusion), calls=%async_computation | async-start | bytes 4718592 | tf_op jit(solution)/shard_map/all_to_all | solution.py:91
  63.8 2.0 %copy-start = (bf16[16,64,1024]{2,1,0:T(8,128)(2,1)}, bf16[16,64,1024]{2,1,0:T(8,128)(2,1)S(1)}, u32[]{:S(2)}) copy-start(bf16[16,64,1024]{2,1,0:T(8,128)(2,1)S(1)} %slice.218) | copy-start | bytes 6291460
  65.8 34.3 %collective-permute-start.1 = (bf16[1040,1024]{1,0:T(8,128)(2,1)}, bf16[1040,1024]{1,0:T(8,128)(2,1)}, u32[]{:S(2)}, u32[]{:S(2)}) collective-permute-start(bf16[1040,1024]{1,0:T(8,128)(2,1)} %pad_maximum_fusion.1), channel_id=1, source_target_pairs={{0,2},{4,0},{8,4},{12,8},{14,12},{10,14},{6,10},{2,6},{1,1},{5,5},... | collective-permute-start | bytes 6389768 | tf_op jit(solution)/shard_map/ppermute | solution.py:23
  71.5 28.7 %collective-permute-start = (bf16[1040,1024]{1,0:T(8,128)(2,1)}, bf16[1040,1024]{1,0:T(8,128)(2,1)}, u32[]{:S(2)}, u32[]{:S(2)}) collective-permute-start(bf16[1040,1024]{1,0:T(8,128)(2,1)} %pad_maximum_fusion.1), channel_id=1, source_target_pairs={{0,1},{4,5},{8,9},{12,13},{14,15},{10,11},{6,7},{2,3},{16,17},{20,... | collective-permute-start | bytes 6389768 | tf_op jit(solution)/shard_map/ppermute | solution.py:23
  88.8 7.2 %copy-start.1 = (bf16[16,64,1024]{2,1,0:T(8,128)(2,1)S(1)}, bf16[16,64,1024]{2,1,0:T(8,128)(2,1)}, u32[]{:S(2)}) copy-start(bf16[16,64,1024]{2,1,0:T(8,128)(2,1)} %copy-done) | copy-start | bytes 6291460
  88.9 28.5 %collective-permute-start.2 = (bf16[528,1024]{1,0:T(8,128)(2,1)S(1)}, bf16[528,1024]{1,0:T(8,128)(2,1)S(1)}, u32[]{:S(2)}, u32[]{:S(2)}) collective-permute-start(bf16[528,1024]{1,0:T(8,128)(2,1)S(1)} %pad_maximum_fusion.2), channel_id=1, source_target_pairs={{0,4},{1,5},{4,8},{5,9},{8,12},{9,13},{12,14},{13,15},{14,10},{15,... | collective-permute-start | bytes 3244040 | tf_op jit(solution)/shard_map/ppermute | solution.py:23
  117.4 5.7 %collective-permute-start.4 = (bf16[528,1024]{1,0:T(8,128)(2,1)S(1)}, bf16[528,1024]{1,0:T(8,128)(2,1)S(1)}, u32[]{:S(2)}, u32[]{:S(2)}) collective-permute-start(bf16[528,1024]{1,0:T(8,128)(2,1)S(1)} %collective-permute-done.2), channel_id=1, source_target_pairs={{0,1},{1,0},{4,5},{5,4},{8,9},{9,8},{12,13},{13,12},{14,15},{15,14... | collective-permute-start | bytes 3244040 | tf_op jit(solution)/shard_map/ppermute | solution.py:23
  117.4 28.8 %collective-permute-start.3 = (bf16[528,1024]{1,0:T(8,128)(2,1)S(1)}, bf16[528,1024]{1,0:T(8,128)(2,1)S(1)}, u32[]{:S(2)}, u32[]{:S(2)}) collective-permute-start(bf16[528,1024]{1,0:T(8,128)(2,1)S(1)} %pad_maximum_fusion.3), channel_id=1, source_target_pairs={{0,4},{1,5},{4,8},{5,9},{8,12},{9,13},{12,14},{13,15},{14,10},{15,... | collective-permute-start | bytes 3244040 | tf_op jit(solution)/shard_map/ppermute | solution.py:23
  146.2 2.7 %collective-permute-start.5 = (bf16[528,1024]{1,0:T(8,128)(2,1)S(1)}, bf16[528,1024]{1,0:T(8,128)(2,1)S(1)}, u32[]{:S(2)}, u32[]{:S(2)}) collective-permute-start(bf16[528,1024]{1,0:T(8,128)(2,1)S(1)} %collective-permute-done.3), channel_id=1, source_target_pairs={{0,1},{1,0},{4,5},{5,4},{8,9},{9,8},{12,13},{13,12},{14,15},{15,14... | collective-permute-start | bytes 3244040 | tf_op jit(solution)/shard_map/ppermute | solution.py:23

commit v14 on v11

--- a/solution.py
+++ b/solution.py
@@ -103,7 +103,7 @@
     half = slot_count // 2
     forward = [(p, (p + 2) % n) for p in range(n)]
     swap = [(p, p ^ 1) for p in range(n)]
-    fwd_a = moved(pack(own[:half], own_ids[:half]), pos2dev, forward)
+    fwd_a = moved(pack(own[:half], own_ids), pos2dev, forward)
     across = moved(pack(own, own_ids), pos2dev, [(p, p + 1) for p in evens])
     total = step_total(own, own_ids, own, own_ids, my_pairs[0], True)
     total, across = lax.optimization_barrier((total, across))
@@ -113,16 +113,20 @@
         for lo in (0, half)
     ]
     total, fwd_a, from_across = lax.optimization_barrier((total, fwd_a, from_across))
-    _, second_half, packed = lax.optimization_barrier(
-        (fwd_a, pack(own[half:], own_ids[half:]), pack(own, own_ids))
-    )
+    _, second_half, packed = lax.optimization_barrier((fwd_a, own[half:], pack(own, own_ids)))
     fwd_b = moved(second_half, pos2dev, forward)
     back2 = moved(packed, pos2dev, [(p, (p - 2) % n) for p in evens] + [(p, p) for p in range(1, n, 2)])
     swapped_a = moved(fwd_a, pos2dev, swap)
 
+    def all_ids(packed_half):
+        return packed_half[half:].reshape(-1)[:slot_count].astype(jnp.int32)
+
+    fwd_all_ids = all_ids(fwd_a)
+    swapped_all_ids = all_ids(swapped_a)
+
     def half_steps(fwd, swapped, lo, total):
-        fwd_held, fwd_ids = unpack(fwd)
-        swapped_held, swapped_ids = unpack(swapped)
+        fwd_held, fwd_ids = fwd[:half], fwd_all_ids[lo : lo + half]
+        swapped_held, swapped_ids = swapped[:half], swapped_all_ids[lo : lo + half]
         q0 = lo // 128
         total = total + step_total(own, own_ids, fwd_held, fwd_ids, my_pairs[2], False, q0)
         from_swap = step_total(own, own_ids, swapped_held, swapped_ids, my_pairs[1], False, q0)
@@ -130,7 +134,7 @@
 
     def last_step(swapped, lo):
         back2_held, back2_ids = unpack(back2)
-        swapped_held, swapped_ids = unpack(swapped)
+        swapped_held, swapped_ids = swapped[:half], swapped_all_ids[lo : lo + half]
         return step_total(
             back2_held,
             back2_ids,

time: 152 us -> 151 us (level)
  waiting for transfers between devices: 73.3 us -> 71.7 us
    ppermute x6, waiting for transfers between devices: 32.2 us -> 30.6 us  [moved(): return lax.ppermute(x, 'blk', [(pos2dev[a], pos2dev[b]) for a, b in moves])]
where the time goes in v14:
time: 151 us; the launch traced here: 150 us
  waiting for transfers between devices  71.7 us (47%)
  starting transfers between devices  24.5 us (16%)
  matrix products  21.4 us (14%)
  other arithmetic  12.9 us (9%)
  blocking collectives  11.4 us (8%)
  between operations  4.21 us (3%)
  local copies, waits for them, and re-layouts  4.07 us (3%)
    all_to_all x1, waiting for transfers between devices, body(): lax.all_to_all(payload, 'blk', split_axis=0, concat_axis=0, tiled=True)  41.2 us
    ppermute x6, waiting for transfers between devices, moved(): return lax.ppermute(x, 'blk', [(pos2dev[a], pos2dev[b]) for a, b in moves])  30.6 us
    dot_general x9, matrix products, step_total(): lax.dot_general(local, remote, (((1,), (1,)), ((), ())), preferred_elemen...  18.8 us
    ppermute x6, starting transfers between devices, moved(): return lax.ppermute(x, 'blk', [(pos2dev[a], pos2dev[b]) for a, b in moves])  17 us
    all_to_all x1, blocking collectives, body(): lax.all_to_all(totals, 'blk', split_axis=0, concat_axis=0, tiled=True)  11.4 us
    all_to_all x1, starting transfers between devices, body(): lax.all_to_all(payload, 'blk', split_axis=0, concat_axis=0, tiled=True)  7.52 us
  transfers between devices with their start and end apart: 7, of which 4 were waited for; matrix products, arithmetic and copies ran while one was open for 12% of the time, Pallas kernels for 0%

profile of v14, /device:TPU:0, one launch (start us, length us, event | category | flops | bytes accessed | tf_op | source)
XLA Modules:
  0.0 150.2 jit_solution(7469733844815389516)
XLA Ops:
  0.0 0.8 convert.13
  0.8 0.1 copy.72
  1.0 0.1 reshape.391
  1.1 2.0 %fusion.2 = f32[960]{0:T(1024)S(1)} fusion(bf16[960,1024]{1,0:T(8,128)(2,1)} %param.7), kind=kLoop, calls=%fused_computation.7 | loop fusion | flops 2948160 | bytes 1969920 | tf_op jit(solution)/shard_map/reduce_sum | solution.py:69
  3.1 1.2 convert_reduce_fusion
  4.3 0.7 fusion.39
  5.1 0.6 select_reduce_fusion
  5.7 0.1 sub.11
  5.8 0.1 pad.21.clone
  6.0 2.6 %fusion.9 = bf16[1024,1024]{1,0:T(8,128)(2,1)S(1)} fusion(bf16[960,1024]{1,0:T(8,128)(2,1)S(1)} %copy-done.2, f32[960]{0:T(1024)S(1)} %add_rsqrt_fusion, s32[960]{0:T(1024)S(1)} %get-tuple-element.44), kind=kOutput, calls=%fused_computation.38 | convolution fusion | flops 2018246656 | bytes 4070912 | tf_op jit(solution)/shard_map/dot_general | solution.py:77
  8.6 1.7 %pad_maximum_fusion = bf16[16,65,1024]{2,1,0:T(8,128)(2,1)} fusion(bf16[16,1,1024]{2,1,0:T(2,128)(2,1)S(1)} %copy.73, bf16[16,64,1024]{2,1,0:T(8,128)(2,1)S(1)} %bitcast.119), kind=kLoop, calls=%fused_computation.18 | loop fusion | flops 4259840 | bytes 4259840 | tf_op jit(solution)/shard_map/concatenate | solution.py:90
  10.3 7.5 %all-to-all-start = ((bf16[16,65,1024]{2,1,0:T(8,128)(2,1)}), bf16[16,65,1024]{2,1,0:T(8,128)(2,1)S(1)}, u32[]{:S(2)}, u32[]{:S(2)}) async-start(bf16[16,65,1024]{2,1,0:T(8,128)(2,1)} %pad_maximum_fusion), calls=%async_computation | async-start | bytes 4718592 | tf_op jit(solution)/shard_map/all_to_all | solution.py:91
  17.8 0.6 dynamic_slice.9
  22.3 41.2 %all-to-all-done = bf16[16,65,1024]{2,1,0:T(8,128)(2,1)S(1)} async-done(((bf16[16,65,1024]{2,1,0:T(8,128)(2,1)}), bf16[16,65,1024]{2,1,0:T(8,128)(2,1)S(1)}, u32[]{:S(2)}, u32[]{:S(2)}) %all-to-all-start) | async-done | bytes 2129952 | tf_op jit(solution)/shard_map/all_to_all | solution.py:91
  63.5 0.1 reshape.323
  63.6 0.2 slice.209
  63.9 1.6 %pad_maximum_fusion.1 = bf16[1040,1024]{1,0:T(8,128)(2,1)} fusion(bf16[16,1024]{1,0:T(8,128)(2,1)S(1)} %reshape.313, bf16[1024,1024]{1,0:T(8,128)(2,1)S(1)} %bitcast.110), kind=kLoop, calls=%fused_computation.19 | loop fusion | flops 4259840 | bytes 4259840 | tf_op jit(solution)/shard_map/concatenate | solution.py:47
  65.5 0.3 copy-done
  65.8 4.0 %collective-permute-start = (bf16[1040,1024]{1,0:T(8,128)(2,1)}, bf16[1040,1024]{1,0:T(8,128)(2,1)}, u32[]{:S(2)}, u32[]{:S(2)}) collective-permute-start(bf16[1040,1024]{1,0:T(8,128)(2,1)} %pad_maximum_fusion.1), channel_id=1, source_target_pairs={{0,1},{4,5},{8,9},{12,13},{14,15},{10,11},{6,7},{2,3},{16,17},{20,... | collective-permute-start | bytes 6389768 | tf_op jit(solution)/shard_map/ppermute | solution.py:23
  69.8 0.1 slice.210
  69.9 0.1 copy.75
  70.0 0.1 constant_dynamic-slice_fusion.1
  70.1 0.1 copy.77
  70.2 0.1 copy.76
  70.3 0.1 convert_reduce_fusion.1
  70.4 0.1 copy.79
  70.5 0.1 copy.78
  70.6 0.1 convert_reduce_fusion.4
  70.7 0.2 fusion.42
  70.9 0.1 pad_maximum_fusion.2
  71.0 6.9 %collective-permute-start.1 = (bf16[528,1024]{1,0:T(8,128)(2,1)S(1)}, bf16[528,1024]{1,0:T(8,128)(2,1)S(1)}, u32[]{:S(2)}, u32[]{:S(2)}) collective-permute-start(bf16[528,1024]{1,0:T(8,128)(2,1)S(1)} %pad_maximum_fusion.2), channel_id=1, source_target_pairs={{0,4},{1,5},{4,8},{5,9},{8,12},{9,13},{12,14},{13,15},{14,10},{15,... | collective-permute-start | bytes 3244040 | tf_op jit(solution)/shard_map/ppermute | solution.py:23
  77.9 3.2 %bitcast_reduce_fusion = f32[1024,8]{0,1:T(8,128)S(1)} fusion(bf16[1024,1024]{1,0:T(8,128)(2,1)S(1)} %bitcast.111, s32[1024]{0:T(1024)S(1)} %reshape.323, pred[1024]{0:T(1024)(128)(4,1)S(1)} %broadcast_compare_fusion.1), kind=kOutput, calls=%fused_computation.2 | convolution fusion | flops 2155864064 | bytes 2135040 | tf_op jit(solution)/shard_map/dot_general | solution.py:30
  81.1 0.1 fusion.25
  81.2 0.7 slice_convert_fusion.4
  82.0 2.9 %bitcast_reduce_fusion.7 = f32[1024,4]{0,1:T(4,128)S(1)} fusion(bf16[1024,1024]{1,0:T(8,128)(2,1)S(1)} %bitcast.112, bf16[1040,1024]{1,0:T(8,128)(2,1)} %collective-permute-done, s32[1024]{0:T(1024)S(1)} %reshape.323, s32[512]{0:T(512)S(1)} %bitcast.143, pred[1024]{0:T(1024)(128)(4,1)S(1)} %broadcast_compare_fusion.1), kind=kOutput, calls=%fused_computation.26 | convolution fusion | flops 1076359168 | bytes 3169280 | tf_op jit(solution)/shard_map/dot_general | solution.py:30
  84.8 0.1 fusion.32
  84.9 2.9 %bitcast_reduce_fusion.8 = f32[1024,4]{0,1:T(4,128)S(1)} fusion(bf16[1024,1024]{1,0:T(8,128)(2,1)S(1)} %bitcast.113, bf16[1040,1024]{1,0:T(8,128)(2,1)} %collective-permute-done, s32[1024]{0:T(1024)S(1)} %reshape.323, s32[512]{0:T(512)S(1)} %bitcast.142, pred[1024]{0:T(1024)(128)(4,1)S(1)} %broadcast_compare_fusion.1), kind=kOutput, calls=%fused_computation.27 | convolution fusion | flops 1076359168 | bytes 3169280 | tf_op jit(solution)/shard_map/dot_general | solution.py:30
  87.8 0.1 fusion.33
  87.9 11.4 %collective-permute-done.1 = bf16[528,1024]{1,0:T(8,128)(2,1)S(1)} collective-permute-done((bf16[528,1024]{1,0:T(8,128)(2,1)S(1)}, bf16[528,1024]{1,0:T(8,128)(2,1)S(1)}, u32[]{:S(2)}, u32[]{:S(2)}) %collective-permute-start.1) | collective-permute-done | bytes 1081376 | tf_op jit(solution)/shard_map/ppermute | solution.py:23
  99.3 3.0 %collective-permute-start.2 = (bf16[512,1024]{1,0:T(8,128)(2,1)S(1)}, bf16[512,1024]{1,0:T(8,128)(2,1)S(1)}, u32[]{:S(2)}, u32[]{:S(2)}) collective-permute-start(bf16[512,1024]{1,0:T(8,128)(2,1)S(1)} %bitcast.120), channel_id=1, source_target_pairs={{0,4},{1,5},{4,8},{5,9},{8,12},{9,13},{12,14},{13,15},{14,10},{15,... | collective-permute-start | bytes 3145736 | tf_op jit(solution)/shard_map/ppermute | solution.py:23
  102.3 3.1 %collective-permute-start.5 = (bf16[1040,1024]{1,0:T(8,128)(2,1)}, bf16[1040,1024]{1,0:T(8,128)(2,1)S(1)}, u32[]{:S(2)}, u32[]{:S(2)}) collective-permute-start(bf16[1040,1024]{1,0:T(8,128)(2,1)} %pad_maximum_fusion.1), channel_id=1, source_target_pairs={{0,2},{4,0},{8,4},{12,8},{14,12},{10,14},{6,10},{2,6},{1,1},{5,5},... | collective-permute-start | bytes 6389768 | tf_op jit(solution)/shard_map/ppermute | solution.py:23
  105.4 1.6 %bitcast_reduce_fusion.6 = f32[1024,4]{0,1:T(4,128)S(1)} fusion(bf16[1024,1024]{1,0:T(8,128)(2,1)S(1)} %bitcast.114, bf16[528,1024]{1,0:T(8,128)(2,1)S(1)} %collective-permute-done.1, s32[1024]{0:T(1024)S(1)} %reshape.323, s32[512]{0:T(512)S(1)} %bitcast.144, pred[1024]{0:T(1024)(128)(4,1)S(1)} %broadcast_compare_fusion.1), kind=kOutput, calls=%fused_computation.25 | convolution fusion | flops 1076359168 | bytes 3169280 | tf_op jit(solution)/shard_map/dot_general | solution.py:30
  107.1 0.1 fusion.31
  107.2 1.6 %bitcast_reduce_fusion.5 = f32[1024,4]{0,1:T(4,128)S(1)} fusion(bf16[1024,1024]{1,0:T(8,128)(2,1)S(1)} %bitcast.115, s32[1024]{0:T(1024)S(1)} %reshape.323, s32[512]{0:T(512)S(1)} %bitcast.137, pred[1024]{0:T(1024)(128)(4,1)S(1)} %broadcast_compare_fusion.1, bf16[528,1024]{1,0:T(8,128)(2,1)S(1)} %collective-permute-done.3), kind=kOutput, calls=%fused_computation.24 | convolution fusion | flops 1076359168 | bytes 3169280 | tf_op jit(solution)/shard_map/dot_general | solution.py:30
  108.8 0.1 fusion.30
  108.9 18.2 %collective-permute-done.2 = bf16[512,1024]{1,0:T(8,128)(2,1)S(1)} collective-permute-done((bf16[512,1024]{1,0:T(8,128)(2,1)S(1)}, bf16[512,1024]{1,0:T(8,128)(2,1)S(1)}, u32[]{:S(2)}, u32[]{:S(2)}) %collective-permute-start.2) | collective-permute-done | bytes 1048608 | tf_op jit(solution)/shard_map/ppermute | solution.py:23
  127.1 1.6 %bitcast_reduce_fusion.4 = f32[1024,4]{0,1:T(4,128)S(1)} fusion(bf16[1024,1024]{1,0:T(8,128)(2,1)S(1)} %bitcast.116, bf16[512,1024]{1,0:T(8,128)(2,1)S(1)} %collective-permute-done.2, s32[1024]{0:T(1024)S(1)} %reshape.323, s32[512]{0:T(512)S(1)} %bitcast.141, pred[1024]{0:T(1024)(128)(4,1)S(1)} %broadcast_compare_fusion.1), kind=kOutput, calls=%fused_computation.23 | convolution fusion | flops 1076359168 | bytes 3169280 | tf_op jit(solution)/shard_map/dot_general | solution.py:30
  128.8 0.1 fusion.29
  128.9 0.9 collective-permute-done.4
  129.8 1.7 %bitcast_reduce_fusion.3 = f32[1024,4]{0,1:T(4,128)S(1)} fusion(bf16[1024,1024]{1,0:T(8,128)(2,1)S(1)} %bitcast.117, bf16[512,1024]{1,0:T(8,128)(2,1)S(1)} %collective-permute-done.4, s32[1024]{0:T(1024)S(1)} %reshape.323, s32[512]{0:T(512)S(1)} %bitcast.139, pred[1024]{0:T(1024)(128)(4,1)S(1)} %broadcast_compare_fusion.1), kind=kOutput, calls=%fused_computation.22 | convolution fusion | flops 1076359168 | bytes 3169280 | tf_op jit(solution)/shard_map/dot_general | solution.py:30
  131.4 0.1 fusion.28
  131.6 1.6 %bitcast_reduce_fusion.1 = f32[1024,4]{0,1:T(4,128)S(1)} fusion(bf16[512,1024]{1,0:T(8,128)(2,1)S(1)} %collective-permute-done.4, bf16[1040,1024]{1,0:T(8,128)(2,1)S(1)} %collective-permute-done.5, s32[1024]{0:T(1024)S(1)} %bitcast.123, s32[512]{0:T(512)S(1)} %bitcast.140, pred[1024]{0:T(1024)(128)(4,1)S(1)} %broadcast_compare_fusion), kind=kOutput, calls=%fused_computation.20 | convolution fusion | flops 1076359168 | bytes 3169280 | tf_op jit(solution)/shard_map/dot_general | solution.py:30
  133.2 0.1 fusion.26
  133.3 1.6 %bitcast_reduce_fusion.2 = f32[1024,4]{0,1:T(4,128)S(1)} fusion(bf16[1040,1024]{1,0:T(8,128)(2,1)S(1)} %collective-permute-done.5, s32[1024]{0:T(1024)S(1)} %bitcast.124, s32[512]{0:T(512)S(1)} %bitcast.138, pred[1024]{0:T(1024)(128)(4,1)S(1)} %broadcast_compare_fusion, bf16[528,1024]{1,0:T(8,128)(2,1)S(1)} %collective-permute-done.3), kind=kOutput, calls=%fused_computation.21 | convolution fusion | flops 1076359168 | bytes 3169280 | tf_op jit(solution)/shard_map/dot_general | solution.py:30
  134.9 0.1 fusion.27
  135.0 0.1 stack_reshape.4
  135.1 0.1 select_n.155
  135.2 0.1 reshape.394
  135.3 11.4 %all_to_all.10 = f32[16,1,128]{2,1,0:T(1,128)S(1)} all-to-all(f32[16,1,128]{2,1,0:T(1,128)S(1)} %reshape.394), channel_id=1, replica_groups=mesh['groups'=2,'blk'=16] {'blk'}, dimensions={0} | all-to-all | bytes 16384 | tf_op jit(solution)/shard_map/all_to_all | solution.py:156
  146.6 0.5 broadcast.269
  147.2 0.7 reduce.48
  147.8 0.1 reshape.395
  148.1 1.5 add_reduce_fusion
  149.6 0.6 log1p.3
  (44 shorter events, 0.5 us)
Async XLA Ops:
  0.0 5.9 %copy-start.2 = (bf16[960,1024]{1,0:T(8,128)(2,1)S(1)}, bf16[960,1024]{1,0:T(8,128)(2,1)}, u32[]{:S(2)}) copy-start(bf16[960,1024]{1,0:T(8,128)(2,1)} %param.7) | copy-start | bytes 5898244
  10.3 7.5 %copy-start.3 = (s32[16]{0:T(128)S(1)}, s32[16]{0:T(128)}, u32[]{:S(2)}) copy-start(s32[16]{0:T(128)} %constant.73.clone) | copy-start | bytes 196
  10.3 53.2 %all-to-all-start = ((bf16[16,65,1024]{2,1,0:T(8,128)(2,1)}), bf16[16,65,1024]{2,1,0:T(8,128)(2,1)S(1)}, u32[]{:S(2)}, u32[]{:S(2)}) async-start(bf16[16,65,1024]{2,1,0:T(8,128)(2,1)} %pad_maximum_fusion), calls=%async_computation | async-start | bytes 4718592 | tf_op jit(solution)/shard_map/all_to_all | solution.py:91
  63.8 1.9 %copy-start = (bf16[16,64,1024]{2,1,0:T(8,128)(2,1)}, bf16[16,64,1024]{2,1,0:T(8,128)(2,1)S(1)}, u32[]{:S(2)}) copy-start(bf16[16,64,1024]{2,1,0:T(8,128)(2,1)S(1)} %slice.209) | copy-start | bytes 6291460
  65.8 15.4 %collective-permute-start = (bf16[1040,1024]{1,0:T(8,128)(2,1)}, bf16[1040,1024]{1,0:T(8,128)(2,1)}, u32[]{:S(2)}, u32[]{:S(2)}) collective-permute-start(bf16[1040,1024]{1,0:T(8,128)(2,1)} %pad_maximum_fusion.1), channel_id=1, source_target_pairs={{0,1},{4,5},{8,9},{12,13},{14,15},{10,11},{6,7},{2,3},{16,17},{20,... | collective-permute-start | bytes 6389768 | tf_op jit(solution)/shard_map/ppermute | solution.py:23
  70.9 7.0 %copy-start.1 = (bf16[16,64,1024]{2,1,0:T(8,128)(2,1)S(1)}, bf16[16,64,1024]{2,1,0:T(8,128)(2,1)}, u32[]{:S(2)}) copy-start(bf16[16,64,1024]{2,1,0:T(8,128)(2,1)} %copy-done) | copy-start | bytes 6291460
  71.0 28.3 %collective-permute-start.1 = (bf16[528,1024]{1,0:T(8,128)(2,1)S(1)}, bf16[528,1024]{1,0:T(8,128)(2,1)S(1)}, u32[]{:S(2)}, u32[]{:S(2)}) collective-permute-start(bf16[528,1024]{1,0:T(8,128)(2,1)S(1)} %pad_maximum_fusion.2), channel_id=1, source_target_pairs={{0,4},{1,5},{4,8},{5,9},{8,12},{9,13},{12,14},{13,15},{14,10},{15,... | collective-permute-start | bytes 3244040 | tf_op jit(solution)/shard_map/ppermute | solution.py:23
  99.3 7.9 %collective-permute-start.3 = (bf16[528,1024]{1,0:T(8,128)(2,1)S(1)}, bf16[528,1024]{1,0:T(8,128)(2,1)S(1)}, u32[]{:S(2)}, u32[]{:S(2)}) collective-permute-start(bf16[528,1024]{1,0:T(8,128)(2,1)S(1)} %collective-permute-done.1), channel_id=1, source_target_pairs={{0,1},{1,0},{4,5},{5,4},{8,9},{9,8},{12,13},{13,12},{14,15},{15,14... | collective-permute-start | bytes 3244040 | tf_op jit(solution)/shard_map/ppermute | solution.py:23
  99.3 27.8 %collective-permute-start.2 = (bf16[512,1024]{1,0:T(8,128)(2,1)S(1)}, bf16[512,1024]{1,0:T(8,128)(2,1)S(1)}, u32[]{:S(2)}, u32[]{:S(2)}) collective-permute-start(bf16[512,1024]{1,0:T(8,128)(2,1)S(1)} %bitcast.120), channel_id=1, source_target_pairs={{0,4},{1,5},{4,8},{5,9},{8,12},{9,13},{12,14},{13,15},{14,10},{15,... | collective-permute-start | bytes 3145736 | tf_op jit(solution)/shard_map/ppermute | solution.py:23
  102.3 29.3 %collective-permute-start.5 = (bf16[1040,1024]{1,0:T(8,128)(2,1)}, bf16[1040,1024]{1,0:T(8,128)(2,1)S(1)}, u32[]{:S(2)}, u32[]{:S(2)}) collective-permute-start(bf16[1040,1024]{1,0:T(8,128)(2,1)} %pad_maximum_fusion.1), channel_id=1, source_target_pairs={{0,2},{4,0},{8,4},{12,8},{14,12},{10,14},{6,10},{2,6},{1,1},{5,5},... | collective-permute-start | bytes 6389768 | tf_op jit(solution)/shard_map/ppermute | solution.py:23
  127.1 2.7 %collective-permute-start.4 = (bf16[512,1024]{1,0:T(8,128)(2,1)S(1)}, bf16[512,1024]{1,0:T(8,128)(2,1)S(1)}, u32[]{:S(2)}, u32[]{:S(2)}) collective-permute-start(bf16[512,1024]{1,0:T(8,128)(2,1)S(1)} %collective-permute-done.2), channel_id=1, source_target_pairs={{0,1},{1,0},{4,5},{5,4},{8,9},{9,8},{12,13},{13,12},{14,15},{15,14... | collective-permute-start | bytes 3145736 | tf_op jit(solution)/shard_map/ppermute | solution.py:23

commit v15 on v14

--- a/solution.py
+++ b/solution.py
@@ -74,9 +74,8 @@
     place = jnp.asarray(np.asarray(pos2dev, np.int32))[owners] * capacity + arrival
     slot_index = jnp.arange(slot_count, dtype=jnp.int32)
     hit = place[None, :] == slot_index[:, None]
-    outgoing = jnp.dot(
-        hit.astype(jnp.bfloat16), unit, preferred_element_type=jnp.float32
-    ).astype(jnp.bfloat16)
+    source_row = jnp.sum(jnp.where(hit, row_index[None, :] + 1, 0), axis=1) - 1
+    outgoing = jnp.take(unit, jnp.where(source_row < 0, row_count, source_row), axis=0, mode="fill", fill_value=0)
     outgoing_ids = jnp.sum(jnp.where(hit, clusters[None, :] + 1, 0), axis=1) - 1
     pair_count = pairs[0].size
     side = jnp.concatenate(

time: 151 us -> 158 us (1.046)
  local copies, waits for them, and re-layouts: 4.07 us -> 9.5 us
  other arithmetic: 12.9 us -> 17.4 us
  matrix products: 21.4 us -> 18.8 us
    gather x0 -> x1, local copies, waits for them, and re-layouts: none -> 5.36 us  [body(): jnp.take(unit, jnp.where(source_row < 0, row_count, source_row), axis=0,...]
    dot_general x1 -> x0, matrix products: 2.61 us -> none  [body(): jnp.dot(hit.astype(jnp.bfloat16), unit, preferred_element_type=jnp.float32)]
    convert_element_type x0 -> x1, other arithmetic: none -> 1.93 us  [body(): unit = (value_entries * lax.rsqrt(jnp.mean(value_entries * value_entries,...]
    select_n x0 -> x2, other arithmetic: none -> 1.82 us  [body(): jnp.take(unit, jnp.where(source_row < 0, row_count, source_row), axis=0,...]
where the time goes in v15:
time: 158 us
  waiting for transfers between devices  71.7 us (45%)
  starting transfers between devices  24.5 us (16%)
  matrix products  18.8 us (12%)
  other arithmetic  17.4 us (11%)
  blocking collectives  11.3 us (7%)
  local copies, waits for them, and re-layouts  9.5 us (6%)
  between operations  4.22 us (3%)
    all_to_all x1, waiting for transfers between devices, body(): lax.all_to_all(payload, 'blk', split_axis=0, concat_axis=0, tiled=True)  41.2 us
    ppermute x6, waiting for transfers between devices, moved(): return lax.ppermute(x, 'blk', [(pos2dev[a], pos2dev[b]) for a, b in moves])  30.6 us
    dot_general x9, matrix products, step_total(): lax.dot_general(local, remote, (((1,), (1,)), ((), ())), preferred_elemen...  18.8 us
    ppermute x6, starting transfers between devices, moved(): return lax.ppermute(x, 'blk', [(pos2dev[a], pos2dev[b]) for a, b in moves])  17 us
    all_to_all x1, blocking collectives, body(): lax.all_to_all(totals, 'blk', split_axis=0, concat_axis=0, tiled=True)  11.3 us
    all_to_all x1, starting transfers between devices, body(): lax.all_to_all(payload, 'blk', split_axis=0, concat_axis=0, tiled=True)  7.52 us
    gather x1, local copies, waits for them, and re-layouts, body(): jnp.take(unit, jnp.where(source_row < 0, row_count, source_row), axis=0,...  5.36 us
  transfers between devices with their start and end apart: 7, of which 4 were waited for; matrix products, arithmetic and copies ran while one was open for 12% of the time, Pallas kernels for 0%

profile of v15, /device:TPU:0, one launch (start us, length us, event | category | flops | bytes accessed | tf_op | source)
XLA Modules:
  0.0 157.5 jit_solution(12892609533340507940)
XLA Ops:
  0.0 0.7 broadcast_add_fusion
  0.7 0.7 convert.13
  1.4 0.1 copy.74
  1.5 0.1 reshape.438
  1.6 2.0 %fusion.2 = f32[960]{0:T(1024)S(1)} fusion(bf16[960,1024]{1,0:T(8,128)(2,1)} %param.7), kind=kLoop, calls=%fused_computation.8 | loop fusion | flops 2948160 | bytes 1969920 | tf_op jit(solution)/shard_map/reduce_sum | solution.py:69
  3.6 1.2 convert_reduce_fusion
  4.9 0.7 fusion.32
  5.6 0.8 select_reduce_fusion.1
  6.5 0.1 sub.20
  6.6 0.1 pad.21.clone
  6.8 1.9 %fusion.3 = bf16[960,1024]{1,0:T(8,128)(2,1)S(1)} fusion(bf16[960,1024]{1,0:T(8,128)(2,1)} %param.7, f32[960]{0:T(1024)S(1)} %add_rsqrt_fusion), kind=kLoop, calls=%fused_computation.9 | loop fusion | flops 2949120 | bytes 3936000 | tf_op jit(solution)/shard_map/convert_element_type | solution.py:70
  8.7 5.4 %gather_fusion = bf16[1024,1024]{1,0:T(8,128)(2,1)} fusion(bf16[960,1024]{1,0:T(8,128)(2,1)S(1)} %fusion.3, s32[1024]{0:T(1024)S(1)} %broadcast_clamp_fusion), kind=kCustom, calls=%fused_computation | custom fusion | bytes 4198400 | tf_op jit(solution)/shard_map/jit(_take)/gather | solution.py:78
  14.1 1.8 %broadcast_select_fusion = bf16[16,64,1024]{2,1,0:T(8,128)(2,1)S(1)} fusion(bf16[16,64,1024]{2,1,0:T(8,128)(2,1)} %bitcast.112, pred[16,64]{1,0:T(8,128)(4,1)S(1)} %compare_and_fusion), kind=kLoop, calls=%fused_computation.37 | loop fusion | flops 1048576 | bytes 4195328 | tf_op jit(solution)/shard_map/jit(_take)/select_n | solution.py:78
  15.9 1.7 %pad_maximum_fusion = bf16[16,65,1024]{2,1,0:T(8,128)(2,1)} fusion(bf16[16,1,1024]{2,1,0:T(2,128)(2,1)S(1)} %copy.75, bf16[16,64,1024]{2,1,0:T(8,128)(2,1)S(1)} %broadcast_select_fusion), kind=kLoop, calls=%fused_computation.19 | loop fusion | flops 4259840 | bytes 4259840 | tf_op jit(solution)/shard_map/concatenate | solution.py:89
  17.6 7.5 %all-to-all-start = ((bf16[16,65,1024]{2,1,0:T(8,128)(2,1)}), bf16[16,65,1024]{2,1,0:T(8,128)(2,1)S(1)}, u32[]{:S(2)}, u32[]{:S(2)}) async-start(bf16[16,65,1024]{2,1,0:T(8,128)(2,1)} %pad_maximum_fusion), calls=%async_computation | async-start | bytes 4718592 | tf_op jit(solution)/shard_map/all_to_all | solution.py:90
  25.2 0.6 dynamic_slice.9
  29.7 41.2 %all-to-all-done = bf16[16,65,1024]{2,1,0:T(8,128)(2,1)S(1)} async-done(((bf16[16,65,1024]{2,1,0:T(8,128)(2,1)}), bf16[16,65,1024]{2,1,0:T(8,128)(2,1)S(1)}, u32[]{:S(2)}, u32[]{:S(2)}) %all-to-all-start) | async-done | bytes 2129952 | tf_op jit(solution)/shard_map/all_to_all | solution.py:90
  71.0 0.2 slice.211
  71.2 1.6 %pad_maximum_fusion.1 = bf16[1040,1024]{1,0:T(8,128)(2,1)} fusion(bf16[16,1024]{1,0:T(8,128)(2,1)S(1)} %reshape.352, bf16[1024,1024]{1,0:T(8,128)(2,1)S(1)} %bitcast.113), kind=kLoop, calls=%fused_computation.20 | loop fusion | flops 4259840 | bytes 4259840 | tf_op jit(solution)/shard_map/concatenate | solution.py:47
  72.8 0.3 copy-done
  73.1 4.0 %collective-permute-start = (bf16[1040,1024]{1,0:T(8,128)(2,1)}, bf16[1040,1024]{1,0:T(8,128)(2,1)}, u32[]{:S(2)}, u32[]{:S(2)}) collective-permute-start(bf16[1040,1024]{1,0:T(8,128)(2,1)} %pad_maximum_fusion.1), channel_id=1, source_target_pairs={{0,1},{4,5},{8,9},{12,13},{14,15},{10,11},{6,7},{2,3},{16,17},{20,... | collective-permute-start | bytes 6389768 | tf_op jit(solution)/shard_map/ppermute | solution.py:23
  77.1 0.1 slice.212
  77.2 0.1 copy.77
  77.3 0.1 constant_dynamic-slice_fusion.1
  77.5 0.1 copy.79
  77.6 0.1 copy.78
  77.7 0.1 convert_reduce_fusion.1
  77.7 0.1 copy.81
  77.8 0.1 copy.80
  78.0 0.1 convert_reduce_fusion.4
  78.1 0.2 fusion.35
  78.3 6.9 %collective-permute-start.1 = (bf16[528,1024]{1,0:T(8,128)(2,1)S(1)}, bf16[528,1024]{1,0:T(8,128)(2,1)S(1)}, u32[]{:S(2)}, u32[]{:S(2)}) collective-permute-start(bf16[528,1024]{1,0:T(8,128)(2,1)S(1)} %pad_maximum_fusion.2), channel_id=1, source_target_pairs={{0,4},{1,5},{4,8},{5,9},{8,12},{9,13},{12,14},{13,15},{14,10},{15,... | collective-permute-start | bytes 3244040 | tf_op jit(solution)/shard_map/ppermute | solution.py:23
  85.3 3.2 %bitcast_reduce_fusion = f32[1024,8]{0,1:T(8,128)S(1)} fusion(bf16[1024,1024]{1,0:T(8,128)(2,1)S(1)} %bitcast.114, s32[1024]{0:T(1024)S(1)} %reshape.362, pred[1024]{0:T(1024)(128)(4,1)S(1)} %broadcast_compare_fusion.1), kind=kOutput, calls=%fused_computation.3 | convolution fusion | flops 2155864064 | bytes 2135040 | tf_op jit(solution)/shard_map/dot_general | solution.py:30
  88.5 0.1 fusion.18
  88.6 0.7 slice_convert_fusion.4
  89.3 2.9 %bitcast_reduce_fusion.7 = f32[1024,4]{0,1:T(4,128)S(1)} fusion(bf16[1024,1024]{1,0:T(8,128)(2,1)S(1)} %bitcast.115, bf16[1040,1024]{1,0:T(8,128)(2,1)} %collective-permute-done, s32[1024]{0:T(1024)S(1)} %reshape.362, s32[512]{0:T(512)S(1)} %bitcast.147, pred[1024]{0:T(1024)(128)(4,1)S(1)} %broadcast_compare_fusion.1), kind=kOutput, calls=%fused_computation.27 | convolution fusion | flops 1076359168 | bytes 3169280 | tf_op jit(solution)/shard_map/dot_general | solution.py:30
  92.2 0.1 fusion.25
  92.3 2.9 %bitcast_reduce_fusion.8 = f32[1024,4]{0,1:T(4,128)S(1)} fusion(bf16[1024,1024]{1,0:T(8,128)(2,1)S(1)} %bitcast.116, bf16[1040,1024]{1,0:T(8,128)(2,1)} %collective-permute-done, s32[1024]{0:T(1024)S(1)} %reshape.362, s32[512]{0:T(512)S(1)} %bitcast.146, pred[1024]{0:T(1024)(128)(4,1)S(1)} %broadcast_compare_fusion.1), kind=kOutput, calls=%fused_computation.28 | convolution fusion | flops 1076359168 | bytes 3169280 | tf_op jit(solution)/shard_map/dot_general | solution.py:30
  95.1 0.1 fusion.26
  95.2 11.4 %collective-permute-done.1 = bf16[528,1024]{1,0:T(8,128)(2,1)S(1)} collective-permute-done((bf16[528,1024]{1,0:T(8,128)(2,1)S(1)}, bf16[528,1024]{1,0:T(8,128)(2,1)S(1)}, u32[]{:S(2)}, u32[]{:S(2)}) %collective-permute-start.1) | collective-permute-done | bytes 1081376 | tf_op jit(solution)/shard_map/ppermute | solution.py:23
  106.6 3.0 %collective-permute-start.2 = (bf16[512,1024]{1,0:T(8,128)(2,1)S(1)}, bf16[512,1024]{1,0:T(8,128)(2,1)S(1)}, u32[]{:S(2)}, u32[]{:S(2)}) collective-permute-start(bf16[512,1024]{1,0:T(8,128)(2,1)S(1)} %bitcast.122), channel_id=1, source_target_pairs={{0,4},{1,5},{4,8},{5,9},{8,12},{9,13},{12,14},{13,15},{14,10},{15,... | collective-permute-start | bytes 3145736 | tf_op jit(solution)/shard_map/ppermute | solution.py:23
  109.6 3.1 %collective-permute-start.5 = (bf16[1040,1024]{1,0:T(8,128)(2,1)}, bf16[1040,1024]{1,0:T(8,128)(2,1)S(1)}, u32[]{:S(2)}, u32[]{:S(2)}) collective-permute-start(bf16[1040,1024]{1,0:T(8,128)(2,1)} %pad_maximum_fusion.1), channel_id=1, source_target_pairs={{0,2},{4,0},{8,4},{12,8},{14,12},{10,14},{6,10},{2,6},{1,1},{5,5},... | collective-permute-start | bytes 6389768 | tf_op jit(solution)/shard_map/ppermute | solution.py:23
  112.8 1.6 %bitcast_reduce_fusion.6 = f32[1024,4]{0,1:T(4,128)S(1)} fusion(bf16[1024,1024]{1,0:T(8,128)(2,1)S(1)} %bitcast.117, bf16[528,1024]{1,0:T(8,128)(2,1)S(1)} %collective-permute-done.1, s32[1024]{0:T(1024)S(1)} %reshape.362, s32[512]{0:T(512)S(1)} %bitcast.148, pred[1024]{0:T(1024)(128)(4,1)S(1)} %broadcast_compare_fusion.1), kind=kOutput, calls=%fused_computation.26 | convolution fusion | flops 1076359168 | bytes 3169280 | tf_op jit(solution)/shard_map/dot_general | solution.py:30
  114.4 0.1 fusion.24
  114.5 1.6 %bitcast_reduce_fusion.5 = f32[1024,4]{0,1:T(4,128)S(1)} fusion(bf16[1024,1024]{1,0:T(8,128)(2,1)S(1)} %bitcast.118, s32[1024]{0:T(1024)S(1)} %reshape.362, s32[512]{0:T(512)S(1)} %bitcast.141, pred[1024]{0:T(1024)(128)(4,1)S(1)} %broadcast_compare_fusion.1, bf16[528,1024]{1,0:T(8,128)(2,1)S(1)} %collective-permute-done.3), kind=kOutput, calls=%fused_computation.25 | convolution fusion | flops 1076359168 | bytes 3169280 | tf_op jit(solution)/shard_map/dot_general | solution.py:30
  116.2 0.1 fusion.23
  116.3 18.2 %collective-permute-done.2 = bf16[512,1024]{1,0:T(8,128)(2,1)S(1)} collective-permute-done((bf16[512,1024]{1,0:T(8,128)(2,1)S(1)}, bf16[512,1024]{1,0:T(8,128)(2,1)S(1)}, u32[]{:S(2)}, u32[]{:S(2)}) %collective-permute-start.2) | collective-permute-done | bytes 1048608 | tf_op jit(solution)/shard_map/ppermute | solution.py:23
  134.5 1.6 %bitcast_reduce_fusion.4 = f32[1024,4]{0,1:T(4,128)S(1)} fusion(bf16[1024,1024]{1,0:T(8,128)(2,1)S(1)} %bitcast.119, bf16[512,1024]{1,0:T(8,128)(2,1)S(1)} %collective-permute-done.2, s32[1024]{0:T(1024)S(1)} %reshape.362, s32[512]{0:T(512)S(1)} %bitcast.145, pred[1024]{0:T(1024)(128)(4,1)S(1)} %broadcast_compare_fusion.1), kind=kOutput, calls=%fused_computation.24 | convolution fusion | flops 1076359168 | bytes 3169280 | tf_op jit(solution)/shard_map/dot_general | solution.py:30
  136.1 0.1 fusion.22
  136.2 0.9 collective-permute-done.4
  137.1 1.7 %bitcast_reduce_fusion.3 = f32[1024,4]{0,1:T(4,128)S(1)} fusion(bf16[1024,1024]{1,0:T(8,128)(2,1)S(1)} %bitcast.120, bf16[512,1024]{1,0:T(8,128)(2,1)S(1)} %collective-permute-done.4, s32[1024]{0:T(1024)S(1)} %reshape.362, s32[512]{0:T(512)S(1)} %bitcast.143, pred[1024]{0:T(1024)(128)(4,1)S(1)} %broadcast_compare_fusion.1), kind=kOutput, calls=%fused_computation.23 | convolution fusion | flops 1076359168 | bytes 3169280 | tf_op jit(solution)/shard_map/dot_general | solution.py:30
  138.8 0.1 fusion.21
  138.9 1.6 %bitcast_reduce_fusion.1 = f32[1024,4]{0,1:T(4,128)S(1)} fusion(bf16[512,1024]{1,0:T(8,128)(2,1)S(1)} %collective-permute-done.4, bf16[1040,1024]{1,0:T(8,128)(2,1)S(1)} %collective-permute-done.5, s32[1024]{0:T(1024)S(1)} %bitcast.126, s32[512]{0:T(512)S(1)} %bitcast.144, pred[1024]{0:T(1024)(128)(4,1)S(1)} %broadcast_compare_fusion), kind=kOutput, calls=%fused_computation.21 | convolution fusion | flops 1076359168 | bytes 3169280 | tf_op jit(solution)/shard_map/dot_general | solution.py:30
  140.6 0.1 fusion.19
  140.6 1.6 %bitcast_reduce_fusion.2 = f32[1024,4]{0,1:T(4,128)S(1)} fusion(bf16[1040,1024]{1,0:T(8,128)(2,1)S(1)} %collective-permute-done.5, s32[1024]{0:T(1024)S(1)} %bitcast.127, s32[512]{0:T(512)S(1)} %bitcast.142, pred[1024]{0:T(1024)(128)(4,1)S(1)} %broadcast_compare_fusion, bf16[528,1024]{1,0:T(8,128)(2,1)S(1)} %collective-permute-done.3), kind=kOutput, calls=%fused_computation.22 | convolution fusion | flops 1076359168 | bytes 3169280 | tf_op jit(solution)/shard_map/dot_general | solution.py:30
  142.4 0.1 stack_reshape.4
  142.4 0.1 select_n.202
  142.6 0.1 reshape.441
  142.6 11.3 %all_to_all.10 = f32[16,1,128]{2,1,0:T(1,128)S(1)} all-to-all(f32[16,1,128]{2,1,0:T(1,128)S(1)} %reshape.441), channel_id=1, replica_groups=mesh['groups'=2,'blk'=16] {'blk'}, dimensions={0} | all-to-all | bytes 16384 | tf_op jit(solution)/shard_map/all_to_all | solution.py:155
  154.0 0.5 broadcast.345
  154.5 0.7 reduce.48
  155.2 0.1 reshape.442
  155.4 1.5 add_reduce_fusion
  156.9 0.6 log1p.3
  (50 shorter events, 0.8 us)
Async XLA Ops:
  17.6 7.5 %copy-start.2 = (s32[16]{0:T(128)S(1)}, s32[16]{0:T(128)}, u32[]{:S(2)}) copy-start(s32[16]{0:T(128)} %constant.90.clone) | copy-start | bytes 196
  17.6 53.2 %all-to-all-start = ((bf16[16,65,1024]{2,1,0:T(8,128)(2,1)}), bf16[16,65,1024]{2,1,0:T(8,128)(2,1)S(1)}, u32[]{:S(2)}, u32[]{:S(2)}) async-start(bf16[16,65,1024]{2,1,0:T(8,128)(2,1)} %pad_maximum_fusion), calls=%async_computation | async-start | bytes 4718592 | tf_op jit(solution)/shard_map/all_to_all | solution.py:90
  71.2 1.9 %copy-start = (bf16[16,64,1024]{2,1,0:T(8,128)(2,1)}, bf16[16,64,1024]{2,1,0:T(8,128)(2,1)S(1)}, u32[]{:S(2)}) copy-start(bf16[16,64,1024]{2,1,0:T(8,128)(2,1)S(1)} %slice.211) | copy-start | bytes 6291460
  73.1 15.4 %collective-permute-start = (bf16[1040,1024]{1,0:T(8,128)(2,1)}, bf16[1040,1024]{1,0:T(8,128)(2,1)}, u32[]{:S(2)}, u32[]{:S(2)}) collective-permute-start(bf16[1040,1024]{1,0:T(8,128)(2,1)} %pad_maximum_fusion.1), channel_id=1, source_target_pairs={{0,1},{4,5},{8,9},{12,13},{14,15},{10,11},{6,7},{2,3},{16,17},{20,... | collective-permute-start | bytes 6389768 | tf_op jit(solution)/shard_map/ppermute | solution.py:23
  78.2 7.0 %copy-start.1 = (bf16[16,64,1024]{2,1,0:T(8,128)(2,1)S(1)}, bf16[16,64,1024]{2,1,0:T(8,128)(2,1)}, u32[]{:S(2)}) copy-start(bf16[16,64,1024]{2,1,0:T(8,128)(2,1)} %copy-done) | copy-start | bytes 6291460
  78.3 28.3 %collective-permute-start.1 = (bf16[528,1024]{1,0:T(8,128)(2,1)S(1)}, bf16[528,1024]{1,0:T(8,128)(2,1)S(1)}, u32[]{:S(2)}, u32[]{:S(2)}) collective-permute-start(bf16[528,1024]{1,0:T(8,128)(2,1)S(1)} %pad_maximum_fusion.2), channel_id=1, source_target_pairs={{0,4},{1,5},{4,8},{5,9},{8,12},{9,13},{12,14},{13,15},{14,10},{15,... | collective-permute-start | bytes 3244040 | tf_op jit(solution)/shard_map/ppermute | solution.py:23
  106.6 7.9 %collective-permute-start.3 = (bf16[528,1024]{1,0:T(8,128)(2,1)S(1)}, bf16[528,1024]{1,0:T(8,128)(2,1)S(1)}, u32[]{:S(2)}, u32[]{:S(2)}) collective-permute-start(bf16[528,1024]{1,0:T(8,128)(2,1)S(1)} %collective-permute-done.1), channel_id=1, source_target_pairs={{0,1},{1,0},{4,5},{5,4},{8,9},{9,8},{12,13},{13,12},{14,15},{15,14... | collective-permute-start | bytes 3244040 | tf_op jit(solution)/shard_map/ppermute | solution.py:23
  106.6 27.8 %collective-permute-start.2 = (bf16[512,1024]{1,0:T(8,128)(2,1)S(1)}, bf16[512,1024]{1,0:T(8,128)(2,1)S(1)}, u32[]{:S(2)}, u32[]{:S(2)}) collective-permute-start(bf16[512,1024]{1,0:T(8,128)(2,1)S(1)} %bitcast.122), channel_id=1, source_target_pairs={{0,4},{1,5},{4,8},{5,9},{8,12},{9,13},{12,14},{13,15},{14,10},{15,... | collective-permute-start | bytes 3145736 | tf_op jit(solution)/shard_map/ppermute | solution.py:23
  109.6 29.3 %collective-permute-start.5 = (bf16[1040,1024]{1,0:T(8,128)(2,1)}, bf16[1040,1024]{1,0:T(8,128)(2,1)S(1)}, u32[]{:S(2)}, u32[]{:S(2)}) collective-permute-start(bf16[1040,1024]{1,0:T(8,128)(2,1)} %pad_maximum_fusion.1), channel_id=1, source_target_pairs={{0,2},{4,0},{8,4},{12,8},{14,12},{10,14},{6,10},{2,6},{1,1},{5,5},... | collective-permute-start | bytes 6389768 | tf_op jit(solution)/shard_map/ppermute | solution.py:23
  134.5 2.7 %collective-permute-start.4 = (bf16[512,1024]{1,0:T(8,128)(2,1)S(1)}, bf16[512,1024]{1,0:T(8,128)(2,1)S(1)}, u32[]{:S(2)}, u32[]{:S(2)}) collective-permute-start(bf16[512,1024]{1,0:T(8,128)(2,1)S(1)} %collective-permute-done.2), channel_id=1, source_target_pairs={{0,1},{1,0},{4,5},{5,4},{8,9},{9,8},{12,13},{13,12},{14,15},{15,14... | collective-permute-start | bytes 3145736 | tf_op jit(solution)/shard_map/ppermute | solution.py:23

commit v16 on v14

--- a/solution.py
+++ b/solution.py
@@ -103,11 +103,14 @@
     half = slot_count // 2
     forward = [(p, (p + 2) % n) for p in range(n)]
     swap = [(p, p ^ 1) for p in range(n)]
-    fwd_a = moved(pack(own[:half], own_ids), pos2dev, forward)
-    across = moved(pack(own, own_ids), pos2dev, [(p, p + 1) for p in evens])
+    lead_half = pack(own[:half], own_ids)
+    fwd_a = moved(lead_half, pos2dev, forward)
+    across_a = moved(lead_half, pos2dev, [(p, p + 1) for p in evens])
+    across_b = moved(own[half:], pos2dev, [(p, p + 1) for p in evens])
     total = step_total(own, own_ids, own, own_ids, my_pairs[0], True)
-    total, across = lax.optimization_barrier((total, across))
-    across_held, across_ids = unpack(across)
+    total, across_a, across_b = lax.optimization_barrier((total, across_a, across_b))
+    across_held = jnp.concatenate([across_a[:half], across_b], axis=0)
+    across_ids = across_a[half:].reshape(-1)[:slot_count].astype(jnp.int32)
     from_across = [
         step_total(own, own_ids, across_held[lo : lo + half], across_ids[lo : lo + half], my_pairs[1], False, lo // 128)
         for lo in (0, half)

time: 151 us -> 149 us (0.987)
  waiting for transfers between devices: 71.7 us -> 64 us
  local copies, waits for them, and re-layouts: 4.07 us -> 8 us
  other arithmetic: 12.9 us -> 14.5 us
    ppermute x6 -> x7, waiting for transfers between devices: 30.6 us -> 22.9 us  [moved(): return lax.ppermute(x, 'blk', [(pos2dev[a], pos2dev[b]) for a, b in moves])]
    ppermute x6 -> x7, starting transfers between devices: 17 us -> 18 us  [moved(): return lax.ppermute(x, 'blk', [(pos2dev[a], pos2dev[b]) for a, b in moves])]
  transfers between devices with their start and end apart: 7 -> 8, of which waited for: 4 -> 4; matrix products, arithmetic and copies ran while one was open for 12% -> 16% of each run, Pallas kernels for 0% -> 0%
where the time goes in v16:
time: 149 us; the launch traced here: 148 us
  waiting for transfers between devices  64 us (43%)
  starting transfers between devices  25.5 us (17%)
  matrix products  21.4 us (14%)
  other arithmetic  14.5 us (10%)
  blocking collectives  11.3 us (8%)
  local copies, waits for them, and re-layouts  8 us (5%)
  between operations  3.68 us (2%)
    all_to_all x1, waiting for transfers between devices, body(): lax.all_to_all(payload, 'blk', split_axis=0, concat_axis=0, tiled=True)  41.2 us
    ppermute x7, waiting for transfers between devices, moved(): return lax.ppermute(x, 'blk', [(pos2dev[a], pos2dev[b]) for a, b in moves])  22.9 us
    dot_general x9, matrix products, step_total(): lax.dot_general(local, remote, (((1,), (1,)), ((), ())), preferred_elemen...  18.8 us
    ppermute x7, starting transfers between devices, moved(): return lax.ppermute(x, 'blk', [(pos2dev[a], pos2dev[b]) for a, b in moves])  18 us
    all_to_all x1, blocking collectives, body(): lax.all_to_all(totals, 'blk', split_axis=0, concat_axis=0, tiled=True)  11.3 us
    all_to_all x1, starting transfers between devices, body(): lax.all_to_all(payload, 'blk', split_axis=0, concat_axis=0, tiled=True)  7.52 us
  transfers between devices with their start and end apart: 8, of which 4 were waited for; matrix products, arithmetic and copies ran while one was open for 16% of the time, Pallas kernels for 0%

profile of v16, /device:TPU:0, one launch (start us, length us, event | category | flops | bytes accessed | tf_op | source)
XLA Modules:
  0.0 148.4 jit_solution(4455455815900430646)
XLA Ops:
  0.0 0.8 convert.13
  0.8 0.1 copy.72
  1.0 0.1 reshape.390
  1.1 2.0 %fusion.2 = f32[960]{0:T(1024)S(1)} fusion(bf16[960,1024]{1,0:T(8,128)(2,1)} %param.7), kind=kLoop, calls=%fused_computation.7 | loop fusion | flops 2948160 | bytes 1969920 | tf_op jit(solution)/shard_map/reduce_sum | solution.py:69
  3.1 1.2 convert_reduce_fusion
  4.3 1.3 fusion.38
  5.7 0.6 select_reduce_fusion
  6.3 0.1 sub.11
  6.5 2.6 %fusion.9 = bf16[1024,1024]{1,0:T(8,128)(2,1)S(1)} fusion(bf16[960,1024]{1,0:T(8,128)(2,1)S(1)} %copy-done, f32[960]{0:T(1024)S(1)} %add_rsqrt_fusion, s32[960]{0:T(1024)S(1)} %get-tuple-element.46), kind=kOutput, calls=%fused_computation.38 | convolution fusion | flops 2018246656 | bytes 4070912 | tf_op jit(solution)/shard_map/dot_general | solution.py:77
  9.2 1.7 %pad_maximum_fusion = bf16[16,65,1024]{2,1,0:T(8,128)(2,1)} fusion(bf16[16,1,1024]{2,1,0:T(2,128)(2,1)S(1)} %copy.73, bf16[16,64,1024]{2,1,0:T(8,128)(2,1)S(1)} %bitcast.120), kind=kLoop, calls=%fused_computation.18 | loop fusion | flops 4259840 | bytes 4259840 | tf_op jit(solution)/shard_map/concatenate | solution.py:90
  10.8 7.5 %all-to-all-start = ((bf16[16,65,1024]{2,1,0:T(8,128)(2,1)}), bf16[16,65,1024]{2,1,0:T(8,128)(2,1)S(1)}, u32[]{:S(2)}, u32[]{:S(2)}) async-start(bf16[16,65,1024]{2,1,0:T(8,128)(2,1)} %pad_maximum_fusion), calls=%async_computation | async-start | bytes 4718592 | tf_op jit(solution)/shard_map/all_to_all | solution.py:91
  18.4 0.6 dynamic_slice.9
  22.4 0.5 iota_add_fusion
  22.9 41.2 %all-to-all-done = bf16[16,65,1024]{2,1,0:T(8,128)(2,1)S(1)} async-done(((bf16[16,65,1024]{2,1,0:T(8,128)(2,1)}), bf16[16,65,1024]{2,1,0:T(8,128)(2,1)S(1)}, u32[]{:S(2)}, u32[]{:S(2)}) %all-to-all-start) | async-done | bytes 2129952 | tf_op jit(solution)/shard_map/all_to_all | solution.py:91
  64.2 0.6 copy-done.2
  64.8 1.2 fusion.41
  66.0 7.8 %collective-permute-start.2 = (bf16[528,1024]{1,0:T(8,128)(2,1)S(1)}, bf16[528,1024]{1,0:T(8,128)(2,1)}, u32[]{:S(2)}, u32[]{:S(2)}) collective-permute-start(bf16[528,1024]{1,0:T(8,128)(2,1)S(1)} %pad_maximum_fusion.2), channel_id=1, source_target_pairs={{0,4},{1,5},{4,8},{5,9},{8,12},{9,13},{12,14},{13,15},{14,10},{15,... | collective-permute-start | bytes 3244040 | tf_op jit(solution)/shard_map/ppermute | solution.py:23
  73.8 2.5 %collective-permute-start = (bf16[528,1024]{1,0:T(8,128)(2,1)S(1)}, bf16[528,1024]{1,0:T(8,128)(2,1)}, u32[]{:S(2)}, u32[]{:S(2)}) collective-permute-start(bf16[528,1024]{1,0:T(8,128)(2,1)S(1)} %pad_maximum_fusion.2), channel_id=1, source_target_pairs={{0,1},{4,5},{8,9},{12,13},{14,15},{10,11},{6,7},{2,3},{16,17},{20,... | collective-permute-start | bytes 3244040 | tf_op jit(solution)/shard_map/ppermute | solution.py:23
  76.4 0.1 slice.204
  76.4 0.1 copy.75
  76.6 0.7 constant_dynamic-slice_fusion.1
  77.3 0.8 copy.77
  78.1 0.8 copy.76
  78.9 0.8 copy.79
  79.7 0.1 copy.78
  79.8 1.3 collective-permute-start.1
  81.2 0.7 convert_reduce_fusion.4
  81.9 0.1 convert_reduce_fusion.1
  82.0 0.2 slice.203
  82.2 0.4 copy-done.3
  82.7 3.2 %bitcast_reduce_fusion = f32[1024,8]{0,1:T(8,128)S(1)} fusion(bf16[1024,1024]{1,0:T(8,128)(2,1)S(1)} %bitcast.111, s32[1024]{0:T(1024)S(1)} %copy-done.3, pred[1024]{0:T(1024)(128)(4,1)S(1)} %broadcast_compare_fusion.1), kind=kOutput, calls=%fused_computation.2 | convolution fusion | flops 2155864064 | bytes 2135040 | tf_op jit(solution)/shard_map/dot_general | solution.py:30
  85.8 0.1 fusion.24
  85.9 0.7 slice_convert_fusion.4
  86.7 1.6 %bitcast_reduce_fusion.7 = f32[1024,4]{0,1:T(4,128)S(1)} fusion(bf16[1024,1024]{1,0:T(8,128)(2,1)S(1)} %bitcast.112, bf16[512,1024]{1,0:T(8,128)(2,1)S(1)} %collective-permute-done.1, s32[1024]{0:T(1024)S(1)} %copy-done.3, s32[512]{0:T(512)S(1)} %bitcast.145, pred[1024]{0:T(1024)(128)(4,1)S(1)} %broadcast_compare_fusion.1), kind=kOutput, calls=%fused_computation.26 | convolution fusion | flops 1076359168 | bytes 3169280 | tf_op jit(solution)/shard_map/dot_general | solution.py:30
  88.3 0.1 fusion.31
  88.4 2.9 %bitcast_reduce_fusion.8 = f32[1024,4]{0,1:T(4,128)S(1)} fusion(bf16[1024,1024]{1,0:T(8,128)(2,1)S(1)} %bitcast.113, bf16[528,1024]{1,0:T(8,128)(2,1)} %collective-permute-done, s32[1024]{0:T(1024)S(1)} %copy-done.3, s32[512]{0:T(512)S(1)} %bitcast.144, pred[1024]{0:T(1024)(128)(4,1)S(1)} %broadcast_compare_fusion.1), kind=kOutput, calls=%fused_computation.27 | convolution fusion | flops 1076359168 | bytes 3169280 | tf_op jit(solution)/shard_map/dot_general | solution.py:30
  91.3 0.1 fusion.32
  91.3 5.7 %collective-permute-done.2 = bf16[528,1024]{1,0:T(8,128)(2,1)} collective-permute-done((bf16[528,1024]{1,0:T(8,128)(2,1)S(1)}, bf16[528,1024]{1,0:T(8,128)(2,1)}, u32[]{:S(2)}, u32[]{:S(2)}) %collective-permute-start.2) | collective-permute-done | bytes 1081376 | tf_op jit(solution)/shard_map/ppermute | solution.py:23
  97.0 0.2 pad_maximum_fusion.1
  97.2 3.0 %collective-permute-start.3 = (bf16[512,1024]{1,0:T(8,128)(2,1)S(1)}, bf16[512,1024]{1,0:T(8,128)(2,1)S(1)}, u32[]{:S(2)}, u32[]{:S(2)}) collective-permute-start(bf16[512,1024]{1,0:T(8,128)(2,1)S(1)} %bitcast.122), channel_id=1, source_target_pairs={{0,4},{1,5},{4,8},{5,9},{8,12},{9,13},{12,14},{13,15},{14,10},{15,... | collective-permute-start | bytes 3145736 | tf_op jit(solution)/shard_map/ppermute | solution.py:23
  100.2 3.2 %collective-permute-start.6 = (bf16[1040,1024]{1,0:T(8,128)(2,1)S(1)}, bf16[1040,1024]{1,0:T(8,128)(2,1)S(1)}, u32[]{:S(2)}, u32[]{:S(2)}) collective-permute-start(bf16[1040,1024]{1,0:T(8,128)(2,1)S(1)} %pad_maximum_fusion.1), channel_id=1, source_target_pairs={{0,2},{4,0},{8,4},{12,8},{14,12},{10,14},{6,10},{2,6},{1,1},{5,5},... | collective-permute-start | bytes 6389768 | tf_op jit(solution)/shard_map/ppermute | solution.py:23
  103.5 0.7 slice_convert_fusion.3
  104.2 2.9 %bitcast_reduce_fusion.6 = f32[1024,4]{0,1:T(4,128)S(1)} fusion(bf16[1024,1024]{1,0:T(8,128)(2,1)S(1)} %bitcast.115, bf16[528,1024]{1,0:T(8,128)(2,1)} %collective-permute-done.2, s32[1024]{0:T(1024)S(1)} %copy-done.3, s32[512]{0:T(512)S(1)} %bitcast.146, pred[1024]{0:T(1024)(128)(4,1)S(1)} %broadcast_compare_fusion.1), kind=kOutput, calls=%fused_computation.25 | convolution fusion | flops 1076359168 | bytes 3169280 | tf_op jit(solution)/shard_map/dot_general | solution.py:30
  107.1 0.1 fusion.30
  107.2 1.6 %bitcast_reduce_fusion.5 = f32[1024,4]{0,1:T(4,128)S(1)} fusion(bf16[1024,1024]{1,0:T(8,128)(2,1)S(1)} %bitcast.116, s32[1024]{0:T(1024)S(1)} %copy-done.3, s32[512]{0:T(512)S(1)} %bitcast.139, pred[1024]{0:T(1024)(128)(4,1)S(1)} %broadcast_compare_fusion.1, bf16[528,1024]{1,0:T(8,128)(2,1)S(1)} %collective-permute-done.4), kind=kOutput, calls=%fused_computation.24 | convolution fusion | flops 1076359168 | bytes 3169280 | tf_op jit(solution)/shard_map/dot_general | solution.py:30
  108.8 0.1 fusion.29
  108.9 16.3 %collective-permute-done.3 = bf16[512,1024]{1,0:T(8,128)(2,1)S(1)} collective-permute-done((bf16[512,1024]{1,0:T(8,128)(2,1)S(1)}, bf16[512,1024]{1,0:T(8,128)(2,1)S(1)}, u32[]{:S(2)}, u32[]{:S(2)}) %collective-permute-start.3) | collective-permute-done | bytes 1048608 | tf_op jit(solution)/shard_map/ppermute | solution.py:23
  125.2 1.7 %bitcast_reduce_fusion.4 = f32[1024,4]{0,1:T(4,128)S(1)} fusion(bf16[1024,1024]{1,0:T(8,128)(2,1)S(1)} %bitcast.117, bf16[512,1024]{1,0:T(8,128)(2,1)S(1)} %collective-permute-done.3, s32[1024]{0:T(1024)S(1)} %copy-done.3, s32[512]{0:T(512)S(1)} %bitcast.143, pred[1024]{0:T(1024)(128)(4,1)S(1)} %broadcast_compare_fusion.1), kind=kOutput, calls=%fused_computation.23 | convolution fusion | flops 1076359168 | bytes 3169280 | tf_op jit(solution)/shard_map/dot_general | solution.py:30
  126.9 0.1 fusion.28
  127.0 0.9 collective-permute-done.5
  127.8 1.6 %bitcast_reduce_fusion.3 = f32[1024,4]{0,1:T(4,128)S(1)} fusion(bf16[1024,1024]{1,0:T(8,128)(2,1)S(1)} %bitcast.118, bf16[512,1024]{1,0:T(8,128)(2,1)S(1)} %collective-permute-done.5, s32[1024]{0:T(1024)S(1)} %copy-done.3, s32[512]{0:T(512)S(1)} %bitcast.141, pred[1024]{0:T(1024)(128)(4,1)S(1)} %broadcast_compare_fusion.1), kind=kOutput, calls=%fused_computation.22 | convolution fusion | flops 1076359168 | bytes 3169280 | tf_op jit(solution)/shard_map/dot_general | solution.py:30
  129.5 0.1 fusion.27
  129.6 1.7 %bitcast_reduce_fusion.1 = f32[1024,4]{0,1:T(4,128)S(1)} fusion(bf16[512,1024]{1,0:T(8,128)(2,1)S(1)} %collective-permute-done.5, bf16[1040,1024]{1,0:T(8,128)(2,1)S(1)} %collective-permute-done.6, s32[1024]{0:T(1024)S(1)} %bitcast.125, s32[512]{0:T(512)S(1)} %bitcast.142, pred[1024]{0:T(1024)(128)(4,1)S(1)} %broadcast_compare_fusion), kind=kOutput, calls=%fused_computation.20 | convolution fusion | flops 1076359168 | bytes 3169280 | tf_op jit(solution)/shard_map/dot_general | solution.py:30
  131.2 0.1 fusion.25
  131.3 1.7 %bitcast_reduce_fusion.2 = f32[1024,4]{0,1:T(4,128)S(1)} fusion(bf16[1040,1024]{1,0:T(8,128)(2,1)S(1)} %collective-permute-done.6, s32[1024]{0:T(1024)S(1)} %bitcast.126, s32[512]{0:T(512)S(1)} %bitcast.140, pred[1024]{0:T(1024)(128)(4,1)S(1)} %broadcast_compare_fusion, bf16[528,1024]{1,0:T(8,128)(2,1)S(1)} %collective-permute-done.4), kind=kOutput, calls=%fused_computation.21 | convolution fusion | flops 1076359168 | bytes 3169280 | tf_op jit(solution)/shard_map/dot_general | solution.py:30
  133.1 0.1 stack_reshape.4
  133.2 0.1 select_n.155
  133.3 0.1 reshape.393
  133.4 11.3 %all_to_all.10 = f32[16,1,128]{2,1,0:T(1,128)S(1)} all-to-all(f32[16,1,128]{2,1,0:T(1,128)S(1)} %reshape.393), channel_id=1, replica_groups=mesh['groups'=2,'blk'=16] {'blk'}, dimensions={0} | all-to-all | bytes 16384 | tf_op jit(solution)/shard_map/all_to_all | solution.py:159
  144.7 0.6 broadcast.269
  145.3 0.7 reduce.48
  146.0 0.1 reshape.394
  146.3 1.5 %add_reduce_fusion = f32[960]{0:T(1024)S(1)} fusion(f32[1024]{0:T(1024)S(1)} %broadcast_in_dim.79, s32[960]{0:T(1024)S(1)} %copy-done.6, f32[1024]{0:T(1024)S(1)} %broadcast_in_dim.71, s32[960]{0:T(1024)S(1)} %copy-done.5), kind=kLoop, calls=%fused_computation.9 | loop fusion | flops 5897280 | bytes 19712 | tf_op jit(solution)/shard_map/reduce_sum | solution.py:162
  147.8 0.6 log1p.3
  (54 shorter events, 0.8 us)
Async XLA Ops:
  0.0 6.5 %copy-start = (bf16[960,1024]{1,0:T(8,128)(2,1)S(1)}, bf16[960,1024]{1,0:T(8,128)(2,1)}, u32[]{:S(2)}) copy-start(bf16[960,1024]{1,0:T(8,128)(2,1)} %param.7) | copy-start | bytes 5898244
  5.7 3.5 %copy-start.4 = (s32[960]{0:T(1024)}, s32[960]{0:T(1024)S(1)}, u32[]{:S(2)}) copy-start(s32[960]{0:T(1024)S(1)} %get-tuple-element.46) | copy-start | bytes 11524
  10.8 7.5 %copy-start.7 = (s32[16]{0:T(128)S(1)}, s32[16]{0:T(128)}, u32[]{:S(2)}) copy-start(s32[16]{0:T(128)} %constant.73.clone) | copy-start | bytes 196
  10.8 53.2 %all-to-all-start = ((bf16[16,65,1024]{2,1,0:T(8,128)(2,1)}), bf16[16,65,1024]{2,1,0:T(8,128)(2,1)S(1)}, u32[]{:S(2)}, u32[]{:S(2)}) async-start(bf16[16,65,1024]{2,1,0:T(8,128)(2,1)} %pad_maximum_fusion), calls=%async_computation | async-start | bytes 4718592 | tf_op jit(solution)/shard_map/all_to_all | solution.py:91
  64.1 0.6 copy-start.2
  66.0 31.0 %collective-permute-start.2 = (bf16[528,1024]{1,0:T(8,128)(2,1)S(1)}, bf16[528,1024]{1,0:T(8,128)(2,1)}, u32[]{:S(2)}, u32[]{:S(2)}) collective-permute-start(bf16[528,1024]{1,0:T(8,128)(2,1)S(1)} %pad_maximum_fusion.2), channel_id=1, source_target_pairs={{0,4},{1,5},{4,8},{5,9},{8,12},{9,13},{12,14},{13,15},{14,10},{15,... | collective-permute-start | bytes 3244040 | tf_op jit(solution)/shard_map/ppermute | solution.py:23
  73.8 12.1 %collective-permute-start = (bf16[528,1024]{1,0:T(8,128)(2,1)S(1)}, bf16[528,1024]{1,0:T(8,128)(2,1)}, u32[]{:S(2)}, u32[]{:S(2)}) collective-permute-start(bf16[528,1024]{1,0:T(8,128)(2,1)S(1)} %pad_maximum_fusion.2), channel_id=1, source_target_pairs={{0,1},{4,5},{8,9},{12,13},{14,15},{10,11},{6,7},{2,3},{16,17},{20,... | collective-permute-start | bytes 3244040 | tf_op jit(solution)/shard_map/ppermute | solution.py:23
  79.8 6.1 %collective-permute-start.1 = (bf16[512,1024]{1,0:T(8,128)(2,1)}, bf16[512,1024]{1,0:T(8,128)(2,1)S(1)}, u32[]{:S(2)}, u32[]{:S(2)}) collective-permute-start(bf16[512,1024]{1,0:T(8,128)(2,1)} %bitcast.121), channel_id=1, source_target_pairs={{0,1},{4,5},{8,9},{12,13},{14,15},{10,11},{6,7},{2,3},{16,17},{20,... | collective-permute-start | bytes 3145736 | tf_op jit(solution)/shard_map/ppermute | solution.py:23
  82.0 0.7 copy-start.3
  91.3 5.9 %copy-start.1 = (bf16[8,64,1024]{2,1,0:T(8,128)(2,1)S(1)}, bf16[8,64,1024]{2,1,0:T(8,128)(2,1)}, u32[]{:S(2)}) copy-start(bf16[8,64,1024]{2,1,0:T(8,128)(2,1)} %get-tuple-element.39) | copy-start | bytes 3145732
  97.0 10.1 %collective-permute-start.4 = (bf16[528,1024]{1,0:T(8,128)(2,1)}, bf16[528,1024]{1,0:T(8,128)(2,1)S(1)}, u32[]{:S(2)}, u32[]{:S(2)}) collective-permute-start(bf16[528,1024]{1,0:T(8,128)(2,1)} %collective-permute-done.2), channel_id=1, source_target_pairs={{0,1},{1,0},{4,5},{5,4},{8,9},{9,8},{12,13},{13,12},{14,15},{15,14... | collective-permute-start | bytes 3244040 | tf_op jit(solution)/shard_map/ppermute | solution.py:23
  97.2 28.0 %collective-permute-start.3 = (bf16[512,1024]{1,0:T(8,128)(2,1)S(1)}, bf16[512,1024]{1,0:T(8,128)(2,1)S(1)}, u32[]{:S(2)}, u32[]{:S(2)}) collective-permute-start(bf16[512,1024]{1,0:T(8,128)(2,1)S(1)} %bitcast.122), channel_id=1, source_target_pairs={{0,4},{1,5},{4,8},{5,9},{8,12},{9,13},{12,14},{13,15},{14,10},{15,... | collective-permute-start | bytes 3145736 | tf_op jit(solution)/shard_map/ppermute | solution.py:23
  100.2 29.3 %collective-permute-start.6 = (bf16[1040,1024]{1,0:T(8,128)(2,1)S(1)}, bf16[1040,1024]{1,0:T(8,128)(2,1)S(1)}, u32[]{:S(2)}, u32[]{:S(2)}) collective-permute-start(bf16[1040,1024]{1,0:T(8,128)(2,1)S(1)} %pad_maximum_fusion.1), channel_id=1, source_target_pairs={{0,2},{4,0},{8,4},{12,8},{14,12},{10,14},{6,10},{2,6},{1,1},{5,5},... | collective-permute-start | bytes 6389768 | tf_op jit(solution)/shard_map/ppermute | solution.py:23
  125.2 2.7 %collective-permute-start.5 = (bf16[512,1024]{1,0:T(8,128)(2,1)S(1)}, bf16[512,1024]{1,0:T(8,128)(2,1)S(1)}, u32[]{:S(2)}, u32[]{:S(2)}) collective-permute-start(bf16[512,1024]{1,0:T(8,128)(2,1)S(1)} %collective-permute-done.3), channel_id=1, source_target_pairs={{0,1},{1,0},{4,5},{5,4},{8,9},{9,8},{12,13},{13,12},{14,15},{15,14... | collective-permute-start | bytes 3145736 | tf_op jit(solution)/shard_map/ppermute | solution.py:23
  131.3 15.0 %copy-start.5 = (s32[960]{0:T(1024)S(1)}, s32[960]{0:T(1024)}, u32[]{:S(2)}) copy-start(s32[960]{0:T(1024)} %copy-done.4) | copy-start | bytes 11524
  131.3 15.0 %copy-start.6 = (s32[960]{0:T(1024)S(1)}, s32[960]{0:T(1024)}, u32[]{:S(2)}) copy-start(s32[960]{0:T(1024)} %get-tuple-element.45) | copy-start | bytes 11524

commit v17 on v16

--- a/solution.py
+++ b/solution.py
@@ -157,13 +157,12 @@
     forward_part = jnp.where(odd, 0.0, last)
     totals = jnp.stack([total.reshape(device_count, capacity), forward_part.reshape(device_count, capacity)], axis=1)
     returned = lax.all_to_all(totals, "blk", split_axis=0, concat_axis=0, tiled=True)
-    behind = jnp.asarray(np.asarray(pos2dev, np.int32))[(owners - 2) % device_count] * capacity + arrival
-    behind = jnp.where(owners % 2 == 0, behind, -1)
-    both = jnp.sum(
-        jnp.where(place[:, None] == slot_index[None, :], returned[:, 0].reshape(-1)[None, :], 0.0)
-        + jnp.where(behind[:, None] == slot_index[None, :], returned[:, 1].reshape(-1)[None, :], 0.0),
-        axis=1,
-    )
+    ring_dev = jnp.asarray(np.asarray(pos2dev, np.int32))
+    source_dev = jnp.stack([ring_dev[owners], jnp.where(owners % 2 == 0, ring_dev[(owners - 2) % device_count], -1)], axis=1)
+    dev_pick = (source_dev[:, :, None] == jnp.arange(device_count, dtype=jnp.int32)).astype(jnp.float32)
+    by_row = jnp.einsum("rpe,epa->ra", dev_pick, returned, precision=lax.Precision.HIGHEST)
+    slot_in = jnp.arange(capacity, dtype=jnp.int32)
+    both = jnp.sum(jnp.where(arrival[:, None] == slot_in[None, :], by_row, 0.0), axis=1)
     return jnp.log1p(both)
 
 

time: 149 us -> 149 us (level)
  blocking collectives: 11.3 us -> 0 us
  waiting for transfers between devices: 64 us -> 70.3 us
  starting transfers between devices: 25.5 us -> 30.6 us
  other arithmetic: 14.5 us -> 13 us
    all_to_all x1 -> x0, blocking collectives: 11.3 us -> none  [body(): lax.all_to_all(totals, 'blk', split_axis=0, concat_axis=0, tiled=True)]
    all_to_all x0 -> x1, waiting for transfers between devices: none -> 6.37 us  [body(): lax.all_to_all(totals, 'blk', split_axis=0, concat_axis=0, tiled=True)]
    all_to_all x0 -> x1, starting transfers between devices: none -> 5.15 us  [body(): lax.all_to_all(totals, 'blk', split_axis=0, concat_axis=0, tiled=True)]
  transfers between devices with their start and end apart: 8 -> 9, of which waited for: 4 -> 5; matrix products, arithmetic and copies ran while one was open for 16% -> 16% of each run, Pallas kernels for 0% -> 0%
where the time goes in v17:
time: 149 us; the launch traced here: 148 us
  waiting for transfers between devices  70.3 us (47%)
  starting transfers between devices  30.6 us (21%)
  matrix products  21.7 us (15%)
  other arithmetic  13 us (9%)
  local copies, waits for them, and re-layouts  8.39 us (6%)
  between operations  3.72 us (2%)
    all_to_all x1, waiting for transfers between devices, body(): lax.all_to_all(payload, 'blk', split_axis=0, concat_axis=0, tiled=True)  41.1 us
    ppermute x7, waiting for transfers between devices, moved(): return lax.ppermute(x, 'blk', [(pos2dev[a], pos2dev[b]) for a, b in moves])  22.8 us
    dot_general x9, matrix products, step_total(): lax.dot_general(local, remote, (((1,), (1,)), ((), ())), preferred_elemen...  18.8 us
    ppermute x7, starting transfers between devices, moved(): return lax.ppermute(x, 'blk', [(pos2dev[a], pos2dev[b]) for a, b in moves])  18 us
    all_to_all x1, starting transfers between devices, body(): lax.all_to_all(payload, 'blk', split_axis=0, concat_axis=0, tiled=True)  7.51 us
    all_to_all x1, waiting for transfers between devices, body(): lax.all_to_all(totals, 'blk', split_axis=0, concat_axis=0, tiled=True)  6.37 us
    all_to_all x1, starting transfers between devices, body(): lax.all_to_all(totals, 'blk', split_axis=0, concat_axis=0, tiled=True)  5.15 us
  transfers between devices with their start and end apart: 9, of which 5 were waited for; matrix products, arithmetic and copies ran while one was open for 16% of the time, Pallas kernels for 0%

profile of v17, /device:TPU:0, one launch (start us, length us, event | category | flops | bytes accessed | tf_op | source)
XLA Modules:
  0.0 147.8 jit_solution(16590140014210258808)
XLA Ops:
  0.0 1.3 convert_reduce_fusion
  1.3 0.7 convert.13
  2.0 0.1 copy.76
  2.2 0.1 reshape.373
  2.3 2.0 %fusion.2 = f32[960]{0:T(1024)S(1)} fusion(bf16[960,1024]{1,0:T(8,128)(2,1)} %param.7), kind=kLoop, calls=%fused_computation.7 | loop fusion | flops 2948160 | bytes 1969920 | tf_op jit(solution)/shard_map/reduce_sum | solution.py:69
  4.3 1.3 multiply_add_fusion
  5.6 0.6 select_reduce_fusion
  6.2 0.1 sub.12
  6.5 2.6 %fusion.9 = bf16[1024,1024]{1,0:T(8,128)(2,1)S(1)} fusion(bf16[960,1024]{1,0:T(8,128)(2,1)S(1)} %copy-done, f32[960]{0:T(1024)S(1)} %add_rsqrt_fusion, s32[960]{0:T(1024)S(1)} %get-tuple-element.37), kind=kOutput, calls=%fused_computation.35 | convolution fusion | flops 2018246656 | bytes 4070912 | tf_op jit(solution)/shard_map/dot_general | solution.py:77
  9.1 1.7 %pad_maximum_fusion = bf16[16,65,1024]{2,1,0:T(8,128)(2,1)} fusion(bf16[16,1,1024]{2,1,0:T(2,128)(2,1)S(1)} %copy.77, bf16[16,64,1024]{2,1,0:T(8,128)(2,1)S(1)} %bitcast.128), kind=kLoop, calls=%fused_computation.15 | loop fusion | flops 4259840 | bytes 4259840 | tf_op jit(solution)/shard_map/concatenate | solution.py:90
  10.8 7.5 %all-to-all-start = ((bf16[16,65,1024]{2,1,0:T(8,128)(2,1)}), bf16[16,65,1024]{2,1,0:T(8,128)(2,1)S(1)}, u32[]{:S(2)}, u32[]{:S(2)}) async-start(bf16[16,65,1024]{2,1,0:T(8,128)(2,1)} %pad_maximum_fusion), calls=%async_computation | async-start | bytes 4718592 | tf_op jit(solution)/shard_map/all_to_all | solution.py:91
  18.3 0.6 dynamic_slice.9
  22.3 0.6 iota_add_fusion
  22.9 41.1 %all-to-all-done = bf16[16,65,1024]{2,1,0:T(8,128)(2,1)S(1)} async-done(((bf16[16,65,1024]{2,1,0:T(8,128)(2,1)}), bf16[16,65,1024]{2,1,0:T(8,128)(2,1)S(1)}, u32[]{:S(2)}, u32[]{:S(2)}) %all-to-all-start) | async-done | bytes 2129952 | tf_op jit(solution)/shard_map/all_to_all | solution.py:91
  64.1 0.6 copy-done.2
  64.7 1.2 fusion.42
  65.9 7.8 %collective-permute-start.2 = (bf16[528,1024]{1,0:T(8,128)(2,1)S(1)}, bf16[528,1024]{1,0:T(8,128)(2,1)}, u32[]{:S(2)}, u32[]{:S(2)}) collective-permute-start(bf16[528,1024]{1,0:T(8,128)(2,1)S(1)} %pad_maximum_fusion.2), channel_id=1, source_target_pairs={{0,4},{1,5},{4,8},{5,9},{8,12},{9,13},{12,14},{13,15},{14,10},{15,... | collective-permute-start | bytes 3244040 | tf_op jit(solution)/shard_map/ppermute | solution.py:23
  73.7 2.5 %collective-permute-start = (bf16[528,1024]{1,0:T(8,128)(2,1)S(1)}, bf16[528,1024]{1,0:T(8,128)(2,1)}, u32[]{:S(2)}, u32[]{:S(2)}) collective-permute-start(bf16[528,1024]{1,0:T(8,128)(2,1)S(1)} %pad_maximum_fusion.2), channel_id=1, source_target_pairs={{0,1},{4,5},{8,9},{12,13},{14,15},{10,11},{6,7},{2,3},{16,17},{20,... | collective-permute-start | bytes 3244040 | tf_op jit(solution)/shard_map/ppermute | solution.py:23
  76.3 0.1 slice.196
  76.4 0.1 copy.79
  76.5 0.7 constant_dynamic-slice_fusion
  77.2 0.8 copy.81
  78.0 0.8 copy.80
  78.8 0.8 copy.83
  79.6 0.1 copy.82
  79.7 1.3 collective-permute-start.1
  81.1 0.7 convert_reduce_fusion.4
  81.8 0.1 convert_reduce_fusion.1
  82.0 0.2 slice.195
  82.2 0.4 copy-done.3
  82.6 3.2 %bitcast_reduce_fusion = f32[1024,8]{0,1:T(8,128)S(1)} fusion(bf16[1024,1024]{1,0:T(8,128)(2,1)S(1)} %bitcast.119, s32[1024]{0:T(1024)S(1)} %copy-done.3, pred[1024]{0:T(1024)(128)(4,1)S(1)} %broadcast_compare_fusion.1), kind=kOutput, calls=%fused_computation.2 | convolution fusion | flops 2155864064 | bytes 2135040 | tf_op jit(solution)/shard_map/dot_general | solution.py:30
  85.8 0.1 fusion.27
  85.9 0.7 slice_convert_fusion.4
  86.6 1.6 %bitcast_reduce_fusion.7 = f32[1024,4]{0,1:T(4,128)S(1)} fusion(bf16[1024,1024]{1,0:T(8,128)(2,1)S(1)} %bitcast.120, bf16[512,1024]{1,0:T(8,128)(2,1)S(1)} %collective-permute-done.1, s32[1024]{0:T(1024)S(1)} %copy-done.3, s32[512]{0:T(512)S(1)} %bitcast.155, pred[1024]{0:T(1024)(128)(4,1)S(1)} %broadcast_compare_fusion.1), kind=kOutput, calls=%fused_computation.23 | convolution fusion | flops 1076359168 | bytes 3169280 | tf_op jit(solution)/shard_map/dot_general | solution.py:30
  88.3 0.1 fusion.34
  88.4 2.9 %bitcast_reduce_fusion.8 = f32[1024,4]{0,1:T(4,128)S(1)} fusion(bf16[1024,1024]{1,0:T(8,128)(2,1)S(1)} %bitcast.121, bf16[528,1024]{1,0:T(8,128)(2,1)} %collective-permute-done, s32[1024]{0:T(1024)S(1)} %copy-done.3, s32[512]{0:T(512)S(1)} %bitcast.154, pred[1024]{0:T(1024)(128)(4,1)S(1)} %broadcast_compare_fusion.1), kind=kOutput, calls=%fused_computation.24 | convolution fusion | flops 1076359168 | bytes 3169280 | tf_op jit(solution)/shard_map/dot_general | solution.py:30
  91.2 0.1 fusion.35
  91.3 5.6 %collective-permute-done.2 = bf16[528,1024]{1,0:T(8,128)(2,1)} collective-permute-done((bf16[528,1024]{1,0:T(8,128)(2,1)S(1)}, bf16[528,1024]{1,0:T(8,128)(2,1)}, u32[]{:S(2)}, u32[]{:S(2)}) %collective-permute-start.2) | collective-permute-done | bytes 1081376 | tf_op jit(solution)/shard_map/ppermute | solution.py:23
  96.9 0.2 pad_maximum_fusion.1
  97.1 3.0 %collective-permute-start.3 = (bf16[512,1024]{1,0:T(8,128)(2,1)S(1)}, bf16[512,1024]{1,0:T(8,128)(2,1)S(1)}, u32[]{:S(2)}, u32[]{:S(2)}) collective-permute-start(bf16[512,1024]{1,0:T(8,128)(2,1)S(1)} %bitcast.130), channel_id=1, source_target_pairs={{0,4},{1,5},{4,8},{5,9},{8,12},{9,13},{12,14},{13,15},{14,10},{15,... | collective-permute-start | bytes 3145736 | tf_op jit(solution)/shard_map/ppermute | solution.py:23
  100.2 3.2 %collective-permute-start.6 = (bf16[1040,1024]{1,0:T(8,128)(2,1)S(1)}, bf16[1040,1024]{1,0:T(8,128)(2,1)S(1)}, u32[]{:S(2)}, u32[]{:S(2)}) collective-permute-start(bf16[1040,1024]{1,0:T(8,128)(2,1)S(1)} %pad_maximum_fusion.1), channel_id=1, source_target_pairs={{0,2},{4,0},{8,4},{12,8},{14,12},{10,14},{6,10},{2,6},{1,1},{5,5},... | collective-permute-start | bytes 6389768 | tf_op jit(solution)/shard_map/ppermute | solution.py:23
  103.4 0.7 slice_convert_fusion.3
  104.1 2.9 %bitcast_reduce_fusion.6 = f32[1024,4]{0,1:T(4,128)S(1)} fusion(bf16[1024,1024]{1,0:T(8,128)(2,1)S(1)} %bitcast.123, bf16[528,1024]{1,0:T(8,128)(2,1)} %collective-permute-done.2, s32[1024]{0:T(1024)S(1)} %copy-done.3, s32[512]{0:T(512)S(1)} %bitcast.156, pred[1024]{0:T(1024)(128)(4,1)S(1)} %broadcast_compare_fusion.1), kind=kOutput, calls=%fused_computation.22 | convolution fusion | flops 1076359168 | bytes 3169280 | tf_op jit(solution)/shard_map/dot_general | solution.py:30
  107.0 0.1 fusion.33
  107.1 1.6 %bitcast_reduce_fusion.5 = f32[1024,4]{0,1:T(4,128)S(1)} fusion(bf16[1024,1024]{1,0:T(8,128)(2,1)S(1)} %bitcast.124, s32[1024]{0:T(1024)S(1)} %copy-done.3, s32[512]{0:T(512)S(1)} %bitcast.149, pred[1024]{0:T(1024)(128)(4,1)S(1)} %broadcast_compare_fusion.1, bf16[528,1024]{1,0:T(8,128)(2,1)S(1)} %collective-permute-done.4), kind=kOutput, calls=%fused_computation.21 | convolution fusion | flops 1076359168 | bytes 3169280 | tf_op jit(solution)/shard_map/dot_general | solution.py:30
  108.8 16.3 %collective-permute-done.3 = bf16[512,1024]{1,0:T(8,128)(2,1)S(1)} collective-permute-done((bf16[512,1024]{1,0:T(8,128)(2,1)S(1)}, bf16[512,1024]{1,0:T(8,128)(2,1)S(1)}, u32[]{:S(2)}, u32[]{:S(2)}) %collective-permute-start.3) | collective-permute-done | bytes 1048608 | tf_op jit(solution)/shard_map/ppermute | solution.py:23
  125.1 1.7 %bitcast_reduce_fusion.4 = f32[1024,4]{0,1:T(4,128)S(1)} fusion(bf16[1024,1024]{1,0:T(8,128)(2,1)S(1)} %bitcast.125, bf16[512,1024]{1,0:T(8,128)(2,1)S(1)} %collective-permute-done.3, s32[1024]{0:T(1024)S(1)} %copy-done.3, s32[512]{0:T(512)S(1)} %bitcast.153, pred[1024]{0:T(1024)(128)(4,1)S(1)} %broadcast_compare_fusion.1), kind=kOutput, calls=%fused_computation.20 | convolution fusion | flops 1076359168 | bytes 3169280 | tf_op jit(solution)/shard_map/dot_general | solution.py:30
  126.9 0.9 collective-permute-done.5
  127.8 1.6 %bitcast_reduce_fusion.3 = f32[1024,4]{0,1:T(4,128)S(1)} fusion(bf16[1024,1024]{1,0:T(8,128)(2,1)S(1)} %bitcast.126, bf16[512,1024]{1,0:T(8,128)(2,1)S(1)} %collective-permute-done.5, s32[1024]{0:T(1024)S(1)} %copy-done.3, s32[512]{0:T(512)S(1)} %bitcast.151, pred[1024]{0:T(1024)(128)(4,1)S(1)} %broadcast_compare_fusion.1), kind=kOutput, calls=%fused_computation.19 | convolution fusion | flops 1076359168 | bytes 3169280 | tf_op jit(solution)/shard_map/dot_general | solution.py:30
  129.4 0.1 fusion.30
  129.5 1.6 %bitcast_reduce_fusion.1 = f32[1024,4]{0,1:T(4,128)S(1)} fusion(bf16[512,1024]{1,0:T(8,128)(2,1)S(1)} %collective-permute-done.5, bf16[1040,1024]{1,0:T(8,128)(2,1)S(1)} %collective-permute-done.6, s32[1024]{0:T(1024)S(1)} %bitcast.133, s32[512]{0:T(512)S(1)} %bitcast.152, pred[1024]{0:T(1024)(128)(4,1)S(1)} %broadcast_compare_fusion), kind=kOutput, calls=%fused_computation.17 | convolution fusion | flops 1076359168 | bytes 3169280 | tf_op jit(solution)/shard_map/dot_general | solution.py:30
  131.2 0.1 fusion.28
  131.3 1.6 %bitcast_reduce_fusion.2 = f32[1024,4]{0,1:T(4,128)S(1)} fusion(bf16[1040,1024]{1,0:T(8,128)(2,1)S(1)} %collective-permute-done.6, s32[1024]{0:T(1024)S(1)} %bitcast.134, s32[512]{0:T(512)S(1)} %bitcast.150, pred[1024]{0:T(1024)(128)(4,1)S(1)} %broadcast_compare_fusion, bf16[528,1024]{1,0:T(8,128)(2,1)S(1)} %collective-permute-done.4), kind=kOutput, calls=%fused_computation.18 | convolution fusion | flops 1076359168 | bytes 3169280 | tf_op jit(solution)/shard_map/dot_general | solution.py:30
  132.9 0.1 fusion.29
  133.0 0.1 stack_reshape.4
  133.1 0.1 select_n.157
  133.2 0.7 reshape.375
  133.9 5.1 %all-to-all-start.1 = ((f32[16,1,128]{2,1,0:T(1,128)}), f32[16,1,128]{2,1,0:T(1,128)S(1)}, u32[]{:S(2)}, u32[]{:S(2)}) async-start(f32[16,1,128]{2,1,0:T(1,128)} %reshape.375), calls=%async_computation.1 | async-start | bytes 16384 | tf_op jit(solution)/shard_map/all_to_all | solution.py:159
  139.1 6.4 %all-to-all-done.1 = f32[16,1,128]{2,1,0:T(1,128)S(1)} async-done(((f32[16,1,128]{2,1,0:T(1,128)}), f32[16,1,128]{2,1,0:T(1,128)S(1)}, u32[]{:S(2)}, u32[]{:S(2)}) %all-to-all-start.1) | async-done | bytes 8224 | tf_op jit(solution)/shard_map/all_to_all | solution.py:159
  145.4 0.6 broadcast.271
  146.0 0.7 reduce.40
  146.7 0.1 reshape.376
  146.8 0.3 fusion.21
  147.2 0.6 log1p.3
  (55 shorter events, 0.7 us)
Async XLA Ops:
  0.0 6.5 %copy-start = (bf16[960,1024]{1,0:T(8,128)(2,1)S(1)}, bf16[960,1024]{1,0:T(8,128)(2,1)}, u32[]{:S(2)}) copy-start(bf16[960,1024]{1,0:T(8,128)(2,1)} %param.7) | copy-start | bytes 5898244
  1.3 7.8 %copy-start.6 = (s32[960]{0:T(1024)}, s32[960]{0:T(1024)S(1)}, u32[]{:S(2)}) copy-start(s32[960]{0:T(1024)S(1)} %convert_reduce_fusion) | copy-start | bytes 11524
  10.8 7.5 %copy-start.8 = (s32[16]{0:T(128)S(1)}, s32[16]{0:T(128)}, u32[]{:S(2)}) copy-start(s32[16]{0:T(128)} %constant.73.clone) | copy-start | bytes 196
  10.8 53.2 %all-to-all-start = ((bf16[16,65,1024]{2,1,0:T(8,128)(2,1)}), bf16[16,65,1024]{2,1,0:T(8,128)(2,1)S(1)}, u32[]{:S(2)}, u32[]{:S(2)}) async-start(bf16[16,65,1024]{2,1,0:T(8,128)(2,1)} %pad_maximum_fusion), calls=%async_computation | async-start | bytes 4718592 | tf_op jit(solution)/shard_map/all_to_all | solution.py:91
  64.1 0.6 copy-start.2
  65.9 31.0 %collective-permute-start.2 = (bf16[528,1024]{1,0:T(8,128)(2,1)S(1)}, bf16[528,1024]{1,0:T(8,128)(2,1)}, u32[]{:S(2)}, u32[]{:S(2)}) collective-permute-start(bf16[528,1024]{1,0:T(8,128)(2,1)S(1)} %pad_maximum_fusion.2), channel_id=1, source_target_pairs={{0,4},{1,5},{4,8},{5,9},{8,12},{9,13},{12,14},{13,15},{14,10},{15,... | collective-permute-start | bytes 3244040 | tf_op jit(solution)/shard_map/ppermute | solution.py:23
  73.7 12.2 %collective-permute-start = (bf16[528,1024]{1,0:T(8,128)(2,1)S(1)}, bf16[528,1024]{1,0:T(8,128)(2,1)}, u32[]{:S(2)}, u32[]{:S(2)}) collective-permute-start(bf16[528,1024]{1,0:T(8,128)(2,1)S(1)} %pad_maximum_fusion.2), channel_id=1, source_target_pairs={{0,1},{4,5},{8,9},{12,13},{14,15},{10,11},{6,7},{2,3},{16,17},{20,... | collective-permute-start | bytes 3244040 | tf_op jit(solution)/shard_map/ppermute | solution.py:23
  79.7 6.1 %collective-permute-start.1 = (bf16[512,1024]{1,0:T(8,128)(2,1)}, bf16[512,1024]{1,0:T(8,128)(2,1)S(1)}, u32[]{:S(2)}, u32[]{:S(2)}) collective-permute-start(bf16[512,1024]{1,0:T(8,128)(2,1)} %bitcast.129), channel_id=1, source_target_pairs={{0,1},{4,5},{8,9},{12,13},{14,15},{10,11},{6,7},{2,3},{16,17},{20,... | collective-permute-start | bytes 3145736 | tf_op jit(solution)/shard_map/ppermute | solution.py:23
  81.9 0.7 copy-start.3
  91.3 5.8 %copy-start.1 = (bf16[8,64,1024]{2,1,0:T(8,128)(2,1)S(1)}, bf16[8,64,1024]{2,1,0:T(8,128)(2,1)}, u32[]{:S(2)}) copy-start(bf16[8,64,1024]{2,1,0:T(8,128)(2,1)} %get-tuple-element.39) | copy-start | bytes 3145732
  96.9 10.1 %collective-permute-start.4 = (bf16[528,1024]{1,0:T(8,128)(2,1)}, bf16[528,1024]{1,0:T(8,128)(2,1)S(1)}, u32[]{:S(2)}, u32[]{:S(2)}) collective-permute-start(bf16[528,1024]{1,0:T(8,128)(2,1)} %collective-permute-done.2), channel_id=1, source_target_pairs={{0,1},{1,0},{4,5},{5,4},{8,9},{9,8},{12,13},{13,12},{14,15},{15,14... | collective-permute-start | bytes 3244040 | tf_op jit(solution)/shard_map/ppermute | solution.py:23
  97.1 28.0 %collective-permute-start.3 = (bf16[512,1024]{1,0:T(8,128)(2,1)S(1)}, bf16[512,1024]{1,0:T(8,128)(2,1)S(1)}, u32[]{:S(2)}, u32[]{:S(2)}) collective-permute-start(bf16[512,1024]{1,0:T(8,128)(2,1)S(1)} %bitcast.130), channel_id=1, source_target_pairs={{0,4},{1,5},{4,8},{5,9},{8,12},{9,13},{12,14},{13,15},{14,10},{15,... | collective-permute-start | bytes 3145736 | tf_op jit(solution)/shard_map/ppermute | solution.py:23
  100.2 29.3 %collective-permute-start.6 = (bf16[1040,1024]{1,0:T(8,128)(2,1)S(1)}, bf16[1040,1024]{1,0:T(8,128)(2,1)S(1)}, u32[]{:S(2)}, u32[]{:S(2)}) collective-permute-start(bf16[1040,1024]{1,0:T(8,128)(2,1)S(1)} %pad_maximum_fusion.1), channel_id=1, source_target_pairs={{0,2},{4,0},{8,4},{12,8},{14,12},{10,14},{6,10},{2,6},{1,1},{5,5},... | collective-permute-start | bytes 6389768 | tf_op jit(solution)/shard_map/ppermute | solution.py:23
  125.1 2.7 %collective-permute-start.5 = (bf16[512,1024]{1,0:T(8,128)(2,1)S(1)}, bf16[512,1024]{1,0:T(8,128)(2,1)S(1)}, u32[]{:S(2)}, u32[]{:S(2)}) collective-permute-start(bf16[512,1024]{1,0:T(8,128)(2,1)S(1)} %collective-permute-done.3), channel_id=1, source_target_pairs={{0,1},{1,0},{4,5},{5,4},{8,9},{9,8},{12,13},{13,12},{14,15},{15,14... | collective-permute-start | bytes 3145736 | tf_op jit(solution)/shard_map/ppermute | solution.py:23
  131.2 7.8 %copy-start.4 = (s32[960]{0:T(1024)S(1)}, s32[960]{0:T(1024)}, u32[]{:S(2)}) copy-start(s32[960]{0:T(1024)} %get-tuple-element.38) | copy-start | bytes 11524
  131.2 7.8 %copy-start.5 = (s32[960]{0:T(1024)S(1)}, s32[960]{0:T(1024)}, u32[]{:S(2)}) copy-start(s32[960]{0:T(1024)} %get-tuple-element.53) | copy-start | bytes 11524
  131.2 15.6 %copy-start.7 = (s32[960]{0:T(1024)S(1)}, s32[960]{0:T(1024)}, u32[]{:S(2)}) copy-start(s32[960]{0:T(1024)} %copy-done.6) | copy-start | bytes 11524
  133.9 11.6 %all-to-all-start.1 = ((f32[16,1,128]{2,1,0:T(1,128)}), f32[16,1,128]{2,1,0:T(1,128)S(1)}, u32[]{:S(2)}, u32[]{:S(2)}) async-start(f32[16,1,128]{2,1,0:T(1,128)} %reshape.375), calls=%async_computation.1 | async-start | bytes 16384 | tf_op jit(solution)/shard_map/all_to_all | solution.py:159

commit v18 on v16

--- a/solution.py
+++ b/solution.py
@@ -155,13 +155,20 @@
     last = last_step(swapped_a, 0) + last_step(swapped_b, half)
     total = total + jnp.where(odd, last, 0.0)
     forward_part = jnp.where(odd, 0.0, last)
-    totals = jnp.stack([total.reshape(device_count, capacity), forward_part.reshape(device_count, capacity)], axis=1)
+    totals = jnp.stack([total.reshape(device_count, capacity), forward_part.reshape(device_count, capacity)], axis=1).reshape(device_count, 1, 2 * capacity)
     returned = lax.all_to_all(totals, "blk", split_axis=0, concat_axis=0, tiled=True)
-    behind = jnp.asarray(np.asarray(pos2dev, np.int32))[(owners - 2) % device_count] * capacity + arrival
-    behind = jnp.where(owners % 2 == 0, behind, -1)
+    ring_dev = jnp.asarray(np.asarray(pos2dev, np.int32))
+    dev_index = jnp.arange(device_count, dtype=jnp.int32)
+    own_dev = (ring_dev[owners][:, None] == dev_index).astype(jnp.float32)
+    behind_dev = jnp.where(owners % 2 == 0, ring_dev[(owners - 2) % device_count], -1)
+    behind_dev = (behind_dev[:, None] == dev_index).astype(jnp.float32)
+    flat = returned.reshape(device_count, 1, 2 * capacity)
+    from_owner = jnp.einsum("re,eok->rk", own_dev, flat, precision=lax.Precision.HIGHEST)
+    from_behind = jnp.einsum("re,eok->rk", behind_dev, flat, precision=lax.Precision.HIGHEST)
+    column = jnp.arange(2 * capacity, dtype=jnp.int32)[None, :]
     both = jnp.sum(
-        jnp.where(place[:, None] == slot_index[None, :], returned[:, 0].reshape(-1)[None, :], 0.0)
-        + jnp.where(behind[:, None] == slot_index[None, :], returned[:, 1].reshape(-1)[None, :], 0.0),
+        jnp.where(column == arrival[:, None], from_owner, 0.0)
+        + jnp.where(column == arrival[:, None] + capacity, from_behind, 0.0),
         axis=1,
     )
     return jnp.log1p(both)

time: 149 us -> 148 us (level)
  other arithmetic: 14.5 us -> 12.2 us
  matrix products: 21.4 us -> 23.1 us
    dot_general x0 -> x2, matrix products: none -> 1.76 us  [the longest x1 1.21 us: body(): jnp.einsum('re,eok->rk', behind_dev, flat, precision=lax.Precision.HIGHEST)]
where the time goes in v18:
time: 148 us; the launch traced here: 147 us
  waiting for transfers between devices  64.1 us (43%)
  starting transfers between devices  25.5 us (17%)
  matrix products  23.1 us (16%)
  other arithmetic  12.2 us (8%)
  blocking collectives  11.3 us (8%)
  local copies, waits for them, and re-layouts  7.16 us (5%)
  between operations  3.71 us (3%)
    all_to_all x1, waiting for transfers between devices, body(): lax.all_to_all(payload, 'blk', split_axis=0, concat_axis=0, tiled=True)  41.2 us
    ppermute x7, waiting for transfers between devices, moved(): return lax.ppermute(x, 'blk', [(pos2dev[a], pos2dev[b]) for a, b in moves])  22.9 us
    dot_general x9, matrix products, step_total(): lax.dot_general(local, remote, (((1,), (1,)), ((), ())), preferred_elemen...  18.8 us
    ppermute x7, starting transfers between devices, moved(): return lax.ppermute(x, 'blk', [(pos2dev[a], pos2dev[b]) for a, b in moves])  18 us
    all_to_all x1, blocking collectives, body(): lax.all_to_all(totals, 'blk', split_axis=0, concat_axis=0, tiled=True)  11.3 us
    all_to_all x1, starting transfers between devices, body(): lax.all_to_all(payload, 'blk', split_axis=0, concat_axis=0, tiled=True)  7.52 us
  transfers between devices with their start and end apart: 8, of which 4 were waited for; matrix products, arithmetic and copies ran while one was open for 16% of the time, Pallas kernels for 0%

profile of v18, /device:TPU:0, one launch (start us, length us, event | category | flops | bytes accessed | tf_op | source)
XLA Modules:
  0.0 147.0 jit_solution(3077642067073813217)
XLA Ops:
  0.0 1.3 convert_reduce_fusion
  1.3 0.7 convert.13
  2.0 0.1 copy.76
  2.2 0.1 reshape.382
  2.3 2.0 %fusion.2 = f32[960]{0:T(1024)S(1)} fusion(bf16[960,1024]{1,0:T(8,128)(2,1)} %param.7), kind=kLoop, calls=%fused_computation.7 | loop fusion | flops 2948160 | bytes 1969920 | tf_op jit(solution)/shard_map/reduce_sum | solution.py:69
  4.3 1.3 multiply_add_fusion
  5.6 0.6 select_reduce_fusion
  6.2 0.1 sub.11
  6.3 0.1 pad.20.clone
  6.5 2.6 %fusion.9 = bf16[1024,1024]{1,0:T(8,128)(2,1)S(1)} fusion(bf16[960,1024]{1,0:T(8,128)(2,1)S(1)} %copy-done, f32[960]{0:T(1024)S(1)} %add_rsqrt_fusion, s32[960]{0:T(1024)S(1)} %get-tuple-element.37), kind=kOutput, calls=%fused_computation.35 | convolution fusion | flops 2018246656 | bytes 4070912 | tf_op jit(solution)/shard_map/dot_general | solution.py:77
  9.1 1.7 %pad_maximum_fusion = bf16[16,65,1024]{2,1,0:T(8,128)(2,1)} fusion(bf16[16,1,1024]{2,1,0:T(2,128)(2,1)S(1)} %copy.77, bf16[16,64,1024]{2,1,0:T(8,128)(2,1)S(1)} %bitcast.124), kind=kLoop, calls=%fused_computation.15 | loop fusion | flops 4259840 | bytes 4259840 | tf_op jit(solution)/shard_map/concatenate | solution.py:90
  10.8 7.5 %all-to-all-start = ((bf16[16,65,1024]{2,1,0:T(8,128)(2,1)}), bf16[16,65,1024]{2,1,0:T(8,128)(2,1)S(1)}, u32[]{:S(2)}, u32[]{:S(2)}) async-start(bf16[16,65,1024]{2,1,0:T(8,128)(2,1)} %pad_maximum_fusion), calls=%async_computation | async-start | bytes 4718592 | tf_op jit(solution)/shard_map/all_to_all | solution.py:91
  18.3 0.6 dynamic_slice.9
  22.3 0.5 iota_add_fusion
  22.8 41.2 %all-to-all-done = bf16[16,65,1024]{2,1,0:T(8,128)(2,1)S(1)} async-done(((bf16[16,65,1024]{2,1,0:T(8,128)(2,1)}), bf16[16,65,1024]{2,1,0:T(8,128)(2,1)S(1)}, u32[]{:S(2)}, u32[]{:S(2)}) %all-to-all-start) | async-done | bytes 2129952 | tf_op jit(solution)/shard_map/all_to_all | solution.py:91
  64.1 0.6 copy-done.2
  64.7 1.2 fusion.42
  66.0 7.8 %collective-permute-start.2 = (bf16[528,1024]{1,0:T(8,128)(2,1)S(1)}, bf16[528,1024]{1,0:T(8,128)(2,1)}, u32[]{:S(2)}, u32[]{:S(2)}) collective-permute-start(bf16[528,1024]{1,0:T(8,128)(2,1)S(1)} %pad_maximum_fusion.2), channel_id=1, source_target_pairs={{0,4},{1,5},{4,8},{5,9},{8,12},{9,13},{12,14},{13,15},{14,10},{15,... | collective-permute-start | bytes 3244040 | tf_op jit(solution)/shard_map/ppermute | solution.py:23
  73.8 2.5 %collective-permute-start = (bf16[528,1024]{1,0:T(8,128)(2,1)S(1)}, bf16[528,1024]{1,0:T(8,128)(2,1)}, u32[]{:S(2)}, u32[]{:S(2)}) collective-permute-start(bf16[528,1024]{1,0:T(8,128)(2,1)S(1)} %pad_maximum_fusion.2), channel_id=1, source_target_pairs={{0,1},{4,5},{8,9},{12,13},{14,15},{10,11},{6,7},{2,3},{16,17},{20,... | collective-permute-start | bytes 3244040 | tf_op jit(solution)/shard_map/ppermute | solution.py:23
  76.3 0.1 slice.196
  76.4 0.1 copy.79
  76.5 0.7 constant_dynamic-slice_fusion.1
  77.2 0.8 copy.81
  78.0 0.8 copy.80
  78.8 0.8 copy.83
  79.7 0.1 copy.82
  79.8 1.3 collective-permute-start.1
  81.1 0.7 convert_reduce_fusion.4
  81.8 0.1 convert_reduce_fusion.1
  81.9 0.2 slice.195
  82.1 0.4 copy-done.3
  82.6 3.2 %bitcast_reduce_fusion = f32[1024,8]{0,1:T(8,128)S(1)} fusion(bf16[1024,1024]{1,0:T(8,128)(2,1)S(1)} %bitcast.115, s32[1024]{0:T(1024)S(1)} %copy-done.3, pred[1024]{0:T(1024)(128)(4,1)S(1)} %broadcast_compare_fusion.1), kind=kOutput, calls=%fused_computation.2 | convolution fusion | flops 2155864064 | bytes 2135040 | tf_op jit(solution)/shard_map/dot_general | solution.py:30
  85.8 0.1 fusion.28
  85.9 0.7 slice_convert_fusion.4
  86.6 1.6 %bitcast_reduce_fusion.7 = f32[1024,4]{0,1:T(4,128)S(1)} fusion(bf16[1024,1024]{1,0:T(8,128)(2,1)S(1)} %bitcast.116, bf16[512,1024]{1,0:T(8,128)(2,1)S(1)} %collective-permute-done.1, s32[1024]{0:T(1024)S(1)} %copy-done.3, s32[512]{0:T(512)S(1)} %bitcast.152, pred[1024]{0:T(1024)(128)(4,1)S(1)} %broadcast_compare_fusion.1), kind=kOutput, calls=%fused_computation.23 | convolution fusion | flops 1076359168 | bytes 3169280 | tf_op jit(solution)/shard_map/dot_general | solution.py:30
  88.2 0.1 fusion.35
  88.3 2.9 %bitcast_reduce_fusion.8 = f32[1024,4]{0,1:T(4,128)S(1)} fusion(bf16[1024,1024]{1,0:T(8,128)(2,1)S(1)} %bitcast.117, bf16[528,1024]{1,0:T(8,128)(2,1)} %collective-permute-done, s32[1024]{0:T(1024)S(1)} %copy-done.3, s32[512]{0:T(512)S(1)} %bitcast.151, pred[1024]{0:T(1024)(128)(4,1)S(1)} %broadcast_compare_fusion.1), kind=kOutput, calls=%fused_computation.24 | convolution fusion | flops 1076359168 | bytes 3169280 | tf_op jit(solution)/shard_map/dot_general | solution.py:30
  91.2 0.1 fusion.36
  91.3 5.7 %collective-permute-done.2 = bf16[528,1024]{1,0:T(8,128)(2,1)} collective-permute-done((bf16[528,1024]{1,0:T(8,128)(2,1)S(1)}, bf16[528,1024]{1,0:T(8,128)(2,1)}, u32[]{:S(2)}, u32[]{:S(2)}) %collective-permute-start.2) | collective-permute-done | bytes 1081376 | tf_op jit(solution)/shard_map/ppermute | solution.py:23
  96.9 0.2 pad_maximum_fusion.1
  97.1 3.0 %collective-permute-start.3 = (bf16[512,1024]{1,0:T(8,128)(2,1)S(1)}, bf16[512,1024]{1,0:T(8,128)(2,1)S(1)}, u32[]{:S(2)}, u32[]{:S(2)}) collective-permute-start(bf16[512,1024]{1,0:T(8,128)(2,1)S(1)} %bitcast.126), channel_id=1, source_target_pairs={{0,4},{1,5},{4,8},{5,9},{8,12},{9,13},{12,14},{13,15},{14,10},{15,... | collective-permute-start | bytes 3145736 | tf_op jit(solution)/shard_map/ppermute | solution.py:23
  100.2 3.2 %collective-permute-start.6 = (bf16[1040,1024]{1,0:T(8,128)(2,1)S(1)}, bf16[1040,1024]{1,0:T(8,128)(2,1)S(1)}, u32[]{:S(2)}, u32[]{:S(2)}) collective-permute-start(bf16[1040,1024]{1,0:T(8,128)(2,1)S(1)} %pad_maximum_fusion.1), channel_id=1, source_target_pairs={{0,2},{4,0},{8,4},{12,8},{14,12},{10,14},{6,10},{2,6},{1,1},{5,5},... | collective-permute-start | bytes 6389768 | tf_op jit(solution)/shard_map/ppermute | solution.py:23
  103.4 0.7 slice_convert_fusion.3
  104.1 2.9 %bitcast_reduce_fusion.6 = f32[1024,4]{0,1:T(4,128)S(1)} fusion(bf16[1024,1024]{1,0:T(8,128)(2,1)S(1)} %bitcast.119, bf16[528,1024]{1,0:T(8,128)(2,1)} %collective-permute-done.2, s32[1024]{0:T(1024)S(1)} %copy-done.3, s32[512]{0:T(512)S(1)} %bitcast.153, pred[1024]{0:T(1024)(128)(4,1)S(1)} %broadcast_compare_fusion.1), kind=kOutput, calls=%fused_computation.22 | convolution fusion | flops 1076359168 | bytes 3169280 | tf_op jit(solution)/shard_map/dot_general | solution.py:30
  107.0 0.1 fusion.34
  107.1 1.6 %bitcast_reduce_fusion.5 = f32[1024,4]{0,1:T(4,128)S(1)} fusion(bf16[1024,1024]{1,0:T(8,128)(2,1)S(1)} %bitcast.120, s32[1024]{0:T(1024)S(1)} %copy-done.3, s32[512]{0:T(512)S(1)} %bitcast.146, pred[1024]{0:T(1024)(128)(4,1)S(1)} %broadcast_compare_fusion.1, bf16[528,1024]{1,0:T(8,128)(2,1)S(1)} %collective-permute-done.4), kind=kOutput, calls=%fused_computation.21 | convolution fusion | flops 1076359168 | bytes 3169280 | tf_op jit(solution)/shard_map/dot_general | solution.py:30
  108.8 0.1 fusion.33
  108.8 16.3 %collective-permute-done.3 = bf16[512,1024]{1,0:T(8,128)(2,1)S(1)} collective-permute-done((bf16[512,1024]{1,0:T(8,128)(2,1)S(1)}, bf16[512,1024]{1,0:T(8,128)(2,1)S(1)}, u32[]{:S(2)}, u32[]{:S(2)}) %collective-permute-start.3) | collective-permute-done | bytes 1048608 | tf_op jit(solution)/shard_map/ppermute | solution.py:23
  125.1 1.7 %bitcast_reduce_fusion.4 = f32[1024,4]{0,1:T(4,128)S(1)} fusion(bf16[1024,1024]{1,0:T(8,128)(2,1)S(1)} %bitcast.121, bf16[512,1024]{1,0:T(8,128)(2,1)S(1)} %collective-permute-done.3, s32[1024]{0:T(1024)S(1)} %copy-done.3, s32[512]{0:T(512)S(1)} %bitcast.150, pred[1024]{0:T(1024)(128)(4,1)S(1)} %broadcast_compare_fusion.1), kind=kOutput, calls=%fused_computation.20 | convolution fusion | flops 1076359168 | bytes 3169280 | tf_op jit(solution)/shard_map/dot_general | solution.py:30
  126.8 0.1 fusion.32
  126.9 0.9 collective-permute-done.5
  127.8 1.6 %bitcast_reduce_fusion.3 = f32[1024,4]{0,1:T(4,128)S(1)} fusion(bf16[1024,1024]{1,0:T(8,128)(2,1)S(1)} %bitcast.122, bf16[512,1024]{1,0:T(8,128)(2,1)S(1)} %collective-permute-done.5, s32[1024]{0:T(1024)S(1)} %copy-done.3, s32[512]{0:T(512)S(1)} %bitcast.148, pred[1024]{0:T(1024)(128)(4,1)S(1)} %broadcast_compare_fusion.1), kind=kOutput, calls=%fused_computation.19 | convolution fusion | flops 1076359168 | bytes 3169280 | tf_op jit(solution)/shard_map/dot_general | solution.py:30
  129.4 0.1 fusion.31
  129.5 1.6 %bitcast_reduce_fusion.1 = f32[1024,4]{0,1:T(4,128)S(1)} fusion(bf16[512,1024]{1,0:T(8,128)(2,1)S(1)} %collective-permute-done.5, bf16[1040,1024]{1,0:T(8,128)(2,1)S(1)} %collective-permute-done.6, s32[1024]{0:T(1024)S(1)} %bitcast.132, s32[512]{0:T(512)S(1)} %bitcast.149, pred[1024]{0:T(1024)(128)(4,1)S(1)} %broadcast_compare_fusion), kind=kOutput, calls=%fused_computation.17 | convolution fusion | flops 1076359168 | bytes 3169280 | tf_op jit(solution)/shard_map/dot_general | solution.py:30
  131.2 0.1 fusion.29
  131.3 1.6 %bitcast_reduce_fusion.2 = f32[1024,4]{0,1:T(4,128)S(1)} fusion(bf16[1040,1024]{1,0:T(8,128)(2,1)S(1)} %collective-permute-done.6, s32[1024]{0:T(1024)S(1)} %bitcast.133, s32[512]{0:T(512)S(1)} %bitcast.147, pred[1024]{0:T(1024)(128)(4,1)S(1)} %broadcast_compare_fusion, bf16[528,1024]{1,0:T(8,128)(2,1)S(1)} %collective-permute-done.4), kind=kOutput, calls=%fused_computation.18 | convolution fusion | flops 1076359168 | bytes 3169280 | tf_op jit(solution)/shard_map/dot_general | solution.py:30
  132.9 0.1 fusion.30
  133.0 0.1 stack_reshape.4
  133.1 0.1 select_n.156
  133.2 0.1 reshape.323
  133.3 11.3 %all_to_all.10 = f32[16,1,128]{2,1,0:T(1,128)S(1)} all-to-all(f32[16,1,128]{2,1,0:T(1,128)S(1)} %bitcast.130), channel_id=1, replica_groups=mesh['groups'=2,'blk'=16] {'blk'}, dimensions={0} | all-to-all | bytes 16384 | tf_op jit(solution)/shard_map/all_to_all | solution.py:159
  144.6 1.2 convolution_select_fusion
  145.9 0.6 fusion.21
  146.4 0.6 log1p.3
  (53 shorter events, 0.5 us)
Async XLA Ops:
  0.0 6.5 %copy-start = (bf16[960,1024]{1,0:T(8,128)(2,1)S(1)}, bf16[960,1024]{1,0:T(8,128)(2,1)}, u32[]{:S(2)}) copy-start(bf16[960,1024]{1,0:T(8,128)(2,1)} %param.7) | copy-start | bytes 5898244
  1.3 7.8 %copy-start.6 = (s32[960]{0:T(1024)}, s32[960]{0:T(1024)S(1)}, u32[]{:S(2)}) copy-start(s32[960]{0:T(1024)S(1)} %convert_reduce_fusion) | copy-start | bytes 11524
  10.8 7.5 %copy-start.9 = (s32[16]{0:T(128)S(1)}, s32[16]{0:T(128)}, u32[]{:S(2)}) copy-start(s32[16]{0:T(128)} %constant.74.clone) | copy-start | bytes 196
  10.8 53.2 %all-to-all-start = ((bf16[16,65,1024]{2,1,0:T(8,128)(2,1)}), bf16[16,65,1024]{2,1,0:T(8,128)(2,1)S(1)}, u32[]{:S(2)}, u32[]{:S(2)}) async-start(bf16[16,65,1024]{2,1,0:T(8,128)(2,1)} %pad_maximum_fusion), calls=%async_computation | async-start | bytes 4718592 | tf_op jit(solution)/shard_map/all_to_all | solution.py:91
  64.1 0.6 copy-start.2
  66.0 31.0 %collective-permute-start.2 = (bf16[528,1024]{1,0:T(8,128)(2,1)S(1)}, bf16[528,1024]{1,0:T(8,128)(2,1)}, u32[]{:S(2)}, u32[]{:S(2)}) collective-permute-start(bf16[528,1024]{1,0:T(8,128)(2,1)S(1)} %pad_maximum_fusion.2), channel_id=1, source_target_pairs={{0,4},{1,5},{4,8},{5,9},{8,12},{9,13},{12,14},{13,15},{14,10},{15,... | collective-permute-start | bytes 3244040 | tf_op jit(solution)/shard_map/ppermute | solution.py:23
  73.8 12.1 %collective-permute-start = (bf16[528,1024]{1,0:T(8,128)(2,1)S(1)}, bf16[528,1024]{1,0:T(8,128)(2,1)}, u32[]{:S(2)}, u32[]{:S(2)}) collective-permute-start(bf16[528,1024]{1,0:T(8,128)(2,1)S(1)} %pad_maximum_fusion.2), channel_id=1, source_target_pairs={{0,1},{4,5},{8,9},{12,13},{14,15},{10,11},{6,7},{2,3},{16,17},{20,... | collective-permute-start | bytes 3244040 | tf_op jit(solution)/shard_map/ppermute | solution.py:23
  79.8 6.1 %collective-permute-start.1 = (bf16[512,1024]{1,0:T(8,128)(2,1)}, bf16[512,1024]{1,0:T(8,128)(2,1)S(1)}, u32[]{:S(2)}, u32[]{:S(2)}) collective-permute-start(bf16[512,1024]{1,0:T(8,128)(2,1)} %bitcast.125), channel_id=1, source_target_pairs={{0,1},{4,5},{8,9},{12,13},{14,15},{10,11},{6,7},{2,3},{16,17},{20,... | collective-permute-start | bytes 3145736 | tf_op jit(solution)/shard_map/ppermute | solution.py:23
  81.9 0.7 copy-start.3
  91.3 5.9 %copy-start.1 = (bf16[8,64,1024]{2,1,0:T(8,128)(2,1)S(1)}, bf16[8,64,1024]{2,1,0:T(8,128)(2,1)}, u32[]{:S(2)}) copy-start(bf16[8,64,1024]{2,1,0:T(8,128)(2,1)} %get-tuple-element.39) | copy-start | bytes 3145732
  96.9 10.1 %collective-permute-start.4 = (bf16[528,1024]{1,0:T(8,128)(2,1)}, bf16[528,1024]{1,0:T(8,128)(2,1)S(1)}, u32[]{:S(2)}, u32[]{:S(2)}) collective-permute-start(bf16[528,1024]{1,0:T(8,128)(2,1)} %collective-permute-done.2), channel_id=1, source_target_pairs={{0,1},{1,0},{4,5},{5,4},{8,9},{9,8},{12,13},{13,12},{14,15},{15,14... | collective-permute-start | bytes 3244040 | tf_op jit(solution)/shard_map/ppermute | solution.py:23
  97.1 28.0 %collective-permute-start.3 = (bf16[512,1024]{1,0:T(8,128)(2,1)S(1)}, bf16[512,1024]{1,0:T(8,128)(2,1)S(1)}, u32[]{:S(2)}, u32[]{:S(2)}) collective-permute-start(bf16[512,1024]{1,0:T(8,128)(2,1)S(1)} %bitcast.126), channel_id=1, source_target_pairs={{0,4},{1,5},{4,8},{5,9},{8,12},{9,13},{12,14},{13,15},{14,10},{15,... | collective-permute-start | bytes 3145736 | tf_op jit(solution)/shard_map/ppermute | solution.py:23
  100.2 29.3 %collective-permute-start.6 = (bf16[1040,1024]{1,0:T(8,128)(2,1)S(1)}, bf16[1040,1024]{1,0:T(8,128)(2,1)S(1)}, u32[]{:S(2)}, u32[]{:S(2)}) collective-permute-start(bf16[1040,1024]{1,0:T(8,128)(2,1)S(1)} %pad_maximum_fusion.1), channel_id=1, source_target_pairs={{0,2},{4,0},{8,4},{12,8},{14,12},{10,14},{6,10},{2,6},{1,1},{5,5},... | collective-permute-start | bytes 6389768 | tf_op jit(solution)/shard_map/ppermute | solution.py:23
  125.1 2.7 %collective-permute-start.5 = (bf16[512,1024]{1,0:T(8,128)(2,1)S(1)}, bf16[512,1024]{1,0:T(8,128)(2,1)S(1)}, u32[]{:S(2)}, u32[]{:S(2)}) collective-permute-start(bf16[512,1024]{1,0:T(8,128)(2,1)S(1)} %collective-permute-done.3), channel_id=1, source_target_pairs={{0,1},{1,0},{4,5},{5,4},{8,9},{9,8},{12,13},{13,12},{14,15},{15,14... | collective-permute-start | bytes 3145736 | tf_op jit(solution)/shard_map/ppermute | solution.py:23
  131.3 13.4 %copy-start.4 = (s32[960]{0:T(1024)S(1)}, s32[960]{0:T(1024)}, u32[]{:S(2)}) copy-start(s32[960]{0:T(1024)} %get-tuple-element.47) | copy-start | bytes 11524
  131.3 13.4 %copy-start.5 = (s32[960]{0:T(1024)S(1)}, s32[960]{0:T(1024)}, u32[]{:S(2)}) copy-start(s32[960]{0:T(1024)} %get-tuple-element.48) | copy-start | bytes 11524
  131.3 14.6 %copy-start.7 = (s32[960]{0:T(1024)S(1)}, s32[960]{0:T(1024)}, u32[]{:S(2)}) copy-start(s32[960]{0:T(1024)} %copy-done.6) | copy-start | bytes 11524
  131.3 14.6 %copy-start.8 = (s32[960]{0:T(1024)S(1)}, s32[960]{0:T(1024)}, u32[]{:S(2)}) copy-start(s32[960]{0:T(1024)} %get-tuple-element.38) | copy-start | bytes 11524

commit v19 on v18

--- a/solution.py
+++ b/solution.py
@@ -69,8 +69,10 @@
         * lax.rsqrt(jnp.mean(value_entries * value_entries, axis=1, keepdims=True) + 1e-06)
     ).astype(jnp.bfloat16)
     row_index = jnp.arange(row_count, dtype=jnp.int32)
-    earlier = (owners[None, :] == owners[:, None]) & (row_index[None, :] < row_index[:, None])
-    arrival = jnp.sum(earlier.astype(jnp.int32), axis=1)
+    owner_hot = (owners[:, None] == jnp.arange(device_count, dtype=jnp.int32)).astype(jnp.bfloat16)
+    before = (row_index[None, :] < row_index[:, None]).astype(jnp.bfloat16)
+    prior = jnp.dot(before, owner_hot, preferred_element_type=jnp.float32)
+    arrival = jnp.sum(prior * owner_hot.astype(jnp.float32), axis=1).astype(jnp.int32)
     place = jnp.asarray(np.asarray(pos2dev, np.int32))[owners] * capacity + arrival
     slot_index = jnp.arange(slot_count, dtype=jnp.int32)
     hit = place[None, :] == slot_index[:, None]

time: 148 us -> 148 us (level)
  blocking collectives: 11.3 us -> 0 us
  waiting for transfers between devices: 64.1 us -> 70.5 us
  starting transfers between devices: 25.5 us -> 30.6 us
  other arithmetic: 12.2 us -> 10.1 us
    all_to_all x1 -> x0, blocking collectives: 11.3 us -> none  [body(): lax.all_to_all(totals, 'blk', split_axis=0, concat_axis=0, tiled=True)]
    all_to_all x0 -> x1, waiting for transfers between devices: none -> 6.39 us  [body(): lax.all_to_all(totals, 'blk', split_axis=0, concat_axis=0, tiled=True)]
    all_to_all x0 -> x1, starting transfers between devices: none -> 5.14 us  [body(): lax.all_to_all(totals, 'blk', split_axis=0, concat_axis=0, tiled=True)]
  transfers between devices with their start and end apart: 8 -> 9, of which waited for: 4 -> 5; matrix products, arithmetic and copies ran while one was open for 16% -> 16% of each run, Pallas kernels for 0% -> 0%
where the time goes in v19:
time: 148 us; the launch traced here: 147 us
  waiting for transfers between devices  70.5 us (48%)
  starting transfers between devices  30.6 us (21%)
  matrix products  24.4 us (16%)
  other arithmetic  10.1 us (7%)
  local copies, waits for them, and re-layouts  7.76 us (5%)
  between operations  3.74 us (3%)
    all_to_all x1, waiting for transfers between devices, body(): lax.all_to_all(payload, 'blk', split_axis=0, concat_axis=0, tiled=True)  41.2 us
    ppermute x7, waiting for transfers between devices, moved(): return lax.ppermute(x, 'blk', [(pos2dev[a], pos2dev[b]) for a, b in moves])  22.9 us
    dot_general x9, matrix products, step_total(): lax.dot_general(local, remote, (((1,), (1,)), ((), ())), preferred_elemen...  18.8 us
    ppermute x7, starting transfers between devices, moved(): return lax.ppermute(x, 'blk', [(pos2dev[a], pos2dev[b]) for a, b in moves])  18 us
    all_to_all x1, starting transfers between devices, body(): lax.all_to_all(payload, 'blk', split_axis=0, concat_axis=0, tiled=True)  7.52 us
    all_to_all x1, waiting for transfers between devices, body(): lax.all_to_all(totals, 'blk', split_axis=0, concat_axis=0, tiled=True)  6.39 us
    all_to_all x1, starting transfers between devices, body(): lax.all_to_all(totals, 'blk', split_axis=0, concat_axis=0, tiled=True)  5.14 us
  transfers between devices with their start and end apart: 9, of which 5 were waited for; matrix products, arithmetic and copies ran while one was open for 16% of the time, Pallas kernels for 0%

profile of v19, /device:TPU:0, one launch (start us, length us, event | category | flops | bytes accessed | tf_op | source)
XLA Modules:
  0.0 147.2 jit_solution(13532607715632069906)
XLA Ops:
  0.0 1.3 fusion.23
  1.3 0.7 convert.13
  2.0 0.1 copy.76
  2.2 0.1 reshape.384
  2.3 2.0 %fusion.2 = f32[960]{0:T(1024)S(1)} fusion(bf16[960,1024]{1,0:T(8,128)(2,1)} %param.7), kind=kLoop, calls=%fused_computation.7 | loop fusion | flops 2948160 | bytes 1969920 | tf_op jit(solution)/shard_map/reduce_sum | solution.py:69
  4.3 0.6 multiply_add_fusion
  4.9 0.6 select_reduce_fusion
  5.6 0.1 sub.11
  5.8 2.6 %fusion.9 = bf16[1024,1024]{1,0:T(8,128)(2,1)S(1)} fusion(bf16[960,1024]{1,0:T(8,128)(2,1)S(1)} %copy-done, f32[960]{0:T(1024)S(1)} %add_rsqrt_fusion, s32[960]{0:T(1024)S(1)} %get-tuple-element.37), kind=kOutput, calls=%fused_computation.34 | convolution fusion | flops 2018246656 | bytes 4070912 | tf_op jit(solution)/shard_map/dot_general | solution.py:79
  8.4 1.7 %pad_maximum_fusion = bf16[16,65,1024]{2,1,0:T(8,128)(2,1)} fusion(bf16[16,1,1024]{2,1,0:T(2,128)(2,1)S(1)} %copy.77, bf16[16,64,1024]{2,1,0:T(8,128)(2,1)S(1)} %bitcast.124), kind=kLoop, calls=%fused_computation.14 | loop fusion | flops 4259840 | bytes 4259840 | tf_op jit(solution)/shard_map/concatenate | solution.py:92
  10.1 7.5 %all-to-all-start = ((bf16[16,65,1024]{2,1,0:T(8,128)(2,1)}), bf16[16,65,1024]{2,1,0:T(8,128)(2,1)S(1)}, u32[]{:S(2)}, u32[]{:S(2)}) async-start(bf16[16,65,1024]{2,1,0:T(8,128)(2,1)} %pad_maximum_fusion), calls=%async_computation | async-start | bytes 4718592 | tf_op jit(solution)/shard_map/all_to_all | solution.py:93
  17.6 0.6 dynamic_slice.9
  21.6 0.5 iota_add_fusion
  22.1 41.2 %all-to-all-done = bf16[16,65,1024]{2,1,0:T(8,128)(2,1)S(1)} async-done(((bf16[16,65,1024]{2,1,0:T(8,128)(2,1)}), bf16[16,65,1024]{2,1,0:T(8,128)(2,1)S(1)}, u32[]{:S(2)}, u32[]{:S(2)}) %all-to-all-start) | async-done | bytes 2129952 | tf_op jit(solution)/shard_map/all_to_all | solution.py:93
  63.4 0.6 copy-done.2
  64.0 1.2 fusion.46
  65.3 7.8 %collective-permute-start.2 = (bf16[528,1024]{1,0:T(8,128)(2,1)S(1)}, bf16[528,1024]{1,0:T(8,128)(2,1)}, u32[]{:S(2)}, u32[]{:S(2)}) collective-permute-start(bf16[528,1024]{1,0:T(8,128)(2,1)S(1)} %pad_maximum_fusion.2), channel_id=1, source_target_pairs={{0,4},{1,5},{4,8},{5,9},{8,12},{9,13},{12,14},{13,15},{14,10},{15,... | collective-permute-start | bytes 3244040 | tf_op jit(solution)/shard_map/ppermute | solution.py:23
  73.1 2.5 %collective-permute-start = (bf16[528,1024]{1,0:T(8,128)(2,1)S(1)}, bf16[528,1024]{1,0:T(8,128)(2,1)}, u32[]{:S(2)}, u32[]{:S(2)}) collective-permute-start(bf16[528,1024]{1,0:T(8,128)(2,1)S(1)} %pad_maximum_fusion.2), channel_id=1, source_target_pairs={{0,1},{4,5},{8,9},{12,13},{14,15},{10,11},{6,7},{2,3},{16,17},{20,... | collective-permute-start | bytes 3244040 | tf_op jit(solution)/shard_map/ppermute | solution.py:23
  75.6 0.1 slice.196
  75.7 0.1 copy.79
  75.8 0.7 constant_dynamic-slice_fusion.1
  76.5 0.8 copy.81
  77.4 0.8 copy.80
  78.2 0.8 copy.83
  79.0 0.1 copy.82
  79.1 1.3 collective-permute-start.1
  80.4 0.7 convert_reduce_fusion.3
  81.1 0.1 convert_reduce_fusion
  81.2 0.2 slice.195
  81.5 0.4 copy-done.3
  81.9 3.2 %bitcast_reduce_fusion = f32[1024,8]{0,1:T(8,128)S(1)} fusion(bf16[1024,1024]{1,0:T(8,128)(2,1)S(1)} %bitcast.115, s32[1024]{0:T(1024)S(1)} %copy-done.3, pred[1024]{0:T(1024)(128)(4,1)S(1)} %broadcast_compare_fusion.1), kind=kOutput, calls=%fused_computation.2 | convolution fusion | flops 2155864064 | bytes 2135040 | tf_op jit(solution)/shard_map/dot_general | solution.py:30
  85.1 0.1 fusion.31
  85.2 0.7 slice_convert_fusion.4
  85.9 1.6 %bitcast_reduce_fusion.7 = f32[1024,4]{0,1:T(4,128)S(1)} fusion(bf16[1024,1024]{1,0:T(8,128)(2,1)S(1)} %bitcast.116, bf16[512,1024]{1,0:T(8,128)(2,1)S(1)} %collective-permute-done.1, s32[1024]{0:T(1024)S(1)} %copy-done.3, s32[512]{0:T(512)S(1)} %bitcast.151, pred[1024]{0:T(1024)(128)(4,1)S(1)} %broadcast_compare_fusion.1), kind=kOutput, calls=%fused_computation.22 | convolution fusion | flops 1076359168 | bytes 3169280 | tf_op jit(solution)/shard_map/dot_general | solution.py:30
  87.5 0.1 fusion.39
  87.6 2.9 %bitcast_reduce_fusion.8 = f32[1024,4]{0,1:T(4,128)S(1)} fusion(bf16[1024,1024]{1,0:T(8,128)(2,1)S(1)} %bitcast.117, bf16[528,1024]{1,0:T(8,128)(2,1)} %collective-permute-done, s32[1024]{0:T(1024)S(1)} %copy-done.3, s32[512]{0:T(512)S(1)} %bitcast.150, pred[1024]{0:T(1024)(128)(4,1)S(1)} %broadcast_compare_fusion.1), kind=kOutput, calls=%fused_computation.23 | convolution fusion | flops 1076359168 | bytes 3169280 | tf_op jit(solution)/shard_map/dot_general | solution.py:30
  90.5 0.1 fusion.40
  90.6 5.7 %collective-permute-done.2 = bf16[528,1024]{1,0:T(8,128)(2,1)} collective-permute-done((bf16[528,1024]{1,0:T(8,128)(2,1)S(1)}, bf16[528,1024]{1,0:T(8,128)(2,1)}, u32[]{:S(2)}, u32[]{:S(2)}) %collective-permute-start.2) | collective-permute-done | bytes 1081376 | tf_op jit(solution)/shard_map/ppermute | solution.py:23
  96.3 0.2 pad_maximum_fusion.1
  96.5 3.0 %collective-permute-start.3 = (bf16[512,1024]{1,0:T(8,128)(2,1)S(1)}, bf16[512,1024]{1,0:T(8,128)(2,1)S(1)}, u32[]{:S(2)}, u32[]{:S(2)}) collective-permute-start(bf16[512,1024]{1,0:T(8,128)(2,1)S(1)} %bitcast.126), channel_id=1, source_target_pairs={{0,4},{1,5},{4,8},{5,9},{8,12},{9,13},{12,14},{13,15},{14,10},{15,... | collective-permute-start | bytes 3145736 | tf_op jit(solution)/shard_map/ppermute | solution.py:23
  99.5 3.2 %collective-permute-start.6 = (bf16[1040,1024]{1,0:T(8,128)(2,1)S(1)}, bf16[1040,1024]{1,0:T(8,128)(2,1)S(1)}, u32[]{:S(2)}, u32[]{:S(2)}) collective-permute-start(bf16[1040,1024]{1,0:T(8,128)(2,1)S(1)} %pad_maximum_fusion.1), channel_id=1, source_target_pairs={{0,2},{4,0},{8,4},{12,8},{14,12},{10,14},{6,10},{2,6},{1,1},{5,5},... | collective-permute-start | bytes 6389768 | tf_op jit(solution)/shard_map/ppermute | solution.py:23
  102.7 0.7 slice_convert_fusion.3
  103.5 2.9 %bitcast_reduce_fusion.6 = f32[1024,4]{0,1:T(4,128)S(1)} fusion(bf16[1024,1024]{1,0:T(8,128)(2,1)S(1)} %bitcast.119, bf16[528,1024]{1,0:T(8,128)(2,1)} %collective-permute-done.2, s32[1024]{0:T(1024)S(1)} %copy-done.3, s32[512]{0:T(512)S(1)} %bitcast.152, pred[1024]{0:T(1024)(128)(4,1)S(1)} %broadcast_compare_fusion.1), kind=kOutput, calls=%fused_computation.21 | convolution fusion | flops 1076359168 | bytes 3169280 | tf_op jit(solution)/shard_map/dot_general | solution.py:30
  106.3 0.1 fusion.38
  106.4 1.6 %bitcast_reduce_fusion.5 = f32[1024,4]{0,1:T(4,128)S(1)} fusion(bf16[1024,1024]{1,0:T(8,128)(2,1)S(1)} %bitcast.120, s32[1024]{0:T(1024)S(1)} %copy-done.3, s32[512]{0:T(512)S(1)} %bitcast.145, pred[1024]{0:T(1024)(128)(4,1)S(1)} %broadcast_compare_fusion.1, bf16[528,1024]{1,0:T(8,128)(2,1)S(1)} %collective-permute-done.4), kind=kOutput, calls=%fused_computation.20 | convolution fusion | flops 1076359168 | bytes 3169280 | tf_op jit(solution)/shard_map/dot_general | solution.py:30
  108.1 0.1 fusion.37
  108.2 16.3 %collective-permute-done.3 = bf16[512,1024]{1,0:T(8,128)(2,1)S(1)} collective-permute-done((bf16[512,1024]{1,0:T(8,128)(2,1)S(1)}, bf16[512,1024]{1,0:T(8,128)(2,1)S(1)}, u32[]{:S(2)}, u32[]{:S(2)}) %collective-permute-start.3) | collective-permute-done | bytes 1048608 | tf_op jit(solution)/shard_map/ppermute | solution.py:23
  124.5 1.7 %bitcast_reduce_fusion.4 = f32[1024,4]{0,1:T(4,128)S(1)} fusion(bf16[1024,1024]{1,0:T(8,128)(2,1)S(1)} %bitcast.121, bf16[512,1024]{1,0:T(8,128)(2,1)S(1)} %collective-permute-done.3, s32[1024]{0:T(1024)S(1)} %copy-done.3, s32[512]{0:T(512)S(1)} %bitcast.149, pred[1024]{0:T(1024)(128)(4,1)S(1)} %broadcast_compare_fusion.1), kind=kOutput, calls=%fused_computation.19 | convolution fusion | flops 1076359168 | bytes 3169280 | tf_op jit(solution)/shard_map/dot_general | solution.py:30
  126.1 0.1 fusion.36
  126.2 0.9 collective-permute-done.5
  127.1 1.6 %bitcast_reduce_fusion.3 = f32[1024,4]{0,1:T(4,128)S(1)} fusion(bf16[1024,1024]{1,0:T(8,128)(2,1)S(1)} %bitcast.122, bf16[512,1024]{1,0:T(8,128)(2,1)S(1)} %collective-permute-done.5, s32[1024]{0:T(1024)S(1)} %copy-done.3, s32[512]{0:T(512)S(1)} %bitcast.147, pred[1024]{0:T(1024)(128)(4,1)S(1)} %broadcast_compare_fusion.1), kind=kOutput, calls=%fused_computation.18 | convolution fusion | flops 1076359168 | bytes 3169280 | tf_op jit(solution)/shard_map/dot_general | solution.py:30
  128.8 0.1 fusion.35
  128.9 1.6 %bitcast_reduce_fusion.1 = f32[1024,4]{0,1:T(4,128)S(1)} fusion(bf16[512,1024]{1,0:T(8,128)(2,1)S(1)} %collective-permute-done.5, bf16[1040,1024]{1,0:T(8,128)(2,1)S(1)} %collective-permute-done.6, s32[1024]{0:T(1024)S(1)} %bitcast.131, s32[512]{0:T(512)S(1)} %bitcast.148, pred[1024]{0:T(1024)(128)(4,1)S(1)} %broadcast_compare_fusion), kind=kOutput, calls=%fused_computation.16 | convolution fusion | flops 1076359168 | bytes 3169280 | tf_op jit(solution)/shard_map/dot_general | solution.py:30
  130.5 0.1 fusion.33
  130.6 1.6 %bitcast_reduce_fusion.2 = f32[1024,4]{0,1:T(4,128)S(1)} fusion(bf16[1040,1024]{1,0:T(8,128)(2,1)S(1)} %collective-permute-done.6, s32[1024]{0:T(1024)S(1)} %bitcast.132, s32[512]{0:T(512)S(1)} %bitcast.146, pred[1024]{0:T(1024)(128)(4,1)S(1)} %broadcast_compare_fusion, bf16[528,1024]{1,0:T(8,128)(2,1)S(1)} %collective-permute-done.4), kind=kOutput, calls=%fused_computation.17 | convolution fusion | flops 1076359168 | bytes 3169280 | tf_op jit(solution)/shard_map/dot_general | solution.py:30
  132.3 0.1 fusion.34
  132.3 0.1 stack_reshape.4
  132.4 0.1 select_n.156
  132.5 0.7 reshape.325
  133.2 5.1 %all-to-all-start.1 = ((f32[16,1,128]{2,1,0:T(1,128)}), f32[16,1,128]{2,1,0:T(1,128)S(1)}, u32[]{:S(2)}, u32[]{:S(2)}) async-start(f32[16,1,128]{2,1,0:T(1,128)} %bitcast.28), calls=%async_computation.1 | async-start | bytes 16384 | tf_op jit(solution)/shard_map/all_to_all | solution.py:161
  138.4 6.4 %all-to-all-done.1 = f32[16,1,128]{2,1,0:T(1,128)S(1)} async-done(((f32[16,1,128]{2,1,0:T(1,128)}), f32[16,1,128]{2,1,0:T(1,128)S(1)}, u32[]{:S(2)}, u32[]{:S(2)}) %all-to-all-start.1) | async-done | bytes 8224 | tf_op jit(solution)/shard_map/all_to_all | solution.py:161
  144.8 1.2 convolution_select_fusion
  146.0 0.6 fusion.21
  146.5 0.6 log1p.3
  (59 shorter events, 0.5 us)
Async XLA Ops:
  0.0 4.3 %copy-start.8 = (s32[960]{0:T(1024)S(1)}, s32[960]{0:T(1024)}, u32[]{:S(2)}) copy-start(s32[960]{0:T(1024)} %param.8) | copy-start | bytes 11524
  0.0 5.8 %copy-start = (bf16[960,1024]{1,0:T(8,128)(2,1)S(1)}, bf16[960,1024]{1,0:T(8,128)(2,1)}, u32[]{:S(2)}) copy-start(bf16[960,1024]{1,0:T(8,128)(2,1)} %param.7) | copy-start | bytes 5898244
  0.0 4.3 %copy-start.9 = (s32[960]{0:T(1024)S(1)}, s32[960]{0:T(1024)}, u32[]{:S(2)}) copy-start(s32[960]{0:T(1024)} %param.9) | copy-start | bytes 11524
  1.3 7.1 %copy-start.6 = (f32[960]{0:T(1024)}, f32[960]{0:T(1024)S(1)}, u32[]{:S(2)}) copy-start(f32[960]{0:T(1024)S(1)} %fusion.23) | copy-start | bytes 11524
  10.1 7.5 %copy-start.11 = (s32[16]{0:T(128)S(1)}, s32[16]{0:T(128)}, u32[]{:S(2)}) copy-start(s32[16]{0:T(128)} %constant.74.clone) | copy-start | bytes 196
  10.1 53.2 %all-to-all-start = ((bf16[16,65,1024]{2,1,0:T(8,128)(2,1)}), bf16[16,65,1024]{2,1,0:T(8,128)(2,1)S(1)}, u32[]{:S(2)}, u32[]{:S(2)}) async-start(bf16[16,65,1024]{2,1,0:T(8,128)(2,1)} %pad_maximum_fusion), calls=%async_computation | async-start | bytes 4718592 | tf_op jit(solution)/shard_map/all_to_all | solution.py:93
  63.4 0.6 copy-start.2
  65.3 31.0 %collective-permute-start.2 = (bf16[528,1024]{1,0:T(8,128)(2,1)S(1)}, bf16[528,1024]{1,0:T(8,128)(2,1)}, u32[]{:S(2)}, u32[]{:S(2)}) collective-permute-start(bf16[528,1024]{1,0:T(8,128)(2,1)S(1)} %pad_maximum_fusion.2), channel_id=1, source_target_pairs={{0,4},{1,5},{4,8},{5,9},{8,12},{9,13},{12,14},{13,15},{14,10},{15,... | collective-permute-start | bytes 3244040 | tf_op jit(solution)/shard_map/ppermute | solution.py:23
  73.1 12.1 %collective-permute-start = (bf16[528,1024]{1,0:T(8,128)(2,1)S(1)}, bf16[528,1024]{1,0:T(8,128)(2,1)}, u32[]{:S(2)}, u32[]{:S(2)}) collective-permute-start(bf16[528,1024]{1,0:T(8,128)(2,1)S(1)} %pad_maximum_fusion.2), channel_id=1, source_target_pairs={{0,1},{4,5},{8,9},{12,13},{14,15},{10,11},{6,7},{2,3},{16,17},{20,... | collective-permute-start | bytes 3244040 | tf_op jit(solution)/shard_map/ppermute | solution.py:23
  79.1 6.1 %collective-permute-start.1 = (bf16[512,1024]{1,0:T(8,128)(2,1)}, bf16[512,1024]{1,0:T(8,128)(2,1)S(1)}, u32[]{:S(2)}, u32[]{:S(2)}) collective-permute-start(bf16[512,1024]{1,0:T(8,128)(2,1)} %bitcast.125), channel_id=1, source_target_pairs={{0,1},{4,5},{8,9},{12,13},{14,15},{10,11},{6,7},{2,3},{16,17},{20,... | collective-permute-start | bytes 3145736 | tf_op jit(solution)/shard_map/ppermute | solution.py:23
  81.2 0.7 copy-start.3
  90.6 5.9 %copy-start.1 = (bf16[8,64,1024]{2,1,0:T(8,128)(2,1)S(1)}, bf16[8,64,1024]{2,1,0:T(8,128)(2,1)}, u32[]{:S(2)}) copy-start(bf16[8,64,1024]{2,1,0:T(8,128)(2,1)} %get-tuple-element.39) | copy-start | bytes 3145732
  96.3 10.1 %collective-permute-start.4 = (bf16[528,1024]{1,0:T(8,128)(2,1)}, bf16[528,1024]{1,0:T(8,128)(2,1)S(1)}, u32[]{:S(2)}, u32[]{:S(2)}) collective-permute-start(bf16[528,1024]{1,0:T(8,128)(2,1)} %collective-permute-done.2), channel_id=1, source_target_pairs={{0,1},{1,0},{4,5},{5,4},{8,9},{9,8},{12,13},{13,12},{14,15},{15,14... | collective-permute-start | bytes 3244040 | tf_op jit(solution)/shard_map/ppermute | solution.py:23
  96.5 28.0 %collective-permute-start.3 = (bf16[512,1024]{1,0:T(8,128)(2,1)S(1)}, bf16[512,1024]{1,0:T(8,128)(2,1)S(1)}, u32[]{:S(2)}, u32[]{:S(2)}) collective-permute-start(bf16[512,1024]{1,0:T(8,128)(2,1)S(1)} %bitcast.126), channel_id=1, source_target_pairs={{0,4},{1,5},{4,8},{5,9},{8,12},{9,13},{12,14},{13,15},{14,10},{15,... | collective-permute-start | bytes 3145736 | tf_op jit(solution)/shard_map/ppermute | solution.py:23
  99.5 29.3 %collective-permute-start.6 = (bf16[1040,1024]{1,0:T(8,128)(2,1)S(1)}, bf16[1040,1024]{1,0:T(8,128)(2,1)S(1)}, u32[]{:S(2)}, u32[]{:S(2)}) collective-permute-start(bf16[1040,1024]{1,0:T(8,128)(2,1)S(1)} %pad_maximum_fusion.1), channel_id=1, source_target_pairs={{0,2},{4,0},{8,4},{12,8},{14,12},{10,14},{6,10},{2,6},{1,1},{5,5},... | collective-permute-start | bytes 6389768 | tf_op jit(solution)/shard_map/ppermute | solution.py:23
  124.5 2.7 %collective-permute-start.5 = (bf16[512,1024]{1,0:T(8,128)(2,1)S(1)}, bf16[512,1024]{1,0:T(8,128)(2,1)S(1)}, u32[]{:S(2)}, u32[]{:S(2)}) collective-permute-start(bf16[512,1024]{1,0:T(8,128)(2,1)S(1)} %collective-permute-done.3), channel_id=1, source_target_pairs={{0,1},{1,0},{4,5},{5,4},{8,9},{9,8},{12,13},{13,12},{14,15},{15,14... | collective-permute-start | bytes 3145736 | tf_op jit(solution)/shard_map/ppermute | solution.py:23
  130.6 7.8 %copy-start.7 = (f32[960]{0:T(1024)S(1)}, f32[960]{0:T(1024)}, u32[]{:S(2)}) copy-start(f32[960]{0:T(1024)} %copy-done.6) | copy-start | bytes 11524
  130.6 14.2 %copy-start.4 = (s32[960]{0:T(1024)S(1)}, s32[960]{0:T(1024)}, u32[]{:S(2)}) copy-start(s32[960]{0:T(1024)} %get-tuple-element.47) | copy-start | bytes 11524
  130.6 14.2 %copy-start.5 = (s32[960]{0:T(1024)S(1)}, s32[960]{0:T(1024)}, u32[]{:S(2)}) copy-start(s32[960]{0:T(1024)} %get-tuple-element.48) | copy-start | bytes 11524
  130.6 15.4 %copy-start.10 = (s32[960]{0:T(1024)S(1)}, s32[960]{0:T(1024)}, u32[]{:S(2)}) copy-start(s32[960]{0:T(1024)} %get-tuple-element.38) | copy-start | bytes 11524
  133.2 11.6 %all-to-all-start.1 = ((f32[16,1,128]{2,1,0:T(1,128)}), f32[16,1,128]{2,1,0:T(1,128)S(1)}, u32[]{:S(2)}, u32[]{:S(2)}) async-start(f32[16,1,128]{2,1,0:T(1,128)} %bitcast.28), calls=%async_computation.1 | async-start | bytes 16384 | tf_op jit(solution)/shard_map/all_to_all | solution.py:161

commit v20 on v18

--- a/solution.py
+++ b/solution.py
@@ -63,11 +63,9 @@
     position = jnp.asarray(dev2pos)[lax.axis_index("blk")]
     odd = (position % 2) == 1
 
-    value_entries = embeddings.astype(jnp.float32)
-    unit = (
-        value_entries
-        * lax.rsqrt(jnp.mean(value_entries * value_entries, axis=1, keepdims=True) + 1e-06)
-    ).astype(jnp.bfloat16)
+    square_sum = jnp.einsum("rf,rf->r", embeddings, embeddings, preferred_element_type=jnp.float32)
+    scale = lax.rsqrt(square_sum * (1.0 / feature_span) + 1e-06)
+    unit = (embeddings.astype(jnp.float32) * scale[:, None]).astype(jnp.bfloat16)
     row_index = jnp.arange(row_count, dtype=jnp.int32)
     earlier = (owners[None, :] == owners[:, None]) & (row_index[None, :] < row_index[:, None])
     arrival = jnp.sum(earlier.astype(jnp.int32), axis=1)

time: 148 us -> 148 us (level)
    dot_general x0 -> x1, other arithmetic: none -> 2 us  [body(): jnp.einsum('rf,rf->r', embeddings, embeddings, preferred_element_type=jnp...]
    reduce_sum x1 -> x0, other arithmetic: 2 us -> none  [body(): jnp.mean(value_entries * value_entries, axis=1, keepdims=True) + 1e-06]
where the time goes in v20:
time: 148 us; the launch traced here: 147 us
  waiting for transfers between devices  64.1 us (43%)
  starting transfers between devices  25.5 us (17%)
  matrix products  23.1 us (16%)
  other arithmetic  12.2 us (8%)
  blocking collectives  11.3 us (8%)
  local copies, waits for them, and re-layouts  7.16 us (5%)
  between operations  3.71 us (3%)
    all_to_all x1, waiting for transfers between devices, body(): lax.all_to_all(payload, 'blk', split_axis=0, concat_axis=0, tiled=True)  41.2 us
    ppermute x7, waiting for transfers between devices, moved(): return lax.ppermute(x, 'blk', [(pos2dev[a], pos2dev[b]) for a, b in moves])  22.9 us
    dot_general x9, matrix products, step_total(): lax.dot_general(local, remote, (((1,), (1,)), ((), ())), preferred_elemen...  18.8 us
    ppermute x7, starting transfers between devices, moved(): return lax.ppermute(x, 'blk', [(pos2dev[a], pos2dev[b]) for a, b in moves])  18 us
    all_to_all x1, blocking collectives, body(): lax.all_to_all(totals, 'blk', split_axis=0, concat_axis=0, tiled=True)  11.3 us
    all_to_all x1, starting transfers between devices, body(): lax.all_to_all(payload, 'blk', split_axis=0, concat_axis=0, tiled=True)  7.52 us
  transfers between devices with their start and end apart: 8, of which 4 were waited for; matrix products, arithmetic and copies ran while one was open for 16% of the time, Pallas kernels for 0%

profile of v20, /device:TPU:0, one launch (start us, length us, event | category | flops | bytes accessed | tf_op | source)
XLA Modules:
  0.0 147.0 jit_solution(3077642067073813217)
XLA Ops:
  0.0 1.3 convert_reduce_fusion
  1.3 0.7 convert.13
  2.0 0.1 copy.76
  2.2 0.1 reshape.377
  2.3 2.0 %fusion.3 = f32[960]{0:T(1024)S(1)} fusion(bf16[960,1024]{1,0:T(8,128)(2,1)} %param.7), kind=kLoop, calls=%fused_computation.8 | loop fusion | flops 2948160 | bytes 1969920 | tf_op jit(solution)/shard_map/rf,rf->r/dot_general | solution.py:66
  4.3 1.3 multiply_add_fusion
  5.6 0.6 select_reduce_fusion
  6.2 0.1 sub.11
  6.3 0.1 pad.20.clone
  6.5 2.6 %fusion.9 = bf16[1024,1024]{1,0:T(8,128)(2,1)S(1)} fusion(bf16[960,1024]{1,0:T(8,128)(2,1)S(1)} %copy-done, f32[960]{0:T(1024)S(1)} %add_rsqrt_fusion, s32[960]{0:T(1024)S(1)} %get-tuple-element.37), kind=kOutput, calls=%fused_computation.35 | convolution fusion | flops 2018246656 | bytes 4070912 | tf_op jit(solution)/shard_map/dot_general | solution.py:75
  9.1 1.7 %pad_maximum_fusion = bf16[16,65,1024]{2,1,0:T(8,128)(2,1)} fusion(bf16[16,1,1024]{2,1,0:T(2,128)(2,1)S(1)} %copy.77, bf16[16,64,1024]{2,1,0:T(8,128)(2,1)S(1)} %bitcast.124), kind=kLoop, calls=%fused_computation.15 | loop fusion | flops 4259840 | bytes 4259840 | tf_op jit(solution)/shard_map/concatenate | solution.py:88
  10.8 7.5 %all-to-all-start = ((bf16[16,65,1024]{2,1,0:T(8,128)(2,1)}), bf16[16,65,1024]{2,1,0:T(8,128)(2,1)S(1)}, u32[]{:S(2)}, u32[]{:S(2)}) async-start(bf16[16,65,1024]{2,1,0:T(8,128)(2,1)} %pad_maximum_fusion), calls=%async_computation | async-start | bytes 4718592 | tf_op jit(solution)/shard_map/all_to_all | solution.py:89
  18.3 0.6 dynamic_slice.9
  22.3 0.5 iota_add_fusion
  22.8 41.2 %all-to-all-done = bf16[16,65,1024]{2,1,0:T(8,128)(2,1)S(1)} async-done(((bf16[16,65,1024]{2,1,0:T(8,128)(2,1)}), bf16[16,65,1024]{2,1,0:T(8,128)(2,1)S(1)}, u32[]{:S(2)}, u32[]{:S(2)}) %all-to-all-start) | async-done | bytes 2129952 | tf_op jit(solution)/shard_map/all_to_all | solution.py:89
  64.1 0.6 copy-done.2
  64.7 1.2 fusion.42
  66.0 7.8 %collective-permute-start.2 = (bf16[528,1024]{1,0:T(8,128)(2,1)S(1)}, bf16[528,1024]{1,0:T(8,128)(2,1)}, u32[]{:S(2)}, u32[]{:S(2)}) collective-permute-start(bf16[528,1024]{1,0:T(8,128)(2,1)S(1)} %pad_maximum_fusion.2), channel_id=1, source_target_pairs={{0,4},{1,5},{4,8},{5,9},{8,12},{9,13},{12,14},{13,15},{14,10},{15,... | collective-permute-start | bytes 3244040 | tf_op jit(solution)/shard_map/ppermute | solution.py:23
  73.8 2.5 %collective-permute-start = (bf16[528,1024]{1,0:T(8,128)(2,1)S(1)}, bf16[528,1024]{1,0:T(8,128)(2,1)}, u32[]{:S(2)}, u32[]{:S(2)}) collective-permute-start(bf16[528,1024]{1,0:T(8,128)(2,1)S(1)} %pad_maximum_fusion.2), channel_id=1, source_target_pairs={{0,1},{4,5},{8,9},{12,13},{14,15},{10,11},{6,7},{2,3},{16,17},{20,... | collective-permute-start | bytes 3244040 | tf_op jit(solution)/shard_map/ppermute | solution.py:23
  76.3 0.1 slice.196
  76.4 0.1 copy.79
  76.5 0.7 constant_dynamic-slice_fusion.1
  77.2 0.8 copy.81
  78.0 0.8 copy.80
  78.8 0.8 copy.83
  79.7 0.1 copy.82
  79.8 1.3 collective-permute-start.1
  81.1 0.7 convert_reduce_fusion.4
  81.8 0.1 convert_reduce_fusion.1
  81.9 0.2 slice.195
  82.1 0.4 copy-done.3
  82.6 3.2 %bitcast_reduce_fusion = f32[1024,8]{0,1:T(8,128)S(1)} fusion(bf16[1024,1024]{1,0:T(8,128)(2,1)S(1)} %bitcast.115, s32[1024]{0:T(1024)S(1)} %copy-done.3, pred[1024]{0:T(1024)(128)(4,1)S(1)} %broadcast_compare_fusion.1), kind=kOutput, calls=%fused_computation.2 | convolution fusion | flops 2155864064 | bytes 2135040 | tf_op jit(solution)/shard_map/dot_general | solution.py:30
  85.8 0.1 fusion.28
  85.9 0.7 slice_convert_fusion.4
  86.6 1.6 %bitcast_reduce_fusion.7 = f32[1024,4]{0,1:T(4,128)S(1)} fusion(bf16[1024,1024]{1,0:T(8,128)(2,1)S(1)} %bitcast.116, bf16[512,1024]{1,0:T(8,128)(2,1)S(1)} %collective-permute-done.1, s32[1024]{0:T(1024)S(1)} %copy-done.3, s32[512]{0:T(512)S(1)} %bitcast.152, pred[1024]{0:T(1024)(128)(4,1)S(1)} %broadcast_compare_fusion.1), kind=kOutput, calls=%fused_computation.23 | convolution fusion | flops 1076359168 | bytes 3169280 | tf_op jit(solution)/shard_map/dot_general | solution.py:30
  88.2 0.1 fusion.35
  88.3 2.9 %bitcast_reduce_fusion.8 = f32[1024,4]{0,1:T(4,128)S(1)} fusion(bf16[1024,1024]{1,0:T(8,128)(2,1)S(1)} %bitcast.117, bf16[528,1024]{1,0:T(8,128)(2,1)} %collective-permute-done, s32[1024]{0:T(1024)S(1)} %copy-done.3, s32[512]{0:T(512)S(1)} %bitcast.151, pred[1024]{0:T(1024)(128)(4,1)S(1)} %broadcast_compare_fusion.1), kind=kOutput, calls=%fused_computation.24 | convolution fusion | flops 1076359168 | bytes 3169280 | tf_op jit(solution)/shard_map/dot_general | solution.py:30
  91.2 0.1 fusion.36
  91.3 5.7 %collective-permute-done.2 = bf16[528,1024]{1,0:T(8,128)(2,1)} collective-permute-done((bf16[528,1024]{1,0:T(8,128)(2,1)S(1)}, bf16[528,1024]{1,0:T(8,128)(2,1)}, u32[]{:S(2)}, u32[]{:S(2)}) %collective-permute-start.2) | collective-permute-done | bytes 1081376 | tf_op jit(solution)/shard_map/ppermute | solution.py:23
  96.9 0.2 pad_maximum_fusion.1
  97.1 3.0 %collective-permute-start.3 = (bf16[512,1024]{1,0:T(8,128)(2,1)S(1)}, bf16[512,1024]{1,0:T(8,128)(2,1)S(1)}, u32[]{:S(2)}, u32[]{:S(2)}) collective-permute-start(bf16[512,1024]{1,0:T(8,128)(2,1)S(1)} %bitcast.126), channel_id=1, source_target_pairs={{0,4},{1,5},{4,8},{5,9},{8,12},{9,13},{12,14},{13,15},{14,10},{15,... | collective-permute-start | bytes 3145736 | tf_op jit(solution)/shard_map/ppermute | solution.py:23
  100.2 3.2 %collective-permute-start.6 = (bf16[1040,1024]{1,0:T(8,128)(2,1)S(1)}, bf16[1040,1024]{1,0:T(8,128)(2,1)S(1)}, u32[]{:S(2)}, u32[]{:S(2)}) collective-permute-start(bf16[1040,1024]{1,0:T(8,128)(2,1)S(1)} %pad_maximum_fusion.1), channel_id=1, source_target_pairs={{0,2},{4,0},{8,4},{12,8},{14,12},{10,14},{6,10},{2,6},{1,1},{5,5},... | collective-permute-start | bytes 6389768 | tf_op jit(solution)/shard_map/ppermute | solution.py:23
  103.4 0.7 slice_convert_fusion.3
  104.1 2.9 %bitcast_reduce_fusion.6 = f32[1024,4]{0,1:T(4,128)S(1)} fusion(bf16[1024,1024]{1,0:T(8,128)(2,1)S(1)} %bitcast.119, bf16[528,1024]{1,0:T(8,128)(2,1)} %collective-permute-done.2, s32[1024]{0:T(1024)S(1)} %copy-done.3, s32[512]{0:T(512)S(1)} %bitcast.153, pred[1024]{0:T(1024)(128)(4,1)S(1)} %broadcast_compare_fusion.1), kind=kOutput, calls=%fused_computation.22 | convolution fusion | flops 1076359168 | bytes 3169280 | tf_op jit(solution)/shard_map/dot_general | solution.py:30
  107.0 0.1 fusion.34
  107.1 1.6 %bitcast_reduce_fusion.5 = f32[1024,4]{0,1:T(4,128)S(1)} fusion(bf16[1024,1024]{1,0:T(8,128)(2,1)S(1)} %bitcast.120, s32[1024]{0:T(1024)S(1)} %copy-done.3, s32[512]{0:T(512)S(1)} %bitcast.146, pred[1024]{0:T(1024)(128)(4,1)S(1)} %broadcast_compare_fusion.1, bf16[528,1024]{1,0:T(8,128)(2,1)S(1)} %collective-permute-done.4), kind=kOutput, calls=%fused_computation.21 | convolution fusion | flops 1076359168 | bytes 3169280 | tf_op jit(solution)/shard_map/dot_general | solution.py:30
  108.8 0.1 fusion.33
  108.8 16.3 %collective-permute-done.3 = bf16[512,1024]{1,0:T(8,128)(2,1)S(1)} collective-permute-done((bf16[512,1024]{1,0:T(8,128)(2,1)S(1)}, bf16[512,1024]{1,0:T(8,128)(2,1)S(1)}, u32[]{:S(2)}, u32[]{:S(2)}) %collective-permute-start.3) | collective-permute-done | bytes 1048608 | tf_op jit(solution)/shard_map/ppermute | solution.py:23
  125.1 1.7 %bitcast_reduce_fusion.4 = f32[1024,4]{0,1:T(4,128)S(1)} fusion(bf16[1024,1024]{1,0:T(8,128)(2,1)S(1)} %bitcast.121, bf16[512,1024]{1,0:T(8,128)(2,1)S(1)} %collective-permute-done.3, s32[1024]{0:T(1024)S(1)} %copy-done.3, s32[512]{0:T(512)S(1)} %bitcast.150, pred[1024]{0:T(1024)(128)(4,1)S(1)} %broadcast_compare_fusion.1), kind=kOutput, calls=%fused_computation.20 | convolution fusion | flops 1076359168 | bytes 3169280 | tf_op jit(solution)/shard_map/dot_general | solution.py:30
  126.8 0.1 fusion.32
  126.9 0.9 collective-permute-done.5
  127.8 1.6 %bitcast_reduce_fusion.3 = f32[1024,4]{0,1:T(4,128)S(1)} fusion(bf16[1024,1024]{1,0:T(8,128)(2,1)S(1)} %bitcast.122, bf16[512,1024]{1,0:T(8,128)(2,1)S(1)} %collective-permute-done.5, s32[1024]{0:T(1024)S(1)} %copy-done.3, s32[512]{0:T(512)S(1)} %bitcast.148, pred[1024]{0:T(1024)(128)(4,1)S(1)} %broadcast_compare_fusion.1), kind=kOutput, calls=%fused_computation.19 | convolution fusion | flops 1076359168 | bytes 3169280 | tf_op jit(solution)/shard_map/dot_general | solution.py:30
  129.4 0.1 fusion.31
  129.5 1.6 %bitcast_reduce_fusion.1 = f32[1024,4]{0,1:T(4,128)S(1)} fusion(bf16[512,1024]{1,0:T(8,128)(2,1)S(1)} %collective-permute-done.5, bf16[1040,1024]{1,0:T(8,128)(2,1)S(1)} %collective-permute-done.6, s32[1024]{0:T(1024)S(1)} %bitcast.132, s32[512]{0:T(512)S(1)} %bitcast.149, pred[1024]{0:T(1024)(128)(4,1)S(1)} %broadcast_compare_fusion), kind=kOutput, calls=%fused_computation.17 | convolution fusion | flops 1076359168 | bytes 3169280 | tf_op jit(solution)/shard_map/dot_general | solution.py:30
  131.2 0.1 fusion.29
  131.3 1.6 %bitcast_reduce_fusion.2 = f32[1024,4]{0,1:T(4,128)S(1)} fusion(bf16[1040,1024]{1,0:T(8,128)(2,1)S(1)} %collective-permute-done.6, s32[1024]{0:T(1024)S(1)} %bitcast.133, s32[512]{0:T(512)S(1)} %bitcast.147, pred[1024]{0:T(1024)(128)(4,1)S(1)} %broadcast_compare_fusion, bf16[528,1024]{1,0:T(8,128)(2,1)S(1)} %collective-permute-done.4), kind=kOutput, calls=%fused_computation.18 | convolution fusion | flops 1076359168 | bytes 3169280 | tf_op jit(solution)/shard_map/dot_general | solution.py:30
  132.9 0.1 fusion.30
  133.0 0.1 stack_reshape.4
  133.1 0.1 select_n.156
  133.2 0.1 reshape.316
  133.3 11.3 %all_to_all.10 = f32[16,1,128]{2,1,0:T(1,128)S(1)} all-to-all(f32[16,1,128]{2,1,0:T(1,128)S(1)} %bitcast.130), channel_id=1, replica_groups=mesh['groups'=2,'blk'=16] {'blk'}, dimensions={0} | all-to-all | bytes 16384 | tf_op jit(solution)/shard_map/all_to_all | solution.py:157
  144.6 1.2 convolution_select_fusion
  145.9 0.6 fusion.21
  146.4 0.6 log1p.3
  (53 shorter events, 0.5 us)
Async XLA Ops:
  0.0 6.5 %copy-start = (bf16[960,1024]{1,0:T(8,128)(2,1)S(1)}, bf16[960,1024]{1,0:T(8,128)(2,1)}, u32[]{:S(2)}) copy-start(bf16[960,1024]{1,0:T(8,128)(2,1)} %param.7) | copy-start | bytes 5898244
  1.3 7.8 %copy-start.6 = (s32[960]{0:T(1024)}, s32[960]{0:T(1024)S(1)}, u32[]{:S(2)}) copy-start(s32[960]{0:T(1024)S(1)} %convert_reduce_fusion) | copy-start | bytes 11524
  10.8 7.5 %copy-start.9 = (s32[16]{0:T(128)S(1)}, s32[16]{0:T(128)}, u32[]{:S(2)}) copy-start(s32[16]{0:T(128)} %constant.73.clone) | copy-start | bytes 196
  10.8 53.2 %all-to-all-start = ((bf16[16,65,1024]{2,1,0:T(8,128)(2,1)}), bf16[16,65,1024]{2,1,0:T(8,128)(2,1)S(1)}, u32[]{:S(2)}, u32[]{:S(2)}) async-start(bf16[16,65,1024]{2,1,0:T(8,128)(2,1)} %pad_maximum_fusion), calls=%async_computation | async-start | bytes 4718592 | tf_op jit(solution)/shard_map/all_to_all | solution.py:89
  64.1 0.6 copy-start.2
  66.0 31.0 %collective-permute-start.2 = (bf16[528,1024]{1,0:T(8,128)(2,1)S(1)}, bf16[528,1024]{1,0:T(8,128)(2,1)}, u32[]{:S(2)}, u32[]{:S(2)}) collective-permute-start(bf16[528,1024]{1,0:T(8,128)(2,1)S(1)} %pad_maximum_fusion.2), channel_id=1, source_target_pairs={{0,4},{1,5},{4,8},{5,9},{8,12},{9,13},{12,14},{13,15},{14,10},{15,... | collective-permute-start | bytes 3244040 | tf_op jit(solution)/shard_map/ppermute | solution.py:23
  73.8 12.1 %collective-permute-start = (bf16[528,1024]{1,0:T(8,128)(2,1)S(1)}, bf16[528,1024]{1,0:T(8,128)(2,1)}, u32[]{:S(2)}, u32[]{:S(2)}) collective-permute-start(bf16[528,1024]{1,0:T(8,128)(2,1)S(1)} %pad_maximum_fusion.2), channel_id=1, source_target_pairs={{0,1},{4,5},{8,9},{12,13},{14,15},{10,11},{6,7},{2,3},{16,17},{20,... | collective-permute-start | bytes 3244040 | tf_op jit(solution)/shard_map/ppermute | solution.py:23
  79.8 6.1 %collective-permute-start.1 = (bf16[512,1024]{1,0:T(8,128)(2,1)}, bf16[512,1024]{1,0:T(8,128)(2,1)S(1)}, u32[]{:S(2)}, u32[]{:S(2)}) collective-permute-start(bf16[512,1024]{1,0:T(8,128)(2,1)} %bitcast.125), channel_id=1, source_target_pairs={{0,1},{4,5},{8,9},{12,13},{14,15},{10,11},{6,7},{2,3},{16,17},{20,... | collective-permute-start | bytes 3145736 | tf_op jit(solution)/shard_map/ppermute | solution.py:23
  81.9 0.7 copy-start.3
  91.3 5.9 %copy-start.1 = (bf16[8,64,1024]{2,1,0:T(8,128)(2,1)S(1)}, bf16[8,64,1024]{2,1,0:T(8,128)(2,1)}, u32[]{:S(2)}) copy-start(bf16[8,64,1024]{2,1,0:T(8,128)(2,1)} %get-tuple-element.39) | copy-start | bytes 3145732
  96.9 10.1 %collective-permute-start.4 = (bf16[528,1024]{1,0:T(8,128)(2,1)}, bf16[528,1024]{1,0:T(8,128)(2,1)S(1)}, u32[]{:S(2)}, u32[]{:S(2)}) collective-permute-start(bf16[528,1024]{1,0:T(8,128)(2,1)} %collective-permute-done.2), channel_id=1, source_target_pairs={{0,1},{1,0},{4,5},{5,4},{8,9},{9,8},{12,13},{13,12},{14,15},{15,14... | collective-permute-start | bytes 3244040 | tf_op jit(solution)/shard_map/ppermute | solution.py:23
  97.1 28.0 %collective-permute-start.3 = (bf16[512,1024]{1,0:T(8,128)(2,1)S(1)}, bf16[512,1024]{1,0:T(8,128)(2,1)S(1)}, u32[]{:S(2)}, u32[]{:S(2)}) collective-permute-start(bf16[512,1024]{1,0:T(8,128)(2,1)S(1)} %bitcast.126), channel_id=1, source_target_pairs={{0,4},{1,5},{4,8},{5,9},{8,12},{9,13},{12,14},{13,15},{14,10},{15,... | collective-permute-start | bytes 3145736 | tf_op jit(solution)/shard_map/ppermute | solution.py:23
  100.2 29.3 %collective-permute-start.6 = (bf16[1040,1024]{1,0:T(8,128)(2,1)S(1)}, bf16[1040,1024]{1,0:T(8,128)(2,1)S(1)}, u32[]{:S(2)}, u32[]{:S(2)}) collective-permute-start(bf16[1040,1024]{1,0:T(8,128)(2,1)S(1)} %pad_maximum_fusion.1), channel_id=1, source_target_pairs={{0,2},{4,0},{8,4},{12,8},{14,12},{10,14},{6,10},{2,6},{1,1},{5,5},... | collective-permute-start | bytes 6389768 | tf_op jit(solution)/shard_map/ppermute | solution.py:23
  125.1 2.7 %collective-permute-start.5 = (bf16[512,1024]{1,0:T(8,128)(2,1)S(1)}, bf16[512,1024]{1,0:T(8,128)(2,1)S(1)}, u32[]{:S(2)}, u32[]{:S(2)}) collective-permute-start(bf16[512,1024]{1,0:T(8,128)(2,1)S(1)} %collective-permute-done.3), channel_id=1, source_target_pairs={{0,1},{1,0},{4,5},{5,4},{8,9},{9,8},{12,13},{13,12},{14,15},{15,14... | collective-permute-start | bytes 3145736 | tf_op jit(solution)/shard_map/ppermute | solution.py:23
  131.3 13.4 %copy-start.4 = (s32[960]{0:T(1024)S(1)}, s32[960]{0:T(1024)}, u32[]{:S(2)}) copy-start(s32[960]{0:T(1024)} %get-tuple-element.47) | copy-start | bytes 11524
  131.3 13.4 %copy-start.5 = (s32[960]{0:T(1024)S(1)}, s32[960]{0:T(1024)}, u32[]{:S(2)}) copy-start(s32[960]{0:T(1024)} %get-tuple-element.48) | copy-start | bytes 11524
  131.3 14.6 %copy-start.7 = (s32[960]{0:T(1024)S(1)}, s32[960]{0:T(1024)}, u32[]{:S(2)}) copy-start(s32[960]{0:T(1024)} %copy-done.6) | copy-start | bytes 11524
  131.3 14.6 %copy-start.8 = (s32[960]{0:T(1024)S(1)}, s32[960]{0:T(1024)}, u32[]{:S(2)}) copy-start(s32[960]{0:T(1024)} %get-tuple-element.38) | copy-start | bytes 11524
